TPU v7x, 128 devices: a whole 4x4x4 slice. The times are simulated.
128 devices in a mesh: az: 16 (over z, y), rg: 8 (over x, core).
Axes of the slice: x: 4, y: 4, z: 4, core: 2. Of those that a mesh axis runs over, the one named last changes fastest.
Arguments:
- master_phasor_raster: bfloat16 [2, 2560, 10240], P(None, ('az', 'rg')), may hold values from -6 to 6
- slave_phasor_raster: bfloat16 [2, 2560, 10240], P(None, ('az', 'rg')), may hold values from -6 to 6
- segment_track_trim: int32 [16, 2], replicated, may hold values from 0 to 16
- segment_slant_trim: int32 [16, 2], replicated, may hold values from 0 to 96
Outputs:
- phase: float32 [512, 2048], P('az', 'rg')
- weight: float32 [512, 2048], P('az', 'rg')
Inputs may be any that keep to these rules, and one draw needn't show every extreme that they name: segment_track_trim rows hold invalid line counts at the start and end of each burst. segment_slant_trim rows hold invalid column counts at the near and far range edge of each burst.
All inputs are finite; a program needn't handle non-finite values.
Results may differ from a plain program's by a relative error of at most 0.0003.
Values may be sent and summed in bfloat16 or wider, within the bound.
No kernel may reach another device: no remote copies, remote signals or barrier semaphores. Data moves between devices by JAX's collectives and lax.ppermute only.
A program may use at most 128 MiB of HBM per device.

v0:
```python
import jax
import jax.numpy as jnp
from jax import lax
from jax.sharding import PartitionSpec as P

LOOK = 5
LEVELS = 6
ITERS = 3
SWEEPS = 4
SEGMENT_HEIGHT = 160
GATHER_LEVEL = 1


OMEGA = 0.6
MU = 0.01


def neighbours(v):
    n_az = lax.axis_size("az")
    n_rg = lax.axis_size("rg")
    above = lax.ppermute(v[..., -1:, :], "az", [(i, i + 1) for i in range(n_az - 1)])
    below = lax.ppermute(v[..., :1, :], "az", [(i + 1, i) for i in range(n_az - 1)])
    left = lax.ppermute(v[..., :, -1:], "rg", [(i, i + 1) for i in range(n_rg - 1)])
    right = lax.ppermute(v[..., :, :1], "rg", [(i + 1, i) for i in range(n_rg - 1)])
    north = jnp.concatenate([above, v[..., :-1, :]], axis=-2)
    south = jnp.concatenate([v[..., 1:, :], below], axis=-2)
    west = jnp.concatenate([left, v[..., :, :-1]], axis=-1)
    east = jnp.concatenate([v[..., :, 1:], right], axis=-1)
    return north, south, west, east


def apply_halo(vector, operators):
    east, west, south, north, diagonal = operators
    v_n, v_s, v_w, v_e = neighbours(vector)
    return diagonal * vector - east * v_e - west * v_w - south * v_s - north * v_n


def apply_padded(vector, operators):
    east, west, south, north, diagonal = operators
    padded = jnp.pad(vector, 1)
    return (diagonal * vector - east * padded[1:-1, 2:] - west * padded[1:-1, :-2]
            - south * padded[2:, 1:-1] - north * padded[:-2, 1:-1])


def mean_multilook(leading, trailing, row_ok, col_ok):
    valid_mask = (row_ok[:, None] & col_ok[None, :]).astype(jnp.float32)
    first_re = leading[0].astype(jnp.float32) * valid_mask
    first_im = leading[1].astype(jnp.float32) * valid_mask
    second_re = trailing[0].astype(jnp.float32) * valid_mask
    second_im = trailing[1].astype(jnp.float32) * valid_mask
    products = jnp.stack(
        [
            first_re * second_re + first_im * second_im,
            first_im * second_re - first_re * second_im,
            first_re * first_re + first_im * first_im,
            second_re * second_re + second_im * second_im,
        ]
    )
    height_rows, width_cols = valid_mask.shape
    span = LOOK * 128
    grouped = products.reshape(4, height_rows, width_cols // span, span)
    cols = jnp.einsum("pikc,cd->pikd", grouped, group_sum(span, LOOK).T, precision=HIGHEST)
    cols = cols.reshape(4, height_rows, width_cols // LOOK)
    return jnp.einsum("ri,pic->prc", group_sum(height_rows, LOOK), cols, precision=HIGHEST)


def edge_terms(left_re, left_im, left_weight, right_re, right_im, right_weight):
    edge_weight = 0.5 * (left_weight + right_weight)
    cross_im = right_im * left_re - right_re * left_im
    power_sum = (
        left_re * left_re + left_im * left_im + right_re * right_re + right_im * right_im + 1.0
    )
    return (edge_weight, 2.0 * cross_im / power_sum)


HIGHEST = lax.Precision.HIGHEST


def group_sum(n, size):
    group = lax.broadcasted_iota(jnp.int32, (n // size, n), 0)
    cell = lax.broadcasted_iota(jnp.int32, (n // size, n), 1)
    return (cell // size == group).astype(jnp.float32)


def pick(n, offset):
    group = lax.broadcasted_iota(jnp.int32, (n // 2, n), 0)
    cell = lax.broadcasted_iota(jnp.int32, (n // 2, n), 1)
    return (cell == 2 * group + offset).astype(jnp.float32)


def sandwich(left, vector, right):
    inner = jnp.dot(left, vector, precision=HIGHEST)
    return jnp.dot(inner, right, precision=HIGHEST)


def restrict_sum(vector):
    rows_now, cols_now = vector.shape
    return sandwich(group_sum(rows_now, 2), vector, group_sum(cols_now, 2).T)


def prolong_copy(vector):
    rows_now, cols_now = vector.shape
    return sandwich(group_sum(2 * rows_now, 2).T, vector, group_sum(2 * cols_now, 2))


def coarsen(east, west, south, north):
    rows_now, cols_now = east.shape
    row_sum = group_sum(rows_now, 2)
    col_sum = group_sum(cols_now, 2).T
    return (
        sandwich(row_sum, east, pick(cols_now, 1).T),
        sandwich(row_sum, west, pick(cols_now, 0).T),
        sandwich(pick(rows_now, 1), south, col_sum),
        sandwich(pick(rows_now, 0), north, col_sum),
    )


def build_levels(east, west, south, north, first_level, last_level):
    levels = {}
    for level in range(first_level, last_level):
        diagonal = east + west + south + north + MU * 4.0**level
        levels[level] = (east, west, south, north, diagonal)
        if level + 1 < LEVELS:
            east, west, south, north = coarsen(east, west, south, north)
    return levels, (east, west, south, north)


def jacobi_sweeps(rhs_vec, operators, apply_fn):
    estimate = OMEGA * rhs_vec / operators[4]
    for sweep_index in range(SWEEPS - 1):
        estimate = estimate + OMEGA * (rhs_vec - apply_fn(estimate, operators)) / operators[4]
    return estimate


def vcycle(rhs_vec, level, levels, apply_fn, stop_fn):
    if level == LEVELS - 1:
        return jacobi_sweeps(rhs_vec, levels[level], apply_fn)
    if stop_fn is not None and level == GATHER_LEVEL:
        return stop_fn(rhs_vec)
    diagonal = levels[level][4]
    estimate = OMEGA * rhs_vec / diagonal
    remain = rhs_vec - apply_fn(estimate, levels[level])
    correction = vcycle(restrict_sum(remain), level + 1, levels, apply_fn, stop_fn)
    estimate = estimate + prolong_copy(correction)
    return estimate + OMEGA * (rhs_vec - apply_fn(estimate, levels[level])) / diagonal


def everyone():
    return lax.axis_size("az") * lax.axis_size("rg")


def gather_strip(blocks):
    n_az = lax.axis_size("az")
    n_rg = lax.axis_size("rg")
    count, h, w = blocks.shape
    sent = jnp.broadcast_to(blocks[None], (n_az, count, h, w))
    got = lax.all_to_all(sent, "az", 0, 0, tiled=True)
    column = got.transpose(1, 0, 2, 3).reshape(count, n_az * h, w)
    left = lax.ppermute(column, "rg", [(i, i + 1) for i in range(n_rg - 1)])
    right = lax.ppermute(column, "rg", [(i + 1, i) for i in range(n_rg - 1)])
    return jnp.concatenate([left, column, right], axis=-1)


def shifted(values, axis):
    pad = [(0, 0)] * values.ndim
    pad[axis] = (1, 0)
    return lax.slice_in_dim(jnp.pad(values, pad), 0, values.shape[axis], axis=axis)


def total(values):
    n = everyone()
    sent = jnp.broadcast_to(values[None], (n, values.shape[0]))
    got = lax.all_to_all(sent, ("az", "rg"), 0, 0, tiled=True)
    return jnp.sum(got, axis=0)


def local(master_phasor_raster, slave_phasor_raster, segment_track_trim, segment_slant_trim):
    n_az = lax.axis_size("az")
    n_range = lax.axis_size("rg")
    segment_ordinal = lax.axis_index("az")
    range_index = lax.axis_index("rg")
    track_trim_width = lax.dynamic_index_in_dim(
        segment_track_trim, segment_ordinal, 0, keepdims=False
    )
    slant_trim_width = lax.dynamic_index_in_dim(
        segment_slant_trim, segment_ordinal, 0, keepdims=False
    )
    lines_here = master_phasor_raster.shape[1]
    slant_sample_total = master_phasor_raster.shape[2]
    along_track_position = range_index * lines_here + jnp.arange(lines_here, dtype=jnp.int32)
    column_index = jnp.arange(slant_sample_total, dtype=jnp.int32)
    row_ok = (along_track_position >= track_trim_width[0]) & (
        along_track_position < SEGMENT_HEIGHT - track_trim_width[1]
    )
    col_ok = (column_index >= slant_trim_width[0]) & (
        column_index < slant_sample_total - slant_trim_width[1]
    )
    pixel_totals = mean_multilook(master_phasor_raster, slave_phasor_raster, row_ok, col_ok)
    look_re, look_im, power_one, power_two = (
        pixel_totals[0],
        pixel_totals[1],
        pixel_totals[2],
        pixel_totals[3],
    )
    weight = 0.05 + 4.0 * (look_re * look_re + look_im * look_im) / jnp.maximum(
        power_one * power_two, 1.0
    )
    fields = jnp.stack([look_re, look_im, weight])
    n_fields, rows_here, cols_all = fields.shape
    cols_here = cols_all // n_range
    fields = fields.reshape(n_fields, rows_here, n_range, cols_here).transpose(2, 0, 1, 3)
    fields = lax.all_to_all(fields, "rg", 0, 0, tiled=True)
    fields = fields.transpose(1, 0, 2, 3).reshape(n_fields, n_range * rows_here, cols_here)
    weight = fields[2]
    shard_height_total = n_range * rows_here

    f_n, f_s, f_w, f_e = neighbours(fields)
    edge_h, grad_h = edge_terms(fields[0], fields[1], fields[2], f_e[0], f_e[1], f_e[2])
    col_global = range_index * cols_here + jnp.arange(cols_here, dtype=jnp.int32)
    keep_h = (col_global <= cols_here * n_range - 2).astype(jnp.float32)
    edge_h = edge_h * keep_h[None, :]
    edge_v, grad_v = edge_terms(fields[0], fields[1], fields[2], f_s[0], f_s[1], f_s[2])
    row_global = segment_ordinal * shard_height_total + jnp.arange(shard_height_total, dtype=jnp.int32)
    keep_v = (row_global <= shard_height_total * n_az - 2).astype(jnp.float32)
    edge_v = edge_v * keep_v[:, None]
    flux_h = edge_h * grad_h
    flux_v = edge_v * grad_v
    e_n, _, e_w, _ = neighbours(jnp.stack([edge_h, flux_h, edge_v, flux_v]))
    west_edge, flux_w, north_edge, flux_n = e_w[0], e_w[1], e_n[2], e_n[3]
    rhs = -(flux_h - flux_w + flux_v - flux_n)

    levels, coarse_edges = build_levels(edge_h, west_edge, south=edge_v, north=north_edge,
                                        first_level=0, last_level=GATHER_LEVEL)
    block_h, block_w = coarse_edges[0].shape
    whole = {}

    def coarse_solve(rhs_vec):
        if not whole:
            got = gather_strip(jnp.stack([coarse_edges[0], coarse_edges[2], rhs_vec]))
            east_s, south_s = got[0], got[1]
            whole["levels"] = build_levels(east_s, shifted(east_s, 1), south_s, shifted(south_s, 0),
                                           GATHER_LEVEL, LEVELS)[0]
            strip_rhs = got[2]
        else:
            strip_rhs = gather_strip(rhs_vec[None])[0]
        strip_x = vcycle(strip_rhs, GATHER_LEVEL, whole["levels"], apply_padded, None)
        return lax.dynamic_slice(strip_x, (segment_ordinal * block_h, block_w), (block_h, block_w))

    def precondition(vector):
        return vcycle(vector, 0, levels, apply_halo, coarse_solve)

    solution = jnp.zeros_like(rhs)
    residual = rhs
    precond = precondition(residual)
    direction = precond
    image_vec = apply_halo(direction, levels[0])
    sums = total(jnp.stack([jnp.sum(residual * precond), jnp.sum(direction * image_vec)]))
    norm_now = sums[0]
    curvature = sums[1]
    for step_index in range(ITERS):
        step_length = norm_now / curvature
        solution = solution + step_length * direction
        if step_index + 1 < ITERS:
            residual = residual - step_length * image_vec
            precond = precondition(residual)
            image_z = apply_halo(precond, levels[0])
            sums = total(jnp.stack([jnp.sum(residual * precond), jnp.sum(precond * image_z),
                                    jnp.sum(precond * image_vec)]))
            norm_next = sums[0]
            ratio = norm_next / norm_now
            direction = precond + ratio * direction
            image_vec = image_z + ratio * image_vec
            curvature = sums[1] + 2.0 * ratio * sums[2] + ratio * ratio * curvature
            norm_now = norm_next
    return (solution, weight)


def solution(mesh):
    return jax.shard_map(
        local,
        mesh=mesh,
        in_specs=(P(None, ("az", "rg"), None), P(None, ("az", "rg"), None), P(), P()),
        out_specs=(P("az", "rg"), P("az", "rg")),
        check_vma=False,
    )
```

profile of v0, /device:TPU:1, one launch (start us, length us, event | category | flops | bytes accessed | tf_op | source)
XLA Modules:
  0.0 344.6 jit_solution(3004726579563990975)
XLA Ops:
  5.1 14.6 %add_reduce_fusion.2 = (f32[20,10240]{1,0:T(8,128)S(1)}, f32[20,10240]{1,0:T(8,128)S(1)}, f32[20,10240]{1,0:T(8,128)S(1)}, f32[20,10240]{1,0:T(8,128)S(1)}) fusion(bf16[2,20,10240]{2,0,1:T(2,128)(2,1)} %param.4, pred[10240]{0:T(1024)(128)(4,1)S(1)} %fusion.309, pred[20]{0:T(512)(128)(4,1)S(1)} %compare_and_fusion.8, bf16[2,20,10240]{2,0,1:T(2,128)(2,1)} %param.5), kind=kLoop, calls=%fused_computation.34 | loop fusion | flops 4300800 | bytes 4925460 | tf_op jit(solution)/shard_map/add | solution.py:53
  24.2 5.8 %all-to-all-start = ((f32[8,3,4,256]{3,2,1,0:T(4,128)}), f32[8,3,4,256]{3,2,1,0:T(4,128)S(1)}, u32[]{:S(2)}, u32[]{:S(2)}) async-start(f32[8,3,4,256]{3,2,1,0:T(4,128)} %maximum_bitcast_fusion.2), calls=%async_computation | async-start | bytes 196608 | tf_op jit(solution)/shard_map/all_to_all | solution.py:212
  30.3 4.7 %all-to-all-done = f32[8,3,4,256]{3,2,1,0:T(4,128)S(1)} async-done(((f32[8,3,4,256]{3,2,1,0:T(4,128)}), f32[8,3,4,256]{3,2,1,0:T(4,128)S(1)}, u32[]{:S(2)}, u32[]{:S(2)}) %all-to-all-start) | async-done | bytes 98336 | tf_op jit(solution)/shard_map/all_to_all | solution.py:212
  41.9 4.0 %collective-permute-start.3 = (f32[4,1,256]{2,1,0:T(1,128)S(1)}, f32[4,1,256]{2,1,0:T(1,128)S(1)}, u32[]{:S(2)}, u32[]{:S(2)}) collective-permute-start(f32[4,1,256]{2,1,0:T(1,128)S(1)} %pad_maximum_fusion.8), channel_id=1, source_target_pairs={{0,8},{8,16},{16,24},{24,32},{32,40},{40,48},{48,56},{56,64},{64,7... | collective-permute-start | bytes 12296 | tf_op jit(solution)/shard_map/ppermute | solution.py:21
  54.2 4.5 %collective-permute-start.5 = (f32[32,1]{1,0:T(8,128)S(1)}, f32[32,1]{1,0:T(8,128)S(1)}, u32[]{:S(2)}, u32[]{:S(2)}) collective-permute-start(f32[32,1]{1,0:T(8,128)S(1)} %get-tuple-element.117), channel_id=1, source_target_pairs={{0,1},{1,2},{2,3},{3,4},{4,5},{5,6},{6,7},{8,9},{9,10},{10,11},{11... | collective-permute-start | bytes 392 | tf_op jit(solution)/shard_map/ppermute | solution.py:23
  65.1 10.6 %all-to-all-start.1 = ((f32[16,3,16,128]{3,2,1,0:T(8,128)}), f32[16,3,16,128]{3,2,1,0:T(8,128)S(1)}, u32[]{:S(2)}, u32[]{:S(2)}) async-start(f32[16,3,16,128]{3,2,1,0:T(8,128)} %broadcast_in_dim.12), calls=%async_computation.1 | async-start | bytes 786432 | tf_op jit(solution)/shard_map/all_to_all | solution.py:157
  75.8 9.1 %all-to-all-done.1 = f32[16,3,16,128]{3,2,1,0:T(8,128)S(1)} async-done(((f32[16,3,16,128]{3,2,1,0:T(8,128)}), f32[16,3,16,128]{3,2,1,0:T(8,128)S(1)}, u32[]{:S(2)}, u32[]{:S(2)}) %all-to-all-start.1) | async-done | bytes 393248 | tf_op jit(solution)/shard_map/all_to_all | solution.py:157
  86.8 4.2 %collective-permute-start.8 = (f32[3,256,128]{2,1,0:T(8,128)S(1)}, f32[3,256,128]{2,1,0:T(8,128)S(1)}, u32[]{:S(2)}, u32[]{:S(2)}) collective-permute-start(f32[3,256,128]{2,1,0:T(8,128)S(1)} %bitcast.325), channel_id=1, source_target_pairs={{0,1},{1,2},{2,3},{3,4},{4,5},{5,6},{6,7},{8,9},{9,10},{10,11},{11... | collective-permute-start | bytes 1179656 | tf_op jit(solution)/shard_map/ppermute | solution.py:159
  112.7 4.7 %collective-permute-start.11 = (f32[32,1]{1,0:T(8,128)S(1)}, f32[32,1]{1,0:T(8,128)S(1)}, u32[]{:S(2)}, u32[]{:S(2)}) collective-permute-start(f32[32,1]{1,0:T(8,128)S(1)} %get-tuple-element.109), channel_id=1, source_target_pairs={{0,1},{1,2},{2,3},{3,4},{4,5},{5,6},{6,7},{8,9},{9,10},{10,11},{11... | collective-permute-start | bytes 392 | tf_op jit(solution)/shard_map/ppermute | solution.py:23
  124.0 4.9 %collective-permute-start.17 = (f32[1,256]{1,0:T(1,128)S(1)}, f32[1,256]{1,0:T(1,128)S(1)}, u32[]{:S(2)}, u32[]{:S(2)}) collective-permute-start(f32[1,256]{1,0:T(1,128)S(1)} %get-tuple-element.104), channel_id=1, source_target_pairs={{0,8},{8,16},{16,24},{24,32},{32,40},{40,48},{48,56},{56,64},{64,7... | collective-permute-start | bytes 3080 | tf_op jit(solution)/shard_map/ppermute | solution.py:21
  130.8 3.6 %collective-permute-start.15 = (f32[32,1]{1,0:T(8,128)S(1)}, f32[32,1]{1,0:T(8,128)S(1)}, u32[]{:S(2)}, u32[]{:S(2)}) collective-permute-start(f32[32,1]{1,0:T(8,128)S(1)} %get-tuple-element.100), channel_id=1, source_target_pairs={{0,1},{1,2},{2,3},{3,4},{4,5},{5,6},{6,7},{8,9},{9,10},{10,11},{11... | collective-permute-start | bytes 392 | tf_op jit(solution)/shard_map/ppermute | solution.py:23
  137.5 19.5 %all_to_all.38 = f32[128,1,2]{2,1,0:T(1,128)S(1)} all-to-all(f32[128,1,2]{2,1,0:T(1,128)S(1)} %broadcast_in_dim.13), channel_id=1, replica_groups=mesh['az'=16,'rg'=8] {'az','rg'}, dimensions={0} | all-to-all | bytes 2048 | tf_op jit(solution)/shard_map/all_to_all | solution.py:173
  171.2 13.4 %all_to_all.39 = f32[16,1,16,128]{3,2,1,0:T(8,128)S(1)} all-to-all(f32[16,1,16,128]{3,2,1,0:T(8,128)S(1)} %broadcast_in_dim.14), channel_id=1, replica_groups=mesh['az'=16,'rg'=8] {'az'}, dimensions={0} | all-to-all | bytes 262144 | tf_op jit(solution)/shard_map/all_to_all | solution.py:157
  186.5 3.9 %collective-permute-start.22 = (f32[1,256,128]{2,1,0:T(8,128)S(1)}, f32[1,256,128]{2,1,0:T(8,128)S(1)}, u32[]{:S(2)}, u32[]{:S(2)}) collective-permute-start(f32[1,256,128]{2,1,0:T(8,128)S(1)} %bitcast.316), channel_id=1, source_target_pairs={{0,1},{1,2},{2,3},{3,4},{4,5},{5,6},{6,7},{8,9},{9,10},{10,11},{11... | collective-permute-start | bytes 393224 | tf_op jit(solution)/shard_map/ppermute | solution.py:159
  202.1 4.6 %collective-permute-start.25 = (f32[32,1]{1,0:T(8,128)S(1)}, f32[32,1]{1,0:T(8,128)S(1)}, u32[]{:S(2)}, u32[]{:S(2)}) collective-permute-start(f32[32,1]{1,0:T(8,128)S(1)} %get-tuple-element.85), channel_id=1, source_target_pairs={{0,1},{1,2},{2,3},{3,4},{4,5},{5,6},{6,7},{8,9},{9,10},{10,11},{11... | collective-permute-start | bytes 392 | tf_op jit(solution)/shard_map/ppermute | solution.py:23
  213.3 4.9 %collective-permute-start.31 = (f32[1,256]{1,0:T(1,128)S(1)}, f32[1,256]{1,0:T(1,128)S(1)}, u32[]{:S(2)}, u32[]{:S(2)}) collective-permute-start(f32[1,256]{1,0:T(1,128)S(1)} %get-tuple-element.80), channel_id=1, source_target_pairs={{0,8},{8,16},{16,24},{24,32},{32,40},{40,48},{48,56},{56,64},{64,7... | collective-permute-start | bytes 3080 | tf_op jit(solution)/shard_map/ppermute | solution.py:21
  220.1 3.6 %collective-permute-start.29 = (f32[32,1]{1,0:T(8,128)S(1)}, f32[32,1]{1,0:T(8,128)S(1)}, u32[]{:S(2)}, u32[]{:S(2)}) collective-permute-start(f32[32,1]{1,0:T(8,128)S(1)} %get-tuple-element.76), channel_id=1, source_target_pairs={{0,1},{1,2},{2,3},{3,4},{4,5},{5,6},{6,7},{8,9},{9,10},{10,11},{11... | collective-permute-start | bytes 392 | tf_op jit(solution)/shard_map/ppermute | solution.py:23
  227.4 19.8 %all_to_all.40 = f32[128,1,3]{2,1,0:T(1,128)S(1)} all-to-all(f32[128,1,3]{2,1,0:T(1,128)S(1)} %broadcast_in_dim.15), channel_id=1, replica_groups=mesh['az'=16,'rg'=8] {'az','rg'}, dimensions={0} | all-to-all | bytes 3072 | tf_op jit(solution)/shard_map/all_to_all | solution.py:173
  264.0 13.4 %all_to_all.41 = f32[16,1,16,128]{3,2,1,0:T(8,128)S(1)} all-to-all(f32[16,1,16,128]{3,2,1,0:T(8,128)S(1)} %broadcast_in_dim.16), channel_id=1, replica_groups=mesh['az'=16,'rg'=8] {'az'}, dimensions={0} | all-to-all | bytes 262144 | tf_op jit(solution)/shard_map/all_to_all | solution.py:157
  279.3 3.6 %collective-permute-start.36 = (f32[1,256,128]{2,1,0:T(8,128)S(1)}, f32[1,256,128]{2,1,0:T(8,128)S(1)}, u32[]{:S(2)}, u32[]{:S(2)}) collective-permute-start(f32[1,256,128]{2,1,0:T(8,128)S(1)} %bitcast.310), channel_id=1, source_target_pairs={{0,1},{1,2},{2,3},{3,4},{4,5},{5,6},{6,7},{8,9},{9,10},{10,11},{11... | collective-permute-start | bytes 393224 | tf_op jit(solution)/shard_map/ppermute | solution.py:159
  294.9 4.6 %collective-permute-start.39 = (f32[32,1]{1,0:T(8,128)S(1)}, f32[32,1]{1,0:T(8,128)S(1)}, u32[]{:S(2)}, u32[]{:S(2)}) collective-permute-start(f32[32,1]{1,0:T(8,128)S(1)} %get-tuple-element.61), channel_id=1, source_target_pairs={{0,1},{1,2},{2,3},{3,4},{4,5},{5,6},{6,7},{8,9},{9,10},{10,11},{11... | collective-permute-start | bytes 392 | tf_op jit(solution)/shard_map/ppermute | solution.py:23
  306.1 4.9 %collective-permute-start.45 = (f32[1,256]{1,0:T(1,128)S(1)}, f32[1,256]{1,0:T(1,128)S(1)}, u32[]{:S(2)}, u32[]{:S(2)}) collective-permute-start(f32[1,256]{1,0:T(1,128)S(1)} %get-tuple-element.56), channel_id=1, source_target_pairs={{0,8},{8,16},{16,24},{24,32},{32,40},{40,48},{48,56},{56,64},{64,7... | collective-permute-start | bytes 3080 | tf_op jit(solution)/shard_map/ppermute | solution.py:21
  312.9 3.6 %collective-permute-start.43 = (f32[32,1]{1,0:T(8,128)S(1)}, f32[32,1]{1,0:T(8,128)S(1)}, u32[]{:S(2)}, u32[]{:S(2)}) collective-permute-start(f32[32,1]{1,0:T(8,128)S(1)} %get-tuple-element.52), channel_id=1, source_target_pairs={{0,1},{1,2},{2,3},{3,4},{4,5},{5,6},{6,7},{8,9},{9,10},{10,11},{11... | collective-permute-start | bytes 392 | tf_op jit(solution)/shard_map/ppermute | solution.py:23
  320.2 19.8 %all_to_all.42 = f32[128,1,3]{2,1,0:T(1,128)S(1)} all-to-all(f32[128,1,3]{2,1,0:T(1,128)S(1)} %broadcast_in_dim.17), channel_id=1, replica_groups=mesh['az'=16,'rg'=8] {'az','rg'}, dimensions={0} | all-to-all | bytes 3072 | tf_op jit(solution)/shard_map/all_to_all | solution.py:173
  (334 shorter events, 142.5 us)
Async XLA Ops:
  24.2 10.8 %all-to-all-start = ((f32[8,3,4,256]{3,2,1,0:T(4,128)}), f32[8,3,4,256]{3,2,1,0:T(4,128)S(1)}, u32[]{:S(2)}, u32[]{:S(2)}) async-start(f32[8,3,4,256]{3,2,1,0:T(4,128)} %maximum_bitcast_fusion.2), calls=%async_computation | async-start | bytes 196608 | tf_op jit(solution)/shard_map/all_to_all | solution.py:212
  41.9 7.6 %collective-permute-start.3 = (f32[4,1,256]{2,1,0:T(1,128)S(1)}, f32[4,1,256]{2,1,0:T(1,128)S(1)}, u32[]{:S(2)}, u32[]{:S(2)}) collective-permute-start(f32[4,1,256]{2,1,0:T(1,128)S(1)} %pad_maximum_fusion.8), channel_id=1, source_target_pairs={{0,8},{8,16},{16,24},{24,32},{32,40},{40,48},{48,56},{56,64},{64,7... | collective-permute-start | bytes 12296 | tf_op jit(solution)/shard_map/ppermute | solution.py:21
  49.7 14.1 %collective-permute-start.7 = (f32[1,256]{1,0:T(1,128)S(1)}, f32[1,256]{1,0:T(1,128)S(1)}, u32[]{:S(2)}, u32[]{:S(2)}) collective-permute-start(f32[1,256]{1,0:T(1,128)S(1)} %get-tuple-element.113), channel_id=1, source_target_pairs={{0,8},{8,16},{16,24},{24,32},{32,40},{40,48},{48,56},{56,64},{64,7... | collective-permute-start | bytes 3080 | tf_op jit(solution)/shard_map/ppermute | solution.py:21
  52.9 10.9 %collective-permute-start.6 = (f32[1,256]{1,0:T(1,128)S(1)}, f32[1,256]{1,0:T(1,128)S(1)}, u32[]{:S(2)}, u32[]{:S(2)}) collective-permute-start(f32[1,256]{1,0:T(1,128)S(1)} %get-tuple-element.114), channel_id=1, source_target_pairs={{8,0},{16,8},{24,16},{32,24},{40,32},{48,40},{56,48},{64,56},{72,6... | collective-permute-start | bytes 3080 | tf_op jit(solution)/shard_map/ppermute | solution.py:22
  54.2 7.2 %collective-permute-start.5 = (f32[32,1]{1,0:T(8,128)S(1)}, f32[32,1]{1,0:T(8,128)S(1)}, u32[]{:S(2)}, u32[]{:S(2)}) collective-permute-start(f32[32,1]{1,0:T(8,128)S(1)} %get-tuple-element.117), channel_id=1, source_target_pairs={{0,1},{1,2},{2,3},{3,4},{4,5},{5,6},{6,7},{8,9},{9,10},{10,11},{11... | collective-permute-start | bytes 392 | tf_op jit(solution)/shard_map/ppermute | solution.py:23
  65.1 19.7 %all-to-all-start.1 = ((f32[16,3,16,128]{3,2,1,0:T(8,128)}), f32[16,3,16,128]{3,2,1,0:T(8,128)S(1)}, u32[]{:S(2)}, u32[]{:S(2)}) async-start(f32[16,3,16,128]{3,2,1,0:T(8,128)} %broadcast_in_dim.12), calls=%async_computation.1 | async-start | bytes 786432 | tf_op jit(solution)/shard_map/all_to_all | solution.py:157
  84.9 9.5 %collective-permute-start.9 = (f32[3,256,128]{2,1,0:T(8,128)S(1)}, f32[3,256,128]{2,1,0:T(8,128)S(1)}, u32[]{:S(2)}, u32[]{:S(2)}) collective-permute-start(f32[3,256,128]{2,1,0:T(8,128)S(1)} %bitcast.324), channel_id=1, source_target_pairs={{1,0},{2,1},{3,2},{4,3},{5,4},{6,5},{7,6},{9,8},{10,9},{11,10},{12... | collective-permute-start | bytes 1179656 | tf_op jit(solution)/shard_map/ppermute | solution.py:160
  86.8 8.7 %collective-permute-start.8 = (f32[3,256,128]{2,1,0:T(8,128)S(1)}, f32[3,256,128]{2,1,0:T(8,128)S(1)}, u32[]{:S(2)}, u32[]{:S(2)}) collective-permute-start(f32[3,256,128]{2,1,0:T(8,128)S(1)} %bitcast.325), channel_id=1, source_target_pairs={{0,1},{1,2},{2,3},{3,4},{4,5},{5,6},{6,7},{8,9},{9,10},{10,11},{11... | collective-permute-start | bytes 1179656 | tf_op jit(solution)/shard_map/ppermute | solution.py:159
  109.2 13.2 %collective-permute-start.13 = (f32[1,256]{1,0:T(1,128)S(1)}, f32[1,256]{1,0:T(1,128)S(1)}, u32[]{:S(2)}, u32[]{:S(2)}) collective-permute-start(f32[1,256]{1,0:T(1,128)S(1)} %get-tuple-element.105), channel_id=1, source_target_pairs={{0,8},{8,16},{16,24},{24,32},{32,40},{40,48},{48,56},{56,64},{64,7... | collective-permute-start | bytes 3080 | tf_op jit(solution)/shard_map/ppermute | solution.py:21
  111.4 11.0 %collective-permute-start.12 = (f32[1,256]{1,0:T(1,128)S(1)}, f32[1,256]{1,0:T(1,128)S(1)}, u32[]{:S(2)}, u32[]{:S(2)}) collective-permute-start(f32[1,256]{1,0:T(1,128)S(1)} %get-tuple-element.106), channel_id=1, source_target_pairs={{8,0},{16,8},{24,16},{32,24},{40,32},{48,40},{56,48},{64,56},{72,6... | collective-permute-start | bytes 3080 | tf_op jit(solution)/shard_map/ppermute | solution.py:22
  122.7 12.6 %collective-permute-start.16 = (f32[1,256]{1,0:T(1,128)S(1)}, f32[1,256]{1,0:T(1,128)S(1)}, u32[]{:S(2)}, u32[]{:S(2)}) collective-permute-start(f32[1,256]{1,0:T(1,128)S(1)} %get-tuple-element.103), channel_id=1, source_target_pairs={{8,0},{16,8},{24,16},{32,24},{40,32},{48,40},{56,48},{64,56},{72,6... | collective-permute-start | bytes 3080 | tf_op jit(solution)/shard_map/ppermute | solution.py:22
  124.0 11.3 %collective-permute-start.17 = (f32[1,256]{1,0:T(1,128)S(1)}, f32[1,256]{1,0:T(1,128)S(1)}, u32[]{:S(2)}, u32[]{:S(2)}) collective-permute-start(f32[1,256]{1,0:T(1,128)S(1)} %get-tuple-element.104), channel_id=1, source_target_pairs={{0,8},{8,16},{16,24},{24,32},{32,40},{40,48},{48,56},{56,64},{64,7... | collective-permute-start | bytes 3080 | tf_op jit(solution)/shard_map/ppermute | solution.py:21
  159.1 11.6 %collective-permute-start.21 = (f32[1,256]{1,0:T(1,128)S(1)}, f32[1,256]{1,0:T(1,128)S(1)}, u32[]{:S(2)}, u32[]{:S(2)}) collective-permute-start(f32[1,256]{1,0:T(1,128)S(1)} %get-tuple-element.89), channel_id=1, source_target_pairs={{0,8},{8,16},{16,24},{24,32},{32,40},{40,48},{48,56},{56,64},{64,7... | collective-permute-start | bytes 3080 | tf_op jit(solution)/shard_map/ppermute | solution.py:21
  161.4 9.4 %collective-permute-start.20 = (f32[1,256]{1,0:T(1,128)S(1)}, f32[1,256]{1,0:T(1,128)S(1)}, u32[]{:S(2)}, u32[]{:S(2)}) collective-permute-start(f32[1,256]{1,0:T(1,128)S(1)} %get-tuple-element.90), channel_id=1, source_target_pairs={{8,0},{16,8},{24,16},{32,24},{40,32},{48,40},{56,48},{64,56},{72,6... | collective-permute-start | bytes 3080 | tf_op jit(solution)/shard_map/ppermute | solution.py:22
  198.6 13.2 %collective-permute-start.27 = (f32[1,256]{1,0:T(1,128)S(1)}, f32[1,256]{1,0:T(1,128)S(1)}, u32[]{:S(2)}, u32[]{:S(2)}) collective-permute-start(f32[1,256]{1,0:T(1,128)S(1)} %get-tuple-element.81), channel_id=1, source_target_pairs={{0,8},{8,16},{16,24},{24,32},{32,40},{40,48},{48,56},{56,64},{64,7... | collective-permute-start | bytes 3080 | tf_op jit(solution)/shard_map/ppermute | solution.py:21
  200.8 11.0 %collective-permute-start.26 = (f32[1,256]{1,0:T(1,128)S(1)}, f32[1,256]{1,0:T(1,128)S(1)}, u32[]{:S(2)}, u32[]{:S(2)}) collective-permute-start(f32[1,256]{1,0:T(1,128)S(1)} %get-tuple-element.82), channel_id=1, source_target_pairs={{8,0},{16,8},{24,16},{32,24},{40,32},{48,40},{56,48},{64,56},{72,6... | collective-permute-start | bytes 3080 | tf_op jit(solution)/shard_map/ppermute | solution.py:22
  212.0 12.6 %collective-permute-start.30 = (f32[1,256]{1,0:T(1,128)S(1)}, f32[1,256]{1,0:T(1,128)S(1)}, u32[]{:S(2)}, u32[]{:S(2)}) collective-permute-start(f32[1,256]{1,0:T(1,128)S(1)} %get-tuple-element.79), channel_id=1, source_target_pairs={{8,0},{16,8},{24,16},{32,24},{40,32},{48,40},{56,48},{64,56},{72,6... | collective-permute-start | bytes 3080 | tf_op jit(solution)/shard_map/ppermute | solution.py:22
  213.3 11.3 %collective-permute-start.31 = (f32[1,256]{1,0:T(1,128)S(1)}, f32[1,256]{1,0:T(1,128)S(1)}, u32[]{:S(2)}, u32[]{:S(2)}) collective-permute-start(f32[1,256]{1,0:T(1,128)S(1)} %get-tuple-element.80), channel_id=1, source_target_pairs={{0,8},{8,16},{16,24},{24,32},{32,40},{40,48},{48,56},{56,64},{64,7... | collective-permute-start | bytes 3080 | tf_op jit(solution)/shard_map/ppermute | solution.py:21
  252.0 11.6 %collective-permute-start.35 = (f32[1,256]{1,0:T(1,128)S(1)}, f32[1,256]{1,0:T(1,128)S(1)}, u32[]{:S(2)}, u32[]{:S(2)}) collective-permute-start(f32[1,256]{1,0:T(1,128)S(1)} %get-tuple-element.65), channel_id=1, source_target_pairs={{0,8},{8,16},{16,24},{24,32},{32,40},{40,48},{48,56},{56,64},{64,7... | collective-permute-start | bytes 3080 | tf_op jit(solution)/shard_map/ppermute | solution.py:21
  254.2 9.4 %collective-permute-start.34 = (f32[1,256]{1,0:T(1,128)S(1)}, f32[1,256]{1,0:T(1,128)S(1)}, u32[]{:S(2)}, u32[]{:S(2)}) collective-permute-start(f32[1,256]{1,0:T(1,128)S(1)} %get-tuple-element.66), channel_id=1, source_target_pairs={{8,0},{16,8},{24,16},{32,24},{40,32},{48,40},{56,48},{64,56},{72,6... | collective-permute-start | bytes 3080 | tf_op jit(solution)/shard_map/ppermute | solution.py:22
  291.4 13.2 %collective-permute-start.41 = (f32[1,256]{1,0:T(1,128)S(1)}, f32[1,256]{1,0:T(1,128)S(1)}, u32[]{:S(2)}, u32[]{:S(2)}) collective-permute-start(f32[1,256]{1,0:T(1,128)S(1)} %get-tuple-element.57), channel_id=1, source_target_pairs={{0,8},{8,16},{16,24},{24,32},{32,40},{40,48},{48,56},{56,64},{64,7... | collective-permute-start | bytes 3080 | tf_op jit(solution)/shard_map/ppermute | solution.py:21
  293.6 11.0 %collective-permute-start.40 = (f32[1,256]{1,0:T(1,128)S(1)}, f32[1,256]{1,0:T(1,128)S(1)}, u32[]{:S(2)}, u32[]{:S(2)}) collective-permute-start(f32[1,256]{1,0:T(1,128)S(1)} %get-tuple-element.58), channel_id=1, source_target_pairs={{8,0},{16,8},{24,16},{32,24},{40,32},{48,40},{56,48},{64,56},{72,6... | collective-permute-start | bytes 3080 | tf_op jit(solution)/shard_map/ppermute | solution.py:22
  304.8 12.6 %collective-permute-start.44 = (f32[1,256]{1,0:T(1,128)S(1)}, f32[1,256]{1,0:T(1,128)S(1)}, u32[]{:S(2)}, u32[]{:S(2)}) collective-permute-start(f32[1,256]{1,0:T(1,128)S(1)} %get-tuple-element.55), channel_id=1, source_target_pairs={{8,0},{16,8},{24,16},{32,24},{40,32},{48,40},{56,48},{64,56},{72,6... | collective-permute-start | bytes 3080 | tf_op jit(solution)/shard_map/ppermute | solution.py:22
  306.1 11.3 %collective-permute-start.45 = (f32[1,256]{1,0:T(1,128)S(1)}, f32[1,256]{1,0:T(1,128)S(1)}, u32[]{:S(2)}, u32[]{:S(2)}) collective-permute-start(f32[1,256]{1,0:T(1,128)S(1)} %get-tuple-element.56), channel_id=1, source_target_pairs={{0,8},{8,16},{16,24},{24,32},{32,40},{40,48},{48,56},{56,64},{64,7... | collective-permute-start | bytes 3080 | tf_op jit(solution)/shard_map/ppermute | solution.py:21
  (26 other events, 155.9 us)
where the time goes:
time: 347 us; the launch traced here: 345 us
  starting transfers between devices  137 us (39%)
  blocking collectives  85.8 us (25%)
  waiting for transfers between devices  45.8 us (13%)
  other arithmetic  28.3 us (8%)
  matrix products  27.9 us (8%)
  between operations  11.7 us (3%)
  local copies, waits for them, and re-layouts  7.85 us (2%)
    all_to_all x3, blocking collectives, total(): got = lax.all_to_all(sent, ('az', 'rg'), 0, 0, tiled=True)  59.1 us
    ppermute x10, starting transfers between devices, neighbours(): lax.ppermute(v[..., :, -1:], 'rg', [(i, i + 1) for i in range(n_rg - 1)])  37.5 us
    ppermute x10, starting transfers between devices, neighbours(): lax.ppermute(v[..., -1:, :], 'az', [(i, i + 1) for i in range(n_az - 1)])  32.9 us
    all_to_all x2, blocking collectives, gather_strip(): got = lax.all_to_all(sent, 'az', 0, 0, tiled=True)  26.7 us
    ppermute x10, waiting for transfers between devices, neighbours(): lax.ppermute(v[..., :, :1], 'rg', [(i + 1, i) for i in range(n_rg - 1)])  20.3 us
    ppermute x10, starting transfers between devices, neighbours(): lax.ppermute(v[..., :, :1], 'rg', [(i + 1, i) for i in range(n_rg - 1)])  20 us
    add x1, other arithmetic, mean_multilook(): first_re * second_re + first_im * second_im  14.6 us
    dot_general x48, matrix products, sandwich(): inner = jnp.dot(left, vector, precision=HIGHEST)  14.6 us
  transfers between devices with their start and end apart: 48, of which 19 were waited for; matrix products, arithmetic and copies ran while one was open for 0% of the time, Pallas kernels for 0%

commit v1 on v0

--- a/solution.py
+++ b/solution.py
@@ -33,6 +33,23 @@
     east, west, south, north, diagonal = operators
     v_n, v_s, v_w, v_e = neighbours(vector)
     return diagonal * vector - east * v_e - west * v_w - south * v_s - north * v_n
+
+
+def extended(v, width):
+    n_az = lax.axis_size("az")
+    n_rg = lax.axis_size("rg")
+    above = lax.ppermute(v[..., -width:, :], "az", [(i, i + 1) for i in range(n_az - 1)])
+    below = lax.ppermute(v[..., :width, :], "az", [(i + 1, i) for i in range(n_az - 1)])
+    v = jnp.concatenate([above, v, below], axis=-2)
+    left = lax.ppermute(v[..., :, -width:], "rg", [(i, i + 1) for i in range(n_rg - 1)])
+    right = lax.ppermute(v[..., :, :width], "rg", [(i + 1, i) for i in range(n_rg - 1)])
+    return jnp.concatenate([left, v, right], axis=-1)
+
+
+def apply_inner(padded, operators):
+    east, west, south, north, diagonal = operators
+    return (diagonal * padded[1:-1, 1:-1] - east * padded[1:-1, 2:] - west * padded[1:-1, :-2]
+            - south * padded[2:, 1:-1] - north * padded[:-2, 1:-1])
 
 
 def apply_padded(vector, operators):
@@ -234,6 +251,10 @@
     block_h, block_w = coarse_edges[0].shape
     whole = {}
 
+    ops_wide = extended(jnp.stack(levels[0]), 2)
+    diag_wide = jnp.where(ops_wide[4] > 0, ops_wide[4], 1.0)
+    ring_ops = tuple(ops_wide[k, 1:-1, 1:-1] for k in range(4)) + (diag_wide[1:-1, 1:-1],)
+
     def coarse_solve(rhs_vec):
         if not whole:
             got = gather_strip(jnp.stack([coarse_edges[0], coarse_edges[2], rhs_vec]))
@@ -244,16 +265,22 @@
         else:
             strip_rhs = gather_strip(rhs_vec[None])[0]
         strip_x = vcycle(strip_rhs, GATHER_LEVEL, whole["levels"], apply_padded, None)
-        return lax.dynamic_slice(strip_x, (segment_ordinal * block_h, block_w), (block_h, block_w))
-
-    def precondition(vector):
-        return vcycle(vector, 0, levels, apply_halo, coarse_solve)
+        strip_x = jnp.pad(strip_x, ((1, 1), (0, 0)))
+        return lax.dynamic_slice(strip_x, (segment_ordinal * block_h, block_w - 1),
+                                 (block_h + 2, block_w + 2))
+
+    def precondition(rhs_vec):
+        rhs_wide = extended(rhs_vec, 2)
+        estimate = OMEGA * rhs_wide / diag_wide
+        remain = rhs_vec - apply_inner(estimate[1:-1, 1:-1], levels[0])
+        estimate = estimate + prolong_copy(coarse_solve(restrict_sum(remain)))
+        ring = estimate[1:-1, 1:-1] + OMEGA * (rhs_wide[1:-1, 1:-1] - apply_inner(estimate, ring_ops)) / ring_ops[4]
+        return ring[1:-1, 1:-1], apply_inner(ring, levels[0])
 
     solution = jnp.zeros_like(rhs)
     residual = rhs
-    precond = precondition(residual)
+    precond, image_vec = precondition(residual)
     direction = precond
-    image_vec = apply_halo(direction, levels[0])
     sums = total(jnp.stack([jnp.sum(residual * precond), jnp.sum(direction * image_vec)]))
     norm_now = sums[0]
     curvature = sums[1]
@@ -262,8 +289,7 @@
         solution = solution + step_length * direction
         if step_index + 1 < ITERS:
             residual = residual - step_length * image_vec
-            precond = precondition(residual)
-            image_z = apply_halo(precond, levels[0])
+            precond, image_z = precondition(residual)
             sums = total(jnp.stack([jnp.sum(residual * precond), jnp.sum(precond * image_z),
                                     jnp.sum(precond * image_vec)]))
             norm_next = sums[0]

time: 347 us -> 285 us (0.82)
  starting transfers between devices: 137 us -> 90 us
  blocking collectives: 85.8 us -> 67.5 us
  waiting for transfers between devices: 45.8 us -> 50.7 us
    ppermute x0 -> x16, starting transfers between devices: none -> 42.6 us  [the longest x4 16.4 us: extended(): lax.ppermute(v[..., :, -width:], 'rg', [(i, i + 1) for i in range(n_rg -...]
    ppermute x10 -> x1, starting transfers between devices: 37.5 us -> 3.84 us  [neighbours(): lax.ppermute(v[..., :, -1:], 'rg', [(i, i + 1) for i in range(n_rg - 1)])]
    ppermute x10 -> x1, starting transfers between devices: 32.9 us -> 3.2 us  [neighbours(): lax.ppermute(v[..., -1:, :], 'az', [(i, i + 1) for i in range(n_az - 1)])]
    ppermute x10 -> x1, waiting for transfers between devices: 20.3 us -> 1.29 us  [neighbours(): lax.ppermute(v[..., :, :1], 'rg', [(i + 1, i) for i in range(n_rg - 1)])]
    all_to_all x3, blocking collectives: 59.1 us -> 40.5 us  [total(): got = lax.all_to_all(sent, ('az', 'rg'), 0, 0, tiled=True)]
    ppermute x0 -> x16, waiting for transfers between devices: none -> 17.9 us  [the longest x4 9.26 us: extended(): lax.ppermute(v[..., :, :width], 'rg', [(i + 1, i) for i in range(n_rg - 1)])]
    ppermute x10 -> x1, starting transfers between devices: 20 us -> 2.73 us  [neighbours(): lax.ppermute(v[..., :, :1], 'rg', [(i + 1, i) for i in range(n_rg - 1)])]
    ppermute x10 -> x1, starting transfers between devices: 12.9 us -> 1.29 us  [neighbours(): lax.ppermute(v[..., :1, :], 'az', [(i + 1, i) for i in range(n_az - 1)])]
  transfers between devices with their start and end apart: 48 -> 28, of which waited for: 19 -> 15; matrix products, arithmetic and copies ran while one was open for 0% -> 1% of each run, Pallas kernels for 0% -> 0%
where the time goes in v1:
time: 285 us; the launch traced here: 284 us
  starting transfers between devices  90 us (32%)
  blocking collectives  67.5 us (24%)
  waiting for transfers between devices  50.7 us (18%)
  other arithmetic  30 us (11%)
  matrix products  27 us (9%)
  between operations  11.6 us (4%)
  local copies, waits for them, and re-layouts  6.7 us (2%)
    all_to_all x3, blocking collectives, total(): got = lax.all_to_all(sent, ('az', 'rg'), 0, 0, tiled=True)  40.5 us
    all_to_all x2, blocking collectives, gather_strip(): got = lax.all_to_all(sent, 'az', 0, 0, tiled=True)  27.1 us
    ppermute x4, starting transfers between devices, extended(): lax.ppermute(v[..., :, -width:], 'rg', [(i, i + 1) for i in range(n_rg -...  16.4 us
    add x1, other arithmetic, mean_multilook(): first_re * second_re + first_im * second_im  14.5 us
    dot_general x48, matrix products, sandwich(): inner = jnp.dot(left, vector, precision=HIGHEST)  13.6 us
    all_to_all x1, starting transfers between devices, gather_strip(): got = lax.all_to_all(sent, 'az', 0, 0, tiled=True)  13.4 us
    ppermute x4, starting transfers between devices, extended(): lax.ppermute(v[..., -width:, :], 'az', [(i, i + 1) for i in range(n_az -...  13.4 us
    ppermute x3, waiting for transfers between devices, gather_strip(): right = lax.ppermute(column, 'rg', [(i + 1, i) for i in range(n_rg - 1)])  12.9 us
  transfers between devices with their start and end apart: 28, of which 15 were waited for; matrix products, arithmetic and copies ran while one was open for 1% of the time, Pallas kernels for 0%

profile of v1, /device:TPU:1, one launch (start us, length us, event | category | flops | bytes accessed | tf_op | source)
XLA Modules:
  0.0 283.6 jit_solution(4936357015003433160)
XLA Ops:
  5.1 14.5 %add_reduce_fusion.2 = (f32[20,10240]{1,0:T(8,128)S(1)}, f32[20,10240]{1,0:T(8,128)S(1)}, f32[20,10240]{1,0:T(8,128)S(1)}, f32[20,10240]{1,0:T(8,128)S(1)}) fusion(bf16[2,20,10240]{2,0,1:T(2,128)(2,1)} %param.4, pred[10240]{0:T(1024)(128)(4,1)S(1)} %fusion.364, pred[20]{0:T(512)(128)(4,1)S(1)} %compare_and_fusion.9, bf16[2,20,10240]{2,0,1:T(2,128)(2,1)} %param.5), kind=kLoop, calls=%fused_computation.34 | loop fusion | flops 4300800 | bytes 4925460 | tf_op jit(solution)/shard_map/add | solution.py:70
  24.1 5.8 %all-to-all-start = ((f32[8,3,4,256]{3,2,1,0:T(4,128)}), f32[8,3,4,256]{3,2,1,0:T(4,128)S(1)}, u32[]{:S(2)}, u32[]{:S(2)}) async-start(f32[8,3,4,256]{3,2,1,0:T(4,128)} %maximum_bitcast_fusion.4), calls=%async_computation | async-start | bytes 196608 | tf_op jit(solution)/shard_map/all_to_all | solution.py:229
  30.2 4.6 %all-to-all-done = f32[8,3,4,256]{3,2,1,0:T(4,128)S(1)} async-done(((f32[8,3,4,256]{3,2,1,0:T(4,128)}), f32[8,3,4,256]{3,2,1,0:T(4,128)S(1)}, u32[]{:S(2)}, u32[]{:S(2)}) %all-to-all-start) | async-done | bytes 98336 | tf_op jit(solution)/shard_map/all_to_all | solution.py:229
  42.6 3.8 %collective-permute-start.2 = (f32[4,32,1]{2,1,0:T(8,128)S(1)}, f32[4,32,1]{2,1,0:T(8,128)S(1)}, u32[]{:S(2)}, u32[]{:S(2)}) collective-permute-start(f32[4,32,1]{2,1,0:T(8,128)S(1)} %slice.1052), channel_id=1, source_target_pairs={{0,1},{1,2},{2,3},{3,4},{4,5},{5,6},{6,7},{8,9},{9,10},{10,11},{11... | collective-permute-start | bytes 1544 | tf_op jit(solution)/shard_map/ppermute | solution.py:23
  46.5 3.2 %collective-permute-start.3 = (f32[4,1,256]{2,1,0:T(1,128)S(1)}, f32[4,1,256]{2,1,0:T(1,128)S(1)}, u32[]{:S(2)}, u32[]{:S(2)}) collective-permute-start(f32[4,1,256]{2,1,0:T(1,128)S(1)} %pad_maximum_fusion.16), channel_id=1, source_target_pairs={{0,8},{8,16},{16,24},{24,32},{32,40},{40,48},{48,56},{56,64},{64,7... | collective-permute-start | bytes 12296 | tf_op jit(solution)/shard_map/ppermute | solution.py:21
  50.5 3.6 %collective-permute-start.4 = (f32[2,256]{1,0:T(2,128)S(1)}, f32[2,256]{1,0:T(2,128)S(1)}, u32[]{:S(2)}, u32[]{:S(2)}) collective-permute-start(f32[2,256]{1,0:T(2,128)S(1)} %get-tuple-element.59), channel_id=1, source_target_pairs={{0,8},{8,16},{16,24},{24,32},{32,40},{40,48},{48,56},{56,64},{64,7... | collective-permute-start | bytes 6152 | tf_op jit(solution)/shard_map/ppermute | solution.py:41
  55.5 5.2 %collective-permute-start.8 = (f32[5,2,256]{2,1,0:T(2,128)S(1)}, f32[5,2,256]{2,1,0:T(2,128)S(1)}, u32[]{:S(2)}, u32[]{:S(2)}) collective-permute-start(f32[5,2,256]{2,1,0:T(2,128)S(1)} %get-tuple-element.41), channel_id=1, source_target_pairs={{0,8},{8,16},{16,24},{24,32},{32,40},{40,48},{48,56},{56,64},{64,7... | collective-permute-start | bytes 30728 | tf_op jit(solution)/shard_map/ppermute | solution.py:41
  65.6 4.5 %collective-permute-start.10 = (f32[5,36,2]{2,1,0:T(8,128)S(1)}, f32[5,36,2]{2,1,0:T(8,128)S(1)}, u32[]{:S(2)}, u32[]{:S(2)}) collective-permute-start(f32[5,36,2]{2,1,0:T(8,128)S(1)} %get-tuple-element.39), channel_id=1, source_target_pairs={{0,1},{1,2},{2,3},{3,4},{4,5},{5,6},{6,7},{8,9},{9,10},{10,11},{11... | collective-permute-start | bytes 4328 | tf_op jit(solution)/shard_map/ppermute | solution.py:44
  72.1 3.6 %collective-permute-start.6 = (f32[36,2]{1,0:T(8,128)S(1)}, f32[36,2]{1,0:T(8,128)S(1)}, u32[]{:S(2)}, u32[]{:S(2)}) collective-permute-start(f32[36,2]{1,0:T(8,128)S(1)} %get-tuple-element.53), channel_id=1, source_target_pairs={{0,1},{1,2},{2,3},{3,4},{4,5},{5,6},{6,7},{8,9},{9,10},{10,11},{11... | collective-permute-start | bytes 872 | tf_op jit(solution)/shard_map/ppermute | solution.py:44
  82.1 13.4 %all-to-all-start.1 = ((f32[16,3,16,128]{3,2,1,0:T(8,128)}), f32[16,3,16,128]{3,2,1,0:T(8,128)S(1)}, u32[]{:S(2)}, u32[]{:S(2)}) async-start(f32[16,3,16,128]{3,2,1,0:T(8,128)} %broadcast_in_dim.17), calls=%async_computation.1 | async-start | bytes 786432 | tf_op jit(solution)/shard_map/all_to_all | solution.py:174
  95.6 9.0 %all-to-all-done.1 = f32[16,3,16,128]{3,2,1,0:T(8,128)S(1)} async-done(((f32[16,3,16,128]{3,2,1,0:T(8,128)}), f32[16,3,16,128]{3,2,1,0:T(8,128)S(1)}, u32[]{:S(2)}, u32[]{:S(2)}) %all-to-all-start.1) | async-done | bytes 393248 | tf_op jit(solution)/shard_map/all_to_all | solution.py:174
  104.6 4.1 %collective-permute-start.12 = (f32[3,256,128]{2,1,0:T(8,128)S(1)}, f32[3,256,128]{2,1,0:T(8,128)S(1)}, u32[]{:S(2)}, u32[]{:S(2)}) collective-permute-start(f32[3,256,128]{2,1,0:T(8,128)S(1)} %bitcast.400), channel_id=1, source_target_pairs={{0,1},{1,2},{2,3},{3,4},{4,5},{5,6},{6,7},{8,9},{9,10},{10,11},{11... | collective-permute-start | bytes 1179656 | tf_op jit(solution)/shard_map/ppermute | solution.py:176
  113.4 4.4 %collective-permute-done.13 = f32[3,256,128]{2,1,0:T(8,128)S(1)} collective-permute-done((f32[3,256,128]{2,1,0:T(8,128)S(1)}, f32[3,256,128]{2,1,0:T(8,128)S(1)}, u32[]{:S(2)}, u32[]{:S(2)}) %collective-permute-start.13) | collective-permute-done | bytes 393248 | tf_op jit(solution)/shard_map/ppermute | solution.py:177
  134.0 12.5 %all_to_all.38 = f32[128,1,2]{2,1,0:T(1,128)S(1)} all-to-all(f32[128,1,2]{2,1,0:T(1,128)S(1)} %broadcast_in_dim.18), channel_id=1, replica_groups=mesh['az'=16,'rg'=8] {'az','rg'}, dimensions={0} | all-to-all | bytes 2048 | tf_op jit(solution)/shard_map/all_to_all | solution.py:190
  155.3 4.1 %collective-permute-start.16 = (f32[36,2]{1,0:T(8,128)S(1)}, f32[36,2]{1,0:T(8,128)S(1)}, u32[]{:S(2)}, u32[]{:S(2)}) collective-permute-start(f32[36,2]{1,0:T(8,128)S(1)} %get-tuple-element.51), channel_id=1, source_target_pairs={{0,1},{1,2},{2,3},{3,4},{4,5},{5,6},{6,7},{8,9},{9,10},{10,11},{11... | collective-permute-start | bytes 872 | tf_op jit(solution)/shard_map/ppermute | solution.py:44
  165.1 13.5 %all_to_all.39 = f32[16,1,16,128]{3,2,1,0:T(8,128)S(1)} all-to-all(f32[16,1,16,128]{3,2,1,0:T(8,128)S(1)} %broadcast_in_dim.19), channel_id=1, replica_groups=mesh['az'=16,'rg'=8] {'az'}, dimensions={0} | all-to-all | bytes 262144 | tf_op jit(solution)/shard_map/all_to_all | solution.py:174
  178.6 3.5 %collective-permute-start.18 = (f32[1,256,128]{2,1,0:T(8,128)S(1)}, f32[1,256,128]{2,1,0:T(8,128)S(1)}, u32[]{:S(2)}, u32[]{:S(2)}) collective-permute-start(f32[1,256,128]{2,1,0:T(8,128)S(1)} %bitcast.408), channel_id=1, source_target_pairs={{0,1},{1,2},{2,3},{3,4},{4,5},{5,6},{6,7},{8,9},{9,10},{10,11},{11... | collective-permute-start | bytes 393224 | tf_op jit(solution)/shard_map/ppermute | solution.py:176
  184.3 4.1 %collective-permute-done.19 = f32[1,256,128]{2,1,0:T(8,128)S(1)} collective-permute-done((f32[1,256,128]{2,1,0:T(8,128)S(1)}, f32[1,256,128]{2,1,0:T(8,128)S(1)}, u32[]{:S(2)}, u32[]{:S(2)}) %collective-permute-start.19) | collective-permute-done | bytes 131104 | tf_op jit(solution)/shard_map/ppermute | solution.py:177
  197.4 14.0 %all_to_all.40 = f32[128,1,3]{2,1,0:T(1,128)S(1)} all-to-all(f32[128,1,3]{2,1,0:T(1,128)S(1)} %broadcast_in_dim.20), channel_id=1, replica_groups=mesh['az'=16,'rg'=8] {'az','rg'}, dimensions={0} | all-to-all | bytes 3072 | tf_op jit(solution)/shard_map/all_to_all | solution.py:190
  222.7 4.1 %collective-permute-start.22 = (f32[36,2]{1,0:T(8,128)S(1)}, f32[36,2]{1,0:T(8,128)S(1)}, u32[]{:S(2)}, u32[]{:S(2)}) collective-permute-start(f32[36,2]{1,0:T(8,128)S(1)} %get-tuple-element.49), channel_id=1, source_target_pairs={{0,1},{1,2},{2,3},{3,4},{4,5},{5,6},{6,7},{8,9},{9,10},{10,11},{11... | collective-permute-start | bytes 872 | tf_op jit(solution)/shard_map/ppermute | solution.py:44
  232.5 13.5 %all_to_all.41 = f32[16,1,16,128]{3,2,1,0:T(8,128)S(1)} all-to-all(f32[16,1,16,128]{3,2,1,0:T(8,128)S(1)} %broadcast_in_dim.21), channel_id=1, replica_groups=mesh['az'=16,'rg'=8] {'az'}, dimensions={0} | all-to-all | bytes 262144 | tf_op jit(solution)/shard_map/all_to_all | solution.py:174
  246.0 3.5 %collective-permute-start.24 = (f32[1,256,128]{2,1,0:T(8,128)S(1)}, f32[1,256,128]{2,1,0:T(8,128)S(1)}, u32[]{:S(2)}, u32[]{:S(2)}) collective-permute-start(f32[1,256,128]{2,1,0:T(8,128)S(1)} %bitcast.403), channel_id=1, source_target_pairs={{0,1},{1,2},{2,3},{3,4},{4,5},{5,6},{6,7},{8,9},{9,10},{10,11},{11... | collective-permute-start | bytes 393224 | tf_op jit(solution)/shard_map/ppermute | solution.py:176
  251.4 4.3 %collective-permute-done.25 = f32[1,256,128]{2,1,0:T(8,128)S(1)} collective-permute-done((f32[1,256,128]{2,1,0:T(8,128)S(1)}, f32[1,256,128]{2,1,0:T(8,128)S(1)}, u32[]{:S(2)}, u32[]{:S(2)}) %collective-permute-start.25) | collective-permute-done | bytes 131104 | tf_op jit(solution)/shard_map/ppermute | solution.py:177
  264.9 14.0 %all_to_all.42 = f32[128,1,3]{2,1,0:T(1,128)S(1)} all-to-all(f32[128,1,3]{2,1,0:T(1,128)S(1)} %broadcast_in_dim.22), channel_id=1, replica_groups=mesh['az'=16,'rg'=8] {'az','rg'}, dimensions={0} | all-to-all | bytes 3072 | tf_op jit(solution)/shard_map/all_to_all | solution.py:190
  (278 shorter events, 100.9 us)
Async XLA Ops:
  24.1 10.8 %all-to-all-start = ((f32[8,3,4,256]{3,2,1,0:T(4,128)}), f32[8,3,4,256]{3,2,1,0:T(4,128)S(1)}, u32[]{:S(2)}, u32[]{:S(2)}) async-start(f32[8,3,4,256]{3,2,1,0:T(4,128)} %maximum_bitcast_fusion.4), calls=%async_computation | async-start | bytes 196608 | tf_op jit(solution)/shard_map/all_to_all | solution.py:229
  35.1 5.4 %collective-permute-start = (f32[3,32,1]{2,1,0:T(8,128)S(1)}, f32[3,32,1]{2,1,0:T(8,128)S(1)}, u32[]{:S(2)}, u32[]{:S(2)}) collective-permute-start(f32[3,32,1]{2,1,0:T(8,128)S(1)} %slice.1039), channel_id=1, source_target_pairs={{1,0},{2,1},{3,2},{4,3},{5,4},{6,5},{7,6},{9,8},{10,9},{11,10},{12... | collective-permute-start | bytes 1160 | tf_op jit(solution)/shard_map/ppermute | solution.py:24
  37.9 4.5 %collective-permute-start.1 = (f32[3,1,256]{2,1,0:T(1,128)S(1)}, f32[3,1,256]{2,1,0:T(1,128)S(1)}, u32[]{:S(2)}, u32[]{:S(2)}) collective-permute-start(f32[3,1,256]{2,1,0:T(1,128)S(1)} %slice.1047), channel_id=1, source_target_pairs={{8,0},{16,8},{24,16},{32,24},{40,32},{48,40},{56,48},{64,56},{72,6... | collective-permute-start | bytes 9224 | tf_op jit(solution)/shard_map/ppermute | solution.py:22
  42.6 7.1 %collective-permute-start.2 = (f32[4,32,1]{2,1,0:T(8,128)S(1)}, f32[4,32,1]{2,1,0:T(8,128)S(1)}, u32[]{:S(2)}, u32[]{:S(2)}) collective-permute-start(f32[4,32,1]{2,1,0:T(8,128)S(1)} %slice.1052), channel_id=1, source_target_pairs={{0,1},{1,2},{2,3},{3,4},{4,5},{5,6},{6,7},{8,9},{9,10},{10,11},{11... | collective-permute-start | bytes 1544 | tf_op jit(solution)/shard_map/ppermute | solution.py:23
  50.5 12.3 %collective-permute-start.4 = (f32[2,256]{1,0:T(2,128)S(1)}, f32[2,256]{1,0:T(2,128)S(1)}, u32[]{:S(2)}, u32[]{:S(2)}) collective-permute-start(f32[2,256]{1,0:T(2,128)S(1)} %get-tuple-element.59), channel_id=1, source_target_pairs={{0,8},{8,16},{16,24},{24,32},{32,40},{40,48},{48,56},{56,64},{64,7... | collective-permute-start | bytes 6152 | tf_op jit(solution)/shard_map/ppermute | solution.py:41
  54.1 8.7 %collective-permute-start.5 = (f32[2,256]{1,0:T(2,128)S(1)}, f32[2,256]{1,0:T(2,128)S(1)}, u32[]{:S(2)}, u32[]{:S(2)}) collective-permute-start(f32[2,256]{1,0:T(2,128)S(1)} %get-tuple-element.60), channel_id=1, source_target_pairs={{8,0},{16,8},{24,16},{32,24},{40,32},{48,40},{56,48},{64,56},{72,6... | collective-permute-start | bytes 6152 | tf_op jit(solution)/shard_map/ppermute | solution.py:42
  55.5 7.4 %collective-permute-start.8 = (f32[5,2,256]{2,1,0:T(2,128)S(1)}, f32[5,2,256]{2,1,0:T(2,128)S(1)}, u32[]{:S(2)}, u32[]{:S(2)}) collective-permute-start(f32[5,2,256]{2,1,0:T(2,128)S(1)} %get-tuple-element.41), channel_id=1, source_target_pairs={{0,8},{8,16},{16,24},{24,32},{32,40},{40,48},{48,56},{56,64},{64,7... | collective-permute-start | bytes 30728 | tf_op jit(solution)/shard_map/ppermute | solution.py:41
  60.8 4.7 %collective-permute-start.9 = (f32[5,2,256]{2,1,0:T(2,128)S(1)}, f32[5,2,256]{2,1,0:T(2,128)S(1)}, u32[]{:S(2)}, u32[]{:S(2)}) collective-permute-start(f32[5,2,256]{2,1,0:T(2,128)S(1)} %get-tuple-element.42), channel_id=1, source_target_pairs={{8,0},{16,8},{24,16},{32,24},{40,32},{48,40},{56,48},{64,56},{72,6... | collective-permute-start | bytes 30728 | tf_op jit(solution)/shard_map/ppermute | solution.py:42
  65.6 12.1 %collective-permute-start.10 = (f32[5,36,2]{2,1,0:T(8,128)S(1)}, f32[5,36,2]{2,1,0:T(8,128)S(1)}, u32[]{:S(2)}, u32[]{:S(2)}) collective-permute-start(f32[5,36,2]{2,1,0:T(8,128)S(1)} %get-tuple-element.39), channel_id=1, source_target_pairs={{0,1},{1,2},{2,3},{3,4},{4,5},{5,6},{6,7},{8,9},{9,10},{10,11},{11... | collective-permute-start | bytes 4328 | tf_op jit(solution)/shard_map/ppermute | solution.py:44
  70.1 7.6 %collective-permute-start.11 = (f32[5,36,2]{2,1,0:T(8,128)S(1)}, f32[5,36,2]{2,1,0:T(8,128)S(1)}, u32[]{:S(2)}, u32[]{:S(2)}) collective-permute-start(f32[5,36,2]{2,1,0:T(8,128)S(1)} %get-tuple-element.40), channel_id=1, source_target_pairs={{1,0},{2,1},{3,2},{4,3},{5,4},{6,5},{7,6},{9,8},{10,9},{11,10},{12... | collective-permute-start | bytes 4328 | tf_op jit(solution)/shard_map/ppermute | solution.py:45
  72.1 5.8 %collective-permute-start.6 = (f32[36,2]{1,0:T(8,128)S(1)}, f32[36,2]{1,0:T(8,128)S(1)}, u32[]{:S(2)}, u32[]{:S(2)}) collective-permute-start(f32[36,2]{1,0:T(8,128)S(1)} %get-tuple-element.53), channel_id=1, source_target_pairs={{0,1},{1,2},{2,3},{3,4},{4,5},{5,6},{6,7},{8,9},{9,10},{10,11},{11... | collective-permute-start | bytes 872 | tf_op jit(solution)/shard_map/ppermute | solution.py:44
  75.7 5.1 %collective-permute-start.7 = (f32[36,2]{1,0:T(8,128)S(1)}, f32[36,2]{1,0:T(8,128)S(1)}, u32[]{:S(2)}, u32[]{:S(2)}) collective-permute-start(f32[36,2]{1,0:T(8,128)S(1)} %get-tuple-element.54), channel_id=1, source_target_pairs={{1,0},{2,1},{3,2},{4,3},{5,4},{6,5},{7,6},{9,8},{10,9},{11,10},{12... | collective-permute-start | bytes 872 | tf_op jit(solution)/shard_map/ppermute | solution.py:45
  82.1 22.5 %all-to-all-start.1 = ((f32[16,3,16,128]{3,2,1,0:T(8,128)}), f32[16,3,16,128]{3,2,1,0:T(8,128)S(1)}, u32[]{:S(2)}, u32[]{:S(2)}) async-start(f32[16,3,16,128]{3,2,1,0:T(8,128)} %broadcast_in_dim.17), calls=%async_computation.1 | async-start | bytes 786432 | tf_op jit(solution)/shard_map/all_to_all | solution.py:174
  104.6 8.8 %collective-permute-start.12 = (f32[3,256,128]{2,1,0:T(8,128)S(1)}, f32[3,256,128]{2,1,0:T(8,128)S(1)}, u32[]{:S(2)}, u32[]{:S(2)}) collective-permute-start(f32[3,256,128]{2,1,0:T(8,128)S(1)} %bitcast.400), channel_id=1, source_target_pairs={{0,1},{1,2},{2,3},{3,4},{4,5},{5,6},{6,7},{8,9},{9,10},{10,11},{11... | collective-permute-start | bytes 1179656 | tf_op jit(solution)/shard_map/ppermute | solution.py:176
  108.7 9.1 %collective-permute-start.13 = (f32[3,256,128]{2,1,0:T(8,128)S(1)}, f32[3,256,128]{2,1,0:T(8,128)S(1)}, u32[]{:S(2)}, u32[]{:S(2)}) collective-permute-start(f32[3,256,128]{2,1,0:T(8,128)S(1)} %bitcast.401), channel_id=1, source_target_pairs={{1,0},{2,1},{3,2},{4,3},{5,4},{6,5},{7,6},{9,8},{10,9},{11,10},{12... | collective-permute-start | bytes 1179656 | tf_op jit(solution)/shard_map/ppermute | solution.py:177
  150.9 4.3 %collective-permute-start.15 = (f32[2,256]{1,0:T(2,128)S(1)}, f32[2,256]{1,0:T(2,128)S(1)}, u32[]{:S(2)}, u32[]{:S(2)}) collective-permute-start(f32[2,256]{1,0:T(2,128)S(1)} %get-tuple-element.58), channel_id=1, source_target_pairs={{8,0},{16,8},{24,16},{32,24},{40,32},{48,40},{56,48},{64,56},{72,6... | collective-permute-start | bytes 6152 | tf_op jit(solution)/shard_map/ppermute | solution.py:42
  155.3 6.1 %collective-permute-start.16 = (f32[36,2]{1,0:T(8,128)S(1)}, f32[36,2]{1,0:T(8,128)S(1)}, u32[]{:S(2)}, u32[]{:S(2)}) collective-permute-start(f32[36,2]{1,0:T(8,128)S(1)} %get-tuple-element.51), channel_id=1, source_target_pairs={{0,1},{1,2},{2,3},{3,4},{4,5},{5,6},{6,7},{8,9},{9,10},{10,11},{11... | collective-permute-start | bytes 872 | tf_op jit(solution)/shard_map/ppermute | solution.py:44
  159.5 5.1 %collective-permute-start.17 = (f32[36,2]{1,0:T(8,128)S(1)}, f32[36,2]{1,0:T(8,128)S(1)}, u32[]{:S(2)}, u32[]{:S(2)}) collective-permute-start(f32[36,2]{1,0:T(8,128)S(1)} %get-tuple-element.52), channel_id=1, source_target_pairs={{1,0},{2,1},{3,2},{4,3},{5,4},{6,5},{7,6},{9,8},{10,9},{11,10},{12... | collective-permute-start | bytes 872 | tf_op jit(solution)/shard_map/ppermute | solution.py:45
  178.6 5.6 %collective-permute-start.18 = (f32[1,256,128]{2,1,0:T(8,128)S(1)}, f32[1,256,128]{2,1,0:T(8,128)S(1)}, u32[]{:S(2)}, u32[]{:S(2)}) collective-permute-start(f32[1,256,128]{2,1,0:T(8,128)S(1)} %bitcast.408), channel_id=1, source_target_pairs={{0,1},{1,2},{2,3},{3,4},{4,5},{5,6},{6,7},{8,9},{9,10},{10,11},{11... | collective-permute-start | bytes 393224 | tf_op jit(solution)/shard_map/ppermute | solution.py:176
  182.1 6.3 %collective-permute-start.19 = (f32[1,256,128]{2,1,0:T(8,128)S(1)}, f32[1,256,128]{2,1,0:T(8,128)S(1)}, u32[]{:S(2)}, u32[]{:S(2)}) collective-permute-start(f32[1,256,128]{2,1,0:T(8,128)S(1)} %bitcast.409), channel_id=1, source_target_pairs={{1,0},{2,1},{3,2},{4,3},{5,4},{6,5},{7,6},{9,8},{10,9},{11,10},{12... | collective-permute-start | bytes 393224 | tf_op jit(solution)/shard_map/ppermute | solution.py:177
  222.7 6.1 %collective-permute-start.22 = (f32[36,2]{1,0:T(8,128)S(1)}, f32[36,2]{1,0:T(8,128)S(1)}, u32[]{:S(2)}, u32[]{:S(2)}) collective-permute-start(f32[36,2]{1,0:T(8,128)S(1)} %get-tuple-element.49), channel_id=1, source_target_pairs={{0,1},{1,2},{2,3},{3,4},{4,5},{5,6},{6,7},{8,9},{9,10},{10,11},{11... | collective-permute-start | bytes 872 | tf_op jit(solution)/shard_map/ppermute | solution.py:44
  226.8 5.1 %collective-permute-start.23 = (f32[36,2]{1,0:T(8,128)S(1)}, f32[36,2]{1,0:T(8,128)S(1)}, u32[]{:S(2)}, u32[]{:S(2)}) collective-permute-start(f32[36,2]{1,0:T(8,128)S(1)} %get-tuple-element.50), channel_id=1, source_target_pairs={{1,0},{2,1},{3,2},{4,3},{5,4},{6,5},{7,6},{9,8},{10,9},{11,10},{12... | collective-permute-start | bytes 872 | tf_op jit(solution)/shard_map/ppermute | solution.py:45
  246.0 5.4 %collective-permute-start.24 = (f32[1,256,128]{2,1,0:T(8,128)S(1)}, f32[1,256,128]{2,1,0:T(8,128)S(1)}, u32[]{:S(2)}, u32[]{:S(2)}) collective-permute-start(f32[1,256,128]{2,1,0:T(8,128)S(1)} %bitcast.403), channel_id=1, source_target_pairs={{0,1},{1,2},{2,3},{3,4},{4,5},{5,6},{6,7},{8,9},{9,10},{10,11},{11... | collective-permute-start | bytes 393224 | tf_op jit(solution)/shard_map/ppermute | solution.py:176
  249.5 6.3 %collective-permute-start.25 = (f32[1,256,128]{2,1,0:T(8,128)S(1)}, f32[1,256,128]{2,1,0:T(8,128)S(1)}, u32[]{:S(2)}, u32[]{:S(2)}) collective-permute-start(f32[1,256,128]{2,1,0:T(8,128)S(1)} %bitcast.404), channel_id=1, source_target_pairs={{1,0},{2,1},{3,2},{4,3},{5,4},{6,5},{7,6},{9,8},{10,9},{11,10},{12... | collective-permute-start | bytes 393224 | tf_op jit(solution)/shard_map/ppermute | solution.py:177
  (5 other events, 30.8 us)

commit v2 on v1

--- a/solution.py
+++ b/solution.py
@@ -222,38 +222,47 @@
     weight = 0.05 + 4.0 * (look_re * look_re + look_im * look_im) / jnp.maximum(
         power_one * power_two, 1.0
     )
+    border = 3
     fields = jnp.stack([look_re, look_im, weight])
     n_fields, rows_here, cols_all = fields.shape
     cols_here = cols_all // n_range
-    fields = fields.reshape(n_fields, rows_here, n_range, cols_here).transpose(2, 0, 1, 3)
+    fields = jnp.pad(fields, ((0, 0), (0, 0), (border, border)))
+    fields = jnp.stack([fields[:, :, c * cols_here:(c + 1) * cols_here + 2 * border] for c in range(n_range)])
     fields = lax.all_to_all(fields, "rg", 0, 0, tiled=True)
-    fields = fields.transpose(1, 0, 2, 3).reshape(n_fields, n_range * rows_here, cols_here)
-    weight = fields[2]
+    fields = fields.transpose(1, 0, 2, 3).reshape(n_fields, n_range * rows_here, cols_here + 2 * border)
     shard_height_total = n_range * rows_here
-
-    f_n, f_s, f_w, f_e = neighbours(fields)
-    edge_h, grad_h = edge_terms(fields[0], fields[1], fields[2], f_e[0], f_e[1], f_e[2])
-    col_global = range_index * cols_here + jnp.arange(cols_here, dtype=jnp.int32)
-    keep_h = (col_global <= cols_here * n_range - 2).astype(jnp.float32)
+    above = lax.ppermute(fields[:, -border:, :], "az", [(i, i + 1) for i in range(n_az - 1)])
+    below = lax.ppermute(fields[:, :border, :], "az", [(i + 1, i) for i in range(n_az - 1)])
+    fields = jnp.concatenate([above, fields, below], axis=1)
+    weight = fields[2, border:-border, border:-border]
+
+    row_global = segment_ordinal * shard_height_total - border + jnp.arange(
+        shard_height_total + 2 * border, dtype=jnp.int32)
+    col_global = range_index * cols_here - border + jnp.arange(cols_here + 2 * border, dtype=jnp.int32)
+    edge_h, grad_h = edge_terms(fields[0, :, :-1], fields[1, :, :-1], fields[2, :, :-1],
+                                fields[0, :, 1:], fields[1, :, 1:], fields[2, :, 1:])
+    keep_h = ((col_global[:-1] >= 0) & (col_global[:-1] <= cols_here * n_range - 2)).astype(jnp.float32)
     edge_h = edge_h * keep_h[None, :]
-    edge_v, grad_v = edge_terms(fields[0], fields[1], fields[2], f_s[0], f_s[1], f_s[2])
-    row_global = segment_ordinal * shard_height_total + jnp.arange(shard_height_total, dtype=jnp.int32)
-    keep_v = (row_global <= shard_height_total * n_az - 2).astype(jnp.float32)
+    edge_v, grad_v = edge_terms(fields[0, :-1], fields[1, :-1], fields[2, :-1],
+                                fields[0, 1:], fields[1, 1:], fields[2, 1:])
+    keep_v = ((row_global[:-1] >= 0) & (row_global[:-1] <= shard_height_total * n_az - 2)).astype(jnp.float32)
     edge_v = edge_v * keep_v[:, None]
     flux_h = edge_h * grad_h
     flux_v = edge_v * grad_v
-    e_n, _, e_w, _ = neighbours(jnp.stack([edge_h, flux_h, edge_v, flux_v]))
-    west_edge, flux_w, north_edge, flux_n = e_w[0], e_w[1], e_n[2], e_n[3]
-    rhs = -(flux_h - flux_w + flux_v - flux_n)
-
-    levels, coarse_edges = build_levels(edge_h, west_edge, south=edge_v, north=north_edge,
+    east_w = edge_h[1:-1, 1:]
+    west_w = edge_h[1:-1, :-1]
+    south_w = edge_v[1:, 1:-1]
+    north_w = edge_v[:-1, 1:-1]
+    diag_wide = east_w + west_w + south_w + north_w + MU * 4.0**0
+    rhs_wide = -(flux_h[1:-1, 1:] - flux_h[1:-1, :-1] + flux_v[1:, 1:-1] - flux_v[:-1, 1:-1])
+    rhs = rhs_wide[2:-2, 2:-2]
+    own = (slice(2, -2), slice(2, -2))
+    levels, coarse_edges = build_levels(east_w[own], west_w[own], south_w[own], north_w[own],
                                         first_level=0, last_level=GATHER_LEVEL)
     block_h, block_w = coarse_edges[0].shape
     whole = {}
 
-    ops_wide = extended(jnp.stack(levels[0]), 2)
-    diag_wide = jnp.where(ops_wide[4] > 0, ops_wide[4], 1.0)
-    ring_ops = tuple(ops_wide[k, 1:-1, 1:-1] for k in range(4)) + (diag_wide[1:-1, 1:-1],)
+    ring_ops = tuple(x[1:-1, 1:-1] for x in (east_w, west_w, south_w, north_w, diag_wide))
 
     def coarse_solve(rhs_vec):
         if not whole:
@@ -269,8 +278,9 @@
         return lax.dynamic_slice(strip_x, (segment_ordinal * block_h, block_w - 1),
                                  (block_h + 2, block_w + 2))
 
-    def precondition(rhs_vec):
-        rhs_wide = extended(rhs_vec, 2)
+    def precondition(rhs_vec, rhs_wide=None):
+        if rhs_wide is None:
+            rhs_wide = extended(rhs_vec, 2)
         estimate = OMEGA * rhs_wide / diag_wide
         remain = rhs_vec - apply_inner(estimate[1:-1, 1:-1], levels[0])
         estimate = estimate + prolong_copy(coarse_solve(restrict_sum(remain)))
@@ -279,7 +289,7 @@
 
     solution = jnp.zeros_like(rhs)
     residual = rhs
-    precond, image_vec = precondition(residual)
+    precond, image_vec = precondition(residual, rhs_wide)
     direction = precond
     sums = total(jnp.stack([jnp.sum(residual * precond), jnp.sum(direction * image_vec)]))
     norm_now = sums[0]

time: 285 us -> 252 us (0.88)
  starting transfers between devices: 90 us -> 62.2 us
  blocking collectives: 67.5 us -> 54.7 us
  other arithmetic: 30 us -> 33.2 us
    all_to_all x3 -> x2, blocking collectives: 40.5 us -> 27.6 us  [total(): got = lax.all_to_all(sent, ('az', 'rg'), 0, 0, tiled=True)]
    all_to_all x0 -> x1, waiting for transfers between devices: none -> 8.91 us  [total(): got = lax.all_to_all(sent, ('az', 'rg'), 0, 0, tiled=True)]
    ppermute x4 -> x2, starting transfers between devices: 13.4 us -> 4.51 us  [extended(): lax.ppermute(v[..., -width:, :], 'az', [(i, i + 1) for i in range(n_az -...]
    ppermute x4 -> x2, starting transfers between devices: 16.4 us -> 8.25 us  [extended(): lax.ppermute(v[..., :, -width:], 'rg', [(i, i + 1) for i in range(n_rg -...]
    ppermute x4 -> x2, starting transfers between devices: 11.1 us -> 4.49 us  [the longest x1 3.2 us: local(): lax.ppermute(fields[:, -border:, :], 'az', [(i, i + 1) for i in range(n_a...]
    all_to_all x0 -> x1, starting transfers between devices: none -> 4.56 us  [total(): got = lax.all_to_all(sent, ('az', 'rg'), 0, 0, tiled=True)]
    all_to_all x1, starting transfers between devices: 13.4 us -> 9.25 us  [gather_strip(): got = lax.all_to_all(sent, 'az', 0, 0, tiled=True)]
    unnamed x3 -> x6, other arithmetic: 0.17 us -> 4.09 us
  transfers between devices with their start and end apart: 28 -> 19, of which waited for: 15 -> 12; matrix products, arithmetic and copies ran while one was open for 1% -> 0% of each run, Pallas kernels for 0% -> 0%
where the time goes in v2:
time: 252 us; the launch traced here: 251 us
  starting transfers between devices  62.2 us (25%)
  blocking collectives  54.7 us (22%)
  waiting for transfers between devices  53.1 us (21%)
  other arithmetic  33.2 us (13%)
  matrix products  27.2 us (11%)
  between operations  11.7 us (5%)
  local copies, waits for them, and re-layouts  8.92 us (4%)
    all_to_all x2, blocking collectives, total(): got = lax.all_to_all(sent, ('az', 'rg'), 0, 0, tiled=True)  27.6 us
    all_to_all x2, blocking collectives, gather_strip(): got = lax.all_to_all(sent, 'az', 0, 0, tiled=True)  27.1 us
    add x1, other arithmetic, mean_multilook(): first_re * second_re + first_im * second_im  14.5 us
    dot_general x48, matrix products, sandwich(): inner = jnp.dot(left, vector, precision=HIGHEST)  13.8 us
    ppermute x3, waiting for transfers between devices, gather_strip(): right = lax.ppermute(column, 'rg', [(i + 1, i) for i in range(n_rg - 1)])  12.9 us
    ppermute x3, starting transfers between devices, gather_strip(): left = lax.ppermute(column, 'rg', [(i, i + 1) for i in range(n_rg - 1)])  12.8 us
    dot_general x48, matrix products, sandwich(): return jnp.dot(inner, right, precision=HIGHEST)  11 us
    all_to_all x1, starting transfers between devices, gather_strip(): got = lax.all_to_all(sent, 'az', 0, 0, tiled=True)  9.25 us
  transfers between devices with their start and end apart: 19, of which 12 were waited for; matrix products, arithmetic and copies ran while one was open for 0% of the time, Pallas kernels for 0%

profile of v2, /device:TPU:1, one launch (start us, length us, event | category | flops | bytes accessed | tf_op | source)
XLA Modules:
  0.0 251.1 jit_solution(11999886867940507416)
XLA Ops:
  5.1 14.5 %add_reduce_fusion.2 = (f32[20,10240]{1,0:T(8,128)S(1)}, f32[20,10240]{1,0:T(8,128)S(1)}, f32[20,10240]{1,0:T(8,128)S(1)}, f32[20,10240]{1,0:T(8,128)S(1)}) fusion(bf16[2,20,10240]{2,0,1:T(2,128)(2,1)} %param.4, pred[10240]{0:T(1024)(128)(4,1)S(1)} %fusion.370, pred[20]{0:T(512)(128)(4,1)S(1)} %compare_and_fusion.9, bf16[2,20,10240]{2,0,1:T(2,128)(2,1)} %param.5), kind=kLoop, calls=%fused_computation.34 | loop fusion | flops 4300800 | bytes 4925460 | tf_op jit(solution)/shard_map/add | solution.py:70
  28.9 5.8 %all-to-all-start = ((f32[8,3,4,262]{3,2,1,0:T(4,128)}), f32[8,3,4,262]{3,2,1,0:T(4,128)S(1)}, u32[]{:S(2)}, u32[]{:S(2)}) async-start(f32[8,3,4,262]{3,2,1,0:T(4,128)} %fusion.551), calls=%async_computation | async-start | bytes 294912 | tf_op jit(solution)/shard_map/all_to_all | solution.py:231
  35.0 5.1 %all-to-all-done = f32[8,3,4,262]{3,2,1,0:T(4,128)S(1)} async-done(((f32[8,3,4,262]{3,2,1,0:T(4,128)}), f32[8,3,4,262]{3,2,1,0:T(4,128)S(1)}, u32[]{:S(2)}, u32[]{:S(2)}) %all-to-all-start) | async-done | bytes 100640 | tf_op jit(solution)/shard_map/all_to_all | solution.py:231
  40.2 3.2 %collective-permute-start = (f32[3,3,262]{2,1,0:T(4,128)S(1)}, f32[3,3,262]{2,1,0:T(4,128)S(1)}, u32[]{:S(2)}, u32[]{:S(2)}) collective-permute-start(f32[3,3,262]{2,1,0:T(4,128)S(1)} %get-tuple-element.29), channel_id=1, source_target_pairs={{0,8},{8,16},{16,24},{24,32},{32,40},{40,48},{48,56},{56,64},{64,7... | collective-permute-start | bytes 28304 | tf_op jit(solution)/shard_map/ppermute | solution.py:234
  44.7 3.2 %collective-permute-done.1 = f32[3,3,262]{2,1,0:T(4,128)S(1)} collective-permute-done((f32[3,3,262]{2,1,0:T(4,128)S(1)}, f32[3,3,262]{2,1,0:T(4,128)S(1)}, u32[]{:S(2)}, u32[]{:S(2)}) %collective-permute-start.1) | collective-permute-done | bytes 9464 | tf_op jit(solution)/shard_map/ppermute | solution.py:235
  50.5 9.2 %all-to-all-start.1 = ((f32[16,3,16,128]{3,2,1,0:T(8,128)}), f32[16,3,16,128]{3,2,1,0:T(8,128)S(1)}, u32[]{:S(2)}, u32[]{:S(2)}) async-start(f32[16,3,16,128]{3,2,1,0:T(8,128)} %broadcast_in_dim.12), calls=%async_computation.1 | async-start | bytes 786432 | tf_op jit(solution)/shard_map/all_to_all | solution.py:174
  59.8 8.2 %all-to-all-done.1 = f32[16,3,16,128]{3,2,1,0:T(8,128)S(1)} async-done(((f32[16,3,16,128]{3,2,1,0:T(8,128)}), f32[16,3,16,128]{3,2,1,0:T(8,128)S(1)}, u32[]{:S(2)}, u32[]{:S(2)}) %all-to-all-start.1) | async-done | bytes 393248 | tf_op jit(solution)/shard_map/all_to_all | solution.py:174
  68.0 5.8 %collective-permute-start.2 = (f32[3,256,128]{2,1,0:T(8,128)S(1)}, f32[3,256,128]{2,1,0:T(8,128)S(1)}, u32[]{:S(2)}, u32[]{:S(2)}) collective-permute-start(f32[3,256,128]{2,1,0:T(8,128)S(1)} %bitcast.225), channel_id=1, source_target_pairs={{0,1},{1,2},{2,3},{3,4},{4,5},{5,6},{6,7},{8,9},{9,10},{10,11},{11... | collective-permute-start | bytes 1179656 | tf_op jit(solution)/shard_map/ppermute | solution.py:176
  78.5 4.4 %collective-permute-done.3 = f32[3,256,128]{2,1,0:T(8,128)S(1)} collective-permute-done((f32[3,256,128]{2,1,0:T(8,128)S(1)}, f32[3,256,128]{2,1,0:T(8,128)S(1)}, u32[]{:S(2)}, u32[]{:S(2)}) %collective-permute-start.3) | collective-permute-done | bytes 393248 | tf_op jit(solution)/shard_map/ppermute | solution.py:177
  99.1 13.6 %all_to_all.38 = f32[128,1,2]{2,1,0:T(1,128)S(1)} all-to-all(f32[128,1,2]{2,1,0:T(1,128)S(1)} %broadcast_in_dim.13), channel_id=1, replica_groups=mesh['az'=16,'rg'=8] {'az','rg'}, dimensions={0} | all-to-all | bytes 2048 | tf_op jit(solution)/shard_map/all_to_all | solution.py:190
  118.4 3.0 %collective-permute-done.5 = f32[2,256]{1,0:T(2,128)S(1)} collective-permute-done((f32[2,256]{1,0:T(2,128)S(1)}, f32[2,256]{1,0:T(2,128)S(1)}, u32[]{:S(2)}, u32[]{:S(2)}) %collective-permute-start.5) | collective-permute-done | bytes 2080 | tf_op jit(solution)/shard_map/ppermute | solution.py:42
  121.5 4.1 %collective-permute-start.6 = (f32[36,2]{1,0:T(8,128)S(1)}, f32[36,2]{1,0:T(8,128)S(1)}, u32[]{:S(2)}, u32[]{:S(2)}) collective-permute-start(f32[36,2]{1,0:T(8,128)S(1)} %get-tuple-element.33), channel_id=1, source_target_pairs={{0,1},{1,2},{2,3},{3,4},{4,5},{5,6},{6,7},{8,9},{9,10},{10,11},{11... | collective-permute-start | bytes 872 | tf_op jit(solution)/shard_map/ppermute | solution.py:44
  127.6 3.2 %collective-permute-done.7 = f32[36,2]{1,0:T(8,128)S(1)} collective-permute-done((f32[36,2]{1,0:T(8,128)S(1)}, f32[36,2]{1,0:T(8,128)S(1)}, u32[]{:S(2)}, u32[]{:S(2)}) %collective-permute-start.7) | collective-permute-done | bytes 320 | tf_op jit(solution)/shard_map/ppermute | solution.py:45
  131.4 13.5 %all_to_all.39 = f32[16,1,16,128]{3,2,1,0:T(8,128)S(1)} all-to-all(f32[16,1,16,128]{3,2,1,0:T(8,128)S(1)} %broadcast_in_dim.14), channel_id=1, replica_groups=mesh['az'=16,'rg'=8] {'az'}, dimensions={0} | all-to-all | bytes 262144 | tf_op jit(solution)/shard_map/all_to_all | solution.py:174
  144.9 3.5 %collective-permute-start.8 = (f32[1,256,128]{2,1,0:T(8,128)S(1)}, f32[1,256,128]{2,1,0:T(8,128)S(1)}, u32[]{:S(2)}, u32[]{:S(2)}) collective-permute-start(f32[1,256,128]{2,1,0:T(8,128)S(1)} %bitcast.233), channel_id=1, source_target_pairs={{0,1},{1,2},{2,3},{3,4},{4,5},{5,6},{6,7},{8,9},{9,10},{10,11},{11... | collective-permute-start | bytes 393224 | tf_op jit(solution)/shard_map/ppermute | solution.py:176
  150.5 4.1 %collective-permute-done.9 = f32[1,256,128]{2,1,0:T(8,128)S(1)} collective-permute-done((f32[1,256,128]{2,1,0:T(8,128)S(1)}, f32[1,256,128]{2,1,0:T(8,128)S(1)}, u32[]{:S(2)}, u32[]{:S(2)}) %collective-permute-start.9) | collective-permute-done | bytes 131104 | tf_op jit(solution)/shard_map/ppermute | solution.py:177
  163.8 14.0 %all_to_all.40 = f32[128,1,3]{2,1,0:T(1,128)S(1)} all-to-all(f32[128,1,3]{2,1,0:T(1,128)S(1)} %broadcast_in_dim.15), channel_id=1, replica_groups=mesh['az'=16,'rg'=8] {'az','rg'}, dimensions={0} | all-to-all | bytes 3072 | tf_op jit(solution)/shard_map/all_to_all | solution.py:190
  189.3 4.1 %collective-permute-start.12 = (f32[36,2]{1,0:T(8,128)S(1)}, f32[36,2]{1,0:T(8,128)S(1)}, u32[]{:S(2)}, u32[]{:S(2)}) collective-permute-start(f32[36,2]{1,0:T(8,128)S(1)} %get-tuple-element.31), channel_id=1, source_target_pairs={{0,1},{1,2},{2,3},{3,4},{4,5},{5,6},{6,7},{8,9},{9,10},{10,11},{11... | collective-permute-start | bytes 872 | tf_op jit(solution)/shard_map/ppermute | solution.py:44
  195.4 3.2 %collective-permute-done.13 = f32[36,2]{1,0:T(8,128)S(1)} collective-permute-done((f32[36,2]{1,0:T(8,128)S(1)}, f32[36,2]{1,0:T(8,128)S(1)}, u32[]{:S(2)}, u32[]{:S(2)}) %collective-permute-start.13) | collective-permute-done | bytes 320 | tf_op jit(solution)/shard_map/ppermute | solution.py:45
  199.1 13.5 %all_to_all.41 = f32[16,1,16,128]{3,2,1,0:T(8,128)S(1)} all-to-all(f32[16,1,16,128]{3,2,1,0:T(8,128)S(1)} %broadcast_in_dim.16), channel_id=1, replica_groups=mesh['az'=16,'rg'=8] {'az'}, dimensions={0} | all-to-all | bytes 262144 | tf_op jit(solution)/shard_map/all_to_all | solution.py:174
  212.6 3.5 %collective-permute-start.14 = (f32[1,256,128]{2,1,0:T(8,128)S(1)}, f32[1,256,128]{2,1,0:T(8,128)S(1)}, u32[]{:S(2)}, u32[]{:S(2)}) collective-permute-start(f32[1,256,128]{2,1,0:T(8,128)S(1)} %bitcast.228), channel_id=1, source_target_pairs={{0,1},{1,2},{2,3},{3,4},{4,5},{5,6},{6,7},{8,9},{9,10},{10,11},{11... | collective-permute-start | bytes 393224 | tf_op jit(solution)/shard_map/ppermute | solution.py:176
  218.1 4.3 %collective-permute-done.15 = f32[1,256,128]{2,1,0:T(8,128)S(1)} collective-permute-done((f32[1,256,128]{2,1,0:T(8,128)S(1)}, f32[1,256,128]{2,1,0:T(8,128)S(1)}, u32[]{:S(2)}, u32[]{:S(2)}) %collective-permute-start.15) | collective-permute-done | bytes 131104 | tf_op jit(solution)/shard_map/ppermute | solution.py:177
  232.1 4.6 %all-to-all-start.6 = ((f32[128,1,3]{2,1,0:T(1,128)}), f32[128,1,3]{2,1,0:T(1,128)S(1)}, u32[]{:S(2)}, u32[]{:S(2)}) async-start(f32[128,1,3]{2,1,0:T(1,128)} %broadcast_in_dim.17), calls=%async_computation.6 | async-start | bytes 131072 | tf_op jit(solution)/shard_map/all_to_all | solution.py:190
  237.4 8.9 %all-to-all-done.6 = f32[128,1,3]{2,1,0:T(1,128)S(1)} async-done(((f32[128,1,3]{2,1,0:T(1,128)}), f32[128,1,3]{2,1,0:T(1,128)S(1)}, u32[]{:S(2)}, u32[]{:S(2)}) %all-to-all-start.6) | async-done | bytes 1568 | tf_op jit(solution)/shard_map/all_to_all | solution.py:190
  (243 shorter events, 78.8 us)
Async XLA Ops:
  28.9 11.2 %all-to-all-start = ((f32[8,3,4,262]{3,2,1,0:T(4,128)}), f32[8,3,4,262]{3,2,1,0:T(4,128)S(1)}, u32[]{:S(2)}, u32[]{:S(2)}) async-start(f32[8,3,4,262]{3,2,1,0:T(4,128)} %fusion.551), calls=%async_computation | async-start | bytes 294912 | tf_op jit(solution)/shard_map/all_to_all | solution.py:231
  40.2 4.5 %collective-permute-start = (f32[3,3,262]{2,1,0:T(4,128)S(1)}, f32[3,3,262]{2,1,0:T(4,128)S(1)}, u32[]{:S(2)}, u32[]{:S(2)}) collective-permute-start(f32[3,3,262]{2,1,0:T(4,128)S(1)} %get-tuple-element.29), channel_id=1, source_target_pairs={{0,8},{8,16},{16,24},{24,32},{32,40},{40,48},{48,56},{56,64},{64,7... | collective-permute-start | bytes 28304 | tf_op jit(solution)/shard_map/ppermute | solution.py:234
  43.4 4.5 %collective-permute-start.1 = (f32[3,3,262]{2,1,0:T(4,128)S(1)}, f32[3,3,262]{2,1,0:T(4,128)S(1)}, u32[]{:S(2)}, u32[]{:S(2)}) collective-permute-start(f32[3,3,262]{2,1,0:T(4,128)S(1)} %get-tuple-element.30), channel_id=1, source_target_pairs={{8,0},{16,8},{24,16},{32,24},{40,32},{48,40},{56,48},{64,56},{72,6... | collective-permute-start | bytes 28304 | tf_op jit(solution)/shard_map/ppermute | solution.py:235
  50.5 17.5 %all-to-all-start.1 = ((f32[16,3,16,128]{3,2,1,0:T(8,128)}), f32[16,3,16,128]{3,2,1,0:T(8,128)S(1)}, u32[]{:S(2)}, u32[]{:S(2)}) async-start(f32[16,3,16,128]{3,2,1,0:T(8,128)} %broadcast_in_dim.12), calls=%async_computation.1 | async-start | bytes 786432 | tf_op jit(solution)/shard_map/all_to_all | solution.py:174
  68.0 10.5 %collective-permute-start.2 = (f32[3,256,128]{2,1,0:T(8,128)S(1)}, f32[3,256,128]{2,1,0:T(8,128)S(1)}, u32[]{:S(2)}, u32[]{:S(2)}) collective-permute-start(f32[3,256,128]{2,1,0:T(8,128)S(1)} %bitcast.225), channel_id=1, source_target_pairs={{0,1},{1,2},{2,3},{3,4},{4,5},{5,6},{6,7},{8,9},{9,10},{10,11},{11... | collective-permute-start | bytes 1179656 | tf_op jit(solution)/shard_map/ppermute | solution.py:176
  73.8 9.1 %collective-permute-start.3 = (f32[3,256,128]{2,1,0:T(8,128)S(1)}, f32[3,256,128]{2,1,0:T(8,128)S(1)}, u32[]{:S(2)}, u32[]{:S(2)}) collective-permute-start(f32[3,256,128]{2,1,0:T(8,128)S(1)} %bitcast.226), channel_id=1, source_target_pairs={{1,0},{2,1},{3,2},{4,3},{5,4},{6,5},{7,6},{9,8},{10,9},{11,10},{12... | collective-permute-start | bytes 1179656 | tf_op jit(solution)/shard_map/ppermute | solution.py:177
  114.8 3.6 %collective-permute-start.4 = (f32[2,256]{1,0:T(2,128)S(1)}, f32[2,256]{1,0:T(2,128)S(1)}, u32[]{:S(2)}, u32[]{:S(2)}) collective-permute-start(f32[2,256]{1,0:T(2,128)S(1)} %get-tuple-element.37), channel_id=1, source_target_pairs={{0,8},{8,16},{16,24},{24,32},{32,40},{40,48},{48,56},{56,64},{64,7... | collective-permute-start | bytes 6152 | tf_op jit(solution)/shard_map/ppermute | solution.py:41
  117.1 4.3 %collective-permute-start.5 = (f32[2,256]{1,0:T(2,128)S(1)}, f32[2,256]{1,0:T(2,128)S(1)}, u32[]{:S(2)}, u32[]{:S(2)}) collective-permute-start(f32[2,256]{1,0:T(2,128)S(1)} %get-tuple-element.38), channel_id=1, source_target_pairs={{8,0},{16,8},{24,16},{32,24},{40,32},{48,40},{56,48},{64,56},{72,6... | collective-permute-start | bytes 6152 | tf_op jit(solution)/shard_map/ppermute | solution.py:42
  121.5 6.1 %collective-permute-start.6 = (f32[36,2]{1,0:T(8,128)S(1)}, f32[36,2]{1,0:T(8,128)S(1)}, u32[]{:S(2)}, u32[]{:S(2)}) collective-permute-start(f32[36,2]{1,0:T(8,128)S(1)} %get-tuple-element.33), channel_id=1, source_target_pairs={{0,1},{1,2},{2,3},{3,4},{4,5},{5,6},{6,7},{8,9},{9,10},{10,11},{11... | collective-permute-start | bytes 872 | tf_op jit(solution)/shard_map/ppermute | solution.py:44
  125.7 5.1 %collective-permute-start.7 = (f32[36,2]{1,0:T(8,128)S(1)}, f32[36,2]{1,0:T(8,128)S(1)}, u32[]{:S(2)}, u32[]{:S(2)}) collective-permute-start(f32[36,2]{1,0:T(8,128)S(1)} %get-tuple-element.34), channel_id=1, source_target_pairs={{1,0},{2,1},{3,2},{4,3},{5,4},{6,5},{7,6},{9,8},{10,9},{11,10},{12... | collective-permute-start | bytes 872 | tf_op jit(solution)/shard_map/ppermute | solution.py:45
  144.9 5.6 %collective-permute-start.8 = (f32[1,256,128]{2,1,0:T(8,128)S(1)}, f32[1,256,128]{2,1,0:T(8,128)S(1)}, u32[]{:S(2)}, u32[]{:S(2)}) collective-permute-start(f32[1,256,128]{2,1,0:T(8,128)S(1)} %bitcast.233), channel_id=1, source_target_pairs={{0,1},{1,2},{2,3},{3,4},{4,5},{5,6},{6,7},{8,9},{9,10},{10,11},{11... | collective-permute-start | bytes 393224 | tf_op jit(solution)/shard_map/ppermute | solution.py:176
  148.4 6.3 %collective-permute-start.9 = (f32[1,256,128]{2,1,0:T(8,128)S(1)}, f32[1,256,128]{2,1,0:T(8,128)S(1)}, u32[]{:S(2)}, u32[]{:S(2)}) collective-permute-start(f32[1,256,128]{2,1,0:T(8,128)S(1)} %bitcast.234), channel_id=1, source_target_pairs={{1,0},{2,1},{3,2},{4,3},{5,4},{6,5},{7,6},{9,8},{10,9},{11,10},{12... | collective-permute-start | bytes 393224 | tf_op jit(solution)/shard_map/ppermute | solution.py:177
  182.6 3.6 %collective-permute-start.10 = (f32[2,256]{1,0:T(2,128)S(1)}, f32[2,256]{1,0:T(2,128)S(1)}, u32[]{:S(2)}, u32[]{:S(2)}) collective-permute-start(f32[2,256]{1,0:T(2,128)S(1)} %get-tuple-element.35), channel_id=1, source_target_pairs={{0,8},{8,16},{16,24},{24,32},{32,40},{40,48},{48,56},{56,64},{64,7... | collective-permute-start | bytes 6152 | tf_op jit(solution)/shard_map/ppermute | solution.py:41
  184.9 4.3 %collective-permute-start.11 = (f32[2,256]{1,0:T(2,128)S(1)}, f32[2,256]{1,0:T(2,128)S(1)}, u32[]{:S(2)}, u32[]{:S(2)}) collective-permute-start(f32[2,256]{1,0:T(2,128)S(1)} %get-tuple-element.36), channel_id=1, source_target_pairs={{8,0},{16,8},{24,16},{32,24},{40,32},{48,40},{56,48},{64,56},{72,6... | collective-permute-start | bytes 6152 | tf_op jit(solution)/shard_map/ppermute | solution.py:42
  189.3 6.1 %collective-permute-start.12 = (f32[36,2]{1,0:T(8,128)S(1)}, f32[36,2]{1,0:T(8,128)S(1)}, u32[]{:S(2)}, u32[]{:S(2)}) collective-permute-start(f32[36,2]{1,0:T(8,128)S(1)} %get-tuple-element.31), channel_id=1, source_target_pairs={{0,1},{1,2},{2,3},{3,4},{4,5},{5,6},{6,7},{8,9},{9,10},{10,11},{11... | collective-permute-start | bytes 872 | tf_op jit(solution)/shard_map/ppermute | solution.py:44
  193.4 5.1 %collective-permute-start.13 = (f32[36,2]{1,0:T(8,128)S(1)}, f32[36,2]{1,0:T(8,128)S(1)}, u32[]{:S(2)}, u32[]{:S(2)}) collective-permute-start(f32[36,2]{1,0:T(8,128)S(1)} %get-tuple-element.32), channel_id=1, source_target_pairs={{1,0},{2,1},{3,2},{4,3},{5,4},{6,5},{7,6},{9,8},{10,9},{11,10},{12... | collective-permute-start | bytes 872 | tf_op jit(solution)/shard_map/ppermute | solution.py:45
  212.6 5.4 %collective-permute-start.14 = (f32[1,256,128]{2,1,0:T(8,128)S(1)}, f32[1,256,128]{2,1,0:T(8,128)S(1)}, u32[]{:S(2)}, u32[]{:S(2)}) collective-permute-start(f32[1,256,128]{2,1,0:T(8,128)S(1)} %bitcast.228), channel_id=1, source_target_pairs={{0,1},{1,2},{2,3},{3,4},{4,5},{5,6},{6,7},{8,9},{9,10},{10,11},{11... | collective-permute-start | bytes 393224 | tf_op jit(solution)/shard_map/ppermute | solution.py:176
  216.1 6.3 %collective-permute-start.15 = (f32[1,256,128]{2,1,0:T(8,128)S(1)}, f32[1,256,128]{2,1,0:T(8,128)S(1)}, u32[]{:S(2)}, u32[]{:S(2)}) collective-permute-start(f32[1,256,128]{2,1,0:T(8,128)S(1)} %bitcast.229), channel_id=1, source_target_pairs={{1,0},{2,1},{3,2},{4,3},{5,4},{6,5},{7,6},{9,8},{10,9},{11,10},{12... | collective-permute-start | bytes 393224 | tf_op jit(solution)/shard_map/ppermute | solution.py:177
  232.1 14.2 %all-to-all-start.6 = ((f32[128,1,3]{2,1,0:T(1,128)}), f32[128,1,3]{2,1,0:T(1,128)S(1)}, u32[]{:S(2)}, u32[]{:S(2)}) async-start(f32[128,1,3]{2,1,0:T(1,128)} %broadcast_in_dim.17), calls=%async_computation.6 | async-start | bytes 131072 | tf_op jit(solution)/shard_map/all_to_all | solution.py:190

commit v3 on v2

--- a/solution.py
+++ b/solution.py
@@ -289,7 +289,9 @@
 
     solution = jnp.zeros_like(rhs)
     residual = rhs
-    precond, image_vec = precondition(residual, rhs_wide)
+    residual_wide = rhs_wide
+    precond, image_vec = precondition(residual, residual_wide)
+    image_wide = extended(image_vec, 2) if ITERS > 1 else None
     direction = precond
     sums = total(jnp.stack([jnp.sum(residual * precond), jnp.sum(direction * image_vec)]))
     norm_now = sums[0]
@@ -298,14 +300,18 @@
         step_length = norm_now / curvature
         solution = solution + step_length * direction
         if step_index + 1 < ITERS:
-            residual = residual - step_length * image_vec
-            precond, image_z = precondition(residual)
+            residual_wide = residual_wide - step_length * image_wide
+            residual = residual_wide[2:-2, 2:-2]
+            precond, image_z = precondition(residual, residual_wide)
+            image_z_wide = extended(image_z, 2) if step_index + 2 < ITERS else None
             sums = total(jnp.stack([jnp.sum(residual * precond), jnp.sum(precond * image_z),
                                     jnp.sum(precond * image_vec)]))
             norm_next = sums[0]
             ratio = norm_next / norm_now
             direction = precond + ratio * direction
             image_vec = image_z + ratio * image_vec
+            if image_z_wide is not None:
+                image_wide = image_z_wide + ratio * image_wide
             curvature = sums[1] + 2.0 * ratio * sums[2] + ratio * ratio * curvature
             norm_now = norm_next
     return (solution, weight)

time: 252 us -> 235 us (0.933)
  blocking collectives: 54.7 us -> 26.3 us
  starting transfers between devices: 62.2 us -> 71.2 us
    all_to_all x2 -> x0, blocking collectives: 27.6 us -> none  [total(): got = lax.all_to_all(sent, ('az', 'rg'), 0, 0, tiled=True)]
    all_to_all x1 -> x3, waiting for transfers between devices: 8.91 us -> 18.9 us  [total(): got = lax.all_to_all(sent, ('az', 'rg'), 0, 0, tiled=True)]
    all_to_all x1 -> x3, starting transfers between devices: 4.56 us -> 13.5 us  [total(): got = lax.all_to_all(sent, ('az', 'rg'), 0, 0, tiled=True)]
    ppermute x2, waiting for transfers between devices: 6.04 us -> 0.01 us  [extended(): lax.ppermute(v[..., :width, :], 'az', [(i + 1, i) for i in range(n_az - 1)])]
    ppermute x2, starting transfers between devices: 8.25 us -> 5.68 us  [extended(): lax.ppermute(v[..., :, -width:], 'rg', [(i, i + 1) for i in range(n_rg -...]
    ppermute x2, waiting for transfers between devices: 6.33 us -> 3.78 us  [extended(): lax.ppermute(v[..., :, :width], 'rg', [(i + 1, i) for i in range(n_rg - 1)])]
  transfers between devices with their start and end apart: 19 -> 21, of which waited for: 12 -> 12; matrix products, arithmetic and copies ran while one was open for 0% -> 1% of each run, Pallas kernels for 0% -> 0%
where the time goes in v3:
time: 235 us; the launch traced here: 234 us
  starting transfers between devices  71.2 us (30%)
  waiting for transfers between devices  54.6 us (23%)
  other arithmetic  33.4 us (14%)
  matrix products  27.3 us (12%)
  blocking collectives  26.3 us (11%)
  between operations  11.5 us (5%)
  local copies, waits for them, and re-layouts  10.2 us (4%)
    all_to_all x2, blocking collectives, gather_strip(): got = lax.all_to_all(sent, 'az', 0, 0, tiled=True)  26.3 us
    all_to_all x3, waiting for transfers between devices, total(): got = lax.all_to_all(sent, ('az', 'rg'), 0, 0, tiled=True)  18.9 us
    add x1, other arithmetic, mean_multilook(): first_re * second_re + first_im * second_im  14.5 us
    dot_general x48, matrix products, sandwich(): inner = jnp.dot(left, vector, precision=HIGHEST)  13.8 us
    all_to_all x3, starting transfers between devices, total(): got = lax.all_to_all(sent, ('az', 'rg'), 0, 0, tiled=True)  13.5 us
    ppermute x3, starting transfers between devices, gather_strip(): left = lax.ppermute(column, 'rg', [(i, i + 1) for i in range(n_rg - 1)])  13.3 us
    ppermute x3, waiting for transfers between devices, gather_strip(): right = lax.ppermute(column, 'rg', [(i + 1, i) for i in range(n_rg - 1)])  12.9 us
    dot_general x48, matrix products, sandwich(): return jnp.dot(inner, right, precision=HIGHEST)  11 us
  transfers between devices with their start and end apart: 21, of which 12 were waited for; matrix products, arithmetic and copies ran while one was open for 1% of the time, Pallas kernels for 0%

profile of v3, /device:TPU:1, one launch (start us, length us, event | category | flops | bytes accessed | tf_op | source)
XLA Modules:
  0.0 234.3 jit_solution(7282702436519990266)
XLA Ops:
  5.2 14.5 %add_reduce_fusion.2 = (f32[20,10240]{1,0:T(8,128)S(1)}, f32[20,10240]{1,0:T(8,128)S(1)}, f32[20,10240]{1,0:T(8,128)S(1)}, f32[20,10240]{1,0:T(8,128)S(1)}) fusion(bf16[2,20,10240]{2,0,1:T(2,128)(2,1)} %param.4, pred[10240]{0:T(1024)(128)(4,1)S(1)} %fusion.372, pred[20]{0:T(512)(128)(4,1)S(1)} %compare_and_fusion.9, bf16[2,20,10240]{2,0,1:T(2,128)(2,1)} %param.5), kind=kLoop, calls=%fused_computation.34 | loop fusion | flops 4300800 | bytes 4925460 | tf_op jit(solution)/shard_map/add | solution.py:70
  28.9 5.8 %all-to-all-start = ((f32[8,3,4,262]{3,2,1,0:T(4,128)}), f32[8,3,4,262]{3,2,1,0:T(4,128)S(1)}, u32[]{:S(2)}, u32[]{:S(2)}) async-start(f32[8,3,4,262]{3,2,1,0:T(4,128)} %fusion.555), calls=%async_computation | async-start | bytes 294912 | tf_op jit(solution)/shard_map/all_to_all | solution.py:231
  35.1 5.1 %all-to-all-done = f32[8,3,4,262]{3,2,1,0:T(4,128)S(1)} async-done(((f32[8,3,4,262]{3,2,1,0:T(4,128)}), f32[8,3,4,262]{3,2,1,0:T(4,128)S(1)}, u32[]{:S(2)}, u32[]{:S(2)}) %all-to-all-start) | async-done | bytes 100640 | tf_op jit(solution)/shard_map/all_to_all | solution.py:231
  40.2 3.2 %collective-permute-start = (f32[3,3,262]{2,1,0:T(4,128)S(1)}, f32[3,3,262]{2,1,0:T(4,128)S(1)}, u32[]{:S(2)}, u32[]{:S(2)}) collective-permute-start(f32[3,3,262]{2,1,0:T(4,128)S(1)} %get-tuple-element.29), channel_id=1, source_target_pairs={{0,8},{8,16},{16,24},{24,32},{32,40},{40,48},{48,56},{56,64},{64,7... | collective-permute-start | bytes 28304 | tf_op jit(solution)/shard_map/ppermute | solution.py:234
  44.7 3.2 %collective-permute-done.1 = f32[3,3,262]{2,1,0:T(4,128)S(1)} collective-permute-done((f32[3,3,262]{2,1,0:T(4,128)S(1)}, f32[3,3,262]{2,1,0:T(4,128)S(1)}, u32[]{:S(2)}, u32[]{:S(2)}) %collective-permute-start.1) | collective-permute-done | bytes 9464 | tf_op jit(solution)/shard_map/ppermute | solution.py:235
  50.5 9.2 %all-to-all-start.1 = ((f32[16,3,16,128]{3,2,1,0:T(8,128)}), f32[16,3,16,128]{3,2,1,0:T(8,128)S(1)}, u32[]{:S(2)}, u32[]{:S(2)}) async-start(f32[16,3,16,128]{3,2,1,0:T(8,128)} %broadcast_in_dim.12), calls=%async_computation.1 | async-start | bytes 786432 | tf_op jit(solution)/shard_map/all_to_all | solution.py:174
  59.8 8.2 %all-to-all-done.1 = f32[16,3,16,128]{3,2,1,0:T(8,128)S(1)} async-done(((f32[16,3,16,128]{3,2,1,0:T(8,128)}), f32[16,3,16,128]{3,2,1,0:T(8,128)S(1)}, u32[]{:S(2)}, u32[]{:S(2)}) %all-to-all-start.1) | async-done | bytes 393248 | tf_op jit(solution)/shard_map/all_to_all | solution.py:174
  68.0 5.8 %collective-permute-start.2 = (f32[3,256,128]{2,1,0:T(8,128)S(1)}, f32[3,256,128]{2,1,0:T(8,128)S(1)}, u32[]{:S(2)}, u32[]{:S(2)}) collective-permute-start(f32[3,256,128]{2,1,0:T(8,128)S(1)} %bitcast.225), channel_id=1, source_target_pairs={{0,1},{1,2},{2,3},{3,4},{4,5},{5,6},{6,7},{8,9},{9,10},{10,11},{11... | collective-permute-start | bytes 1179656 | tf_op jit(solution)/shard_map/ppermute | solution.py:176
  78.6 4.4 %collective-permute-done.3 = f32[3,256,128]{2,1,0:T(8,128)S(1)} collective-permute-done((f32[3,256,128]{2,1,0:T(8,128)S(1)}, f32[3,256,128]{2,1,0:T(8,128)S(1)}, u32[]{:S(2)}, u32[]{:S(2)}) %collective-permute-start.3) | collective-permute-done | bytes 393248 | tf_op jit(solution)/shard_map/ppermute | solution.py:177
  99.7 4.2 %all-to-all-start.2 = ((f32[128,1,2]{2,1,0:T(1,128)}), f32[128,1,2]{2,1,0:T(1,128)S(1)}, u32[]{:S(2)}, u32[]{:S(2)}) async-start(f32[128,1,2]{2,1,0:T(1,128)} %broadcast_in_dim.13), calls=%async_computation.2 | async-start | bytes 131072 | tf_op jit(solution)/shard_map/all_to_all | solution.py:190
  103.9 3.3 %collective-permute-start.4 = (f32[2,256]{1,0:T(2,128)S(1)}, f32[2,256]{1,0:T(2,128)S(1)}, u32[]{:S(2)}, u32[]{:S(2)}) collective-permute-start(f32[2,256]{1,0:T(2,128)S(1)} %get-tuple-element.37), channel_id=1, source_target_pairs={{0,8},{8,16},{16,24},{24,32},{32,40},{40,48},{48,56},{56,64},{64,7... | collective-permute-start | bytes 6152 | tf_op jit(solution)/shard_map/ppermute | solution.py:41
  108.5 5.0 %all-to-all-done.2 = f32[128,1,2]{2,1,0:T(1,128)S(1)} async-done(((f32[128,1,2]{2,1,0:T(1,128)}), f32[128,1,2]{2,1,0:T(1,128)S(1)}, u32[]{:S(2)}, u32[]{:S(2)}) %all-to-all-start.2) | async-done | bytes 1056 | tf_op jit(solution)/shard_map/all_to_all | solution.py:190
  114.3 2.8 %collective-permute-start.6 = (f32[36,2]{1,0:T(8,128)S(1)}, f32[36,2]{1,0:T(8,128)S(1)}, u32[]{:S(2)}, u32[]{:S(2)}) collective-permute-start(f32[36,2]{1,0:T(8,128)S(1)} %get-tuple-element.33), channel_id=1, source_target_pairs={{0,1},{1,2},{2,3},{3,4},{4,5},{5,6},{6,7},{8,9},{9,10},{10,11},{11... | collective-permute-start | bytes 872 | tf_op jit(solution)/shard_map/ppermute | solution.py:44
  122.9 14.5 %all_to_all.38 = f32[16,1,16,128]{3,2,1,0:T(8,128)S(1)} all-to-all(f32[16,1,16,128]{3,2,1,0:T(8,128)S(1)} %broadcast_in_dim.14), channel_id=1, replica_groups=mesh['az'=16,'rg'=8] {'az'}, dimensions={0} | all-to-all | bytes 262144 | tf_op jit(solution)/shard_map/all_to_all | solution.py:174
  137.4 3.7 %collective-permute-start.8 = (f32[1,256,128]{2,1,0:T(8,128)S(1)}, f32[1,256,128]{2,1,0:T(8,128)S(1)}, u32[]{:S(2)}, u32[]{:S(2)}) collective-permute-start(f32[1,256,128]{2,1,0:T(8,128)S(1)} %bitcast.233), channel_id=1, source_target_pairs={{0,1},{1,2},{2,3},{3,4},{4,5},{5,6},{6,7},{8,9},{9,10},{10,11},{11... | collective-permute-start | bytes 393224 | tf_op jit(solution)/shard_map/ppermute | solution.py:176
  143.3 4.1 %collective-permute-done.9 = f32[1,256,128]{2,1,0:T(8,128)S(1)} collective-permute-done((f32[1,256,128]{2,1,0:T(8,128)S(1)}, f32[1,256,128]{2,1,0:T(8,128)S(1)}, u32[]{:S(2)}, u32[]{:S(2)}) %collective-permute-start.9) | collective-permute-done | bytes 131104 | tf_op jit(solution)/shard_map/ppermute | solution.py:177
  157.3 4.6 %all-to-all-start.4 = ((f32[128,1,3]{2,1,0:T(1,128)}), f32[128,1,3]{2,1,0:T(1,128)S(1)}, u32[]{:S(2)}, u32[]{:S(2)}) async-start(f32[128,1,3]{2,1,0:T(1,128)} %broadcast_in_dim.15), calls=%async_computation.4 | async-start | bytes 131072 | tf_op jit(solution)/shard_map/all_to_all | solution.py:190
  161.9 3.3 %collective-permute-start.10 = (f32[2,256]{1,0:T(2,128)S(1)}, f32[2,256]{1,0:T(2,128)S(1)}, u32[]{:S(2)}, u32[]{:S(2)}) collective-permute-start(f32[2,256]{1,0:T(2,128)S(1)} %get-tuple-element.35), channel_id=1, source_target_pairs={{0,8},{8,16},{16,24},{24,32},{32,40},{40,48},{48,56},{56,64},{64,7... | collective-permute-start | bytes 6152 | tf_op jit(solution)/shard_map/ppermute | solution.py:41
  166.5 5.0 %all-to-all-done.4 = f32[128,1,3]{2,1,0:T(1,128)S(1)} async-done(((f32[128,1,3]{2,1,0:T(1,128)}), f32[128,1,3]{2,1,0:T(1,128)S(1)}, u32[]{:S(2)}, u32[]{:S(2)}) %all-to-all-start.4) | async-done | bytes 1568 | tf_op jit(solution)/shard_map/all_to_all | solution.py:190
  183.7 11.7 %all_to_all.39 = f32[16,1,16,128]{3,2,1,0:T(8,128)S(1)} all-to-all(f32[16,1,16,128]{3,2,1,0:T(8,128)S(1)} %broadcast_in_dim.16), channel_id=1, replica_groups=mesh['az'=16,'rg'=8] {'az'}, dimensions={0} | all-to-all | bytes 262144 | tf_op jit(solution)/shard_map/all_to_all | solution.py:174
  195.5 3.7 %collective-permute-start.14 = (f32[1,256,128]{2,1,0:T(8,128)S(1)}, f32[1,256,128]{2,1,0:T(8,128)S(1)}, u32[]{:S(2)}, u32[]{:S(2)}) collective-permute-start(f32[1,256,128]{2,1,0:T(8,128)S(1)} %bitcast.228), channel_id=1, source_target_pairs={{0,1},{1,2},{2,3},{3,4},{4,5},{5,6},{6,7},{8,9},{9,10},{10,11},{11... | collective-permute-start | bytes 393224 | tf_op jit(solution)/shard_map/ppermute | solution.py:176
  201.1 4.3 %collective-permute-done.15 = f32[1,256,128]{2,1,0:T(8,128)S(1)} collective-permute-done((f32[1,256,128]{2,1,0:T(8,128)S(1)}, f32[1,256,128]{2,1,0:T(8,128)S(1)}, u32[]{:S(2)}, u32[]{:S(2)}) %collective-permute-start.15) | collective-permute-done | bytes 131104 | tf_op jit(solution)/shard_map/ppermute | solution.py:177
  215.4 4.6 %all-to-all-start.6 = ((f32[128,1,3]{2,1,0:T(1,128)}), f32[128,1,3]{2,1,0:T(1,128)S(1)}, u32[]{:S(2)}, u32[]{:S(2)}) async-start(f32[128,1,3]{2,1,0:T(1,128)} %broadcast_in_dim.17), calls=%async_computation.6 | async-start | bytes 131072 | tf_op jit(solution)/shard_map/all_to_all | solution.py:190
  220.7 8.9 %all-to-all-done.6 = f32[128,1,3]{2,1,0:T(1,128)S(1)} async-done(((f32[128,1,3]{2,1,0:T(1,128)}), f32[128,1,3]{2,1,0:T(1,128)S(1)}, u32[]{:S(2)}, u32[]{:S(2)}) %all-to-all-start.6) | async-done | bytes 1568 | tf_op jit(solution)/shard_map/all_to_all | solution.py:190
  (243 shorter events, 79.4 us)
Async XLA Ops:
  28.9 11.2 %all-to-all-start = ((f32[8,3,4,262]{3,2,1,0:T(4,128)}), f32[8,3,4,262]{3,2,1,0:T(4,128)S(1)}, u32[]{:S(2)}, u32[]{:S(2)}) async-start(f32[8,3,4,262]{3,2,1,0:T(4,128)} %fusion.555), calls=%async_computation | async-start | bytes 294912 | tf_op jit(solution)/shard_map/all_to_all | solution.py:231
  40.2 4.5 %collective-permute-start = (f32[3,3,262]{2,1,0:T(4,128)S(1)}, f32[3,3,262]{2,1,0:T(4,128)S(1)}, u32[]{:S(2)}, u32[]{:S(2)}) collective-permute-start(f32[3,3,262]{2,1,0:T(4,128)S(1)} %get-tuple-element.29), channel_id=1, source_target_pairs={{0,8},{8,16},{16,24},{24,32},{32,40},{40,48},{48,56},{56,64},{64,7... | collective-permute-start | bytes 28304 | tf_op jit(solution)/shard_map/ppermute | solution.py:234
  43.4 4.5 %collective-permute-start.1 = (f32[3,3,262]{2,1,0:T(4,128)S(1)}, f32[3,3,262]{2,1,0:T(4,128)S(1)}, u32[]{:S(2)}, u32[]{:S(2)}) collective-permute-start(f32[3,3,262]{2,1,0:T(4,128)S(1)} %get-tuple-element.30), channel_id=1, source_target_pairs={{8,0},{16,8},{24,16},{32,24},{40,32},{48,40},{56,48},{64,56},{72,6... | collective-permute-start | bytes 28304 | tf_op jit(solution)/shard_map/ppermute | solution.py:235
  50.5 17.5 %all-to-all-start.1 = ((f32[16,3,16,128]{3,2,1,0:T(8,128)}), f32[16,3,16,128]{3,2,1,0:T(8,128)S(1)}, u32[]{:S(2)}, u32[]{:S(2)}) async-start(f32[16,3,16,128]{3,2,1,0:T(8,128)} %broadcast_in_dim.12), calls=%async_computation.1 | async-start | bytes 786432 | tf_op jit(solution)/shard_map/all_to_all | solution.py:174
  68.0 10.5 %collective-permute-start.2 = (f32[3,256,128]{2,1,0:T(8,128)S(1)}, f32[3,256,128]{2,1,0:T(8,128)S(1)}, u32[]{:S(2)}, u32[]{:S(2)}) collective-permute-start(f32[3,256,128]{2,1,0:T(8,128)S(1)} %bitcast.225), channel_id=1, source_target_pairs={{0,1},{1,2},{2,3},{3,4},{4,5},{5,6},{6,7},{8,9},{9,10},{10,11},{11... | collective-permute-start | bytes 1179656 | tf_op jit(solution)/shard_map/ppermute | solution.py:176
  73.9 9.1 %collective-permute-start.3 = (f32[3,256,128]{2,1,0:T(8,128)S(1)}, f32[3,256,128]{2,1,0:T(8,128)S(1)}, u32[]{:S(2)}, u32[]{:S(2)}) collective-permute-start(f32[3,256,128]{2,1,0:T(8,128)S(1)} %bitcast.226), channel_id=1, source_target_pairs={{1,0},{2,1},{3,2},{4,3},{5,4},{6,5},{7,6},{9,8},{10,9},{11,10},{12... | collective-permute-start | bytes 1179656 | tf_op jit(solution)/shard_map/ppermute | solution.py:177
  99.7 13.8 %all-to-all-start.2 = ((f32[128,1,2]{2,1,0:T(1,128)}), f32[128,1,2]{2,1,0:T(1,128)S(1)}, u32[]{:S(2)}, u32[]{:S(2)}) async-start(f32[128,1,2]{2,1,0:T(1,128)} %broadcast_in_dim.13), calls=%async_computation.2 | async-start | bytes 131072 | tf_op jit(solution)/shard_map/all_to_all | solution.py:190
  103.9 10.3 %collective-permute-start.4 = (f32[2,256]{1,0:T(2,128)S(1)}, f32[2,256]{1,0:T(2,128)S(1)}, u32[]{:S(2)}, u32[]{:S(2)}) collective-permute-start(f32[2,256]{1,0:T(2,128)S(1)} %get-tuple-element.37), channel_id=1, source_target_pairs={{0,8},{8,16},{16,24},{24,32},{32,40},{40,48},{48,56},{56,64},{64,7... | collective-permute-start | bytes 6152 | tf_op jit(solution)/shard_map/ppermute | solution.py:41
  107.2 7.0 %collective-permute-start.5 = (f32[2,256]{1,0:T(2,128)S(1)}, f32[2,256]{1,0:T(2,128)S(1)}, u32[]{:S(2)}, u32[]{:S(2)}) collective-permute-start(f32[2,256]{1,0:T(2,128)S(1)} %get-tuple-element.38), channel_id=1, source_target_pairs={{8,0},{16,8},{24,16},{32,24},{40,32},{48,40},{56,48},{64,56},{72,6... | collective-permute-start | bytes 6152 | tf_op jit(solution)/shard_map/ppermute | solution.py:42
  114.3 6.1 %collective-permute-start.6 = (f32[36,2]{1,0:T(8,128)S(1)}, f32[36,2]{1,0:T(8,128)S(1)}, u32[]{:S(2)}, u32[]{:S(2)}) collective-permute-start(f32[36,2]{1,0:T(8,128)S(1)} %get-tuple-element.33), channel_id=1, source_target_pairs={{0,1},{1,2},{2,3},{3,4},{4,5},{5,6},{6,7},{8,9},{9,10},{10,11},{11... | collective-permute-start | bytes 872 | tf_op jit(solution)/shard_map/ppermute | solution.py:44
  117.2 5.1 %collective-permute-start.7 = (f32[36,2]{1,0:T(8,128)S(1)}, f32[36,2]{1,0:T(8,128)S(1)}, u32[]{:S(2)}, u32[]{:S(2)}) collective-permute-start(f32[36,2]{1,0:T(8,128)S(1)} %get-tuple-element.34), channel_id=1, source_target_pairs={{1,0},{2,1},{3,2},{4,3},{5,4},{6,5},{7,6},{9,8},{10,9},{11,10},{12... | collective-permute-start | bytes 872 | tf_op jit(solution)/shard_map/ppermute | solution.py:45
  137.4 5.9 %collective-permute-start.8 = (f32[1,256,128]{2,1,0:T(8,128)S(1)}, f32[1,256,128]{2,1,0:T(8,128)S(1)}, u32[]{:S(2)}, u32[]{:S(2)}) collective-permute-start(f32[1,256,128]{2,1,0:T(8,128)S(1)} %bitcast.233), channel_id=1, source_target_pairs={{0,1},{1,2},{2,3},{3,4},{4,5},{5,6},{6,7},{8,9},{9,10},{10,11},{11... | collective-permute-start | bytes 393224 | tf_op jit(solution)/shard_map/ppermute | solution.py:176
  141.2 6.3 %collective-permute-start.9 = (f32[1,256,128]{2,1,0:T(8,128)S(1)}, f32[1,256,128]{2,1,0:T(8,128)S(1)}, u32[]{:S(2)}, u32[]{:S(2)}) collective-permute-start(f32[1,256,128]{2,1,0:T(8,128)S(1)} %bitcast.234), channel_id=1, source_target_pairs={{1,0},{2,1},{3,2},{4,3},{5,4},{6,5},{7,6},{9,8},{10,9},{11,10},{12... | collective-permute-start | bytes 393224 | tf_op jit(solution)/shard_map/ppermute | solution.py:177
  157.3 14.3 %all-to-all-start.4 = ((f32[128,1,3]{2,1,0:T(1,128)}), f32[128,1,3]{2,1,0:T(1,128)S(1)}, u32[]{:S(2)}, u32[]{:S(2)}) async-start(f32[128,1,3]{2,1,0:T(1,128)} %broadcast_in_dim.15), calls=%async_computation.4 | async-start | bytes 131072 | tf_op jit(solution)/shard_map/all_to_all | solution.py:190
  161.9 13.1 %collective-permute-start.10 = (f32[2,256]{1,0:T(2,128)S(1)}, f32[2,256]{1,0:T(2,128)S(1)}, u32[]{:S(2)}, u32[]{:S(2)}) collective-permute-start(f32[2,256]{1,0:T(2,128)S(1)} %get-tuple-element.35), channel_id=1, source_target_pairs={{0,8},{8,16},{16,24},{24,32},{32,40},{40,48},{48,56},{56,64},{64,7... | collective-permute-start | bytes 6152 | tf_op jit(solution)/shard_map/ppermute | solution.py:41
  165.2 9.8 %collective-permute-start.11 = (f32[2,256]{1,0:T(2,128)S(1)}, f32[2,256]{1,0:T(2,128)S(1)}, u32[]{:S(2)}, u32[]{:S(2)}) collective-permute-start(f32[2,256]{1,0:T(2,128)S(1)} %get-tuple-element.36), channel_id=1, source_target_pairs={{8,0},{16,8},{24,16},{32,24},{40,32},{48,40},{56,48},{64,56},{72,6... | collective-permute-start | bytes 6152 | tf_op jit(solution)/shard_map/ppermute | solution.py:42
  175.1 6.0 %collective-permute-start.12 = (f32[36,2]{1,0:T(8,128)S(1)}, f32[36,2]{1,0:T(8,128)S(1)}, u32[]{:S(2)}, u32[]{:S(2)}) collective-permute-start(f32[36,2]{1,0:T(8,128)S(1)} %get-tuple-element.31), channel_id=1, source_target_pairs={{0,1},{1,2},{2,3},{3,4},{4,5},{5,6},{6,7},{8,9},{9,10},{10,11},{11... | collective-permute-start | bytes 872 | tf_op jit(solution)/shard_map/ppermute | solution.py:44
  178.0 5.1 %collective-permute-start.13 = (f32[36,2]{1,0:T(8,128)S(1)}, f32[36,2]{1,0:T(8,128)S(1)}, u32[]{:S(2)}, u32[]{:S(2)}) collective-permute-start(f32[36,2]{1,0:T(8,128)S(1)} %get-tuple-element.32), channel_id=1, source_target_pairs={{1,0},{2,1},{3,2},{4,3},{5,4},{6,5},{7,6},{9,8},{10,9},{11,10},{12... | collective-permute-start | bytes 872 | tf_op jit(solution)/shard_map/ppermute | solution.py:45
  195.5 5.7 %collective-permute-start.14 = (f32[1,256,128]{2,1,0:T(8,128)S(1)}, f32[1,256,128]{2,1,0:T(8,128)S(1)}, u32[]{:S(2)}, u32[]{:S(2)}) collective-permute-start(f32[1,256,128]{2,1,0:T(8,128)S(1)} %bitcast.228), channel_id=1, source_target_pairs={{0,1},{1,2},{2,3},{3,4},{4,5},{5,6},{6,7},{8,9},{9,10},{10,11},{11... | collective-permute-start | bytes 393224 | tf_op jit(solution)/shard_map/ppermute | solution.py:176
  199.2 6.3 %collective-permute-start.15 = (f32[1,256,128]{2,1,0:T(8,128)S(1)}, f32[1,256,128]{2,1,0:T(8,128)S(1)}, u32[]{:S(2)}, u32[]{:S(2)}) collective-permute-start(f32[1,256,128]{2,1,0:T(8,128)S(1)} %bitcast.229), channel_id=1, source_target_pairs={{1,0},{2,1},{3,2},{4,3},{5,4},{6,5},{7,6},{9,8},{10,9},{11,10},{12... | collective-permute-start | bytes 393224 | tf_op jit(solution)/shard_map/ppermute | solution.py:177
  215.4 14.3 %all-to-all-start.6 = ((f32[128,1,3]{2,1,0:T(1,128)}), f32[128,1,3]{2,1,0:T(1,128)S(1)}, u32[]{:S(2)}, u32[]{:S(2)}) async-start(f32[128,1,3]{2,1,0:T(1,128)} %broadcast_in_dim.17), calls=%async_computation.6 | async-start | bytes 131072 | tf_op jit(solution)/shard_map/all_to_all | solution.py:190

commit v4 on v2

--- a/solution.py
+++ b/solution.py
@@ -222,7 +222,8 @@
     weight = 0.05 + 4.0 * (look_re * look_re + look_im * look_im) / jnp.maximum(
         power_one * power_two, 1.0
     )
-    border = 3
+    widest = 2 * ITERS
+    border = widest + 1
     fields = jnp.stack([look_re, look_im, weight])
     n_fields, rows_here, cols_all = fields.shape
     cols_here = cols_all // n_range
@@ -253,18 +254,24 @@
     west_w = edge_h[1:-1, :-1]
     south_w = edge_v[1:, 1:-1]
     north_w = edge_v[:-1, 1:-1]
-    diag_wide = east_w + west_w + south_w + north_w + MU * 4.0**0
+    diag_w = east_w + west_w + south_w + north_w + MU * 4.0**0
+    ops_w = (east_w, west_w, south_w, north_w, diag_w)
     rhs_wide = -(flux_h[1:-1, 1:] - flux_h[1:-1, :-1] + flux_v[1:, 1:-1] - flux_v[:-1, 1:-1])
-    rhs = rhs_wide[2:-2, 2:-2]
-    own = (slice(2, -2), slice(2, -2))
-    levels, coarse_edges = build_levels(east_w[own], west_w[own], south_w[own], north_w[own],
-                                        first_level=0, last_level=GATHER_LEVEL)
+
+    def crop(values, ring):
+        cut = (values.shape[-2] - shard_height_total) // 2 - ring
+        if cut == 0:
+            return values
+        return values[..., cut:-cut, cut:-cut]
+
+    def ops_at(ring):
+        return tuple(crop(x, ring) for x in ops_w)
+
+    levels, coarse_edges = build_levels(*ops_at(0)[:4], first_level=0, last_level=GATHER_LEVEL)
     block_h, block_w = coarse_edges[0].shape
     whole = {}
 
-    ring_ops = tuple(x[1:-1, 1:-1] for x in (east_w, west_w, south_w, north_w, diag_wide))
-
-    def coarse_solve(rhs_vec):
+    def coarse_solve(rhs_vec, ring):
         if not whole:
             got = gather_strip(jnp.stack([coarse_edges[0], coarse_edges[2], rhs_vec]))
             east_s, south_s = got[0], got[1]
@@ -274,38 +281,43 @@
         else:
             strip_rhs = gather_strip(rhs_vec[None])[0]
         strip_x = vcycle(strip_rhs, GATHER_LEVEL, whole["levels"], apply_padded, None)
-        strip_x = jnp.pad(strip_x, ((1, 1), (0, 0)))
-        return lax.dynamic_slice(strip_x, (segment_ordinal * block_h, block_w - 1),
-                                 (block_h + 2, block_w + 2))
-
-    def precondition(rhs_vec, rhs_wide=None):
-        if rhs_wide is None:
-            rhs_wide = extended(rhs_vec, 2)
-        estimate = OMEGA * rhs_wide / diag_wide
-        remain = rhs_vec - apply_inner(estimate[1:-1, 1:-1], levels[0])
-        estimate = estimate + prolong_copy(coarse_solve(restrict_sum(remain)))
-        ring = estimate[1:-1, 1:-1] + OMEGA * (rhs_wide[1:-1, 1:-1] - apply_inner(estimate, ring_ops)) / ring_ops[4]
-        return ring[1:-1, 1:-1], apply_inner(ring, levels[0])
-
-    solution = jnp.zeros_like(rhs)
-    residual = rhs
-    precond, image_vec = precondition(residual, rhs_wide)
+        coarse_ring = ring // 2
+        strip_x = jnp.pad(strip_x, ((coarse_ring, coarse_ring), (0, 0)))
+        return lax.dynamic_slice(strip_x, (segment_ordinal * block_h, block_w - coarse_ring),
+                                 (block_h + 2 * coarse_ring, block_w + 2 * coarse_ring))
+
+    def precondition(rhs_wide):
+        ring = (rhs_wide.shape[0] - shard_height_total) // 2
+        diag_here = ops_at(ring)[4]
+        estimate = OMEGA * rhs_wide / diag_here
+        remain = crop(rhs_wide, 0) - apply_inner(crop(estimate, 1), levels[0])
+        estimate = estimate + prolong_copy(coarse_solve(restrict_sum(remain), ring))
+        inner = ops_at(ring - 1)
+        smoothed = crop(estimate, ring - 1) + OMEGA * (crop(rhs_wide, ring - 1) - apply_inner(estimate, inner)) / inner[4]
+        return smoothed, apply_inner(smoothed, ops_at(ring - 2))
+
+    residual_wide = rhs_wide
+    precond, image_vec = precondition(residual_wide)
     direction = precond
-    sums = total(jnp.stack([jnp.sum(residual * precond), jnp.sum(direction * image_vec)]))
+    sums = total(jnp.stack([jnp.sum(crop(residual_wide, 0) * crop(precond, 0)),
+                            jnp.sum(crop(direction, 0) * crop(image_vec, 0))]))
     norm_now = sums[0]
     curvature = sums[1]
+    solution = jnp.zeros_like(crop(rhs_wide, 0))
     for step_index in range(ITERS):
         step_length = norm_now / curvature
-        solution = solution + step_length * direction
+        solution = solution + step_length * crop(direction, 0)
         if step_index + 1 < ITERS:
-            residual = residual - step_length * image_vec
-            precond, image_z = precondition(residual)
-            sums = total(jnp.stack([jnp.sum(residual * precond), jnp.sum(precond * image_z),
-                                    jnp.sum(precond * image_vec)]))
+            ring = (image_vec.shape[0] - shard_height_total) // 2
+            residual_wide = crop(residual_wide, ring) - step_length * image_vec
+            precond, image_z = precondition(residual_wide)
+            sums = total(jnp.stack([jnp.sum(crop(residual_wide, 0) * crop(precond, 0)),
+                                    jnp.sum(crop(precond, 0) * crop(image_z, 0)),
+                                    jnp.sum(crop(precond, 0) * crop(image_vec, 0))]))
             norm_next = sums[0]
             ratio = norm_next / norm_now
-            direction = precond + ratio * direction
-            image_vec = image_z + ratio * image_vec
+            direction = precond + ratio * crop(direction, ring - 1)
+            image_vec = image_z + ratio * crop(image_vec, ring - 2)
             curvature = sums[1] + 2.0 * ratio * sums[2] + ratio * ratio * curvature
             norm_now = norm_next
     return (solution, weight)

time: 252 us -> 218 us (0.87)
  blocking collectives: 54.7 us -> 0 us
  waiting for transfers between devices: 53.1 us -> 73.5 us
    all_to_all x4 -> x0, blocking collectives: 54.7 us -> none  [the longest x2 27.6 us: total(): got = lax.all_to_all(sent, ('az', 'rg'), 0, 0, tiled=True)]
    all_to_all x1 -> x3, waiting for transfers between devices: 8.91 us -> 28.6 us  [total(): got = lax.all_to_all(sent, ('az', 'rg'), 0, 0, tiled=True)]
    ppermute x8 -> x0, starting transfers between devices: 19.2 us -> none  [the longest x2 8.25 us: extended(): lax.ppermute(v[..., :, -width:], 'rg', [(i, i + 1) for i in range(n_rg -...]
    all_to_all x1 -> x3, waiting for transfers between devices: 8.19 us -> 21.7 us  [gather_strip(): got = lax.all_to_all(sent, 'az', 0, 0, tiled=True)]
    ppermute x8 -> x0, waiting for transfers between devices: 12.4 us -> none  [the longest x2 6.33 us: extended(): lax.ppermute(v[..., :, :width], 'rg', [(i + 1, i) for i in range(n_rg - 1)])]
    all_to_all x1 -> x3, starting transfers between devices: 4.56 us -> 13.3 us  [total(): got = lax.all_to_all(sent, ('az', 'rg'), 0, 0, tiled=True)]
    all_to_all x1 -> x3, starting transfers between devices: 9.25 us -> 16.3 us  [gather_strip(): got = lax.all_to_all(sent, 'az', 0, 0, tiled=True)]
  transfers between devices with their start and end apart: 19 -> 15, of which waited for: 12 -> 12; matrix products, arithmetic and copies ran while one was open for 0% -> 1% of each run, Pallas kernels for 0% -> 0%
where the time goes in v4:
time: 218 us; the launch traced here: 217 us
  waiting for transfers between devices  73.5 us (34%)
  starting transfers between devices  59.8 us (27%)
  other arithmetic  33.7 us (15%)
  matrix products  27.3 us (13%)
  between operations  11.5 us (5%)
  local copies, waits for them, and re-layouts  11.3 us (5%)
    all_to_all x3, waiting for transfers between devices, total(): got = lax.all_to_all(sent, ('az', 'rg'), 0, 0, tiled=True)  28.6 us
    all_to_all x3, waiting for transfers between devices, gather_strip(): got = lax.all_to_all(sent, 'az', 0, 0, tiled=True)  21.7 us
    all_to_all x3, starting transfers between devices, gather_strip(): got = lax.all_to_all(sent, 'az', 0, 0, tiled=True)  16.3 us
    add x1, other arithmetic, mean_multilook(): first_re * second_re + first_im * second_im  14.5 us
    dot_general x48, matrix products, sandwich(): inner = jnp.dot(left, vector, precision=HIGHEST)  13.8 us
    ppermute x3, starting transfers between devices, gather_strip(): left = lax.ppermute(column, 'rg', [(i, i + 1) for i in range(n_rg - 1)])  13.8 us
    all_to_all x3, starting transfers between devices, total(): got = lax.all_to_all(sent, ('az', 'rg'), 0, 0, tiled=True)  13.3 us
    ppermute x3, waiting for transfers between devices, gather_strip(): right = lax.ppermute(column, 'rg', [(i + 1, i) for i in range(n_rg - 1)])  12.2 us
  transfers between devices with their start and end apart: 15, of which 12 were waited for; matrix products, arithmetic and copies ran while one was open for 1% of the time, Pallas kernels for 0%

profile of v4, /device:TPU:1, one launch (start us, length us, event | category | flops | bytes accessed | tf_op | source)
XLA Modules:
  0.0 217.1 jit_solution(12787506567380007589)
XLA Ops:
  5.1 14.5 %add_reduce_fusion.2 = (f32[20,10240]{1,0:T(8,128)S(1)}, f32[20,10240]{1,0:T(8,128)S(1)}, f32[20,10240]{1,0:T(8,128)S(1)}, f32[20,10240]{1,0:T(8,128)S(1)}) fusion(bf16[2,20,10240]{2,0,1:T(2,128)(2,1)} %param.4, pred[10240]{0:T(1024)(128)(4,1)S(1)} %fusion.380, pred[20]{0:T(512)(128)(4,1)S(1)} %compare_and_fusion.11, bf16[2,20,10240]{2,0,1:T(2,128)(2,1)} %param.5), kind=kLoop, calls=%fused_computation.34 | loop fusion | flops 4300800 | bytes 4925460 | tf_op jit(solution)/shard_map/add | solution.py:70
  28.9 5.8 %all-to-all-start = ((f32[8,3,4,270]{3,2,1,0:T(4,128)}), f32[8,3,4,270]{3,2,1,0:T(4,128)S(1)}, u32[]{:S(2)}, u32[]{:S(2)}) async-start(f32[8,3,4,270]{3,2,1,0:T(4,128)} %fusion.564), calls=%async_computation | async-start | bytes 294912 | tf_op jit(solution)/shard_map/all_to_all | solution.py:232
  35.0 5.1 %all-to-all-done = f32[8,3,4,270]{3,2,1,0:T(4,128)S(1)} async-done(((f32[8,3,4,270]{3,2,1,0:T(4,128)}), f32[8,3,4,270]{3,2,1,0:T(4,128)S(1)}, u32[]{:S(2)}, u32[]{:S(2)}) %all-to-all-start) | async-done | bytes 103712 | tf_op jit(solution)/shard_map/all_to_all | solution.py:232
  40.2 3.2 %collective-permute-start = (f32[3,7,270]{2,1,0:T(8,128)S(1)}, f32[3,7,270]{2,1,0:T(8,128)S(1)}, u32[]{:S(2)}, u32[]{:S(2)}) collective-permute-start(f32[3,7,270]{2,1,0:T(8,128)S(1)} %get-tuple-element.28), channel_id=1, source_target_pairs={{0,8},{8,16},{16,24},{24,32},{32,40},{40,48},{48,56},{56,64},{64,7... | collective-permute-start | bytes 68048 | tf_op jit(solution)/shard_map/ppermute | solution.py:235
  44.7 3.4 %collective-permute-done.1 = f32[3,7,270]{2,1,0:T(8,128)S(1)} collective-permute-done((f32[3,7,270]{2,1,0:T(8,128)S(1)}, f32[3,7,270]{2,1,0:T(8,128)S(1)}, u32[]{:S(2)}, u32[]{:S(2)}) %collective-permute-start.1) | collective-permute-done | bytes 22712 | tf_op jit(solution)/shard_map/ppermute | solution.py:236
  50.7 9.2 %all-to-all-start.1 = ((f32[16,3,16,128]{3,2,1,0:T(8,128)}), f32[16,3,16,128]{3,2,1,0:T(8,128)S(1)}, u32[]{:S(2)}, u32[]{:S(2)}) async-start(f32[16,3,16,128]{3,2,1,0:T(8,128)} %broadcast_in_dim.12), calls=%async_computation.1 | async-start | bytes 786432 | tf_op jit(solution)/shard_map/all_to_all | solution.py:174
  60.0 8.2 %all-to-all-done.1 = f32[16,3,16,128]{3,2,1,0:T(8,128)S(1)} async-done(((f32[16,3,16,128]{3,2,1,0:T(8,128)}), f32[16,3,16,128]{3,2,1,0:T(8,128)S(1)}, u32[]{:S(2)}, u32[]{:S(2)}) %all-to-all-start.1) | async-done | bytes 393248 | tf_op jit(solution)/shard_map/all_to_all | solution.py:174
  68.2 5.8 %collective-permute-start.2 = (f32[3,256,128]{2,1,0:T(8,128)S(1)}, f32[3,256,128]{2,1,0:T(8,128)S(1)}, u32[]{:S(2)}, u32[]{:S(2)}) collective-permute-start(f32[3,256,128]{2,1,0:T(8,128)S(1)} %bitcast.225), channel_id=1, source_target_pairs={{0,1},{1,2},{2,3},{3,4},{4,5},{5,6},{6,7},{8,9},{9,10},{10,11},{11... | collective-permute-start | bytes 1179656 | tf_op jit(solution)/shard_map/ppermute | solution.py:176
  76.2 2.5 %collective-permute-done.2 = f32[3,256,128]{2,1,0:T(8,128)S(1)} collective-permute-done((f32[3,256,128]{2,1,0:T(8,128)S(1)}, f32[3,256,128]{2,1,0:T(8,128)S(1)}, u32[]{:S(2)}, u32[]{:S(2)}) %collective-permute-start.2) | collective-permute-done | bytes 393248 | tf_op jit(solution)/shard_map/ppermute | solution.py:176
  78.8 4.4 %collective-permute-done.3 = f32[3,256,128]{2,1,0:T(8,128)S(1)} collective-permute-done((f32[3,256,128]{2,1,0:T(8,128)S(1)}, f32[3,256,128]{2,1,0:T(8,128)S(1)}, u32[]{:S(2)}, u32[]{:S(2)}) %collective-permute-start.3) | collective-permute-done | bytes 393248 | tf_op jit(solution)/shard_map/ppermute | solution.py:177
  100.1 4.2 %all-to-all-start.2 = ((f32[128,1,2]{2,1,0:T(1,128)}), f32[128,1,2]{2,1,0:T(1,128)S(1)}, u32[]{:S(2)}, u32[]{:S(2)}) async-start(f32[128,1,2]{2,1,0:T(1,128)} %broadcast_in_dim.13), calls=%async_computation.2 | async-start | bytes 131072 | tf_op jit(solution)/shard_map/all_to_all | solution.py:190
  104.3 9.6 %all-to-all-done.2 = f32[128,1,2]{2,1,0:T(1,128)S(1)} async-done(((f32[128,1,2]{2,1,0:T(1,128)}), f32[128,1,2]{2,1,0:T(1,128)S(1)}, u32[]{:S(2)}, u32[]{:S(2)}) %all-to-all-start.2) | async-done | bytes 1056 | tf_op jit(solution)/shard_map/all_to_all | solution.py:190
  117.3 3.5 %all-to-all-start.3 = ((f32[16,1,16,128]{3,2,1,0:T(8,128)}), f32[16,1,16,128]{3,2,1,0:T(8,128)S(1)}, u32[]{:S(2)}, u32[]{:S(2)}) async-start(f32[16,1,16,128]{3,2,1,0:T(8,128)} %broadcast_in_dim.14), calls=%async_computation.3 | async-start | bytes 262144 | tf_op jit(solution)/shard_map/all_to_all | solution.py:174
  120.8 6.8 %all-to-all-done.3 = f32[16,1,16,128]{3,2,1,0:T(8,128)S(1)} async-done(((f32[16,1,16,128]{3,2,1,0:T(8,128)}), f32[16,1,16,128]{3,2,1,0:T(8,128)S(1)}, u32[]{:S(2)}, u32[]{:S(2)}) %all-to-all-start.3) | async-done | bytes 131104 | tf_op jit(solution)/shard_map/all_to_all | solution.py:174
  127.6 4.0 %collective-permute-start.4 = (f32[1,256,128]{2,1,0:T(8,128)S(1)}, f32[1,256,128]{2,1,0:T(8,128)S(1)}, u32[]{:S(2)}, u32[]{:S(2)}) collective-permute-start(f32[1,256,128]{2,1,0:T(8,128)S(1)} %bitcast.233), channel_id=1, source_target_pairs={{0,1},{1,2},{2,3},{3,4},{4,5},{5,6},{6,7},{8,9},{9,10},{10,11},{11... | collective-permute-start | bytes 393224 | tf_op jit(solution)/shard_map/ppermute | solution.py:176
  133.8 4.1 %collective-permute-done.5 = f32[1,256,128]{2,1,0:T(8,128)S(1)} collective-permute-done((f32[1,256,128]{2,1,0:T(8,128)S(1)}, f32[1,256,128]{2,1,0:T(8,128)S(1)}, u32[]{:S(2)}, u32[]{:S(2)}) %collective-permute-start.5) | collective-permute-done | bytes 131104 | tf_op jit(solution)/shard_map/ppermute | solution.py:177
  147.8 4.6 %all-to-all-start.4 = ((f32[128,1,3]{2,1,0:T(1,128)}), f32[128,1,3]{2,1,0:T(1,128)S(1)}, u32[]{:S(2)}, u32[]{:S(2)}) async-start(f32[128,1,3]{2,1,0:T(1,128)} %broadcast_in_dim.15), calls=%async_computation.4 | async-start | bytes 131072 | tf_op jit(solution)/shard_map/all_to_all | solution.py:190
  152.4 9.6 %all-to-all-done.4 = f32[128,1,3]{2,1,0:T(1,128)S(1)} async-done(((f32[128,1,3]{2,1,0:T(1,128)}), f32[128,1,3]{2,1,0:T(1,128)S(1)}, u32[]{:S(2)}, u32[]{:S(2)}) %all-to-all-start.4) | async-done | bytes 1568 | tf_op jit(solution)/shard_map/all_to_all | solution.py:190
  167.9 3.5 %all-to-all-start.5 = ((f32[16,1,16,128]{3,2,1,0:T(8,128)}), f32[16,1,16,128]{3,2,1,0:T(8,128)S(1)}, u32[]{:S(2)}, u32[]{:S(2)}) async-start(f32[16,1,16,128]{3,2,1,0:T(8,128)} %broadcast_in_dim.16), calls=%async_computation.5 | async-start | bytes 262144 | tf_op jit(solution)/shard_map/all_to_all | solution.py:174
  171.4 6.8 %all-to-all-done.5 = f32[16,1,16,128]{3,2,1,0:T(8,128)S(1)} async-done(((f32[16,1,16,128]{3,2,1,0:T(8,128)}), f32[16,1,16,128]{3,2,1,0:T(8,128)S(1)}, u32[]{:S(2)}, u32[]{:S(2)}) %all-to-all-start.5) | async-done | bytes 131104 | tf_op jit(solution)/shard_map/all_to_all | solution.py:174
  178.2 4.0 %collective-permute-start.6 = (f32[1,256,128]{2,1,0:T(8,128)S(1)}, f32[1,256,128]{2,1,0:T(8,128)S(1)}, u32[]{:S(2)}, u32[]{:S(2)}) collective-permute-start(f32[1,256,128]{2,1,0:T(8,128)S(1)} %bitcast.228), channel_id=1, source_target_pairs={{0,1},{1,2},{2,3},{3,4},{4,5},{5,6},{6,7},{8,9},{9,10},{10,11},{11... | collective-permute-start | bytes 393224 | tf_op jit(solution)/shard_map/ppermute | solution.py:176
  184.8 3.7 %collective-permute-done.7 = f32[1,256,128]{2,1,0:T(8,128)S(1)} collective-permute-done((f32[1,256,128]{2,1,0:T(8,128)S(1)}, f32[1,256,128]{2,1,0:T(8,128)S(1)}, u32[]{:S(2)}, u32[]{:S(2)}) %collective-permute-start.7) | collective-permute-done | bytes 131104 | tf_op jit(solution)/shard_map/ppermute | solution.py:177
  198.2 4.6 %all-to-all-start.6 = ((f32[128,1,3]{2,1,0:T(1,128)}), f32[128,1,3]{2,1,0:T(1,128)S(1)}, u32[]{:S(2)}, u32[]{:S(2)}) async-start(f32[128,1,3]{2,1,0:T(1,128)} %broadcast_in_dim.17), calls=%async_computation.6 | async-start | bytes 131072 | tf_op jit(solution)/shard_map/all_to_all | solution.py:190
  202.9 9.4 %all-to-all-done.6 = f32[128,1,3]{2,1,0:T(1,128)S(1)} async-done(((f32[128,1,3]{2,1,0:T(1,128)}), f32[128,1,3]{2,1,0:T(1,128)S(1)}, u32[]{:S(2)}, u32[]{:S(2)}) %all-to-all-start.6) | async-done | bytes 1568 | tf_op jit(solution)/shard_map/all_to_all | solution.py:190
  (235 shorter events, 65.2 us)
Async XLA Ops:
  28.9 11.2 %all-to-all-start = ((f32[8,3,4,270]{3,2,1,0:T(4,128)}), f32[8,3,4,270]{3,2,1,0:T(4,128)S(1)}, u32[]{:S(2)}, u32[]{:S(2)}) async-start(f32[8,3,4,270]{3,2,1,0:T(4,128)} %fusion.564), calls=%async_computation | async-start | bytes 294912 | tf_op jit(solution)/shard_map/all_to_all | solution.py:232
  40.2 4.5 %collective-permute-start = (f32[3,7,270]{2,1,0:T(8,128)S(1)}, f32[3,7,270]{2,1,0:T(8,128)S(1)}, u32[]{:S(2)}, u32[]{:S(2)}) collective-permute-start(f32[3,7,270]{2,1,0:T(8,128)S(1)} %get-tuple-element.28), channel_id=1, source_target_pairs={{0,8},{8,16},{16,24},{24,32},{32,40},{40,48},{48,56},{56,64},{64,7... | collective-permute-start | bytes 68048 | tf_op jit(solution)/shard_map/ppermute | solution.py:235
  43.4 4.7 %collective-permute-start.1 = (f32[3,7,270]{2,1,0:T(8,128)S(1)}, f32[3,7,270]{2,1,0:T(8,128)S(1)}, u32[]{:S(2)}, u32[]{:S(2)}) collective-permute-start(f32[3,7,270]{2,1,0:T(8,128)S(1)} %get-tuple-element.29), channel_id=1, source_target_pairs={{8,0},{16,8},{24,16},{32,24},{40,32},{48,40},{56,48},{64,56},{72,6... | collective-permute-start | bytes 68048 | tf_op jit(solution)/shard_map/ppermute | solution.py:236
  50.7 17.5 %all-to-all-start.1 = ((f32[16,3,16,128]{3,2,1,0:T(8,128)}), f32[16,3,16,128]{3,2,1,0:T(8,128)S(1)}, u32[]{:S(2)}, u32[]{:S(2)}) async-start(f32[16,3,16,128]{3,2,1,0:T(8,128)} %broadcast_in_dim.12), calls=%async_computation.1 | async-start | bytes 786432 | tf_op jit(solution)/shard_map/all_to_all | solution.py:174
  68.2 10.5 %collective-permute-start.2 = (f32[3,256,128]{2,1,0:T(8,128)S(1)}, f32[3,256,128]{2,1,0:T(8,128)S(1)}, u32[]{:S(2)}, u32[]{:S(2)}) collective-permute-start(f32[3,256,128]{2,1,0:T(8,128)S(1)} %bitcast.225), channel_id=1, source_target_pairs={{0,1},{1,2},{2,3},{3,4},{4,5},{5,6},{6,7},{8,9},{9,10},{10,11},{11... | collective-permute-start | bytes 1179656 | tf_op jit(solution)/shard_map/ppermute | solution.py:176
  74.1 9.1 %collective-permute-start.3 = (f32[3,256,128]{2,1,0:T(8,128)S(1)}, f32[3,256,128]{2,1,0:T(8,128)S(1)}, u32[]{:S(2)}, u32[]{:S(2)}) collective-permute-start(f32[3,256,128]{2,1,0:T(8,128)S(1)} %bitcast.226), channel_id=1, source_target_pairs={{1,0},{2,1},{3,2},{4,3},{5,4},{6,5},{7,6},{9,8},{10,9},{11,10},{12... | collective-permute-start | bytes 1179656 | tf_op jit(solution)/shard_map/ppermute | solution.py:177
  100.1 13.8 %all-to-all-start.2 = ((f32[128,1,2]{2,1,0:T(1,128)}), f32[128,1,2]{2,1,0:T(1,128)S(1)}, u32[]{:S(2)}, u32[]{:S(2)}) async-start(f32[128,1,2]{2,1,0:T(1,128)} %broadcast_in_dim.13), calls=%async_computation.2 | async-start | bytes 131072 | tf_op jit(solution)/shard_map/all_to_all | solution.py:190
  117.3 10.3 %all-to-all-start.3 = ((f32[16,1,16,128]{3,2,1,0:T(8,128)}), f32[16,1,16,128]{3,2,1,0:T(8,128)S(1)}, u32[]{:S(2)}, u32[]{:S(2)}) async-start(f32[16,1,16,128]{3,2,1,0:T(8,128)} %broadcast_in_dim.14), calls=%async_computation.3 | async-start | bytes 262144 | tf_op jit(solution)/shard_map/all_to_all | solution.py:174
  127.6 6.2 %collective-permute-start.4 = (f32[1,256,128]{2,1,0:T(8,128)S(1)}, f32[1,256,128]{2,1,0:T(8,128)S(1)}, u32[]{:S(2)}, u32[]{:S(2)}) collective-permute-start(f32[1,256,128]{2,1,0:T(8,128)S(1)} %bitcast.233), channel_id=1, source_target_pairs={{0,1},{1,2},{2,3},{3,4},{4,5},{5,6},{6,7},{8,9},{9,10},{10,11},{11... | collective-permute-start | bytes 393224 | tf_op jit(solution)/shard_map/ppermute | solution.py:176
  131.6 6.3 %collective-permute-start.5 = (f32[1,256,128]{2,1,0:T(8,128)S(1)}, f32[1,256,128]{2,1,0:T(8,128)S(1)}, u32[]{:S(2)}, u32[]{:S(2)}) collective-permute-start(f32[1,256,128]{2,1,0:T(8,128)S(1)} %bitcast.234), channel_id=1, source_target_pairs={{1,0},{2,1},{3,2},{4,3},{5,4},{6,5},{7,6},{9,8},{10,9},{11,10},{12... | collective-permute-start | bytes 393224 | tf_op jit(solution)/shard_map/ppermute | solution.py:177
  147.8 14.2 %all-to-all-start.4 = ((f32[128,1,3]{2,1,0:T(1,128)}), f32[128,1,3]{2,1,0:T(1,128)S(1)}, u32[]{:S(2)}, u32[]{:S(2)}) async-start(f32[128,1,3]{2,1,0:T(1,128)} %broadcast_in_dim.15), calls=%async_computation.4 | async-start | bytes 131072 | tf_op jit(solution)/shard_map/all_to_all | solution.py:190
  167.9 10.3 %all-to-all-start.5 = ((f32[16,1,16,128]{3,2,1,0:T(8,128)}), f32[16,1,16,128]{3,2,1,0:T(8,128)S(1)}, u32[]{:S(2)}, u32[]{:S(2)}) async-start(f32[16,1,16,128]{3,2,1,0:T(8,128)} %broadcast_in_dim.16), calls=%async_computation.5 | async-start | bytes 262144 | tf_op jit(solution)/shard_map/all_to_all | solution.py:174
  178.2 6.6 %collective-permute-start.6 = (f32[1,256,128]{2,1,0:T(8,128)S(1)}, f32[1,256,128]{2,1,0:T(8,128)S(1)}, u32[]{:S(2)}, u32[]{:S(2)}) collective-permute-start(f32[1,256,128]{2,1,0:T(8,128)S(1)} %bitcast.228), channel_id=1, source_target_pairs={{0,1},{1,2},{2,3},{3,4},{4,5},{5,6},{6,7},{8,9},{9,10},{10,11},{11... | collective-permute-start | bytes 393224 | tf_op jit(solution)/shard_map/ppermute | solution.py:176
  182.2 6.3 %collective-permute-start.7 = (f32[1,256,128]{2,1,0:T(8,128)S(1)}, f32[1,256,128]{2,1,0:T(8,128)S(1)}, u32[]{:S(2)}, u32[]{:S(2)}) collective-permute-start(f32[1,256,128]{2,1,0:T(8,128)S(1)} %bitcast.229), channel_id=1, source_target_pairs={{1,0},{2,1},{3,2},{4,3},{5,4},{6,5},{7,6},{9,8},{10,9},{11,10},{12... | collective-permute-start | bytes 393224 | tf_op jit(solution)/shard_map/ppermute | solution.py:177
  198.2 14.2 %all-to-all-start.6 = ((f32[128,1,3]{2,1,0:T(1,128)}), f32[128,1,3]{2,1,0:T(1,128)S(1)}, u32[]{:S(2)}, u32[]{:S(2)}) async-start(f32[128,1,3]{2,1,0:T(1,128)} %broadcast_in_dim.17), calls=%async_computation.6 | async-start | bytes 131072 | tf_op jit(solution)/shard_map/all_to_all | solution.py:190

commit v5 on v4

--- a/solution.py
+++ b/solution.py
@@ -166,16 +166,25 @@
     return lax.axis_size("az") * lax.axis_size("rg")
 
 
-def gather_strip(blocks):
+def gather_strip(blocks, sums=None):
     n_az = lax.axis_size("az")
     n_rg = lax.axis_size("rg")
     count, h, w = blocks.shape
-    sent = jnp.broadcast_to(blocks[None], (n_az, count, h, w))
+    if sums is not None:
+        extra = jnp.zeros((1, h, w), jnp.float32).at[0, 0, :sums.shape[0]].set(sums)
+        blocks = jnp.concatenate([blocks, extra])
+    sent = jnp.broadcast_to(blocks[None], (n_az,) + blocks.shape)
     got = lax.all_to_all(sent, "az", 0, 0, tiled=True)
+    summed = None
+    if sums is not None:
+        column_sums = jnp.sum(got[:, count, 0, :sums.shape[0]], axis=0)
+        rows = lax.all_to_all(jnp.broadcast_to(column_sums[None], (n_rg, sums.shape[0])), "rg", 0, 0, tiled=True)
+        summed = jnp.sum(rows, axis=0)
+        got = got[:, :count]
     column = got.transpose(1, 0, 2, 3).reshape(count, n_az * h, w)
     left = lax.ppermute(column, "rg", [(i, i + 1) for i in range(n_rg - 1)])
     right = lax.ppermute(column, "rg", [(i + 1, i) for i in range(n_rg - 1)])
-    return jnp.concatenate([left, column, right], axis=-1)
+    return jnp.concatenate([left, column, right], axis=-1), summed
 
 
 def shifted(values, axis):
@@ -271,55 +280,73 @@
     block_h, block_w = coarse_edges[0].shape
     whole = {}
 
-    def coarse_solve(rhs_vec, ring):
+    def coarse_solve(rhs_vec, ring, sums):
         if not whole:
-            got = gather_strip(jnp.stack([coarse_edges[0], coarse_edges[2], rhs_vec]))
+            got, summed = gather_strip(jnp.stack([coarse_edges[0], coarse_edges[2], rhs_vec]), sums)
             east_s, south_s = got[0], got[1]
             whole["levels"] = build_levels(east_s, shifted(east_s, 1), south_s, shifted(south_s, 0),
                                            GATHER_LEVEL, LEVELS)[0]
             strip_rhs = got[2]
         else:
-            strip_rhs = gather_strip(rhs_vec[None])[0]
+            got, summed = gather_strip(rhs_vec[None], sums)
+            strip_rhs = got[0]
         strip_x = vcycle(strip_rhs, GATHER_LEVEL, whole["levels"], apply_padded, None)
         coarse_ring = ring // 2
         strip_x = jnp.pad(strip_x, ((coarse_ring, coarse_ring), (0, 0)))
         return lax.dynamic_slice(strip_x, (segment_ordinal * block_h, block_w - coarse_ring),
-                                 (block_h + 2 * coarse_ring, block_w + 2 * coarse_ring))
-
-    def precondition(rhs_wide):
+                                 (block_h + 2 * coarse_ring, block_w + 2 * coarse_ring)), summed
+
+    def precondition(rhs_wide, sums=None):
         ring = (rhs_wide.shape[0] - shard_height_total) // 2
         diag_here = ops_at(ring)[4]
         estimate = OMEGA * rhs_wide / diag_here
         remain = crop(rhs_wide, 0) - apply_inner(crop(estimate, 1), levels[0])
-        estimate = estimate + prolong_copy(coarse_solve(restrict_sum(remain), ring))
+        patch, summed = coarse_solve(restrict_sum(remain), ring, sums)
+        estimate = estimate + prolong_copy(patch)
         inner = ops_at(ring - 1)
         smoothed = crop(estimate, ring - 1) + OMEGA * (crop(rhs_wide, ring - 1) - apply_inner(estimate, inner)) / inner[4]
-        return smoothed, apply_inner(smoothed, ops_at(ring - 2))
+        return smoothed, apply_inner(smoothed, ops_at(ring - 2)), summed
+
+    def ring_of(values):
+        return (values.shape[-2] - shard_height_total) // 2
+
+    def own_sums(*pairs):
+        return jnp.stack([jnp.sum(crop(a, 0) * crop(b, 0)) for a, b in pairs])
 
     residual_wide = rhs_wide
-    precond, image_vec = precondition(residual_wide)
-    direction = precond
-    sums = total(jnp.stack([jnp.sum(crop(residual_wide, 0) * crop(precond, 0)),
-                            jnp.sum(crop(direction, 0) * crop(image_vec, 0))]))
+    precond, image_u, _ = precondition(residual_wide)
+    sums = own_sums((residual_wide, precond), (image_u, precond))
+    if ITERS > 1:
+        pre_image, image_pre, sums = precondition(image_u, sums)
+    else:
+        sums = total(sums)
     norm_now = sums[0]
     curvature = sums[1]
-    solution = jnp.zeros_like(crop(rhs_wide, 0))
-    for step_index in range(ITERS):
-        step_length = norm_now / curvature
+    step_length = norm_now / curvature
+    direction, image_vec = precond, image_u
+    if ITERS > 1:
+        pre_dir, image_pre_dir = pre_image, image_pre
+    solution = step_length * crop(direction, 0)
+    for step_index in range(1, ITERS):
+        residual_wide = crop(residual_wide, ring_of(image_vec)) - step_length * image_vec
+        precond = crop(precond, ring_of(pre_dir)) - step_length * pre_dir
+        image_u = crop(image_u, ring_of(image_pre_dir)) - step_length * image_pre_dir
+        sums = own_sums((residual_wide, precond), (image_u, precond), (precond, image_vec))
+        if step_index + 1 < ITERS:
+            pre_image, image_pre, sums = precondition(image_u, sums)
+        else:
+            sums = total(sums)
+        norm_next = sums[0]
+        ratio = norm_next / norm_now
+        curvature = sums[1] + 2.0 * ratio * sums[2] + ratio * ratio * curvature
+        step_length = norm_next / curvature
+        direction = precond + ratio * crop(direction, ring_of(precond))
+        image_vec = image_u + ratio * crop(image_vec, ring_of(image_u))
+        if step_index + 1 < ITERS:
+            pre_dir = pre_image + ratio * crop(pre_dir, ring_of(pre_image))
+            image_pre_dir = image_pre + ratio * crop(image_pre_dir, ring_of(image_pre))
         solution = solution + step_length * crop(direction, 0)
-        if step_index + 1 < ITERS:
-            ring = (image_vec.shape[0] - shard_height_total) // 2
-            residual_wide = crop(residual_wide, ring) - step_length * image_vec
-            precond, image_z = precondition(residual_wide)
-            sums = total(jnp.stack([jnp.sum(crop(residual_wide, 0) * crop(precond, 0)),
-                                    jnp.sum(crop(precond, 0) * crop(image_z, 0)),
-                                    jnp.sum(crop(precond, 0) * crop(image_vec, 0))]))
-            norm_next = sums[0]
-            ratio = norm_next / norm_now
-            direction = precond + ratio * crop(direction, ring - 1)
-            image_vec = image_z + ratio * crop(image_vec, ring - 2)
-            curvature = sums[1] + 2.0 * ratio * sums[2] + ratio * ratio * curvature
-            norm_now = norm_next
+        norm_now = norm_next
     return (solution, weight)
 
 

time: 218 us -> 194 us (0.89)
  waiting for transfers between devices: 73.5 us -> 50.2 us
    all_to_all x3 -> x1, waiting for transfers between devices: 28.6 us -> 9.42 us  [total(): got = lax.all_to_all(sent, ('az', 'rg'), 0, 0, tiled=True)]
    all_to_all x3 -> x1, starting transfers between devices: 13.3 us -> 5.67 us  [total(): got = lax.all_to_all(sent, ('az', 'rg'), 0, 0, tiled=True)]
    all_to_all x0 -> x2, starting transfers between devices: none -> 7.6 us  [gather_strip(): lax.all_to_all(jnp.broadcast_to(column_sums[None], (n_rg, sums.shape[0]))...]
    ppermute x3, waiting for transfers between devices: 12.2 us -> 4.8 us  [gather_strip(): right = lax.ppermute(column, 'rg', [(i + 1, i) for i in range(n_rg - 1)])]
  transfers between devices with their start and end apart: 15 -> 15, of which waited for: 12 -> 10; matrix products, arithmetic and copies ran while one was open for 1% -> 2% of each run, Pallas kernels for 0% -> 0%
where the time goes in v5:
time: 194 us; the launch traced here: 193 us
  starting transfers between devices  59.2 us (31%)
  waiting for transfers between devices  50.2 us (26%)
  other arithmetic  33.5 us (17%)
  matrix products  27.3 us (14%)
  local copies, waits for them, and re-layouts  11.5 us (6%)
  between operations  11.4 us (6%)
    all_to_all x3, waiting for transfers between devices, gather_strip(): got = lax.all_to_all(sent, 'az', 0, 0, tiled=True)  23.3 us
    all_to_all x3, starting transfers between devices, gather_strip(): got = lax.all_to_all(sent, 'az', 0, 0, tiled=True)  16.3 us
    add x1, other arithmetic, mean_multilook(): first_re * second_re + first_im * second_im  14.5 us
    dot_general x48, matrix products, sandwich(): inner = jnp.dot(left, vector, precision=HIGHEST)  13.8 us
    ppermute x3, starting transfers between devices, gather_strip(): left = lax.ppermute(column, 'rg', [(i, i + 1) for i in range(n_rg - 1)])  13.1 us
    dot_general x48, matrix products, sandwich(): return jnp.dot(inner, right, precision=HIGHEST)  11 us
    all_to_all x1, waiting for transfers between devices, total(): got = lax.all_to_all(sent, ('az', 'rg'), 0, 0, tiled=True)  9.42 us
    all_to_all x2, starting transfers between devices, gather_strip(): lax.all_to_all(jnp.broadcast_to(column_sums[None], (n_rg, sums.shape[0]))...  7.6 us
  transfers between devices with their start and end apart: 15, of which 10 were waited for; matrix products, arithmetic and copies ran while one was open for 2% of the time, Pallas kernels for 0%

profile of v5, /device:TPU:1, one launch (start us, length us, event | category | flops | bytes accessed | tf_op | source)
XLA Modules:
  0.0 193.0 jit_solution(12875168407449823334)
XLA Ops:
  5.1 14.5 %add_reduce_fusion.2 = (f32[20,10240]{1,0:T(8,128)S(1)}, f32[20,10240]{1,0:T(8,128)S(1)}, f32[20,10240]{1,0:T(8,128)S(1)}, f32[20,10240]{1,0:T(8,128)S(1)}) fusion(bf16[2,20,10240]{2,0,1:T(2,128)(2,1)} %param.8, pred[10240]{0:T(1024)(128)(4,1)S(1)} %fusion.379, pred[20]{0:T(512)(128)(4,1)S(1)} %compare_and_fusion.10, bf16[2,20,10240]{2,0,1:T(2,128)(2,1)} %param.9), kind=kLoop, calls=%fused_computation.36 | loop fusion | flops 4300800 | bytes 4925460 | tf_op jit(solution)/shard_map/add | solution.py:70
  28.9 5.8 %all-to-all-start = ((f32[8,3,4,270]{3,2,1,0:T(4,128)}), f32[8,3,4,270]{3,2,1,0:T(4,128)S(1)}, u32[]{:S(2)}, u32[]{:S(2)}) async-start(f32[8,3,4,270]{3,2,1,0:T(4,128)} %fusion.567), calls=%async_computation | async-start | bytes 294912 | tf_op jit(solution)/shard_map/all_to_all | solution.py:241
  35.1 5.0 %all-to-all-done = f32[8,3,4,270]{3,2,1,0:T(4,128)S(1)} async-done(((f32[8,3,4,270]{3,2,1,0:T(4,128)}), f32[8,3,4,270]{3,2,1,0:T(4,128)S(1)}, u32[]{:S(2)}, u32[]{:S(2)}) %all-to-all-start) | async-done | bytes 103712 | tf_op jit(solution)/shard_map/all_to_all | solution.py:241
  40.2 3.2 %collective-permute-start = (f32[3,7,270]{2,1,0:T(8,128)S(1)}, f32[3,7,270]{2,1,0:T(8,128)S(1)}, u32[]{:S(2)}, u32[]{:S(2)}) collective-permute-start(f32[3,7,270]{2,1,0:T(8,128)S(1)} %get-tuple-element.55), channel_id=1, source_target_pairs={{0,8},{8,16},{16,24},{24,32},{32,40},{40,48},{48,56},{56,64},{64,7... | collective-permute-start | bytes 68048 | tf_op jit(solution)/shard_map/ppermute | solution.py:244
  44.7 3.4 %collective-permute-done.1 = f32[3,7,270]{2,1,0:T(8,128)S(1)} collective-permute-done((f32[3,7,270]{2,1,0:T(8,128)S(1)}, f32[3,7,270]{2,1,0:T(8,128)S(1)}, u32[]{:S(2)}, u32[]{:S(2)}) %collective-permute-start.1) | collective-permute-done | bytes 22712 | tf_op jit(solution)/shard_map/ppermute | solution.py:245
  50.7 9.2 %all-to-all-start.1 = ((f32[16,3,16,128]{3,2,1,0:T(8,128)}), f32[16,3,16,128]{3,2,1,0:T(8,128)S(1)}, u32[]{:S(2)}, u32[]{:S(2)}) async-start(f32[16,3,16,128]{3,2,1,0:T(8,128)} %broadcast_in_dim.16), calls=%async_computation.1 | async-start | bytes 786432 | tf_op jit(solution)/shard_map/all_to_all | solution.py:177
  60.0 8.2 %all-to-all-done.1 = f32[16,3,16,128]{3,2,1,0:T(8,128)S(1)} async-done(((f32[16,3,16,128]{3,2,1,0:T(8,128)}), f32[16,3,16,128]{3,2,1,0:T(8,128)S(1)}, u32[]{:S(2)}, u32[]{:S(2)}) %all-to-all-start.1) | async-done | bytes 393248 | tf_op jit(solution)/shard_map/all_to_all | solution.py:177
  68.2 5.8 %collective-permute-start.2 = (f32[3,256,128]{2,1,0:T(8,128)S(1)}, f32[3,256,128]{2,1,0:T(8,128)S(1)}, u32[]{:S(2)}, u32[]{:S(2)}) collective-permute-start(f32[3,256,128]{2,1,0:T(8,128)S(1)} %bitcast.233), channel_id=1, source_target_pairs={{0,1},{1,2},{2,3},{3,4},{4,5},{5,6},{6,7},{8,9},{9,10},{10,11},{11... | collective-permute-start | bytes 1179656 | tf_op jit(solution)/shard_map/ppermute | solution.py:185
  74.1 2.1 %collective-permute-start.3 = (f32[3,256,128]{2,1,0:T(8,128)S(1)}, f32[3,256,128]{2,1,0:T(8,128)S(1)}, u32[]{:S(2)}, u32[]{:S(2)}) collective-permute-start(f32[3,256,128]{2,1,0:T(8,128)S(1)} %bitcast.234), channel_id=1, source_target_pairs={{1,0},{2,1},{3,2},{4,3},{5,4},{6,5},{7,6},{9,8},{10,9},{11,10},{12... | collective-permute-start | bytes 1179656 | tf_op jit(solution)/shard_map/ppermute | solution.py:186
  76.2 2.5 %collective-permute-done.2 = f32[3,256,128]{2,1,0:T(8,128)S(1)} collective-permute-done((f32[3,256,128]{2,1,0:T(8,128)S(1)}, f32[3,256,128]{2,1,0:T(8,128)S(1)}, u32[]{:S(2)}, u32[]{:S(2)}) %collective-permute-start.2) | collective-permute-done | bytes 393248 | tf_op jit(solution)/shard_map/ppermute | solution.py:185
  78.8 4.4 %collective-permute-done.3 = f32[3,256,128]{2,1,0:T(8,128)S(1)} collective-permute-done((f32[3,256,128]{2,1,0:T(8,128)S(1)}, f32[3,256,128]{2,1,0:T(8,128)S(1)}, u32[]{:S(2)}, u32[]{:S(2)}) %collective-permute-start.3) | collective-permute-done | bytes 393248 | tf_op jit(solution)/shard_map/ppermute | solution.py:186
  100.7 3.5 %all-to-all-start.2 = ((f32[16,2,16,128]{3,2,1,0:T(8,128)}), f32[16,2,16,128]{3,2,1,0:T(8,128)S(1)}, u32[]{:S(2)}, u32[]{:S(2)}) async-start(f32[16,2,16,128]{3,2,1,0:T(8,128)} %broadcast_in_dim.18), calls=%async_computation.2 | async-start | bytes 524288 | tf_op jit(solution)/shard_map/all_to_all | solution.py:177
  104.3 7.5 %all-to-all-done.2 = f32[16,2,16,128]{3,2,1,0:T(8,128)S(1)} async-done(((f32[16,2,16,128]{3,2,1,0:T(8,128)}), f32[16,2,16,128]{3,2,1,0:T(8,128)S(1)}, u32[]{:S(2)}, u32[]{:S(2)}) %all-to-all-start.2) | async-done | bytes 262176 | tf_op jit(solution)/shard_map/all_to_all | solution.py:177
  111.8 3.8 %collective-permute-start.4 = (f32[1,256,128]{2,1,0:T(8,128)S(1)}, f32[1,256,128]{2,1,0:T(8,128)S(1)}, u32[]{:S(2)}, u32[]{:S(2)}) collective-permute-start(f32[1,256,128]{2,1,0:T(8,128)S(1)} %bitcast.241), channel_id=1, source_target_pairs={{0,1},{1,2},{2,3},{3,4},{4,5},{5,6},{6,7},{8,9},{9,10},{10,11},{11... | collective-permute-start | bytes 393224 | tf_op jit(solution)/shard_map/ppermute | solution.py:185
  116.2 3.3 %all-to-all-start.3 = ((f32[8,1,2]{2,1,0:T(1,128)}), f32[8,1,2]{2,1,0:T(1,128)S(1)}, u32[]{:S(2)}, u32[]{:S(2)}) async-start(f32[8,1,2]{2,1,0:T(1,128)} %broadcast_in_dim.19), calls=%async_computation.3 | async-start | bytes 8192 | tf_op jit(solution)/shard_map/all_to_all | solution.py:181
  119.4 2.1 %collective-permute-start.5 = (f32[1,256,128]{2,1,0:T(8,128)S(1)}, f32[1,256,128]{2,1,0:T(8,128)S(1)}, u32[]{:S(2)}, u32[]{:S(2)}) collective-permute-start(f32[1,256,128]{2,1,0:T(8,128)S(1)} %bitcast.242), channel_id=1, source_target_pairs={{1,0},{2,1},{3,2},{4,3},{5,4},{6,5},{7,6},{9,8},{10,9},{11,10},{12... | collective-permute-start | bytes 393224 | tf_op jit(solution)/shard_map/ppermute | solution.py:186
  136.2 3.5 %all-to-all-start.4 = ((f32[16,2,16,128]{3,2,1,0:T(8,128)}), f32[16,2,16,128]{3,2,1,0:T(8,128)S(1)}, u32[]{:S(2)}, u32[]{:S(2)}) async-start(f32[16,2,16,128]{3,2,1,0:T(8,128)} %broadcast_in_dim.21), calls=%async_computation.4 | async-start | bytes 524288 | tf_op jit(solution)/shard_map/all_to_all | solution.py:177
  140.5 7.7 %all-to-all-done.4 = f32[16,2,16,128]{3,2,1,0:T(8,128)S(1)} async-done(((f32[16,2,16,128]{3,2,1,0:T(8,128)}), f32[16,2,16,128]{3,2,1,0:T(8,128)S(1)}, u32[]{:S(2)}, u32[]{:S(2)}) %all-to-all-start.4) | async-done | bytes 262176 | tf_op jit(solution)/shard_map/all_to_all | solution.py:177
  148.8 4.3 %all-to-all-start.5 = ((f32[8,1,3]{2,1,0:T(1,128)}), f32[8,1,3]{2,1,0:T(1,128)S(1)}, u32[]{:S(2)}, u32[]{:S(2)}) async-start(f32[8,1,3]{2,1,0:T(1,128)} %broadcast_in_dim.22), calls=%async_computation.5 | async-start | bytes 8192 | tf_op jit(solution)/shard_map/all_to_all | solution.py:181
  153.2 3.5 %collective-permute-start.6 = (f32[1,256,128]{2,1,0:T(8,128)S(1)}, f32[1,256,128]{2,1,0:T(8,128)S(1)}, u32[]{:S(2)}, u32[]{:S(2)}) collective-permute-start(f32[1,256,128]{2,1,0:T(8,128)S(1)} %bitcast.236), channel_id=1, source_target_pairs={{0,1},{1,2},{2,3},{3,4},{4,5},{5,6},{6,7},{8,9},{9,10},{10,11},{11... | collective-permute-start | bytes 393224 | tf_op jit(solution)/shard_map/ppermute | solution.py:185
  156.7 1.9 collective-permute-start.7
  170.3 2.0 %pad_maximum_fusion.5 = f32[3]{0:T(128)S(1)} fusion(f32[1]{0:T(128)} %bitcast.52, f32[1]{0:T(128)} %bitcast.51, f32[1]{0:T(128)} %bitcast.50), kind=kLoop, calls=%fused_computation.1328 | loop fusion | flops 6 | bytes 24 | tf_op jit(solution)/shard_map/stack | solution.py:314
  173.0 5.7 %all-to-all-start.6 = ((f32[128,1,3]{2,1,0:T(1,128)}), f32[128,1,3]{2,1,0:T(1,128)S(1)}, u32[]{:S(2)}, u32[]{:S(2)}) async-start(f32[128,1,3]{2,1,0:T(1,128)} %broadcast_in_dim.23), calls=%async_computation.6 | async-start | bytes 131072 | tf_op jit(solution)/shard_map/all_to_all | solution.py:199
  178.8 9.4 %all-to-all-done.6 = f32[128,1,3]{2,1,0:T(1,128)S(1)} async-done(((f32[128,1,3]{2,1,0:T(1,128)}), f32[128,1,3]{2,1,0:T(1,128)S(1)}, u32[]{:S(2)}, u32[]{:S(2)}) %all-to-all-start.6) | async-done | bytes 1568 | tf_op jit(solution)/shard_map/all_to_all | solution.py:199
  (242 shorter events, 59.1 us)
Async XLA Ops:
  28.9 11.2 %all-to-all-start = ((f32[8,3,4,270]{3,2,1,0:T(4,128)}), f32[8,3,4,270]{3,2,1,0:T(4,128)S(1)}, u32[]{:S(2)}, u32[]{:S(2)}) async-start(f32[8,3,4,270]{3,2,1,0:T(4,128)} %fusion.567), calls=%async_computation | async-start | bytes 294912 | tf_op jit(solution)/shard_map/all_to_all | solution.py:241
  40.2 4.5 %collective-permute-start = (f32[3,7,270]{2,1,0:T(8,128)S(1)}, f32[3,7,270]{2,1,0:T(8,128)S(1)}, u32[]{:S(2)}, u32[]{:S(2)}) collective-permute-start(f32[3,7,270]{2,1,0:T(8,128)S(1)} %get-tuple-element.55), channel_id=1, source_target_pairs={{0,8},{8,16},{16,24},{24,32},{32,40},{40,48},{48,56},{56,64},{64,7... | collective-permute-start | bytes 68048 | tf_op jit(solution)/shard_map/ppermute | solution.py:244
  43.4 4.7 %collective-permute-start.1 = (f32[3,7,270]{2,1,0:T(8,128)S(1)}, f32[3,7,270]{2,1,0:T(8,128)S(1)}, u32[]{:S(2)}, u32[]{:S(2)}) collective-permute-start(f32[3,7,270]{2,1,0:T(8,128)S(1)} %get-tuple-element.56), channel_id=1, source_target_pairs={{8,0},{16,8},{24,16},{32,24},{40,32},{48,40},{56,48},{64,56},{72,6... | collective-permute-start | bytes 68048 | tf_op jit(solution)/shard_map/ppermute | solution.py:245
  50.7 17.5 %all-to-all-start.1 = ((f32[16,3,16,128]{3,2,1,0:T(8,128)}), f32[16,3,16,128]{3,2,1,0:T(8,128)S(1)}, u32[]{:S(2)}, u32[]{:S(2)}) async-start(f32[16,3,16,128]{3,2,1,0:T(8,128)} %broadcast_in_dim.16), calls=%async_computation.1 | async-start | bytes 786432 | tf_op jit(solution)/shard_map/all_to_all | solution.py:177
  68.2 10.5 %collective-permute-start.2 = (f32[3,256,128]{2,1,0:T(8,128)S(1)}, f32[3,256,128]{2,1,0:T(8,128)S(1)}, u32[]{:S(2)}, u32[]{:S(2)}) collective-permute-start(f32[3,256,128]{2,1,0:T(8,128)S(1)} %bitcast.233), channel_id=1, source_target_pairs={{0,1},{1,2},{2,3},{3,4},{4,5},{5,6},{6,7},{8,9},{9,10},{10,11},{11... | collective-permute-start | bytes 1179656 | tf_op jit(solution)/shard_map/ppermute | solution.py:185
  74.1 9.1 %collective-permute-start.3 = (f32[3,256,128]{2,1,0:T(8,128)S(1)}, f32[3,256,128]{2,1,0:T(8,128)S(1)}, u32[]{:S(2)}, u32[]{:S(2)}) collective-permute-start(f32[3,256,128]{2,1,0:T(8,128)S(1)} %bitcast.234), channel_id=1, source_target_pairs={{1,0},{2,1},{3,2},{4,3},{5,4},{6,5},{7,6},{9,8},{10,9},{11,10},{12... | collective-permute-start | bytes 1179656 | tf_op jit(solution)/shard_map/ppermute | solution.py:186
  100.7 11.0 %all-to-all-start.2 = ((f32[16,2,16,128]{3,2,1,0:T(8,128)}), f32[16,2,16,128]{3,2,1,0:T(8,128)S(1)}, u32[]{:S(2)}, u32[]{:S(2)}) async-start(f32[16,2,16,128]{3,2,1,0:T(8,128)} %broadcast_in_dim.18), calls=%async_computation.2 | async-start | bytes 524288 | tf_op jit(solution)/shard_map/all_to_all | solution.py:177
  111.8 13.6 %collective-permute-start.4 = (f32[1,256,128]{2,1,0:T(8,128)S(1)}, f32[1,256,128]{2,1,0:T(8,128)S(1)}, u32[]{:S(2)}, u32[]{:S(2)}) collective-permute-start(f32[1,256,128]{2,1,0:T(8,128)S(1)} %bitcast.241), channel_id=1, source_target_pairs={{0,1},{1,2},{2,3},{3,4},{4,5},{5,6},{6,7},{8,9},{9,10},{10,11},{11... | collective-permute-start | bytes 393224 | tf_op jit(solution)/shard_map/ppermute | solution.py:185
  116.2 7.1 %all-to-all-start.3 = ((f32[8,1,2]{2,1,0:T(1,128)}), f32[8,1,2]{2,1,0:T(1,128)S(1)}, u32[]{:S(2)}, u32[]{:S(2)}) async-start(f32[8,1,2]{2,1,0:T(1,128)} %broadcast_in_dim.19), calls=%async_computation.3 | async-start | bytes 8192 | tf_op jit(solution)/shard_map/all_to_all | solution.py:181
  119.4 6.3 %collective-permute-start.5 = (f32[1,256,128]{2,1,0:T(8,128)S(1)}, f32[1,256,128]{2,1,0:T(8,128)S(1)}, u32[]{:S(2)}, u32[]{:S(2)}) collective-permute-start(f32[1,256,128]{2,1,0:T(8,128)S(1)} %bitcast.242), channel_id=1, source_target_pairs={{1,0},{2,1},{3,2},{4,3},{5,4},{6,5},{7,6},{9,8},{10,9},{11,10},{12... | collective-permute-start | bytes 393224 | tf_op jit(solution)/shard_map/ppermute | solution.py:186
  136.2 12.0 %all-to-all-start.4 = ((f32[16,2,16,128]{3,2,1,0:T(8,128)}), f32[16,2,16,128]{3,2,1,0:T(8,128)S(1)}, u32[]{:S(2)}, u32[]{:S(2)}) async-start(f32[16,2,16,128]{3,2,1,0:T(8,128)} %broadcast_in_dim.21), calls=%async_computation.4 | async-start | bytes 524288 | tf_op jit(solution)/shard_map/all_to_all | solution.py:177
  148.8 9.8 %all-to-all-start.5 = ((f32[8,1,3]{2,1,0:T(1,128)}), f32[8,1,3]{2,1,0:T(1,128)S(1)}, u32[]{:S(2)}, u32[]{:S(2)}) async-start(f32[8,1,3]{2,1,0:T(1,128)} %broadcast_in_dim.22), calls=%async_computation.5 | async-start | bytes 8192 | tf_op jit(solution)/shard_map/all_to_all | solution.py:181
  153.2 10.0 %collective-permute-start.6 = (f32[1,256,128]{2,1,0:T(8,128)S(1)}, f32[1,256,128]{2,1,0:T(8,128)S(1)}, u32[]{:S(2)}, u32[]{:S(2)}) collective-permute-start(f32[1,256,128]{2,1,0:T(8,128)S(1)} %bitcast.236), channel_id=1, source_target_pairs={{0,1},{1,2},{2,3},{3,4},{4,5},{5,6},{6,7},{8,9},{9,10},{10,11},{11... | collective-permute-start | bytes 393224 | tf_op jit(solution)/shard_map/ppermute | solution.py:185
  156.7 6.4 %collective-permute-start.7 = (f32[1,256,128]{2,1,0:T(8,128)S(1)}, f32[1,256,128]{2,1,0:T(8,128)S(1)}, u32[]{:S(2)}, u32[]{:S(2)}) collective-permute-start(f32[1,256,128]{2,1,0:T(8,128)S(1)} %bitcast.237), channel_id=1, source_target_pairs={{1,0},{2,1},{3,2},{4,3},{5,4},{6,5},{7,6},{9,8},{10,9},{11,10},{12... | collective-permute-start | bytes 393224 | tf_op jit(solution)/shard_map/ppermute | solution.py:186
  173.0 15.3 %all-to-all-start.6 = ((f32[128,1,3]{2,1,0:T(1,128)}), f32[128,1,3]{2,1,0:T(1,128)S(1)}, u32[]{:S(2)}, u32[]{:S(2)}) async-start(f32[128,1,3]{2,1,0:T(1,128)} %broadcast_in_dim.23), calls=%async_computation.6 | async-start | bytes 131072 | tf_op jit(solution)/shard_map/all_to_all | solution.py:199

commit v6 on v5

--- a/solution.py
+++ b/solution.py
@@ -2,6 +2,7 @@
 import jax.numpy as jnp
 from jax import lax
 from jax.sharding import PartitionSpec as P
+from jax.experimental import pallas as pl
 
 LOOK = 5
 LEVELS = 6
@@ -59,26 +60,46 @@
             - south * padded[2:, 1:-1] - north * padded[:-2, 1:-1])
 
 
+def multilook_kernel(lead_ref, trail_ref, row_ref, col_ref, out_ref):
+    mask = row_ref[:, 0:1] * col_ref[...]
+    first_re = lead_ref[0].astype(jnp.float32) * mask
+    first_im = lead_ref[1].astype(jnp.float32) * mask
+    second_re = trail_ref[0].astype(jnp.float32) * mask
+    second_im = trail_ref[1].astype(jnp.float32) * mask
+    products = (
+        first_re * second_re + first_im * second_im,
+        first_im * second_re - first_re * second_im,
+        first_re * first_re + first_im * first_im,
+        second_re * second_re + second_im * second_im,
+    )
+    for part, values in enumerate(products):
+        for group in range(out_ref.shape[1]):
+            acc = values[group * LOOK:group * LOOK + 1, :]
+            for offset in range(1, LOOK):
+                acc = acc + values[group * LOOK + offset:group * LOOK + offset + 1, :]
+            out_ref[part, group:group + 1, :] = acc
+
+
 def mean_multilook(leading, trailing, row_ok, col_ok):
-    valid_mask = (row_ok[:, None] & col_ok[None, :]).astype(jnp.float32)
-    first_re = leading[0].astype(jnp.float32) * valid_mask
-    first_im = leading[1].astype(jnp.float32) * valid_mask
-    second_re = trailing[0].astype(jnp.float32) * valid_mask
-    second_im = trailing[1].astype(jnp.float32) * valid_mask
-    products = jnp.stack(
-        [
-            first_re * second_re + first_im * second_im,
-            first_im * second_re - first_re * second_im,
-            first_re * first_re + first_im * first_im,
-            second_re * second_re + second_im * second_im,
-        ]
-    )
-    height_rows, width_cols = valid_mask.shape
+    _, height_rows, width_cols = leading.shape
+    block = 1024
+    rows = pl.pallas_call(
+        multilook_kernel,
+        grid=(width_cols // block,),
+        in_specs=[
+            pl.BlockSpec((2, height_rows, block), lambda j: (0, 0, j)),
+            pl.BlockSpec((2, height_rows, block), lambda j: (0, 0, j)),
+            pl.BlockSpec((height_rows, 128), lambda j: (0, 0)),
+            pl.BlockSpec((1, block), lambda j: (0, j)),
+        ],
+        out_specs=pl.BlockSpec((4, height_rows // LOOK, block), lambda j: (0, 0, j)),
+        out_shape=jax.ShapeDtypeStruct((4, height_rows // LOOK, width_cols), jnp.float32),
+    )(leading, trailing, jnp.broadcast_to(row_ok.astype(jnp.float32)[:, None], (height_rows, 128)),
+      col_ok.astype(jnp.float32)[None, :])
     span = LOOK * 128
-    grouped = products.reshape(4, height_rows, width_cols // span, span)
+    grouped = rows.reshape(4, height_rows // LOOK, width_cols // span, span)
     cols = jnp.einsum("pikc,cd->pikd", grouped, group_sum(span, LOOK).T, precision=HIGHEST)
-    cols = cols.reshape(4, height_rows, width_cols // LOOK)
-    return jnp.einsum("ri,pic->prc", group_sum(height_rows, LOOK), cols, precision=HIGHEST)
+    return cols.reshape(4, height_rows // LOOK, width_cols // LOOK)
 
 
 def edge_terms(left_re, left_im, left_weight, right_re, right_im, right_weight):

time: 194 us -> 190 us (0.979)
  other arithmetic: 33.5 us -> 15.7 us
  local copies, waits for them, and re-layouts: 11.5 us -> 20.2 us
  Pallas kernels: 0 us -> 7.66 us
  waiting for transfers between devices: 50.2 us -> 46 us
  starting transfers between devices: 59.2 us -> 62.3 us
  matrix products: 27.3 us -> 25.3 us
    add x1 -> x0, other arithmetic: 14.5 us -> none  [mean_multilook(): first_re * second_re + first_im * second_im]
    pallas_call x0 -> x1, Pallas kernels: none -> 7.66 us  [mean_multilook(): pl.pallas_call(multilook_kernel, grid=(width_cols // block,), in_specs=[p...]
    unnamed x5 -> x11, local copies, waits for them, and re-layouts: 1.37 us -> 8.35 us
    unnamed x6 -> x0, other arithmetic: 4.08 us -> none
    all_to_all x2, starting transfers between devices: 7.6 us -> 11.1 us  [gather_strip(): lax.all_to_all(jnp.broadcast_to(column_sums[None], (n_rg, sums.shape[0]))...]
    ppermute x3, starting transfers between devices: 13.1 us -> 9.78 us  [gather_strip(): left = lax.ppermute(column, 'rg', [(i, i + 1) for i in range(n_rg - 1)])]
    ppermute x3, starting transfers between devices: 6.16 us -> 9.5 us  [gather_strip(): right = lax.ppermute(column, 'rg', [(i + 1, i) for i in range(n_rg - 1)])]
    convert_element_type x0 -> x2, other arithmetic: none -> 1.94 us  [the longest x1 1.29 us: mean_multilook(): col_ok.astype(jnp.float32)[None, :]]
  transfers between devices with their start and end apart: 15 -> 15, of which waited for: 10 -> 8; matrix products, arithmetic and copies ran while one was open for 2% -> 1% of each run, Pallas kernels for 0% -> 0%
where the time goes in v6:
time: 190 us; the launch traced here: 188 us
  starting transfers between devices  62.3 us (33%)
  waiting for transfers between devices  46 us (24%)
  matrix products  25.3 us (13%)
  local copies, waits for them, and re-layouts  20.2 us (11%)
  other arithmetic  15.7 us (8%)
  between operations  11.3 us (6%)
  Pallas kernels  7.66 us (4%)
    all_to_all x3, waiting for transfers between devices, gather_strip(): got = lax.all_to_all(sent, 'az', 0, 0, tiled=True)  23.7 us
    all_to_all x3, starting transfers between devices, gather_strip(): got = lax.all_to_all(sent, 'az', 0, 0, tiled=True)  16.3 us
    dot_general x48, matrix products, sandwich(): inner = jnp.dot(left, vector, precision=HIGHEST)  13.8 us
    all_to_all x2, starting transfers between devices, gather_strip(): lax.all_to_all(jnp.broadcast_to(column_sums[None], (n_rg, sums.shape[0]))...  11.1 us
    dot_general x48, matrix products, sandwich(): return jnp.dot(inner, right, precision=HIGHEST)  11 us
    ppermute x3, starting transfers between devices, gather_strip(): left = lax.ppermute(column, 'rg', [(i, i + 1) for i in range(n_rg - 1)])  9.78 us
    ppermute x3, starting transfers between devices, gather_strip(): right = lax.ppermute(column, 'rg', [(i + 1, i) for i in range(n_rg - 1)])  9.5 us
    all_to_all x1, waiting for transfers between devices, total(): got = lax.all_to_all(sent, ('az', 'rg'), 0, 0, tiled=True)  9.4 us
  transfers between devices with their start and end apart: 15, of which 8 were waited for; matrix products, arithmetic and copies ran while one was open for 1% of the time, Pallas kernels for 0%

profile of v6, /device:TPU:1, one launch (start us, length us, event | category | flops | bytes accessed | tf_op | source)
XLA Modules:
  0.0 188.5 jit_solution(1619298890456923604)
XLA Ops:
  2.6 2.4 %copy.24.lead_ref = bf16[2,20,10240]{2,1,0:T(8,128)(2,1)} copy(bf16[2,20,10240]{2,0,1:T(2,128)(2,1)} %param.8) | data formatting | bytes 1638400 | tf_op args[0]
  10.1 7.7 %shard_map.59 = f32[4,4,10240]{2,1,0:T(4,128)} custom-call(bf16[2,20,10240]{2,1,0:T(8,128)(2,1)} %copy.24.lead_ref, bf16[2,20,10240]{2,1,0:T(8,128)(2,1)} %copy.25.trail_ref, f32[20,128]{1,0:T(8,128)} %broadcast_in_dim.18.row_ref, f32[1,10240]{1,0:T(1,128)} %and_convert_fusion.col_ref), custom_call_target="tpu_custom_call" | custom-call | tf_op jit(solution)/shard_map/pallas_call | solution.py:86
  25.2 5.8 %all-to-all-start = ((f32[8,3,4,270]{3,2,1,0:T(4,128)}), f32[8,3,4,270]{3,2,1,0:T(4,128)S(1)}, u32[]{:S(2)}, u32[]{:S(2)}) async-start(f32[8,3,4,270]{3,2,1,0:T(4,128)} %fusion.561), calls=%async_computation | async-start | bytes 294912 | tf_op jit(solution)/shard_map/all_to_all | solution.py:262
  31.5 5.0 %all-to-all-done = f32[8,3,4,270]{3,2,1,0:T(4,128)S(1)} async-done(((f32[8,3,4,270]{3,2,1,0:T(4,128)}), f32[8,3,4,270]{3,2,1,0:T(4,128)S(1)}, u32[]{:S(2)}, u32[]{:S(2)}) %all-to-all-start) | async-done | bytes 103712 | tf_op jit(solution)/shard_map/all_to_all | solution.py:262
  36.6 3.2 %collective-permute-start = (f32[3,7,270]{2,1,0:T(8,128)S(1)}, f32[3,7,270]{2,1,0:T(8,128)S(1)}, u32[]{:S(2)}, u32[]{:S(2)}) collective-permute-start(f32[3,7,270]{2,1,0:T(8,128)S(1)} %get-tuple-element.51), channel_id=1, source_target_pairs={{0,8},{8,16},{16,24},{24,32},{32,40},{40,48},{48,56},{56,64},{64,7... | collective-permute-start | bytes 68048 | tf_op jit(solution)/shard_map/ppermute | solution.py:265
  41.1 3.4 %collective-permute-done.1 = f32[3,7,270]{2,1,0:T(8,128)S(1)} collective-permute-done((f32[3,7,270]{2,1,0:T(8,128)S(1)}, f32[3,7,270]{2,1,0:T(8,128)S(1)}, u32[]{:S(2)}, u32[]{:S(2)}) %collective-permute-start.1) | collective-permute-done | bytes 22712 | tf_op jit(solution)/shard_map/ppermute | solution.py:266
  47.1 9.2 %all-to-all-start.1 = ((f32[16,3,16,128]{3,2,1,0:T(8,128)}), f32[16,3,16,128]{3,2,1,0:T(8,128)S(1)}, u32[]{:S(2)}, u32[]{:S(2)}) async-start(f32[16,3,16,128]{3,2,1,0:T(8,128)} %broadcast_in_dim.19), calls=%async_computation.1 | async-start | bytes 786432 | tf_op jit(solution)/shard_map/all_to_all | solution.py:198
  56.4 8.2 %all-to-all-done.1 = f32[16,3,16,128]{3,2,1,0:T(8,128)S(1)} async-done(((f32[16,3,16,128]{3,2,1,0:T(8,128)}), f32[16,3,16,128]{3,2,1,0:T(8,128)S(1)}, u32[]{:S(2)}, u32[]{:S(2)}) %all-to-all-start.1) | async-done | bytes 393248 | tf_op jit(solution)/shard_map/all_to_all | solution.py:198
  64.6 5.7 %collective-permute-start.3 = (f32[3,256,128]{2,1,0:T(8,128)S(1)}, f32[3,256,128]{2,1,0:T(8,128)S(1)}, u32[]{:S(2)}, u32[]{:S(2)}) collective-permute-start(f32[3,256,128]{2,1,0:T(8,128)S(1)} %bitcast.193), channel_id=1, source_target_pairs={{1,0},{2,1},{3,2},{4,3},{5,4},{6,5},{7,6},{9,8},{10,9},{11,10},{12... | collective-permute-start | bytes 1179656 | tf_op jit(solution)/shard_map/ppermute | solution.py:207
  70.3 2.3 %collective-permute-start.2 = (f32[3,256,128]{2,1,0:T(8,128)S(1)}, f32[3,256,128]{2,1,0:T(8,128)S(1)}, u32[]{:S(2)}, u32[]{:S(2)}) collective-permute-start(f32[3,256,128]{2,1,0:T(8,128)S(1)} %bitcast.194), channel_id=1, source_target_pairs={{0,1},{1,2},{2,3},{3,4},{4,5},{5,6},{6,7},{8,9},{9,10},{10,11},{11... | collective-permute-start | bytes 1179656 | tf_op jit(solution)/shard_map/ppermute | solution.py:206
  72.6 3.3 %collective-permute-done.3 = f32[3,256,128]{2,1,0:T(8,128)S(1)} collective-permute-done((f32[3,256,128]{2,1,0:T(8,128)S(1)}, f32[3,256,128]{2,1,0:T(8,128)S(1)}, u32[]{:S(2)}, u32[]{:S(2)}) %collective-permute-start.3) | collective-permute-done | bytes 393248 | tf_op jit(solution)/shard_map/ppermute | solution.py:207
  94.6 3.5 %all-to-all-start.2 = ((f32[16,2,16,128]{3,2,1,0:T(8,128)}), f32[16,2,16,128]{3,2,1,0:T(8,128)S(1)}, u32[]{:S(2)}, u32[]{:S(2)}) async-start(f32[16,2,16,128]{3,2,1,0:T(8,128)} %broadcast_in_dim.21), calls=%async_computation.2 | async-start | bytes 524288 | tf_op jit(solution)/shard_map/all_to_all | solution.py:198
  98.2 7.5 %all-to-all-done.2 = f32[16,2,16,128]{3,2,1,0:T(8,128)S(1)} async-done(((f32[16,2,16,128]{3,2,1,0:T(8,128)}), f32[16,2,16,128]{3,2,1,0:T(8,128)S(1)}, u32[]{:S(2)}, u32[]{:S(2)}) %all-to-all-start.2) | async-done | bytes 262176 | tf_op jit(solution)/shard_map/all_to_all | solution.py:198
  106.3 5.9 %all-to-all-start.3 = ((f32[8,1,2]{2,1,0:T(1,128)}), f32[8,1,2]{2,1,0:T(1,128)S(1)}, u32[]{:S(2)}, u32[]{:S(2)}) async-start(f32[8,1,2]{2,1,0:T(1,128)} %broadcast_in_dim.22), calls=%async_computation.3 | async-start | bytes 8192 | tf_op jit(solution)/shard_map/all_to_all | solution.py:202
  112.2 1.9 %collective-permute-start.5 = (f32[1,256,128]{2,1,0:T(8,128)S(1)}, f32[1,256,128]{2,1,0:T(8,128)S(1)}, u32[]{:S(2)}, u32[]{:S(2)}) collective-permute-start(f32[1,256,128]{2,1,0:T(8,128)S(1)} %bitcast.201), channel_id=1, source_target_pairs={{1,0},{2,1},{3,2},{4,3},{5,4},{6,5},{7,6},{9,8},{10,9},{11,10},{12... | collective-permute-start | bytes 393224 | tf_op jit(solution)/shard_map/ppermute | solution.py:207
  114.1 3.9 %collective-permute-start.4 = (f32[1,256,128]{2,1,0:T(8,128)S(1)}, f32[1,256,128]{2,1,0:T(8,128)S(1)}, u32[]{:S(2)}, u32[]{:S(2)}) collective-permute-start(f32[1,256,128]{2,1,0:T(8,128)S(1)} %bitcast.202), channel_id=1, source_target_pairs={{0,1},{1,2},{2,3},{3,4},{4,5},{5,6},{6,7},{8,9},{9,10},{10,11},{11... | collective-permute-start | bytes 393224 | tf_op jit(solution)/shard_map/ppermute | solution.py:206
  127.9 2.0 %maximum_bitcast_fusion.5 = f32[1,1,3]{2,1,0:T(1,128)S(1)} fusion(f32[1]{0:T(128)} %bitcast.38, f32[1]{0:T(128)} %bitcast.37, f32[1]{0:T(128)} %bitcast.36), kind=kLoop, calls=%fused_computation.1278 | loop fusion | flops 6 | bytes 24 | tf_op jit(solution)/shard_map/reshape.48
  130.6 3.5 %all-to-all-start.4 = ((f32[16,2,16,128]{3,2,1,0:T(8,128)}), f32[16,2,16,128]{3,2,1,0:T(8,128)S(1)}, u32[]{:S(2)}, u32[]{:S(2)}) async-start(f32[16,2,16,128]{3,2,1,0:T(8,128)} %broadcast_in_dim.24), calls=%async_computation.4 | async-start | bytes 524288 | tf_op jit(solution)/shard_map/all_to_all | solution.py:198
  134.9 8.1 %all-to-all-done.4 = f32[16,2,16,128]{3,2,1,0:T(8,128)S(1)} async-done(((f32[16,2,16,128]{3,2,1,0:T(8,128)}), f32[16,2,16,128]{3,2,1,0:T(8,128)S(1)}, u32[]{:S(2)}, u32[]{:S(2)}) %all-to-all-start.4) | async-done | bytes 262176 | tf_op jit(solution)/shard_map/all_to_all | solution.py:198
  143.7 5.2 %all-to-all-start.5 = ((f32[8,1,3]{2,1,0:T(1,128)}), f32[8,1,3]{2,1,0:T(1,128)S(1)}, u32[]{:S(2)}, u32[]{:S(2)}) async-start(f32[8,1,3]{2,1,0:T(1,128)} %broadcast_in_dim.25), calls=%async_computation.5 | async-start | bytes 8192 | tf_op jit(solution)/shard_map/all_to_all | solution.py:202
  150.8 3.6 %collective-permute-start.6 = (f32[1,256,128]{2,1,0:T(8,128)S(1)}, f32[1,256,128]{2,1,0:T(8,128)S(1)}, u32[]{:S(2)}, u32[]{:S(2)}) collective-permute-start(f32[1,256,128]{2,1,0:T(8,128)S(1)} %bitcast.197), channel_id=1, source_target_pairs={{0,1},{1,2},{2,3},{3,4},{4,5},{5,6},{6,7},{8,9},{9,10},{10,11},{11... | collective-permute-start | bytes 393224 | tf_op jit(solution)/shard_map/ppermute | solution.py:206
  166.3 2.0 %pad_maximum_fusion.4 = f32[3]{0:T(128)S(1)} fusion(f32[1]{0:T(128)} %bitcast.47, f32[1]{0:T(128)} %bitcast.46, f32[1]{0:T(128)} %bitcast.45), kind=kLoop, calls=%fused_computation.1279 | loop fusion | flops 6 | bytes 24 | tf_op jit(solution)/shard_map/stack | solution.py:335
  168.9 5.3 %all-to-all-start.6 = ((f32[128,1,3]{2,1,0:T(1,128)}), f32[128,1,3]{2,1,0:T(1,128)S(1)}, u32[]{:S(2)}, u32[]{:S(2)}) async-start(f32[128,1,3]{2,1,0:T(1,128)} %broadcast_in_dim.26), calls=%async_computation.6 | async-start | bytes 131072 | tf_op jit(solution)/shard_map/all_to_all | solution.py:220
  174.4 9.4 %all-to-all-done.6 = f32[128,1,3]{2,1,0:T(1,128)S(1)} async-done(((f32[128,1,3]{2,1,0:T(1,128)}), f32[128,1,3]{2,1,0:T(1,128)S(1)}, u32[]{:S(2)}, u32[]{:S(2)}) %all-to-all-start.6) | async-done | bytes 1568 | tf_op jit(solution)/shard_map/all_to_all | solution.py:220
  (239 shorter events, 59.3 us)
Async XLA Ops:
  0.6 4.3 %copy-start = (bf16[2,20,10240]{2,0,1:T(2,128)(2,1)S(1)}, bf16[2,20,10240]{2,0,1:T(2,128)(2,1)}, u32[]{:S(2)}) copy-start(bf16[2,20,10240]{2,0,1:T(2,128)(2,1)} %param.9) | copy-start | bytes 2457604
  25.2 11.2 %all-to-all-start = ((f32[8,3,4,270]{3,2,1,0:T(4,128)}), f32[8,3,4,270]{3,2,1,0:T(4,128)S(1)}, u32[]{:S(2)}, u32[]{:S(2)}) async-start(f32[8,3,4,270]{3,2,1,0:T(4,128)} %fusion.561), calls=%async_computation | async-start | bytes 294912 | tf_op jit(solution)/shard_map/all_to_all | solution.py:262
  36.6 4.5 %collective-permute-start = (f32[3,7,270]{2,1,0:T(8,128)S(1)}, f32[3,7,270]{2,1,0:T(8,128)S(1)}, u32[]{:S(2)}, u32[]{:S(2)}) collective-permute-start(f32[3,7,270]{2,1,0:T(8,128)S(1)} %get-tuple-element.51), channel_id=1, source_target_pairs={{0,8},{8,16},{16,24},{24,32},{32,40},{40,48},{48,56},{56,64},{64,7... | collective-permute-start | bytes 68048 | tf_op jit(solution)/shard_map/ppermute | solution.py:265
  39.8 4.7 %collective-permute-start.1 = (f32[3,7,270]{2,1,0:T(8,128)S(1)}, f32[3,7,270]{2,1,0:T(8,128)S(1)}, u32[]{:S(2)}, u32[]{:S(2)}) collective-permute-start(f32[3,7,270]{2,1,0:T(8,128)S(1)} %get-tuple-element.52), channel_id=1, source_target_pairs={{8,0},{16,8},{24,16},{32,24},{40,32},{48,40},{56,48},{64,56},{72,6... | collective-permute-start | bytes 68048 | tf_op jit(solution)/shard_map/ppermute | solution.py:266
  47.1 17.5 %all-to-all-start.1 = ((f32[16,3,16,128]{3,2,1,0:T(8,128)}), f32[16,3,16,128]{3,2,1,0:T(8,128)S(1)}, u32[]{:S(2)}, u32[]{:S(2)}) async-start(f32[16,3,16,128]{3,2,1,0:T(8,128)} %broadcast_in_dim.19), calls=%async_computation.1 | async-start | bytes 786432 | tf_op jit(solution)/shard_map/all_to_all | solution.py:198
  64.6 11.3 %collective-permute-start.3 = (f32[3,256,128]{2,1,0:T(8,128)S(1)}, f32[3,256,128]{2,1,0:T(8,128)S(1)}, u32[]{:S(2)}, u32[]{:S(2)}) collective-permute-start(f32[3,256,128]{2,1,0:T(8,128)S(1)} %bitcast.193), channel_id=1, source_target_pairs={{1,0},{2,1},{3,2},{4,3},{5,4},{6,5},{7,6},{9,8},{10,9},{11,10},{12... | collective-permute-start | bytes 1179656 | tf_op jit(solution)/shard_map/ppermute | solution.py:207
  70.3 6.8 %collective-permute-start.2 = (f32[3,256,128]{2,1,0:T(8,128)S(1)}, f32[3,256,128]{2,1,0:T(8,128)S(1)}, u32[]{:S(2)}, u32[]{:S(2)}) collective-permute-start(f32[3,256,128]{2,1,0:T(8,128)S(1)} %bitcast.194), channel_id=1, source_target_pairs={{0,1},{1,2},{2,3},{3,4},{4,5},{5,6},{6,7},{8,9},{9,10},{10,11},{11... | collective-permute-start | bytes 1179656 | tf_op jit(solution)/shard_map/ppermute | solution.py:206
  94.6 11.0 %all-to-all-start.2 = ((f32[16,2,16,128]{3,2,1,0:T(8,128)}), f32[16,2,16,128]{3,2,1,0:T(8,128)S(1)}, u32[]{:S(2)}, u32[]{:S(2)}) async-start(f32[16,2,16,128]{3,2,1,0:T(8,128)} %broadcast_in_dim.21), calls=%async_computation.2 | async-start | bytes 524288 | tf_op jit(solution)/shard_map/all_to_all | solution.py:198
  106.3 11.7 %all-to-all-start.3 = ((f32[8,1,2]{2,1,0:T(1,128)}), f32[8,1,2]{2,1,0:T(1,128)S(1)}, u32[]{:S(2)}, u32[]{:S(2)}) async-start(f32[8,1,2]{2,1,0:T(1,128)} %broadcast_in_dim.22), calls=%async_computation.3 | async-start | bytes 8192 | tf_op jit(solution)/shard_map/all_to_all | solution.py:202
  112.2 7.8 %collective-permute-start.5 = (f32[1,256,128]{2,1,0:T(8,128)S(1)}, f32[1,256,128]{2,1,0:T(8,128)S(1)}, u32[]{:S(2)}, u32[]{:S(2)}) collective-permute-start(f32[1,256,128]{2,1,0:T(8,128)S(1)} %bitcast.201), channel_id=1, source_target_pairs={{1,0},{2,1},{3,2},{4,3},{5,4},{6,5},{7,6},{9,8},{10,9},{11,10},{12... | collective-permute-start | bytes 393224 | tf_op jit(solution)/shard_map/ppermute | solution.py:207
  114.1 5.9 %collective-permute-start.4 = (f32[1,256,128]{2,1,0:T(8,128)S(1)}, f32[1,256,128]{2,1,0:T(8,128)S(1)}, u32[]{:S(2)}, u32[]{:S(2)}) collective-permute-start(f32[1,256,128]{2,1,0:T(8,128)S(1)} %bitcast.202), channel_id=1, source_target_pairs={{0,1},{1,2},{2,3},{3,4},{4,5},{5,6},{6,7},{8,9},{9,10},{10,11},{11... | collective-permute-start | bytes 393224 | tf_op jit(solution)/shard_map/ppermute | solution.py:206
  130.6 12.4 %all-to-all-start.4 = ((f32[16,2,16,128]{3,2,1,0:T(8,128)}), f32[16,2,16,128]{3,2,1,0:T(8,128)S(1)}, u32[]{:S(2)}, u32[]{:S(2)}) async-start(f32[16,2,16,128]{3,2,1,0:T(8,128)} %broadcast_in_dim.24), calls=%async_computation.4 | async-start | bytes 524288 | tf_op jit(solution)/shard_map/all_to_all | solution.py:198
  143.7 10.8 %all-to-all-start.5 = ((f32[8,1,3]{2,1,0:T(1,128)}), f32[8,1,3]{2,1,0:T(1,128)S(1)}, u32[]{:S(2)}, u32[]{:S(2)}) async-start(f32[8,1,3]{2,1,0:T(1,128)} %broadcast_in_dim.25), calls=%async_computation.5 | async-start | bytes 8192 | tf_op jit(solution)/shard_map/all_to_all | solution.py:202
  148.9 10.2 %collective-permute-start.7 = (f32[1,256,128]{2,1,0:T(8,128)S(1)}, f32[1,256,128]{2,1,0:T(8,128)S(1)}, u32[]{:S(2)}, u32[]{:S(2)}) collective-permute-start(f32[1,256,128]{2,1,0:T(8,128)S(1)} %bitcast.196), channel_id=1, source_target_pairs={{1,0},{2,1},{3,2},{4,3},{5,4},{6,5},{7,6},{9,8},{10,9},{11,10},{12... | collective-permute-start | bytes 393224 | tf_op jit(solution)/shard_map/ppermute | solution.py:207
  150.8 8.3 %collective-permute-start.6 = (f32[1,256,128]{2,1,0:T(8,128)S(1)}, f32[1,256,128]{2,1,0:T(8,128)S(1)}, u32[]{:S(2)}, u32[]{:S(2)}) collective-permute-start(f32[1,256,128]{2,1,0:T(8,128)S(1)} %bitcast.197), channel_id=1, source_target_pairs={{0,1},{1,2},{2,3},{3,4},{4,5},{5,6},{6,7},{8,9},{9,10},{10,11},{11... | collective-permute-start | bytes 393224 | tf_op jit(solution)/shard_map/ppermute | solution.py:206
  168.9 14.9 %all-to-all-start.6 = ((f32[128,1,3]{2,1,0:T(1,128)}), f32[128,1,3]{2,1,0:T(1,128)S(1)}, u32[]{:S(2)}, u32[]{:S(2)}) async-start(f32[128,1,3]{2,1,0:T(1,128)} %broadcast_in_dim.26), calls=%async_computation.6 | async-start | bytes 131072 | tf_op jit(solution)/shard_map/all_to_all | solution.py:220

commit v7 on v6

--- a/solution.py
+++ b/solution.py
@@ -257,8 +257,11 @@
     fields = jnp.stack([look_re, look_im, weight])
     n_fields, rows_here, cols_all = fields.shape
     cols_here = cols_all // n_range
-    fields = jnp.pad(fields, ((0, 0), (0, 0), (border, border)))
-    fields = jnp.stack([fields[:, :, c * cols_here:(c + 1) * cols_here + 2 * border] for c in range(n_range)])
+    main = fields.reshape(n_fields, rows_here, n_range, cols_here).transpose(2, 0, 1, 3)
+    zero = jnp.zeros((1, n_fields, rows_here, border), jnp.float32)
+    before = jnp.concatenate([zero, main[:-1, :, :, -border:]], axis=0)
+    after = jnp.concatenate([main[1:, :, :, :border], zero], axis=0)
+    fields = jnp.concatenate([before, main, after], axis=-1)
     fields = lax.all_to_all(fields, "rg", 0, 0, tiled=True)
     fields = fields.transpose(1, 0, 2, 3).reshape(n_fields, n_range * rows_here, cols_here + 2 * border)
     shard_height_total = n_range * rows_here

time: 190 us -> 185 us (0.974)
  local copies, waits for them, and re-layouts: 20.2 us -> 15.5 us
    unnamed x11 -> x4, local copies, waits for them, and re-layouts: 8.35 us -> 3.58 us
where the time goes in v7:
time: 185 us; the launch traced here: 184 us
  starting transfers between devices  62.4 us (34%)
  waiting for transfers between devices  46 us (25%)
  matrix products  25.3 us (14%)
  other arithmetic  15.9 us (9%)
  local copies, waits for them, and re-layouts  15.5 us (8%)
  between operations  11.3 us (6%)
  Pallas kernels  7.64 us (4%)
    all_to_all x3, waiting for transfers between devices, gather_strip(): got = lax.all_to_all(sent, 'az', 0, 0, tiled=True)  23.7 us
    all_to_all x3, starting transfers between devices, gather_strip(): got = lax.all_to_all(sent, 'az', 0, 0, tiled=True)  16.3 us
    dot_general x48, matrix products, sandwich(): inner = jnp.dot(left, vector, precision=HIGHEST)  13.8 us
    all_to_all x2, starting transfers between devices, gather_strip(): lax.all_to_all(jnp.broadcast_to(column_sums[None], (n_rg, sums.shape[0]))...  11.3 us
    dot_general x48, matrix products, sandwich(): return jnp.dot(inner, right, precision=HIGHEST)  11 us
    ppermute x3, starting transfers between devices, gather_strip(): left = lax.ppermute(column, 'rg', [(i, i + 1) for i in range(n_rg - 1)])  9.78 us
    ppermute x3, starting transfers between devices, gather_strip(): right = lax.ppermute(column, 'rg', [(i + 1, i) for i in range(n_rg - 1)])  9.5 us
    all_to_all x1, waiting for transfers between devices, total(): got = lax.all_to_all(sent, ('az', 'rg'), 0, 0, tiled=True)  9.43 us
  transfers between devices with their start and end apart: 15, of which 8 were waited for; matrix products, arithmetic and copies ran while one was open for 1% of the time, Pallas kernels for 0%

profile of v7, /device:TPU:1, one launch (start us, length us, event | category | flops | bytes accessed | tf_op | source)
XLA Modules:
  0.0 184.1 jit_solution(7205224971167017003)
XLA Ops:
  2.6 2.4 %copy.59.lead_ref = bf16[2,20,10240]{2,1,0:T(8,128)(2,1)} copy(bf16[2,20,10240]{2,0,1:T(2,128)(2,1)} %param.8) | data formatting | bytes 1638400 | tf_op args[0]
  10.1 7.6 %shard_map.59 = f32[4,4,10240]{2,1,0:T(4,128)} custom-call(bf16[2,20,10240]{2,1,0:T(8,128)(2,1)} %copy.59.lead_ref, bf16[2,20,10240]{2,1,0:T(8,128)(2,1)} %copy.60.trail_ref, f32[20,128]{1,0:T(8,128)} %broadcast_in_dim.18.row_ref, f32[1,10240]{1,0:T(1,128)} %and_convert_fusion.col_ref), custom_call_target="tpu_custom_call" | custom-call | tf_op jit(solution)/shard_map/pallas_call | solution.py:86
  20.6 5.8 %all-to-all-start = ((f32[8,3,4,270]{3,2,1,0:T(4,128)}), f32[8,3,4,270]{3,2,1,0:T(4,128)S(1)}, u32[]{:S(2)}, u32[]{:S(2)}) async-start(f32[8,3,4,270]{3,2,1,0:T(4,128)} %copy.61), calls=%async_computation | async-start | bytes 294912 | tf_op jit(solution)/shard_map/all_to_all | solution.py:265
  26.8 5.0 %all-to-all-done = f32[8,3,4,270]{3,2,1,0:T(4,128)S(1)} async-done(((f32[8,3,4,270]{3,2,1,0:T(4,128)}), f32[8,3,4,270]{3,2,1,0:T(4,128)S(1)}, u32[]{:S(2)}, u32[]{:S(2)}) %all-to-all-start) | async-done | bytes 103712 | tf_op jit(solution)/shard_map/all_to_all | solution.py:265
  31.9 3.2 %collective-permute-start = (f32[3,7,270]{2,1,0:T(8,128)S(1)}, f32[3,7,270]{2,1,0:T(8,128)S(1)}, u32[]{:S(2)}, u32[]{:S(2)}) collective-permute-start(f32[3,7,270]{2,1,0:T(8,128)S(1)} %get-tuple-element.51), channel_id=1, source_target_pairs={{0,8},{8,16},{16,24},{24,32},{32,40},{40,48},{48,56},{56,64},{64,7... | collective-permute-start | bytes 68048 | tf_op jit(solution)/shard_map/ppermute | solution.py:268
  36.5 3.4 %collective-permute-done.1 = f32[3,7,270]{2,1,0:T(8,128)S(1)} collective-permute-done((f32[3,7,270]{2,1,0:T(8,128)S(1)}, f32[3,7,270]{2,1,0:T(8,128)S(1)}, u32[]{:S(2)}, u32[]{:S(2)}) %collective-permute-start.1) | collective-permute-done | bytes 22712 | tf_op jit(solution)/shard_map/ppermute | solution.py:269
  42.5 9.2 %all-to-all-start.1 = ((f32[16,3,16,128]{3,2,1,0:T(8,128)}), f32[16,3,16,128]{3,2,1,0:T(8,128)S(1)}, u32[]{:S(2)}, u32[]{:S(2)}) async-start(f32[16,3,16,128]{3,2,1,0:T(8,128)} %broadcast_in_dim.19), calls=%async_computation.1 | async-start | bytes 786432 | tf_op jit(solution)/shard_map/all_to_all | solution.py:198
  51.8 8.2 %all-to-all-done.1 = f32[16,3,16,128]{3,2,1,0:T(8,128)S(1)} async-done(((f32[16,3,16,128]{3,2,1,0:T(8,128)}), f32[16,3,16,128]{3,2,1,0:T(8,128)S(1)}, u32[]{:S(2)}, u32[]{:S(2)}) %all-to-all-start.1) | async-done | bytes 393248 | tf_op jit(solution)/shard_map/all_to_all | solution.py:198
  60.0 5.7 %collective-permute-start.3 = (f32[3,256,128]{2,1,0:T(8,128)S(1)}, f32[3,256,128]{2,1,0:T(8,128)S(1)}, u32[]{:S(2)}, u32[]{:S(2)}) collective-permute-start(f32[3,256,128]{2,1,0:T(8,128)S(1)} %bitcast.163), channel_id=1, source_target_pairs={{1,0},{2,1},{3,2},{4,3},{5,4},{6,5},{7,6},{9,8},{10,9},{11,10},{12... | collective-permute-start | bytes 1179656 | tf_op jit(solution)/shard_map/ppermute | solution.py:207
  65.7 2.3 %collective-permute-start.2 = (f32[3,256,128]{2,1,0:T(8,128)S(1)}, f32[3,256,128]{2,1,0:T(8,128)S(1)}, u32[]{:S(2)}, u32[]{:S(2)}) collective-permute-start(f32[3,256,128]{2,1,0:T(8,128)S(1)} %bitcast.164), channel_id=1, source_target_pairs={{0,1},{1,2},{2,3},{3,4},{4,5},{5,6},{6,7},{8,9},{9,10},{10,11},{11... | collective-permute-start | bytes 1179656 | tf_op jit(solution)/shard_map/ppermute | solution.py:206
  68.0 3.3 %collective-permute-done.3 = f32[3,256,128]{2,1,0:T(8,128)S(1)} collective-permute-done((f32[3,256,128]{2,1,0:T(8,128)S(1)}, f32[3,256,128]{2,1,0:T(8,128)S(1)}, u32[]{:S(2)}, u32[]{:S(2)}) %collective-permute-start.3) | collective-permute-done | bytes 393248 | tf_op jit(solution)/shard_map/ppermute | solution.py:207
  90.0 3.5 %all-to-all-start.2 = ((f32[16,2,16,128]{3,2,1,0:T(8,128)}), f32[16,2,16,128]{3,2,1,0:T(8,128)S(1)}, u32[]{:S(2)}, u32[]{:S(2)}) async-start(f32[16,2,16,128]{3,2,1,0:T(8,128)} %broadcast_in_dim.21), calls=%async_computation.2 | async-start | bytes 524288 | tf_op jit(solution)/shard_map/all_to_all | solution.py:198
  93.6 7.5 %all-to-all-done.2 = f32[16,2,16,128]{3,2,1,0:T(8,128)S(1)} async-done(((f32[16,2,16,128]{3,2,1,0:T(8,128)}), f32[16,2,16,128]{3,2,1,0:T(8,128)S(1)}, u32[]{:S(2)}, u32[]{:S(2)}) %all-to-all-start.2) | async-done | bytes 262176 | tf_op jit(solution)/shard_map/all_to_all | solution.py:198
  101.7 5.9 %all-to-all-start.3 = ((f32[8,1,2]{2,1,0:T(1,128)}), f32[8,1,2]{2,1,0:T(1,128)S(1)}, u32[]{:S(2)}, u32[]{:S(2)}) async-start(f32[8,1,2]{2,1,0:T(1,128)} %broadcast_in_dim.22), calls=%async_computation.3 | async-start | bytes 8192 | tf_op jit(solution)/shard_map/all_to_all | solution.py:202
  107.6 1.9 %collective-permute-start.5 = (f32[1,256,128]{2,1,0:T(8,128)S(1)}, f32[1,256,128]{2,1,0:T(8,128)S(1)}, u32[]{:S(2)}, u32[]{:S(2)}) collective-permute-start(f32[1,256,128]{2,1,0:T(8,128)S(1)} %bitcast.171), channel_id=1, source_target_pairs={{1,0},{2,1},{3,2},{4,3},{5,4},{6,5},{7,6},{9,8},{10,9},{11,10},{12... | collective-permute-start | bytes 393224 | tf_op jit(solution)/shard_map/ppermute | solution.py:207
  109.5 3.9 %collective-permute-start.4 = (f32[1,256,128]{2,1,0:T(8,128)S(1)}, f32[1,256,128]{2,1,0:T(8,128)S(1)}, u32[]{:S(2)}, u32[]{:S(2)}) collective-permute-start(f32[1,256,128]{2,1,0:T(8,128)S(1)} %bitcast.172), channel_id=1, source_target_pairs={{0,1},{1,2},{2,3},{3,4},{4,5},{5,6},{6,7},{8,9},{9,10},{10,11},{11... | collective-permute-start | bytes 393224 | tf_op jit(solution)/shard_map/ppermute | solution.py:206
  123.2 2.0 %maximum_bitcast_fusion.6 = f32[1,1,3]{2,1,0:T(1,128)S(1)} fusion(f32[1]{0:T(128)} %bitcast.31, f32[1]{0:T(128)} %bitcast.30, f32[1]{0:T(128)} %bitcast.29), kind=kLoop, calls=%fused_computation.1263 | loop fusion | flops 6 | bytes 24 | tf_op jit(solution)/shard_map/reshape.49
  125.9 3.5 %all-to-all-start.4 = ((f32[16,2,16,128]{3,2,1,0:T(8,128)}), f32[16,2,16,128]{3,2,1,0:T(8,128)S(1)}, u32[]{:S(2)}, u32[]{:S(2)}) async-start(f32[16,2,16,128]{3,2,1,0:T(8,128)} %broadcast_in_dim.24), calls=%async_computation.4 | async-start | bytes 524288 | tf_op jit(solution)/shard_map/all_to_all | solution.py:198
  130.2 8.1 %all-to-all-done.4 = f32[16,2,16,128]{3,2,1,0:T(8,128)S(1)} async-done(((f32[16,2,16,128]{3,2,1,0:T(8,128)}), f32[16,2,16,128]{3,2,1,0:T(8,128)S(1)}, u32[]{:S(2)}, u32[]{:S(2)}) %all-to-all-start.4) | async-done | bytes 262176 | tf_op jit(solution)/shard_map/all_to_all | solution.py:198
  138.9 5.4 %all-to-all-start.5 = ((f32[8,1,3]{2,1,0:T(1,128)}), f32[8,1,3]{2,1,0:T(1,128)S(1)}, u32[]{:S(2)}, u32[]{:S(2)}) async-start(f32[8,1,3]{2,1,0:T(1,128)} %broadcast_in_dim.25), calls=%async_computation.5 | async-start | bytes 8192 | tf_op jit(solution)/shard_map/all_to_all | solution.py:202
  146.2 3.6 %collective-permute-start.6 = (f32[1,256,128]{2,1,0:T(8,128)S(1)}, f32[1,256,128]{2,1,0:T(8,128)S(1)}, u32[]{:S(2)}, u32[]{:S(2)}) collective-permute-start(f32[1,256,128]{2,1,0:T(8,128)S(1)} %bitcast.167), channel_id=1, source_target_pairs={{0,1},{1,2},{2,3},{3,4},{4,5},{5,6},{6,7},{8,9},{9,10},{10,11},{11... | collective-permute-start | bytes 393224 | tf_op jit(solution)/shard_map/ppermute | solution.py:206
  161.6 2.0 %pad_maximum_fusion.3 = f32[3]{0:T(128)S(1)} fusion(f32[1]{0:T(128)} %bitcast.40, f32[1]{0:T(128)} %bitcast.39, f32[1]{0:T(128)} %bitcast.38), kind=kLoop, calls=%fused_computation.1264 | loop fusion | flops 6 | bytes 24 | tf_op jit(solution)/shard_map/stack | solution.py:338
  164.3 5.3 %all-to-all-start.6 = ((f32[128,1,3]{2,1,0:T(1,128)}), f32[128,1,3]{2,1,0:T(1,128)S(1)}, u32[]{:S(2)}, u32[]{:S(2)}) async-start(f32[128,1,3]{2,1,0:T(1,128)} %broadcast_in_dim.26), calls=%async_computation.6 | async-start | bytes 131072 | tf_op jit(solution)/shard_map/all_to_all | solution.py:220
  169.8 9.4 %all-to-all-done.6 = f32[128,1,3]{2,1,0:T(1,128)S(1)} async-done(((f32[128,1,3]{2,1,0:T(1,128)}), f32[128,1,3]{2,1,0:T(1,128)S(1)}, u32[]{:S(2)}, u32[]{:S(2)}) %all-to-all-start.6) | async-done | bytes 1568 | tf_op jit(solution)/shard_map/all_to_all | solution.py:220
  (234 shorter events, 54.7 us)
Async XLA Ops:
  0.6 4.4 %copy-start = (bf16[2,20,10240]{2,0,1:T(2,128)(2,1)S(1)}, bf16[2,20,10240]{2,0,1:T(2,128)(2,1)}, u32[]{:S(2)}) copy-start(bf16[2,20,10240]{2,0,1:T(2,128)(2,1)} %param.9) | copy-start | bytes 2457604
  20.6 11.2 %all-to-all-start = ((f32[8,3,4,270]{3,2,1,0:T(4,128)}), f32[8,3,4,270]{3,2,1,0:T(4,128)S(1)}, u32[]{:S(2)}, u32[]{:S(2)}) async-start(f32[8,3,4,270]{3,2,1,0:T(4,128)} %copy.61), calls=%async_computation | async-start | bytes 294912 | tf_op jit(solution)/shard_map/all_to_all | solution.py:265
  31.9 4.5 %collective-permute-start = (f32[3,7,270]{2,1,0:T(8,128)S(1)}, f32[3,7,270]{2,1,0:T(8,128)S(1)}, u32[]{:S(2)}, u32[]{:S(2)}) collective-permute-start(f32[3,7,270]{2,1,0:T(8,128)S(1)} %get-tuple-element.51), channel_id=1, source_target_pairs={{0,8},{8,16},{16,24},{24,32},{32,40},{40,48},{48,56},{56,64},{64,7... | collective-permute-start | bytes 68048 | tf_op jit(solution)/shard_map/ppermute | solution.py:268
  35.1 4.7 %collective-permute-start.1 = (f32[3,7,270]{2,1,0:T(8,128)S(1)}, f32[3,7,270]{2,1,0:T(8,128)S(1)}, u32[]{:S(2)}, u32[]{:S(2)}) collective-permute-start(f32[3,7,270]{2,1,0:T(8,128)S(1)} %get-tuple-element.52), channel_id=1, source_target_pairs={{8,0},{16,8},{24,16},{32,24},{40,32},{48,40},{56,48},{64,56},{72,6... | collective-permute-start | bytes 68048 | tf_op jit(solution)/shard_map/ppermute | solution.py:269
  42.5 17.5 %all-to-all-start.1 = ((f32[16,3,16,128]{3,2,1,0:T(8,128)}), f32[16,3,16,128]{3,2,1,0:T(8,128)S(1)}, u32[]{:S(2)}, u32[]{:S(2)}) async-start(f32[16,3,16,128]{3,2,1,0:T(8,128)} %broadcast_in_dim.19), calls=%async_computation.1 | async-start | bytes 786432 | tf_op jit(solution)/shard_map/all_to_all | solution.py:198
  60.0 11.3 %collective-permute-start.3 = (f32[3,256,128]{2,1,0:T(8,128)S(1)}, f32[3,256,128]{2,1,0:T(8,128)S(1)}, u32[]{:S(2)}, u32[]{:S(2)}) collective-permute-start(f32[3,256,128]{2,1,0:T(8,128)S(1)} %bitcast.163), channel_id=1, source_target_pairs={{1,0},{2,1},{3,2},{4,3},{5,4},{6,5},{7,6},{9,8},{10,9},{11,10},{12... | collective-permute-start | bytes 1179656 | tf_op jit(solution)/shard_map/ppermute | solution.py:207
  65.7 6.8 %collective-permute-start.2 = (f32[3,256,128]{2,1,0:T(8,128)S(1)}, f32[3,256,128]{2,1,0:T(8,128)S(1)}, u32[]{:S(2)}, u32[]{:S(2)}) collective-permute-start(f32[3,256,128]{2,1,0:T(8,128)S(1)} %bitcast.164), channel_id=1, source_target_pairs={{0,1},{1,2},{2,3},{3,4},{4,5},{5,6},{6,7},{8,9},{9,10},{10,11},{11... | collective-permute-start | bytes 1179656 | tf_op jit(solution)/shard_map/ppermute | solution.py:206
  90.0 11.0 %all-to-all-start.2 = ((f32[16,2,16,128]{3,2,1,0:T(8,128)}), f32[16,2,16,128]{3,2,1,0:T(8,128)S(1)}, u32[]{:S(2)}, u32[]{:S(2)}) async-start(f32[16,2,16,128]{3,2,1,0:T(8,128)} %broadcast_in_dim.21), calls=%async_computation.2 | async-start | bytes 524288 | tf_op jit(solution)/shard_map/all_to_all | solution.py:198
  101.7 11.7 %all-to-all-start.3 = ((f32[8,1,2]{2,1,0:T(1,128)}), f32[8,1,2]{2,1,0:T(1,128)S(1)}, u32[]{:S(2)}, u32[]{:S(2)}) async-start(f32[8,1,2]{2,1,0:T(1,128)} %broadcast_in_dim.22), calls=%async_computation.3 | async-start | bytes 8192 | tf_op jit(solution)/shard_map/all_to_all | solution.py:202
  107.6 7.7 %collective-permute-start.5 = (f32[1,256,128]{2,1,0:T(8,128)S(1)}, f32[1,256,128]{2,1,0:T(8,128)S(1)}, u32[]{:S(2)}, u32[]{:S(2)}) collective-permute-start(f32[1,256,128]{2,1,0:T(8,128)S(1)} %bitcast.171), channel_id=1, source_target_pairs={{1,0},{2,1},{3,2},{4,3},{5,4},{6,5},{7,6},{9,8},{10,9},{11,10},{12... | collective-permute-start | bytes 393224 | tf_op jit(solution)/shard_map/ppermute | solution.py:207
  109.5 5.8 %collective-permute-start.4 = (f32[1,256,128]{2,1,0:T(8,128)S(1)}, f32[1,256,128]{2,1,0:T(8,128)S(1)}, u32[]{:S(2)}, u32[]{:S(2)}) collective-permute-start(f32[1,256,128]{2,1,0:T(8,128)S(1)} %bitcast.172), channel_id=1, source_target_pairs={{0,1},{1,2},{2,3},{3,4},{4,5},{5,6},{6,7},{8,9},{9,10},{10,11},{11... | collective-permute-start | bytes 393224 | tf_op jit(solution)/shard_map/ppermute | solution.py:206
  125.9 12.4 %all-to-all-start.4 = ((f32[16,2,16,128]{3,2,1,0:T(8,128)}), f32[16,2,16,128]{3,2,1,0:T(8,128)S(1)}, u32[]{:S(2)}, u32[]{:S(2)}) async-start(f32[16,2,16,128]{3,2,1,0:T(8,128)} %broadcast_in_dim.24), calls=%async_computation.4 | async-start | bytes 524288 | tf_op jit(solution)/shard_map/all_to_all | solution.py:198
  138.9 10.9 %all-to-all-start.5 = ((f32[8,1,3]{2,1,0:T(1,128)}), f32[8,1,3]{2,1,0:T(1,128)S(1)}, u32[]{:S(2)}, u32[]{:S(2)}) async-start(f32[8,1,3]{2,1,0:T(1,128)} %broadcast_in_dim.25), calls=%async_computation.5 | async-start | bytes 8192 | tf_op jit(solution)/shard_map/all_to_all | solution.py:202
  144.3 10.0 %collective-permute-start.7 = (f32[1,256,128]{2,1,0:T(8,128)S(1)}, f32[1,256,128]{2,1,0:T(8,128)S(1)}, u32[]{:S(2)}, u32[]{:S(2)}) collective-permute-start(f32[1,256,128]{2,1,0:T(8,128)S(1)} %bitcast.166), channel_id=1, source_target_pairs={{1,0},{2,1},{3,2},{4,3},{5,4},{6,5},{7,6},{9,8},{10,9},{11,10},{12... | collective-permute-start | bytes 393224 | tf_op jit(solution)/shard_map/ppermute | solution.py:207
  146.2 8.1 %collective-permute-start.6 = (f32[1,256,128]{2,1,0:T(8,128)S(1)}, f32[1,256,128]{2,1,0:T(8,128)S(1)}, u32[]{:S(2)}, u32[]{:S(2)}) collective-permute-start(f32[1,256,128]{2,1,0:T(8,128)S(1)} %bitcast.167), channel_id=1, source_target_pairs={{0,1},{1,2},{2,3},{3,4},{4,5},{5,6},{6,7},{8,9},{9,10},{10,11},{11... | collective-permute-start | bytes 393224 | tf_op jit(solution)/shard_map/ppermute | solution.py:206
  164.3 14.9 %all-to-all-start.6 = ((f32[128,1,3]{2,1,0:T(1,128)}), f32[128,1,3]{2,1,0:T(1,128)S(1)}, u32[]{:S(2)}, u32[]{:S(2)}) async-start(f32[128,1,3]{2,1,0:T(1,128)} %broadcast_in_dim.26), calls=%async_computation.6 | async-start | bytes 131072 | tf_op jit(solution)/shard_map/all_to_all | solution.py:220

commit v8 on v7

--- a/solution.py
+++ b/solution.py
@@ -3,6 +3,7 @@
 from jax import lax
 from jax.sharding import PartitionSpec as P
 from jax.experimental import pallas as pl
+from jax.experimental.pallas import tpu as pltpu
 
 LOOK = 5
 LEVELS = 6
@@ -60,8 +61,12 @@
             - south * padded[2:, 1:-1] - north * padded[:-2, 1:-1])
 
 
-def multilook_kernel(lead_ref, trail_ref, row_ref, col_ref, out_ref):
-    mask = row_ref[:, 0:1] * col_ref[...]
+def multilook_kernel(bounds_ref, lead_ref, trail_ref, out_ref):
+    shape = lead_ref.shape[1:]
+    line = lax.broadcasted_iota(jnp.int32, shape, 0)
+    column = pl.program_id(0) * shape[1] + lax.broadcasted_iota(jnp.int32, shape, 1)
+    mask = ((line >= bounds_ref[0]) & (line < bounds_ref[1]) & (column >= bounds_ref[2])
+            & (column < bounds_ref[3])).astype(jnp.float32)
     first_re = lead_ref[0].astype(jnp.float32) * mask
     first_im = lead_ref[1].astype(jnp.float32) * mask
     second_re = trail_ref[0].astype(jnp.float32) * mask
@@ -80,22 +85,20 @@
             out_ref[part, group:group + 1, :] = acc
 
 
-def mean_multilook(leading, trailing, row_ok, col_ok):
+def mean_multilook(leading, trailing, bounds):
     _, height_rows, width_cols = leading.shape
     block = 1024
     rows = pl.pallas_call(
         multilook_kernel,
         grid=(width_cols // block,),
         in_specs=[
+            pl.BlockSpec(memory_space=pltpu.SMEM),
             pl.BlockSpec((2, height_rows, block), lambda j: (0, 0, j)),
             pl.BlockSpec((2, height_rows, block), lambda j: (0, 0, j)),
-            pl.BlockSpec((height_rows, 128), lambda j: (0, 0)),
-            pl.BlockSpec((1, block), lambda j: (0, j)),
         ],
         out_specs=pl.BlockSpec((4, height_rows // LOOK, block), lambda j: (0, 0, j)),
         out_shape=jax.ShapeDtypeStruct((4, height_rows // LOOK, width_cols), jnp.float32),
-    )(leading, trailing, jnp.broadcast_to(row_ok.astype(jnp.float32)[:, None], (height_rows, 128)),
-      col_ok.astype(jnp.float32)[None, :])
+    )(bounds, leading, trailing)
     span = LOOK * 128
     grouped = rows.reshape(4, height_rows // LOOK, width_cols // span, span)
     cols = jnp.einsum("pikc,cd->pikd", grouped, group_sum(span, LOOK).T, precision=HIGHEST)
@@ -234,15 +237,14 @@
     )
     lines_here = master_phasor_raster.shape[1]
     slant_sample_total = master_phasor_raster.shape[2]
-    along_track_position = range_index * lines_here + jnp.arange(lines_here, dtype=jnp.int32)
-    column_index = jnp.arange(slant_sample_total, dtype=jnp.int32)
-    row_ok = (along_track_position >= track_trim_width[0]) & (
-        along_track_position < SEGMENT_HEIGHT - track_trim_width[1]
-    )
-    col_ok = (column_index >= slant_trim_width[0]) & (
-        column_index < slant_sample_total - slant_trim_width[1]
-    )
-    pixel_totals = mean_multilook(master_phasor_raster, slave_phasor_raster, row_ok, col_ok)
+    first_line = range_index * lines_here
+    bounds = jnp.stack([
+        track_trim_width[0] - first_line,
+        SEGMENT_HEIGHT - track_trim_width[1] - first_line,
+        slant_trim_width[0],
+        slant_sample_total - slant_trim_width[1],
+    ]).astype(jnp.int32)
+    pixel_totals = mean_multilook(master_phasor_raster, slave_phasor_raster, bounds)
     look_re, look_im, power_one, power_two = (
         pixel_totals[0],
         pixel_totals[1],

time: 185 us -> 185 us (level)
    convert_element_type x2 -> x0, other arithmetic: 1.94 us -> none  [the longest x1 1.29 us: mean_multilook(): col_ok.astype(jnp.float32)[None, :]]
    another operation x2 -> x3, other arithmetic: 3.41 us -> 4.72 us
where the time goes in v8:
time: 185 us; the launch traced here: 183 us
  starting transfers between devices  62.4 us (34%)
  waiting for transfers between devices  46 us (25%)
  matrix products  25.3 us (14%)
  other arithmetic  15.3 us (8%)
  local copies, waits for them, and re-layouts  14.8 us (8%)
  between operations  12 us (6%)
  Pallas kernels  7.34 us (4%)
    all_to_all x3, waiting for transfers between devices, gather_strip(): got = lax.all_to_all(sent, 'az', 0, 0, tiled=True)  23.7 us
    all_to_all x3, starting transfers between devices, gather_strip(): got = lax.all_to_all(sent, 'az', 0, 0, tiled=True)  16.3 us
    dot_general x48, matrix products, sandwich(): inner = jnp.dot(left, vector, precision=HIGHEST)  13.8 us
    all_to_all x2, starting transfers between devices, gather_strip(): lax.all_to_all(jnp.broadcast_to(column_sums[None], (n_rg, sums.shape[0]))...  11.3 us
    dot_general x48, matrix products, sandwich(): return jnp.dot(inner, right, precision=HIGHEST)  11 us
    ppermute x3, starting transfers between devices, gather_strip(): left = lax.ppermute(column, 'rg', [(i, i + 1) for i in range(n_rg - 1)])  9.78 us
    ppermute x3, starting transfers between devices, gather_strip(): right = lax.ppermute(column, 'rg', [(i + 1, i) for i in range(n_rg - 1)])  9.5 us
    all_to_all x1, waiting for transfers between devices, total(): got = lax.all_to_all(sent, ('az', 'rg'), 0, 0, tiled=True)  9.43 us
  transfers between devices with their start and end apart: 15, of which 8 were waited for; matrix products, arithmetic and copies ran while one was open for 1% of the time, Pallas kernels for 0%

profile of v8, /device:TPU:1, one launch (start us, length us, event | category | flops | bytes accessed | tf_op | source)
XLA Modules:
  0.0 183.2 jit_solution(2302661318534474055)
XLA Ops:
  3.9 2.4 %copy.59.lead_ref = bf16[2,20,10240]{2,1,0:T(8,128)(2,1)} copy(bf16[2,20,10240]{2,0,1:T(2,128)(2,1)} %param.8) | data formatting | bytes 1638400 | tf_op args[0]
  9.5 7.3 %shard_map.59 = f32[4,4,10240]{2,1,0:T(4,128)} custom-call(s32[4]{0:T(128)} %pad_add_fusion.bounds_ref, bf16[2,20,10240]{2,1,0:T(8,128)(2,1)} %copy.59.lead_ref, bf16[2,20,10240]{2,1,0:T(8,128)(2,1)} %copy.60.trail_ref), custom_call_target="tpu_custom_call" | custom-call | tf_op jit(solution)/shard_map/pallas_call | solution.py:91
  19.7 5.8 %all-to-all-start = ((f32[8,3,4,270]{3,2,1,0:T(4,128)}), f32[8,3,4,270]{3,2,1,0:T(4,128)S(1)}, u32[]{:S(2)}, u32[]{:S(2)}) async-start(f32[8,3,4,270]{3,2,1,0:T(4,128)} %copy.61), calls=%async_computation | async-start | bytes 294912 | tf_op jit(solution)/shard_map/all_to_all | solution.py:267
  25.9 5.0 %all-to-all-done = f32[8,3,4,270]{3,2,1,0:T(4,128)S(1)} async-done(((f32[8,3,4,270]{3,2,1,0:T(4,128)}), f32[8,3,4,270]{3,2,1,0:T(4,128)S(1)}, u32[]{:S(2)}, u32[]{:S(2)}) %all-to-all-start) | async-done | bytes 103712 | tf_op jit(solution)/shard_map/all_to_all | solution.py:267
  31.0 3.2 %collective-permute-start = (f32[3,7,270]{2,1,0:T(8,128)S(1)}, f32[3,7,270]{2,1,0:T(8,128)S(1)}, u32[]{:S(2)}, u32[]{:S(2)}) collective-permute-start(f32[3,7,270]{2,1,0:T(8,128)S(1)} %get-tuple-element.51), channel_id=1, source_target_pairs={{0,8},{8,16},{16,24},{24,32},{32,40},{40,48},{48,56},{56,64},{64,7... | collective-permute-start | bytes 68048 | tf_op jit(solution)/shard_map/ppermute | solution.py:270
  35.6 3.4 %collective-permute-done.1 = f32[3,7,270]{2,1,0:T(8,128)S(1)} collective-permute-done((f32[3,7,270]{2,1,0:T(8,128)S(1)}, f32[3,7,270]{2,1,0:T(8,128)S(1)}, u32[]{:S(2)}, u32[]{:S(2)}) %collective-permute-start.1) | collective-permute-done | bytes 22712 | tf_op jit(solution)/shard_map/ppermute | solution.py:271
  41.6 9.2 %all-to-all-start.1 = ((f32[16,3,16,128]{3,2,1,0:T(8,128)}), f32[16,3,16,128]{3,2,1,0:T(8,128)S(1)}, u32[]{:S(2)}, u32[]{:S(2)}) async-start(f32[16,3,16,128]{3,2,1,0:T(8,128)} %broadcast_in_dim.16), calls=%async_computation.1 | async-start | bytes 786432 | tf_op jit(solution)/shard_map/all_to_all | solution.py:201
  50.9 8.2 %all-to-all-done.1 = f32[16,3,16,128]{3,2,1,0:T(8,128)S(1)} async-done(((f32[16,3,16,128]{3,2,1,0:T(8,128)}), f32[16,3,16,128]{3,2,1,0:T(8,128)S(1)}, u32[]{:S(2)}, u32[]{:S(2)}) %all-to-all-start.1) | async-done | bytes 393248 | tf_op jit(solution)/shard_map/all_to_all | solution.py:201
  59.1 5.7 %collective-permute-start.3 = (f32[3,256,128]{2,1,0:T(8,128)S(1)}, f32[3,256,128]{2,1,0:T(8,128)S(1)}, u32[]{:S(2)}, u32[]{:S(2)}) collective-permute-start(f32[3,256,128]{2,1,0:T(8,128)S(1)} %bitcast.165), channel_id=1, source_target_pairs={{1,0},{2,1},{3,2},{4,3},{5,4},{6,5},{7,6},{9,8},{10,9},{11,10},{12... | collective-permute-start | bytes 1179656 | tf_op jit(solution)/shard_map/ppermute | solution.py:210
  64.8 2.3 %collective-permute-start.2 = (f32[3,256,128]{2,1,0:T(8,128)S(1)}, f32[3,256,128]{2,1,0:T(8,128)S(1)}, u32[]{:S(2)}, u32[]{:S(2)}) collective-permute-start(f32[3,256,128]{2,1,0:T(8,128)S(1)} %bitcast.166), channel_id=1, source_target_pairs={{0,1},{1,2},{2,3},{3,4},{4,5},{5,6},{6,7},{8,9},{9,10},{10,11},{11... | collective-permute-start | bytes 1179656 | tf_op jit(solution)/shard_map/ppermute | solution.py:209
  67.1 3.3 %collective-permute-done.3 = f32[3,256,128]{2,1,0:T(8,128)S(1)} collective-permute-done((f32[3,256,128]{2,1,0:T(8,128)S(1)}, f32[3,256,128]{2,1,0:T(8,128)S(1)}, u32[]{:S(2)}, u32[]{:S(2)}) %collective-permute-start.3) | collective-permute-done | bytes 393248 | tf_op jit(solution)/shard_map/ppermute | solution.py:210
  89.1 3.5 %all-to-all-start.2 = ((f32[16,2,16,128]{3,2,1,0:T(8,128)}), f32[16,2,16,128]{3,2,1,0:T(8,128)S(1)}, u32[]{:S(2)}, u32[]{:S(2)}) async-start(f32[16,2,16,128]{3,2,1,0:T(8,128)} %broadcast_in_dim.18), calls=%async_computation.2 | async-start | bytes 524288 | tf_op jit(solution)/shard_map/all_to_all | solution.py:201
  92.7 7.5 %all-to-all-done.2 = f32[16,2,16,128]{3,2,1,0:T(8,128)S(1)} async-done(((f32[16,2,16,128]{3,2,1,0:T(8,128)}), f32[16,2,16,128]{3,2,1,0:T(8,128)S(1)}, u32[]{:S(2)}, u32[]{:S(2)}) %all-to-all-start.2) | async-done | bytes 262176 | tf_op jit(solution)/shard_map/all_to_all | solution.py:201
  100.8 5.9 %all-to-all-start.3 = ((f32[8,1,2]{2,1,0:T(1,128)}), f32[8,1,2]{2,1,0:T(1,128)S(1)}, u32[]{:S(2)}, u32[]{:S(2)}) async-start(f32[8,1,2]{2,1,0:T(1,128)} %broadcast_in_dim.19), calls=%async_computation.3 | async-start | bytes 8192 | tf_op jit(solution)/shard_map/all_to_all | solution.py:205
  108.6 3.9 %collective-permute-start.4 = (f32[1,256,128]{2,1,0:T(8,128)S(1)}, f32[1,256,128]{2,1,0:T(8,128)S(1)}, u32[]{:S(2)}, u32[]{:S(2)}) collective-permute-start(f32[1,256,128]{2,1,0:T(8,128)S(1)} %bitcast.174), channel_id=1, source_target_pairs={{0,1},{1,2},{2,3},{3,4},{4,5},{5,6},{6,7},{8,9},{9,10},{10,11},{11... | collective-permute-start | bytes 393224 | tf_op jit(solution)/shard_map/ppermute | solution.py:209
  122.3 2.0 %maximum_bitcast_fusion.6 = f32[1,1,3]{2,1,0:T(1,128)S(1)} fusion(f32[1]{0:T(128)} %bitcast.33, f32[1]{0:T(128)} %bitcast.32, f32[1]{0:T(128)} %bitcast.31), kind=kLoop, calls=%fused_computation.1262 | loop fusion | flops 6 | bytes 24 | tf_op jit(solution)/shard_map/reshape.49
  125.0 3.5 %all-to-all-start.4 = ((f32[16,2,16,128]{3,2,1,0:T(8,128)}), f32[16,2,16,128]{3,2,1,0:T(8,128)S(1)}, u32[]{:S(2)}, u32[]{:S(2)}) async-start(f32[16,2,16,128]{3,2,1,0:T(8,128)} %broadcast_in_dim.21), calls=%async_computation.4 | async-start | bytes 524288 | tf_op jit(solution)/shard_map/all_to_all | solution.py:201
  129.3 8.1 %all-to-all-done.4 = f32[16,2,16,128]{3,2,1,0:T(8,128)S(1)} async-done(((f32[16,2,16,128]{3,2,1,0:T(8,128)}), f32[16,2,16,128]{3,2,1,0:T(8,128)S(1)}, u32[]{:S(2)}, u32[]{:S(2)}) %all-to-all-start.4) | async-done | bytes 262176 | tf_op jit(solution)/shard_map/all_to_all | solution.py:201
  138.0 5.4 %all-to-all-start.5 = ((f32[8,1,3]{2,1,0:T(1,128)}), f32[8,1,3]{2,1,0:T(1,128)S(1)}, u32[]{:S(2)}, u32[]{:S(2)}) async-start(f32[8,1,3]{2,1,0:T(1,128)} %broadcast_in_dim.22), calls=%async_computation.5 | async-start | bytes 8192 | tf_op jit(solution)/shard_map/all_to_all | solution.py:205
  143.4 1.9 %collective-permute-start.7 = (f32[1,256,128]{2,1,0:T(8,128)S(1)}, f32[1,256,128]{2,1,0:T(8,128)S(1)}, u32[]{:S(2)}, u32[]{:S(2)}) collective-permute-start(f32[1,256,128]{2,1,0:T(8,128)S(1)} %bitcast.168), channel_id=1, source_target_pairs={{1,0},{2,1},{3,2},{4,3},{5,4},{6,5},{7,6},{9,8},{10,9},{11,10},{12... | collective-permute-start | bytes 393224 | tf_op jit(solution)/shard_map/ppermute | solution.py:210
  145.3 3.6 %collective-permute-start.6 = (f32[1,256,128]{2,1,0:T(8,128)S(1)}, f32[1,256,128]{2,1,0:T(8,128)S(1)}, u32[]{:S(2)}, u32[]{:S(2)}) collective-permute-start(f32[1,256,128]{2,1,0:T(8,128)S(1)} %bitcast.169), channel_id=1, source_target_pairs={{0,1},{1,2},{2,3},{3,4},{4,5},{5,6},{6,7},{8,9},{9,10},{10,11},{11... | collective-permute-start | bytes 393224 | tf_op jit(solution)/shard_map/ppermute | solution.py:209
  160.7 2.0 %pad_maximum_fusion.3 = f32[3]{0:T(128)S(1)} fusion(f32[1]{0:T(128)} %bitcast.42, f32[1]{0:T(128)} %bitcast.41, f32[1]{0:T(128)} %bitcast.40), kind=kLoop, calls=%fused_computation.1263 | loop fusion | flops 6 | bytes 24 | tf_op jit(solution)/shard_map/stack | solution.py:340
  163.4 5.3 %all-to-all-start.6 = ((f32[128,1,3]{2,1,0:T(1,128)}), f32[128,1,3]{2,1,0:T(1,128)S(1)}, u32[]{:S(2)}, u32[]{:S(2)}) async-start(f32[128,1,3]{2,1,0:T(1,128)} %broadcast_in_dim.23), calls=%async_computation.6 | async-start | bytes 131072 | tf_op jit(solution)/shard_map/all_to_all | solution.py:223
  168.9 9.4 %all-to-all-done.6 = f32[128,1,3]{2,1,0:T(1,128)S(1)} async-done(((f32[128,1,3]{2,1,0:T(1,128)}), f32[128,1,3]{2,1,0:T(1,128)S(1)}, u32[]{:S(2)}, u32[]{:S(2)}) %all-to-all-start.6) | async-done | bytes 1568 | tf_op jit(solution)/shard_map/all_to_all | solution.py:223
  (232 shorter events, 53.4 us)
Async XLA Ops:
  0.6 5.7 %copy-start = (bf16[2,20,10240]{2,0,1:T(2,128)(2,1)S(1)}, bf16[2,20,10240]{2,0,1:T(2,128)(2,1)}, u32[]{:S(2)}) copy-start(bf16[2,20,10240]{2,0,1:T(2,128)(2,1)} %param.9) | copy-start | bytes 2457604
  19.7 11.2 %all-to-all-start = ((f32[8,3,4,270]{3,2,1,0:T(4,128)}), f32[8,3,4,270]{3,2,1,0:T(4,128)S(1)}, u32[]{:S(2)}, u32[]{:S(2)}) async-start(f32[8,3,4,270]{3,2,1,0:T(4,128)} %copy.61), calls=%async_computation | async-start | bytes 294912 | tf_op jit(solution)/shard_map/all_to_all | solution.py:267
  31.0 4.5 %collective-permute-start = (f32[3,7,270]{2,1,0:T(8,128)S(1)}, f32[3,7,270]{2,1,0:T(8,128)S(1)}, u32[]{:S(2)}, u32[]{:S(2)}) collective-permute-start(f32[3,7,270]{2,1,0:T(8,128)S(1)} %get-tuple-element.51), channel_id=1, source_target_pairs={{0,8},{8,16},{16,24},{24,32},{32,40},{40,48},{48,56},{56,64},{64,7... | collective-permute-start | bytes 68048 | tf_op jit(solution)/shard_map/ppermute | solution.py:270
  34.3 4.7 %collective-permute-start.1 = (f32[3,7,270]{2,1,0:T(8,128)S(1)}, f32[3,7,270]{2,1,0:T(8,128)S(1)}, u32[]{:S(2)}, u32[]{:S(2)}) collective-permute-start(f32[3,7,270]{2,1,0:T(8,128)S(1)} %get-tuple-element.52), channel_id=1, source_target_pairs={{8,0},{16,8},{24,16},{32,24},{40,32},{48,40},{56,48},{64,56},{72,6... | collective-permute-start | bytes 68048 | tf_op jit(solution)/shard_map/ppermute | solution.py:271
  41.6 17.5 %all-to-all-start.1 = ((f32[16,3,16,128]{3,2,1,0:T(8,128)}), f32[16,3,16,128]{3,2,1,0:T(8,128)S(1)}, u32[]{:S(2)}, u32[]{:S(2)}) async-start(f32[16,3,16,128]{3,2,1,0:T(8,128)} %broadcast_in_dim.16), calls=%async_computation.1 | async-start | bytes 786432 | tf_op jit(solution)/shard_map/all_to_all | solution.py:201
  59.1 11.3 %collective-permute-start.3 = (f32[3,256,128]{2,1,0:T(8,128)S(1)}, f32[3,256,128]{2,1,0:T(8,128)S(1)}, u32[]{:S(2)}, u32[]{:S(2)}) collective-permute-start(f32[3,256,128]{2,1,0:T(8,128)S(1)} %bitcast.165), channel_id=1, source_target_pairs={{1,0},{2,1},{3,2},{4,3},{5,4},{6,5},{7,6},{9,8},{10,9},{11,10},{12... | collective-permute-start | bytes 1179656 | tf_op jit(solution)/shard_map/ppermute | solution.py:210
  64.8 6.8 %collective-permute-start.2 = (f32[3,256,128]{2,1,0:T(8,128)S(1)}, f32[3,256,128]{2,1,0:T(8,128)S(1)}, u32[]{:S(2)}, u32[]{:S(2)}) collective-permute-start(f32[3,256,128]{2,1,0:T(8,128)S(1)} %bitcast.166), channel_id=1, source_target_pairs={{0,1},{1,2},{2,3},{3,4},{4,5},{5,6},{6,7},{8,9},{9,10},{10,11},{11... | collective-permute-start | bytes 1179656 | tf_op jit(solution)/shard_map/ppermute | solution.py:209
  89.1 11.0 %all-to-all-start.2 = ((f32[16,2,16,128]{3,2,1,0:T(8,128)}), f32[16,2,16,128]{3,2,1,0:T(8,128)S(1)}, u32[]{:S(2)}, u32[]{:S(2)}) async-start(f32[16,2,16,128]{3,2,1,0:T(8,128)} %broadcast_in_dim.18), calls=%async_computation.2 | async-start | bytes 524288 | tf_op jit(solution)/shard_map/all_to_all | solution.py:201
  100.8 11.7 %all-to-all-start.3 = ((f32[8,1,2]{2,1,0:T(1,128)}), f32[8,1,2]{2,1,0:T(1,128)S(1)}, u32[]{:S(2)}, u32[]{:S(2)}) async-start(f32[8,1,2]{2,1,0:T(1,128)} %broadcast_in_dim.19), calls=%async_computation.3 | async-start | bytes 8192 | tf_op jit(solution)/shard_map/all_to_all | solution.py:205
  106.7 7.7 %collective-permute-start.5 = (f32[1,256,128]{2,1,0:T(8,128)S(1)}, f32[1,256,128]{2,1,0:T(8,128)S(1)}, u32[]{:S(2)}, u32[]{:S(2)}) collective-permute-start(f32[1,256,128]{2,1,0:T(8,128)S(1)} %bitcast.173), channel_id=1, source_target_pairs={{1,0},{2,1},{3,2},{4,3},{5,4},{6,5},{7,6},{9,8},{10,9},{11,10},{12... | collective-permute-start | bytes 393224 | tf_op jit(solution)/shard_map/ppermute | solution.py:210
  108.6 5.8 %collective-permute-start.4 = (f32[1,256,128]{2,1,0:T(8,128)S(1)}, f32[1,256,128]{2,1,0:T(8,128)S(1)}, u32[]{:S(2)}, u32[]{:S(2)}) collective-permute-start(f32[1,256,128]{2,1,0:T(8,128)S(1)} %bitcast.174), channel_id=1, source_target_pairs={{0,1},{1,2},{2,3},{3,4},{4,5},{5,6},{6,7},{8,9},{9,10},{10,11},{11... | collective-permute-start | bytes 393224 | tf_op jit(solution)/shard_map/ppermute | solution.py:209
  125.0 12.4 %all-to-all-start.4 = ((f32[16,2,16,128]{3,2,1,0:T(8,128)}), f32[16,2,16,128]{3,2,1,0:T(8,128)S(1)}, u32[]{:S(2)}, u32[]{:S(2)}) async-start(f32[16,2,16,128]{3,2,1,0:T(8,128)} %broadcast_in_dim.21), calls=%async_computation.4 | async-start | bytes 524288 | tf_op jit(solution)/shard_map/all_to_all | solution.py:201
  138.0 10.9 %all-to-all-start.5 = ((f32[8,1,3]{2,1,0:T(1,128)}), f32[8,1,3]{2,1,0:T(1,128)S(1)}, u32[]{:S(2)}, u32[]{:S(2)}) async-start(f32[8,1,3]{2,1,0:T(1,128)} %broadcast_in_dim.22), calls=%async_computation.5 | async-start | bytes 8192 | tf_op jit(solution)/shard_map/all_to_all | solution.py:205
  143.4 10.0 %collective-permute-start.7 = (f32[1,256,128]{2,1,0:T(8,128)S(1)}, f32[1,256,128]{2,1,0:T(8,128)S(1)}, u32[]{:S(2)}, u32[]{:S(2)}) collective-permute-start(f32[1,256,128]{2,1,0:T(8,128)S(1)} %bitcast.168), channel_id=1, source_target_pairs={{1,0},{2,1},{3,2},{4,3},{5,4},{6,5},{7,6},{9,8},{10,9},{11,10},{12... | collective-permute-start | bytes 393224 | tf_op jit(solution)/shard_map/ppermute | solution.py:210
  145.3 8.1 %collective-permute-start.6 = (f32[1,256,128]{2,1,0:T(8,128)S(1)}, f32[1,256,128]{2,1,0:T(8,128)S(1)}, u32[]{:S(2)}, u32[]{:S(2)}) collective-permute-start(f32[1,256,128]{2,1,0:T(8,128)S(1)} %bitcast.169), channel_id=1, source_target_pairs={{0,1},{1,2},{2,3},{3,4},{4,5},{5,6},{6,7},{8,9},{9,10},{10,11},{11... | collective-permute-start | bytes 393224 | tf_op jit(solution)/shard_map/ppermute | solution.py:209
  163.4 14.9 %all-to-all-start.6 = ((f32[128,1,3]{2,1,0:T(1,128)}), f32[128,1,3]{2,1,0:T(1,128)S(1)}, u32[]{:S(2)}, u32[]{:S(2)}) async-start(f32[128,1,3]{2,1,0:T(1,128)} %broadcast_in_dim.23), calls=%async_computation.6 | async-start | bytes 131072 | tf_op jit(solution)/shard_map/all_to_all | solution.py:223

commit v9 on v8

--- a/solution.py
+++ b/solution.py
@@ -87,7 +87,7 @@
 
 def mean_multilook(leading, trailing, bounds):
     _, height_rows, width_cols = leading.shape
-    block = 1024
+    block = 2560
     rows = pl.pallas_call(
         multilook_kernel,
         grid=(width_cols // block,),

time: 185 us -> 182 us (0.984)
  Pallas kernels: 7.34 us -> 4.69 us
    pallas_call x1, Pallas kernels: 7.34 us -> 4.69 us  [mean_multilook(): pl.pallas_call(multilook_kernel, grid=(width_cols // block,), in_specs=[p...]
where the time goes in v9:
time: 182 us; the launch traced here: 181 us
  starting transfers between devices  62.4 us (34%)
  waiting for transfers between devices  46 us (25%)
  matrix products  25.3 us (14%)
  other arithmetic  15.3 us (8%)
  local copies, waits for them, and re-layouts  14.8 us (8%)
  between operations  12 us (7%)
  Pallas kernels  4.69 us (3%)
    all_to_all x3, waiting for transfers between devices, gather_strip(): got = lax.all_to_all(sent, 'az', 0, 0, tiled=True)  23.7 us
    all_to_all x3, starting transfers between devices, gather_strip(): got = lax.all_to_all(sent, 'az', 0, 0, tiled=True)  16.3 us
    dot_general x48, matrix products, sandwich(): inner = jnp.dot(left, vector, precision=HIGHEST)  13.8 us
    all_to_all x2, starting transfers between devices, gather_strip(): lax.all_to_all(jnp.broadcast_to(column_sums[None], (n_rg, sums.shape[0]))...  11.3 us
    dot_general x48, matrix products, sandwich(): return jnp.dot(inner, right, precision=HIGHEST)  11 us
    ppermute x3, starting transfers between devices, gather_strip(): left = lax.ppermute(column, 'rg', [(i, i + 1) for i in range(n_rg - 1)])  9.78 us
    ppermute x3, starting transfers between devices, gather_strip(): right = lax.ppermute(column, 'rg', [(i + 1, i) for i in range(n_rg - 1)])  9.5 us
    all_to_all x1, waiting for transfers between devices, total(): got = lax.all_to_all(sent, ('az', 'rg'), 0, 0, tiled=True)  9.43 us
  transfers between devices with their start and end apart: 15, of which 8 were waited for; matrix products, arithmetic and copies ran while one was open for 1% of the time, Pallas kernels for 0%

profile of v9, /device:TPU:1, one launch (start us, length us, event | category | flops | bytes accessed | tf_op | source)
XLA Modules:
  0.0 180.5 jit_solution(12183457835051195335)
XLA Ops:
  3.9 2.4 %copy.59.lead_ref = bf16[2,20,10240]{2,1,0:T(8,128)(2,1)} copy(bf16[2,20,10240]{2,0,1:T(2,128)(2,1)} %param.8) | data formatting | bytes 1638400 | tf_op args[0]
  9.5 4.7 %shard_map.59 = f32[4,4,10240]{2,1,0:T(4,128)} custom-call(s32[4]{0:T(128)} %pad_add_fusion.bounds_ref, bf16[2,20,10240]{2,1,0:T(8,128)(2,1)} %copy.59.lead_ref, bf16[2,20,10240]{2,1,0:T(8,128)(2,1)} %copy.60.trail_ref), custom_call_target="tpu_custom_call" | custom-call | tf_op jit(solution)/shard_map/pallas_call | solution.py:91
  17.1 5.8 %all-to-all-start = ((f32[8,3,4,270]{3,2,1,0:T(4,128)}), f32[8,3,4,270]{3,2,1,0:T(4,128)S(1)}, u32[]{:S(2)}, u32[]{:S(2)}) async-start(f32[8,3,4,270]{3,2,1,0:T(4,128)} %copy.61), calls=%async_computation | async-start | bytes 294912 | tf_op jit(solution)/shard_map/all_to_all | solution.py:267
  23.3 5.0 %all-to-all-done = f32[8,3,4,270]{3,2,1,0:T(4,128)S(1)} async-done(((f32[8,3,4,270]{3,2,1,0:T(4,128)}), f32[8,3,4,270]{3,2,1,0:T(4,128)S(1)}, u32[]{:S(2)}, u32[]{:S(2)}) %all-to-all-start) | async-done | bytes 103712 | tf_op jit(solution)/shard_map/all_to_all | solution.py:267
  28.4 3.2 %collective-permute-start = (f32[3,7,270]{2,1,0:T(8,128)S(1)}, f32[3,7,270]{2,1,0:T(8,128)S(1)}, u32[]{:S(2)}, u32[]{:S(2)}) collective-permute-start(f32[3,7,270]{2,1,0:T(8,128)S(1)} %get-tuple-element.51), channel_id=1, source_target_pairs={{0,8},{8,16},{16,24},{24,32},{32,40},{40,48},{48,56},{56,64},{64,7... | collective-permute-start | bytes 68048 | tf_op jit(solution)/shard_map/ppermute | solution.py:270
  32.9 3.4 %collective-permute-done.1 = f32[3,7,270]{2,1,0:T(8,128)S(1)} collective-permute-done((f32[3,7,270]{2,1,0:T(8,128)S(1)}, f32[3,7,270]{2,1,0:T(8,128)S(1)}, u32[]{:S(2)}, u32[]{:S(2)}) %collective-permute-start.1) | collective-permute-done | bytes 22712 | tf_op jit(solution)/shard_map/ppermute | solution.py:271
  38.9 9.2 %all-to-all-start.1 = ((f32[16,3,16,128]{3,2,1,0:T(8,128)}), f32[16,3,16,128]{3,2,1,0:T(8,128)S(1)}, u32[]{:S(2)}, u32[]{:S(2)}) async-start(f32[16,3,16,128]{3,2,1,0:T(8,128)} %broadcast_in_dim.16), calls=%async_computation.1 | async-start | bytes 786432 | tf_op jit(solution)/shard_map/all_to_all | solution.py:201
  48.2 8.2 %all-to-all-done.1 = f32[16,3,16,128]{3,2,1,0:T(8,128)S(1)} async-done(((f32[16,3,16,128]{3,2,1,0:T(8,128)}), f32[16,3,16,128]{3,2,1,0:T(8,128)S(1)}, u32[]{:S(2)}, u32[]{:S(2)}) %all-to-all-start.1) | async-done | bytes 393248 | tf_op jit(solution)/shard_map/all_to_all | solution.py:201
  56.4 5.7 %collective-permute-start.3 = (f32[3,256,128]{2,1,0:T(8,128)S(1)}, f32[3,256,128]{2,1,0:T(8,128)S(1)}, u32[]{:S(2)}, u32[]{:S(2)}) collective-permute-start(f32[3,256,128]{2,1,0:T(8,128)S(1)} %bitcast.165), channel_id=1, source_target_pairs={{1,0},{2,1},{3,2},{4,3},{5,4},{6,5},{7,6},{9,8},{10,9},{11,10},{12... | collective-permute-start | bytes 1179656 | tf_op jit(solution)/shard_map/ppermute | solution.py:210
  62.1 2.3 %collective-permute-start.2 = (f32[3,256,128]{2,1,0:T(8,128)S(1)}, f32[3,256,128]{2,1,0:T(8,128)S(1)}, u32[]{:S(2)}, u32[]{:S(2)}) collective-permute-start(f32[3,256,128]{2,1,0:T(8,128)S(1)} %bitcast.166), channel_id=1, source_target_pairs={{0,1},{1,2},{2,3},{3,4},{4,5},{5,6},{6,7},{8,9},{9,10},{10,11},{11... | collective-permute-start | bytes 1179656 | tf_op jit(solution)/shard_map/ppermute | solution.py:209
  64.4 3.3 %collective-permute-done.3 = f32[3,256,128]{2,1,0:T(8,128)S(1)} collective-permute-done((f32[3,256,128]{2,1,0:T(8,128)S(1)}, f32[3,256,128]{2,1,0:T(8,128)S(1)}, u32[]{:S(2)}, u32[]{:S(2)}) %collective-permute-start.3) | collective-permute-done | bytes 393248 | tf_op jit(solution)/shard_map/ppermute | solution.py:210
  86.4 3.5 %all-to-all-start.2 = ((f32[16,2,16,128]{3,2,1,0:T(8,128)}), f32[16,2,16,128]{3,2,1,0:T(8,128)S(1)}, u32[]{:S(2)}, u32[]{:S(2)}) async-start(f32[16,2,16,128]{3,2,1,0:T(8,128)} %broadcast_in_dim.18), calls=%async_computation.2 | async-start | bytes 524288 | tf_op jit(solution)/shard_map/all_to_all | solution.py:201
  90.0 7.5 %all-to-all-done.2 = f32[16,2,16,128]{3,2,1,0:T(8,128)S(1)} async-done(((f32[16,2,16,128]{3,2,1,0:T(8,128)}), f32[16,2,16,128]{3,2,1,0:T(8,128)S(1)}, u32[]{:S(2)}, u32[]{:S(2)}) %all-to-all-start.2) | async-done | bytes 262176 | tf_op jit(solution)/shard_map/all_to_all | solution.py:201
  98.1 5.9 %all-to-all-start.3 = ((f32[8,1,2]{2,1,0:T(1,128)}), f32[8,1,2]{2,1,0:T(1,128)S(1)}, u32[]{:S(2)}, u32[]{:S(2)}) async-start(f32[8,1,2]{2,1,0:T(1,128)} %broadcast_in_dim.19), calls=%async_computation.3 | async-start | bytes 8192 | tf_op jit(solution)/shard_map/all_to_all | solution.py:205
  104.0 1.9 %collective-permute-start.5 = (f32[1,256,128]{2,1,0:T(8,128)S(1)}, f32[1,256,128]{2,1,0:T(8,128)S(1)}, u32[]{:S(2)}, u32[]{:S(2)}) collective-permute-start(f32[1,256,128]{2,1,0:T(8,128)S(1)} %bitcast.173), channel_id=1, source_target_pairs={{1,0},{2,1},{3,2},{4,3},{5,4},{6,5},{7,6},{9,8},{10,9},{11,10},{12... | collective-permute-start | bytes 393224 | tf_op jit(solution)/shard_map/ppermute | solution.py:210
  106.0 3.9 %collective-permute-start.4 = (f32[1,256,128]{2,1,0:T(8,128)S(1)}, f32[1,256,128]{2,1,0:T(8,128)S(1)}, u32[]{:S(2)}, u32[]{:S(2)}) collective-permute-start(f32[1,256,128]{2,1,0:T(8,128)S(1)} %bitcast.174), channel_id=1, source_target_pairs={{0,1},{1,2},{2,3},{3,4},{4,5},{5,6},{6,7},{8,9},{9,10},{10,11},{11... | collective-permute-start | bytes 393224 | tf_op jit(solution)/shard_map/ppermute | solution.py:209
  119.6 2.0 %maximum_bitcast_fusion.6 = f32[1,1,3]{2,1,0:T(1,128)S(1)} fusion(f32[1]{0:T(128)} %bitcast.33, f32[1]{0:T(128)} %bitcast.32, f32[1]{0:T(128)} %bitcast.31), kind=kLoop, calls=%fused_computation.1262 | loop fusion | flops 6 | bytes 24 | tf_op jit(solution)/shard_map/reshape.49
  122.3 3.5 %all-to-all-start.4 = ((f32[16,2,16,128]{3,2,1,0:T(8,128)}), f32[16,2,16,128]{3,2,1,0:T(8,128)S(1)}, u32[]{:S(2)}, u32[]{:S(2)}) async-start(f32[16,2,16,128]{3,2,1,0:T(8,128)} %broadcast_in_dim.21), calls=%async_computation.4 | async-start | bytes 524288 | tf_op jit(solution)/shard_map/all_to_all | solution.py:201
  126.7 8.1 %all-to-all-done.4 = f32[16,2,16,128]{3,2,1,0:T(8,128)S(1)} async-done(((f32[16,2,16,128]{3,2,1,0:T(8,128)}), f32[16,2,16,128]{3,2,1,0:T(8,128)S(1)}, u32[]{:S(2)}, u32[]{:S(2)}) %all-to-all-start.4) | async-done | bytes 262176 | tf_op jit(solution)/shard_map/all_to_all | solution.py:201
  135.4 5.4 %all-to-all-start.5 = ((f32[8,1,3]{2,1,0:T(1,128)}), f32[8,1,3]{2,1,0:T(1,128)S(1)}, u32[]{:S(2)}, u32[]{:S(2)}) async-start(f32[8,1,3]{2,1,0:T(1,128)} %broadcast_in_dim.22), calls=%async_computation.5 | async-start | bytes 8192 | tf_op jit(solution)/shard_map/all_to_all | solution.py:205
  142.7 3.6 %collective-permute-start.6 = (f32[1,256,128]{2,1,0:T(8,128)S(1)}, f32[1,256,128]{2,1,0:T(8,128)S(1)}, u32[]{:S(2)}, u32[]{:S(2)}) collective-permute-start(f32[1,256,128]{2,1,0:T(8,128)S(1)} %bitcast.169), channel_id=1, source_target_pairs={{0,1},{1,2},{2,3},{3,4},{4,5},{5,6},{6,7},{8,9},{9,10},{10,11},{11... | collective-permute-start | bytes 393224 | tf_op jit(solution)/shard_map/ppermute | solution.py:209
  158.1 2.0 %pad_maximum_fusion.3 = f32[3]{0:T(128)S(1)} fusion(f32[1]{0:T(128)} %bitcast.42, f32[1]{0:T(128)} %bitcast.41, f32[1]{0:T(128)} %bitcast.40), kind=kLoop, calls=%fused_computation.1263 | loop fusion | flops 6 | bytes 24 | tf_op jit(solution)/shard_map/stack | solution.py:340
  160.7 5.3 %all-to-all-start.6 = ((f32[128,1,3]{2,1,0:T(1,128)}), f32[128,1,3]{2,1,0:T(1,128)S(1)}, u32[]{:S(2)}, u32[]{:S(2)}) async-start(f32[128,1,3]{2,1,0:T(1,128)} %broadcast_in_dim.23), calls=%async_computation.6 | async-start | bytes 131072 | tf_op jit(solution)/shard_map/all_to_all | solution.py:223
  166.2 9.4 %all-to-all-done.6 = f32[128,1,3]{2,1,0:T(1,128)S(1)} async-done(((f32[128,1,3]{2,1,0:T(1,128)}), f32[128,1,3]{2,1,0:T(1,128)S(1)}, u32[]{:S(2)}, u32[]{:S(2)}) %all-to-all-start.6) | async-done | bytes 1568 | tf_op jit(solution)/shard_map/all_to_all | solution.py:223
  (232 shorter events, 53.4 us)
Async XLA Ops:
  0.6 5.7 %copy-start = (bf16[2,20,10240]{2,0,1:T(2,128)(2,1)S(1)}, bf16[2,20,10240]{2,0,1:T(2,128)(2,1)}, u32[]{:S(2)}) copy-start(bf16[2,20,10240]{2,0,1:T(2,128)(2,1)} %param.9) | copy-start | bytes 2457604
  17.1 11.2 %all-to-all-start = ((f32[8,3,4,270]{3,2,1,0:T(4,128)}), f32[8,3,4,270]{3,2,1,0:T(4,128)S(1)}, u32[]{:S(2)}, u32[]{:S(2)}) async-start(f32[8,3,4,270]{3,2,1,0:T(4,128)} %copy.61), calls=%async_computation | async-start | bytes 294912 | tf_op jit(solution)/shard_map/all_to_all | solution.py:267
  28.4 4.5 %collective-permute-start = (f32[3,7,270]{2,1,0:T(8,128)S(1)}, f32[3,7,270]{2,1,0:T(8,128)S(1)}, u32[]{:S(2)}, u32[]{:S(2)}) collective-permute-start(f32[3,7,270]{2,1,0:T(8,128)S(1)} %get-tuple-element.51), channel_id=1, source_target_pairs={{0,8},{8,16},{16,24},{24,32},{32,40},{40,48},{48,56},{56,64},{64,7... | collective-permute-start | bytes 68048 | tf_op jit(solution)/shard_map/ppermute | solution.py:270
  31.6 4.7 %collective-permute-start.1 = (f32[3,7,270]{2,1,0:T(8,128)S(1)}, f32[3,7,270]{2,1,0:T(8,128)S(1)}, u32[]{:S(2)}, u32[]{:S(2)}) collective-permute-start(f32[3,7,270]{2,1,0:T(8,128)S(1)} %get-tuple-element.52), channel_id=1, source_target_pairs={{8,0},{16,8},{24,16},{32,24},{40,32},{48,40},{56,48},{64,56},{72,6... | collective-permute-start | bytes 68048 | tf_op jit(solution)/shard_map/ppermute | solution.py:271
  38.9 17.5 %all-to-all-start.1 = ((f32[16,3,16,128]{3,2,1,0:T(8,128)}), f32[16,3,16,128]{3,2,1,0:T(8,128)S(1)}, u32[]{:S(2)}, u32[]{:S(2)}) async-start(f32[16,3,16,128]{3,2,1,0:T(8,128)} %broadcast_in_dim.16), calls=%async_computation.1 | async-start | bytes 786432 | tf_op jit(solution)/shard_map/all_to_all | solution.py:201
  56.4 11.3 %collective-permute-start.3 = (f32[3,256,128]{2,1,0:T(8,128)S(1)}, f32[3,256,128]{2,1,0:T(8,128)S(1)}, u32[]{:S(2)}, u32[]{:S(2)}) collective-permute-start(f32[3,256,128]{2,1,0:T(8,128)S(1)} %bitcast.165), channel_id=1, source_target_pairs={{1,0},{2,1},{3,2},{4,3},{5,4},{6,5},{7,6},{9,8},{10,9},{11,10},{12... | collective-permute-start | bytes 1179656 | tf_op jit(solution)/shard_map/ppermute | solution.py:210
  62.1 6.8 %collective-permute-start.2 = (f32[3,256,128]{2,1,0:T(8,128)S(1)}, f32[3,256,128]{2,1,0:T(8,128)S(1)}, u32[]{:S(2)}, u32[]{:S(2)}) collective-permute-start(f32[3,256,128]{2,1,0:T(8,128)S(1)} %bitcast.166), channel_id=1, source_target_pairs={{0,1},{1,2},{2,3},{3,4},{4,5},{5,6},{6,7},{8,9},{9,10},{10,11},{11... | collective-permute-start | bytes 1179656 | tf_op jit(solution)/shard_map/ppermute | solution.py:209
  86.4 11.0 %all-to-all-start.2 = ((f32[16,2,16,128]{3,2,1,0:T(8,128)}), f32[16,2,16,128]{3,2,1,0:T(8,128)S(1)}, u32[]{:S(2)}, u32[]{:S(2)}) async-start(f32[16,2,16,128]{3,2,1,0:T(8,128)} %broadcast_in_dim.18), calls=%async_computation.2 | async-start | bytes 524288 | tf_op jit(solution)/shard_map/all_to_all | solution.py:201
  98.1 11.7 %all-to-all-start.3 = ((f32[8,1,2]{2,1,0:T(1,128)}), f32[8,1,2]{2,1,0:T(1,128)S(1)}, u32[]{:S(2)}, u32[]{:S(2)}) async-start(f32[8,1,2]{2,1,0:T(1,128)} %broadcast_in_dim.19), calls=%async_computation.3 | async-start | bytes 8192 | tf_op jit(solution)/shard_map/all_to_all | solution.py:205
  104.0 7.7 %collective-permute-start.5 = (f32[1,256,128]{2,1,0:T(8,128)S(1)}, f32[1,256,128]{2,1,0:T(8,128)S(1)}, u32[]{:S(2)}, u32[]{:S(2)}) collective-permute-start(f32[1,256,128]{2,1,0:T(8,128)S(1)} %bitcast.173), channel_id=1, source_target_pairs={{1,0},{2,1},{3,2},{4,3},{5,4},{6,5},{7,6},{9,8},{10,9},{11,10},{12... | collective-permute-start | bytes 393224 | tf_op jit(solution)/shard_map/ppermute | solution.py:210
  106.0 5.8 %collective-permute-start.4 = (f32[1,256,128]{2,1,0:T(8,128)S(1)}, f32[1,256,128]{2,1,0:T(8,128)S(1)}, u32[]{:S(2)}, u32[]{:S(2)}) collective-permute-start(f32[1,256,128]{2,1,0:T(8,128)S(1)} %bitcast.174), channel_id=1, source_target_pairs={{0,1},{1,2},{2,3},{3,4},{4,5},{5,6},{6,7},{8,9},{9,10},{10,11},{11... | collective-permute-start | bytes 393224 | tf_op jit(solution)/shard_map/ppermute | solution.py:209
  122.3 12.4 %all-to-all-start.4 = ((f32[16,2,16,128]{3,2,1,0:T(8,128)}), f32[16,2,16,128]{3,2,1,0:T(8,128)S(1)}, u32[]{:S(2)}, u32[]{:S(2)}) async-start(f32[16,2,16,128]{3,2,1,0:T(8,128)} %broadcast_in_dim.21), calls=%async_computation.4 | async-start | bytes 524288 | tf_op jit(solution)/shard_map/all_to_all | solution.py:201
  135.4 10.9 %all-to-all-start.5 = ((f32[8,1,3]{2,1,0:T(1,128)}), f32[8,1,3]{2,1,0:T(1,128)S(1)}, u32[]{:S(2)}, u32[]{:S(2)}) async-start(f32[8,1,3]{2,1,0:T(1,128)} %broadcast_in_dim.22), calls=%async_computation.5 | async-start | bytes 8192 | tf_op jit(solution)/shard_map/all_to_all | solution.py:205
  140.7 10.0 %collective-permute-start.7 = (f32[1,256,128]{2,1,0:T(8,128)S(1)}, f32[1,256,128]{2,1,0:T(8,128)S(1)}, u32[]{:S(2)}, u32[]{:S(2)}) collective-permute-start(f32[1,256,128]{2,1,0:T(8,128)S(1)} %bitcast.168), channel_id=1, source_target_pairs={{1,0},{2,1},{3,2},{4,3},{5,4},{6,5},{7,6},{9,8},{10,9},{11,10},{12... | collective-permute-start | bytes 393224 | tf_op jit(solution)/shard_map/ppermute | solution.py:210
  142.7 8.1 %collective-permute-start.6 = (f32[1,256,128]{2,1,0:T(8,128)S(1)}, f32[1,256,128]{2,1,0:T(8,128)S(1)}, u32[]{:S(2)}, u32[]{:S(2)}) collective-permute-start(f32[1,256,128]{2,1,0:T(8,128)S(1)} %bitcast.169), channel_id=1, source_target_pairs={{0,1},{1,2},{2,3},{3,4},{4,5},{5,6},{6,7},{8,9},{9,10},{10,11},{11... | collective-permute-start | bytes 393224 | tf_op jit(solution)/shard_map/ppermute | solution.py:209
  160.7 14.9 %all-to-all-start.6 = ((f32[128,1,3]{2,1,0:T(1,128)}), f32[128,1,3]{2,1,0:T(1,128)S(1)}, u32[]{:S(2)}, u32[]{:S(2)}) async-start(f32[128,1,3]{2,1,0:T(1,128)} %broadcast_in_dim.23), calls=%async_computation.6 | async-start | bytes 131072 | tf_op jit(solution)/shard_map/all_to_all | solution.py:223

commit v10 on v9

--- a/solution.py
+++ b/solution.py
@@ -87,7 +87,7 @@
 
 def mean_multilook(leading, trailing, bounds):
     _, height_rows, width_cols = leading.shape
-    block = 2560
+    block = 5120
     rows = pl.pallas_call(
         multilook_kernel,
         grid=(width_cols // block,),

time: 182 us -> 181 us (level)
  no operation moved by 1% of the time
where the time goes in v10:
time: 181 us; the launch traced here: 180 us
  starting transfers between devices  62.4 us (34%)
  waiting for transfers between devices  46 us (25%)
  matrix products  25.3 us (14%)
  other arithmetic  15.3 us (8%)
  local copies, waits for them, and re-layouts  14.8 us (8%)
  between operations  12 us (7%)
  Pallas kernels  4.22 us (2%)
    all_to_all x3, waiting for transfers between devices, gather_strip(): got = lax.all_to_all(sent, 'az', 0, 0, tiled=True)  23.7 us
    all_to_all x3, starting transfers between devices, gather_strip(): got = lax.all_to_all(sent, 'az', 0, 0, tiled=True)  16.3 us
    dot_general x48, matrix products, sandwich(): inner = jnp.dot(left, vector, precision=HIGHEST)  13.8 us
    all_to_all x2, starting transfers between devices, gather_strip(): lax.all_to_all(jnp.broadcast_to(column_sums[None], (n_rg, sums.shape[0]))...  11.3 us
    dot_general x48, matrix products, sandwich(): return jnp.dot(inner, right, precision=HIGHEST)  11 us
    ppermute x3, starting transfers between devices, gather_strip(): left = lax.ppermute(column, 'rg', [(i, i + 1) for i in range(n_rg - 1)])  9.78 us
    ppermute x3, starting transfers between devices, gather_strip(): right = lax.ppermute(column, 'rg', [(i + 1, i) for i in range(n_rg - 1)])  9.5 us
    all_to_all x1, waiting for transfers between devices, total(): got = lax.all_to_all(sent, ('az', 'rg'), 0, 0, tiled=True)  9.43 us
  transfers between devices with their start and end apart: 15, of which 8 were waited for; matrix products, arithmetic and copies ran while one was open for 1% of the time, Pallas kernels for 0%

profile of v10, /device:TPU:1, one launch (start us, length us, event | category | flops | bytes accessed | tf_op | source)
XLA Modules:
  0.0 180.1 jit_solution(1602827907620834482)
XLA Ops:
  3.9 2.4 %copy.59.lead_ref = bf16[2,20,10240]{2,1,0:T(8,128)(2,1)} copy(bf16[2,20,10240]{2,0,1:T(2,128)(2,1)} %param.8) | data formatting | bytes 1638400 | tf_op args[0]
  9.5 4.2 %shard_map.59 = f32[4,4,10240]{2,1,0:T(4,128)} custom-call(s32[4]{0:T(128)} %pad_add_fusion.bounds_ref, bf16[2,20,10240]{2,1,0:T(8,128)(2,1)} %copy.59.lead_ref, bf16[2,20,10240]{2,1,0:T(8,128)(2,1)} %copy.60.trail_ref), custom_call_target="tpu_custom_call" | custom-call | tf_op jit(solution)/shard_map/pallas_call | solution.py:91
  16.6 5.8 %all-to-all-start = ((f32[8,3,4,270]{3,2,1,0:T(4,128)}), f32[8,3,4,270]{3,2,1,0:T(4,128)S(1)}, u32[]{:S(2)}, u32[]{:S(2)}) async-start(f32[8,3,4,270]{3,2,1,0:T(4,128)} %copy.61), calls=%async_computation | async-start | bytes 294912 | tf_op jit(solution)/shard_map/all_to_all | solution.py:267
  22.8 5.0 %all-to-all-done = f32[8,3,4,270]{3,2,1,0:T(4,128)S(1)} async-done(((f32[8,3,4,270]{3,2,1,0:T(4,128)}), f32[8,3,4,270]{3,2,1,0:T(4,128)S(1)}, u32[]{:S(2)}, u32[]{:S(2)}) %all-to-all-start) | async-done | bytes 103712 | tf_op jit(solution)/shard_map/all_to_all | solution.py:267
  27.9 3.2 %collective-permute-start = (f32[3,7,270]{2,1,0:T(8,128)S(1)}, f32[3,7,270]{2,1,0:T(8,128)S(1)}, u32[]{:S(2)}, u32[]{:S(2)}) collective-permute-start(f32[3,7,270]{2,1,0:T(8,128)S(1)} %get-tuple-element.51), channel_id=1, source_target_pairs={{0,8},{8,16},{16,24},{24,32},{32,40},{40,48},{48,56},{56,64},{64,7... | collective-permute-start | bytes 68048 | tf_op jit(solution)/shard_map/ppermute | solution.py:270
  32.5 3.4 %collective-permute-done.1 = f32[3,7,270]{2,1,0:T(8,128)S(1)} collective-permute-done((f32[3,7,270]{2,1,0:T(8,128)S(1)}, f32[3,7,270]{2,1,0:T(8,128)S(1)}, u32[]{:S(2)}, u32[]{:S(2)}) %collective-permute-start.1) | collective-permute-done | bytes 22712 | tf_op jit(solution)/shard_map/ppermute | solution.py:271
  38.5 9.2 %all-to-all-start.1 = ((f32[16,3,16,128]{3,2,1,0:T(8,128)}), f32[16,3,16,128]{3,2,1,0:T(8,128)S(1)}, u32[]{:S(2)}, u32[]{:S(2)}) async-start(f32[16,3,16,128]{3,2,1,0:T(8,128)} %broadcast_in_dim.16), calls=%async_computation.1 | async-start | bytes 786432 | tf_op jit(solution)/shard_map/all_to_all | solution.py:201
  47.8 8.2 %all-to-all-done.1 = f32[16,3,16,128]{3,2,1,0:T(8,128)S(1)} async-done(((f32[16,3,16,128]{3,2,1,0:T(8,128)}), f32[16,3,16,128]{3,2,1,0:T(8,128)S(1)}, u32[]{:S(2)}, u32[]{:S(2)}) %all-to-all-start.1) | async-done | bytes 393248 | tf_op jit(solution)/shard_map/all_to_all | solution.py:201
  56.0 5.7 %collective-permute-start.3 = (f32[3,256,128]{2,1,0:T(8,128)S(1)}, f32[3,256,128]{2,1,0:T(8,128)S(1)}, u32[]{:S(2)}, u32[]{:S(2)}) collective-permute-start(f32[3,256,128]{2,1,0:T(8,128)S(1)} %bitcast.165), channel_id=1, source_target_pairs={{1,0},{2,1},{3,2},{4,3},{5,4},{6,5},{7,6},{9,8},{10,9},{11,10},{12... | collective-permute-start | bytes 1179656 | tf_op jit(solution)/shard_map/ppermute | solution.py:210
  61.6 2.3 %collective-permute-start.2 = (f32[3,256,128]{2,1,0:T(8,128)S(1)}, f32[3,256,128]{2,1,0:T(8,128)S(1)}, u32[]{:S(2)}, u32[]{:S(2)}) collective-permute-start(f32[3,256,128]{2,1,0:T(8,128)S(1)} %bitcast.166), channel_id=1, source_target_pairs={{0,1},{1,2},{2,3},{3,4},{4,5},{5,6},{6,7},{8,9},{9,10},{10,11},{11... | collective-permute-start | bytes 1179656 | tf_op jit(solution)/shard_map/ppermute | solution.py:209
  64.0 3.3 %collective-permute-done.3 = f32[3,256,128]{2,1,0:T(8,128)S(1)} collective-permute-done((f32[3,256,128]{2,1,0:T(8,128)S(1)}, f32[3,256,128]{2,1,0:T(8,128)S(1)}, u32[]{:S(2)}, u32[]{:S(2)}) %collective-permute-start.3) | collective-permute-done | bytes 393248 | tf_op jit(solution)/shard_map/ppermute | solution.py:210
  86.0 3.5 %all-to-all-start.2 = ((f32[16,2,16,128]{3,2,1,0:T(8,128)}), f32[16,2,16,128]{3,2,1,0:T(8,128)S(1)}, u32[]{:S(2)}, u32[]{:S(2)}) async-start(f32[16,2,16,128]{3,2,1,0:T(8,128)} %broadcast_in_dim.18), calls=%async_computation.2 | async-start | bytes 524288 | tf_op jit(solution)/shard_map/all_to_all | solution.py:201
  89.6 7.5 %all-to-all-done.2 = f32[16,2,16,128]{3,2,1,0:T(8,128)S(1)} async-done(((f32[16,2,16,128]{3,2,1,0:T(8,128)}), f32[16,2,16,128]{3,2,1,0:T(8,128)S(1)}, u32[]{:S(2)}, u32[]{:S(2)}) %all-to-all-start.2) | async-done | bytes 262176 | tf_op jit(solution)/shard_map/all_to_all | solution.py:201
  97.7 5.9 %all-to-all-start.3 = ((f32[8,1,2]{2,1,0:T(1,128)}), f32[8,1,2]{2,1,0:T(1,128)S(1)}, u32[]{:S(2)}, u32[]{:S(2)}) async-start(f32[8,1,2]{2,1,0:T(1,128)} %broadcast_in_dim.19), calls=%async_computation.3 | async-start | bytes 8192 | tf_op jit(solution)/shard_map/all_to_all | solution.py:205
  103.6 1.9 %collective-permute-start.5 = (f32[1,256,128]{2,1,0:T(8,128)S(1)}, f32[1,256,128]{2,1,0:T(8,128)S(1)}, u32[]{:S(2)}, u32[]{:S(2)}) collective-permute-start(f32[1,256,128]{2,1,0:T(8,128)S(1)} %bitcast.173), channel_id=1, source_target_pairs={{1,0},{2,1},{3,2},{4,3},{5,4},{6,5},{7,6},{9,8},{10,9},{11,10},{12... | collective-permute-start | bytes 393224 | tf_op jit(solution)/shard_map/ppermute | solution.py:210
  105.5 3.9 %collective-permute-start.4 = (f32[1,256,128]{2,1,0:T(8,128)S(1)}, f32[1,256,128]{2,1,0:T(8,128)S(1)}, u32[]{:S(2)}, u32[]{:S(2)}) collective-permute-start(f32[1,256,128]{2,1,0:T(8,128)S(1)} %bitcast.174), channel_id=1, source_target_pairs={{0,1},{1,2},{2,3},{3,4},{4,5},{5,6},{6,7},{8,9},{9,10},{10,11},{11... | collective-permute-start | bytes 393224 | tf_op jit(solution)/shard_map/ppermute | solution.py:209
  119.2 2.0 %maximum_bitcast_fusion.6 = f32[1,1,3]{2,1,0:T(1,128)S(1)} fusion(f32[1]{0:T(128)} %bitcast.33, f32[1]{0:T(128)} %bitcast.32, f32[1]{0:T(128)} %bitcast.31), kind=kLoop, calls=%fused_computation.1262 | loop fusion | flops 6 | bytes 24 | tf_op jit(solution)/shard_map/reshape.49
  121.9 3.5 %all-to-all-start.4 = ((f32[16,2,16,128]{3,2,1,0:T(8,128)}), f32[16,2,16,128]{3,2,1,0:T(8,128)S(1)}, u32[]{:S(2)}, u32[]{:S(2)}) async-start(f32[16,2,16,128]{3,2,1,0:T(8,128)} %broadcast_in_dim.21), calls=%async_computation.4 | async-start | bytes 524288 | tf_op jit(solution)/shard_map/all_to_all | solution.py:201
  126.2 8.1 %all-to-all-done.4 = f32[16,2,16,128]{3,2,1,0:T(8,128)S(1)} async-done(((f32[16,2,16,128]{3,2,1,0:T(8,128)}), f32[16,2,16,128]{3,2,1,0:T(8,128)S(1)}, u32[]{:S(2)}, u32[]{:S(2)}) %all-to-all-start.4) | async-done | bytes 262176 | tf_op jit(solution)/shard_map/all_to_all | solution.py:201
  134.9 5.4 %all-to-all-start.5 = ((f32[8,1,3]{2,1,0:T(1,128)}), f32[8,1,3]{2,1,0:T(1,128)S(1)}, u32[]{:S(2)}, u32[]{:S(2)}) async-start(f32[8,1,3]{2,1,0:T(1,128)} %broadcast_in_dim.22), calls=%async_computation.5 | async-start | bytes 8192 | tf_op jit(solution)/shard_map/all_to_all | solution.py:205
  142.2 3.6 %collective-permute-start.6 = (f32[1,256,128]{2,1,0:T(8,128)S(1)}, f32[1,256,128]{2,1,0:T(8,128)S(1)}, u32[]{:S(2)}, u32[]{:S(2)}) collective-permute-start(f32[1,256,128]{2,1,0:T(8,128)S(1)} %bitcast.169), channel_id=1, source_target_pairs={{0,1},{1,2},{2,3},{3,4},{4,5},{5,6},{6,7},{8,9},{9,10},{10,11},{11... | collective-permute-start | bytes 393224 | tf_op jit(solution)/shard_map/ppermute | solution.py:209
  157.6 2.0 %pad_maximum_fusion.3 = f32[3]{0:T(128)S(1)} fusion(f32[1]{0:T(128)} %bitcast.42, f32[1]{0:T(128)} %bitcast.41, f32[1]{0:T(128)} %bitcast.40), kind=kLoop, calls=%fused_computation.1263 | loop fusion | flops 6 | bytes 24 | tf_op jit(solution)/shard_map/stack | solution.py:340
  160.3 5.3 %all-to-all-start.6 = ((f32[128,1,3]{2,1,0:T(1,128)}), f32[128,1,3]{2,1,0:T(1,128)S(1)}, u32[]{:S(2)}, u32[]{:S(2)}) async-start(f32[128,1,3]{2,1,0:T(1,128)} %broadcast_in_dim.23), calls=%async_computation.6 | async-start | bytes 131072 | tf_op jit(solution)/shard_map/all_to_all | solution.py:223
  165.8 9.4 %all-to-all-done.6 = f32[128,1,3]{2,1,0:T(1,128)S(1)} async-done(((f32[128,1,3]{2,1,0:T(1,128)}), f32[128,1,3]{2,1,0:T(1,128)S(1)}, u32[]{:S(2)}, u32[]{:S(2)}) %all-to-all-start.6) | async-done | bytes 1568 | tf_op jit(solution)/shard_map/all_to_all | solution.py:223
  (232 shorter events, 53.4 us)
Async XLA Ops:
  0.6 5.7 %copy-start = (bf16[2,20,10240]{2,0,1:T(2,128)(2,1)S(1)}, bf16[2,20,10240]{2,0,1:T(2,128)(2,1)}, u32[]{:S(2)}) copy-start(bf16[2,20,10240]{2,0,1:T(2,128)(2,1)} %param.9) | copy-start | bytes 2457604
  16.6 11.2 %all-to-all-start = ((f32[8,3,4,270]{3,2,1,0:T(4,128)}), f32[8,3,4,270]{3,2,1,0:T(4,128)S(1)}, u32[]{:S(2)}, u32[]{:S(2)}) async-start(f32[8,3,4,270]{3,2,1,0:T(4,128)} %copy.61), calls=%async_computation | async-start | bytes 294912 | tf_op jit(solution)/shard_map/all_to_all | solution.py:267
  27.9 4.5 %collective-permute-start = (f32[3,7,270]{2,1,0:T(8,128)S(1)}, f32[3,7,270]{2,1,0:T(8,128)S(1)}, u32[]{:S(2)}, u32[]{:S(2)}) collective-permute-start(f32[3,7,270]{2,1,0:T(8,128)S(1)} %get-tuple-element.51), channel_id=1, source_target_pairs={{0,8},{8,16},{16,24},{24,32},{32,40},{40,48},{48,56},{56,64},{64,7... | collective-permute-start | bytes 68048 | tf_op jit(solution)/shard_map/ppermute | solution.py:270
  31.1 4.7 %collective-permute-start.1 = (f32[3,7,270]{2,1,0:T(8,128)S(1)}, f32[3,7,270]{2,1,0:T(8,128)S(1)}, u32[]{:S(2)}, u32[]{:S(2)}) collective-permute-start(f32[3,7,270]{2,1,0:T(8,128)S(1)} %get-tuple-element.52), channel_id=1, source_target_pairs={{8,0},{16,8},{24,16},{32,24},{40,32},{48,40},{56,48},{64,56},{72,6... | collective-permute-start | bytes 68048 | tf_op jit(solution)/shard_map/ppermute | solution.py:271
  38.5 17.5 %all-to-all-start.1 = ((f32[16,3,16,128]{3,2,1,0:T(8,128)}), f32[16,3,16,128]{3,2,1,0:T(8,128)S(1)}, u32[]{:S(2)}, u32[]{:S(2)}) async-start(f32[16,3,16,128]{3,2,1,0:T(8,128)} %broadcast_in_dim.16), calls=%async_computation.1 | async-start | bytes 786432 | tf_op jit(solution)/shard_map/all_to_all | solution.py:201
  56.0 11.3 %collective-permute-start.3 = (f32[3,256,128]{2,1,0:T(8,128)S(1)}, f32[3,256,128]{2,1,0:T(8,128)S(1)}, u32[]{:S(2)}, u32[]{:S(2)}) collective-permute-start(f32[3,256,128]{2,1,0:T(8,128)S(1)} %bitcast.165), channel_id=1, source_target_pairs={{1,0},{2,1},{3,2},{4,3},{5,4},{6,5},{7,6},{9,8},{10,9},{11,10},{12... | collective-permute-start | bytes 1179656 | tf_op jit(solution)/shard_map/ppermute | solution.py:210
  61.6 6.8 %collective-permute-start.2 = (f32[3,256,128]{2,1,0:T(8,128)S(1)}, f32[3,256,128]{2,1,0:T(8,128)S(1)}, u32[]{:S(2)}, u32[]{:S(2)}) collective-permute-start(f32[3,256,128]{2,1,0:T(8,128)S(1)} %bitcast.166), channel_id=1, source_target_pairs={{0,1},{1,2},{2,3},{3,4},{4,5},{5,6},{6,7},{8,9},{9,10},{10,11},{11... | collective-permute-start | bytes 1179656 | tf_op jit(solution)/shard_map/ppermute | solution.py:209
  86.0 11.0 %all-to-all-start.2 = ((f32[16,2,16,128]{3,2,1,0:T(8,128)}), f32[16,2,16,128]{3,2,1,0:T(8,128)S(1)}, u32[]{:S(2)}, u32[]{:S(2)}) async-start(f32[16,2,16,128]{3,2,1,0:T(8,128)} %broadcast_in_dim.18), calls=%async_computation.2 | async-start | bytes 524288 | tf_op jit(solution)/shard_map/all_to_all | solution.py:201
  97.7 11.7 %all-to-all-start.3 = ((f32[8,1,2]{2,1,0:T(1,128)}), f32[8,1,2]{2,1,0:T(1,128)S(1)}, u32[]{:S(2)}, u32[]{:S(2)}) async-start(f32[8,1,2]{2,1,0:T(1,128)} %broadcast_in_dim.19), calls=%async_computation.3 | async-start | bytes 8192 | tf_op jit(solution)/shard_map/all_to_all | solution.py:205
  103.6 7.7 %collective-permute-start.5 = (f32[1,256,128]{2,1,0:T(8,128)S(1)}, f32[1,256,128]{2,1,0:T(8,128)S(1)}, u32[]{:S(2)}, u32[]{:S(2)}) collective-permute-start(f32[1,256,128]{2,1,0:T(8,128)S(1)} %bitcast.173), channel_id=1, source_target_pairs={{1,0},{2,1},{3,2},{4,3},{5,4},{6,5},{7,6},{9,8},{10,9},{11,10},{12... | collective-permute-start | bytes 393224 | tf_op jit(solution)/shard_map/ppermute | solution.py:210
  105.5 5.8 %collective-permute-start.4 = (f32[1,256,128]{2,1,0:T(8,128)S(1)}, f32[1,256,128]{2,1,0:T(8,128)S(1)}, u32[]{:S(2)}, u32[]{:S(2)}) collective-permute-start(f32[1,256,128]{2,1,0:T(8,128)S(1)} %bitcast.174), channel_id=1, source_target_pairs={{0,1},{1,2},{2,3},{3,4},{4,5},{5,6},{6,7},{8,9},{9,10},{10,11},{11... | collective-permute-start | bytes 393224 | tf_op jit(solution)/shard_map/ppermute | solution.py:209
  121.9 12.4 %all-to-all-start.4 = ((f32[16,2,16,128]{3,2,1,0:T(8,128)}), f32[16,2,16,128]{3,2,1,0:T(8,128)S(1)}, u32[]{:S(2)}, u32[]{:S(2)}) async-start(f32[16,2,16,128]{3,2,1,0:T(8,128)} %broadcast_in_dim.21), calls=%async_computation.4 | async-start | bytes 524288 | tf_op jit(solution)/shard_map/all_to_all | solution.py:201
  134.9 10.9 %all-to-all-start.5 = ((f32[8,1,3]{2,1,0:T(1,128)}), f32[8,1,3]{2,1,0:T(1,128)S(1)}, u32[]{:S(2)}, u32[]{:S(2)}) async-start(f32[8,1,3]{2,1,0:T(1,128)} %broadcast_in_dim.22), calls=%async_computation.5 | async-start | bytes 8192 | tf_op jit(solution)/shard_map/all_to_all | solution.py:205
  140.3 10.0 %collective-permute-start.7 = (f32[1,256,128]{2,1,0:T(8,128)S(1)}, f32[1,256,128]{2,1,0:T(8,128)S(1)}, u32[]{:S(2)}, u32[]{:S(2)}) collective-permute-start(f32[1,256,128]{2,1,0:T(8,128)S(1)} %bitcast.168), channel_id=1, source_target_pairs={{1,0},{2,1},{3,2},{4,3},{5,4},{6,5},{7,6},{9,8},{10,9},{11,10},{12... | collective-permute-start | bytes 393224 | tf_op jit(solution)/shard_map/ppermute | solution.py:210
  142.2 8.1 %collective-permute-start.6 = (f32[1,256,128]{2,1,0:T(8,128)S(1)}, f32[1,256,128]{2,1,0:T(8,128)S(1)}, u32[]{:S(2)}, u32[]{:S(2)}) collective-permute-start(f32[1,256,128]{2,1,0:T(8,128)S(1)} %bitcast.169), channel_id=1, source_target_pairs={{0,1},{1,2},{2,3},{3,4},{4,5},{5,6},{6,7},{8,9},{9,10},{10,11},{11... | collective-permute-start | bytes 393224 | tf_op jit(solution)/shard_map/ppermute | solution.py:209
  160.3 14.9 %all-to-all-start.6 = ((f32[128,1,3]{2,1,0:T(1,128)}), f32[128,1,3]{2,1,0:T(1,128)S(1)}, u32[]{:S(2)}, u32[]{:S(2)}) async-start(f32[128,1,3]{2,1,0:T(1,128)} %broadcast_in_dim.23), calls=%async_computation.6 | async-start | bytes 131072 | tf_op jit(solution)/shard_map/all_to_all | solution.py:223

commit v11 on v10

--- a/solution.py
+++ b/solution.py
@@ -77,17 +77,20 @@
         first_re * first_re + first_im * first_im,
         second_re * second_re + second_im * second_im,
     )
+    chunks, span = out_ref.shape[2:]
     for part, values in enumerate(products):
         for group in range(out_ref.shape[1]):
             acc = values[group * LOOK:group * LOOK + 1, :]
             for offset in range(1, LOOK):
                 acc = acc + values[group * LOOK + offset:group * LOOK + offset + 1, :]
-            out_ref[part, group:group + 1, :] = acc
+            for chunk in range(chunks):
+                out_ref[part, group, chunk:chunk + 1, :] = acc[:, chunk * span:(chunk + 1) * span]
 
 
 def mean_multilook(leading, trailing, bounds):
     _, height_rows, width_cols = leading.shape
     block = 5120
+    span = LOOK * 128
     rows = pl.pallas_call(
         multilook_kernel,
         grid=(width_cols // block,),
@@ -96,11 +99,10 @@
             pl.BlockSpec((2, height_rows, block), lambda j: (0, 0, j)),
             pl.BlockSpec((2, height_rows, block), lambda j: (0, 0, j)),
         ],
-        out_specs=pl.BlockSpec((4, height_rows // LOOK, block), lambda j: (0, 0, j)),
-        out_shape=jax.ShapeDtypeStruct((4, height_rows // LOOK, width_cols), jnp.float32),
+        out_specs=pl.BlockSpec((4, height_rows // LOOK, block // span, span), lambda j: (0, 0, j, 0)),
+        out_shape=jax.ShapeDtypeStruct((4, height_rows // LOOK, width_cols // span, span), jnp.float32),
     )(bounds, leading, trailing)
-    span = LOOK * 128
-    grouped = rows.reshape(4, height_rows // LOOK, width_cols // span, span)
+    grouped = rows
     cols = jnp.einsum("pikc,cd->pikd", grouped, group_sum(span, LOOK).T, precision=HIGHEST)
     return cols.reshape(4, height_rows // LOOK, width_cols // LOOK)
 

time: 181 us -> 181 us (level)
  no operation moved by 1% of the time
where the time goes in v11:
time: 181 us; the launch traced here: 180 us
  starting transfers between devices  62.4 us (34%)
  waiting for transfers between devices  46 us (25%)
  matrix products  26.3 us (15%)
  other arithmetic  15.3 us (8%)
  local copies, waits for them, and re-layouts  13.4 us (7%)
  between operations  12 us (7%)
  Pallas kernels  4.3 us (2%)
    all_to_all x3, waiting for transfers between devices, gather_strip(): got = lax.all_to_all(sent, 'az', 0, 0, tiled=True)  23.7 us
    all_to_all x3, starting transfers between devices, gather_strip(): got = lax.all_to_all(sent, 'az', 0, 0, tiled=True)  16.3 us
    dot_general x48, matrix products, sandwich(): inner = jnp.dot(left, vector, precision=HIGHEST)  13.8 us
    all_to_all x2, starting transfers between devices, gather_strip(): lax.all_to_all(jnp.broadcast_to(column_sums[None], (n_rg, sums.shape[0]))...  11.3 us
    dot_general x48, matrix products, sandwich(): return jnp.dot(inner, right, precision=HIGHEST)  11 us
    ppermute x3, starting transfers between devices, gather_strip(): left = lax.ppermute(column, 'rg', [(i, i + 1) for i in range(n_rg - 1)])  9.78 us
    ppermute x3, starting transfers between devices, gather_strip(): right = lax.ppermute(column, 'rg', [(i + 1, i) for i in range(n_rg - 1)])  9.5 us
    all_to_all x1, waiting for transfers between devices, total(): got = lax.all_to_all(sent, ('az', 'rg'), 0, 0, tiled=True)  9.43 us
  transfers between devices with their start and end apart: 15, of which 8 were waited for; matrix products, arithmetic and copies ran while one was open for 1% of the time, Pallas kernels for 0%

profile of v11, /device:TPU:1, one launch (start us, length us, event | category | flops | bytes accessed | tf_op | source)
XLA Modules:
  0.0 179.7 jit_solution(6439110527162943487)
XLA Ops:
  3.9 2.4 %copy.59.lead_ref = bf16[2,20,10240]{2,1,0:T(8,128)(2,1)} copy(bf16[2,20,10240]{2,0,1:T(2,128)(2,1)} %param.8) | data formatting | bytes 1638400 | tf_op args[0]
  9.5 4.3 %shard_map.59 = f32[4,4,16,640]{3,2,1,0:T(8,128)} custom-call(s32[4]{0:T(128)} %pad_add_fusion.bounds_ref, bf16[2,20,10240]{2,1,0:T(8,128)(2,1)} %copy.59.lead_ref, bf16[2,20,10240]{2,1,0:T(8,128)(2,1)} %copy.60.trail_ref), custom_call_target="tpu_custom_call" | custom-call | tf_op jit(solution)/shard_map/pallas_call | solution.py:94
  16.3 5.8 %all-to-all-start = ((f32[8,3,4,270]{3,2,1,0:T(4,128)}), f32[8,3,4,270]{3,2,1,0:T(4,128)S(1)}, u32[]{:S(2)}, u32[]{:S(2)}) async-start(f32[8,3,4,270]{3,2,1,0:T(4,128)} %copy.61), calls=%async_computation | async-start | bytes 294912 | tf_op jit(solution)/shard_map/all_to_all | solution.py:269
  22.6 5.0 %all-to-all-done = f32[8,3,4,270]{3,2,1,0:T(4,128)S(1)} async-done(((f32[8,3,4,270]{3,2,1,0:T(4,128)}), f32[8,3,4,270]{3,2,1,0:T(4,128)S(1)}, u32[]{:S(2)}, u32[]{:S(2)}) %all-to-all-start) | async-done | bytes 103712 | tf_op jit(solution)/shard_map/all_to_all | solution.py:269
  27.7 3.2 %collective-permute-start = (f32[3,7,270]{2,1,0:T(8,128)S(1)}, f32[3,7,270]{2,1,0:T(8,128)S(1)}, u32[]{:S(2)}, u32[]{:S(2)}) collective-permute-start(f32[3,7,270]{2,1,0:T(8,128)S(1)} %get-tuple-element.51), channel_id=1, source_target_pairs={{0,8},{8,16},{16,24},{24,32},{32,40},{40,48},{48,56},{56,64},{64,7... | collective-permute-start | bytes 68048 | tf_op jit(solution)/shard_map/ppermute | solution.py:272
  32.2 3.4 %collective-permute-done.1 = f32[3,7,270]{2,1,0:T(8,128)S(1)} collective-permute-done((f32[3,7,270]{2,1,0:T(8,128)S(1)}, f32[3,7,270]{2,1,0:T(8,128)S(1)}, u32[]{:S(2)}, u32[]{:S(2)}) %collective-permute-start.1) | collective-permute-done | bytes 22712 | tf_op jit(solution)/shard_map/ppermute | solution.py:273
  38.2 9.2 %all-to-all-start.1 = ((f32[16,3,16,128]{3,2,1,0:T(8,128)}), f32[16,3,16,128]{3,2,1,0:T(8,128)S(1)}, u32[]{:S(2)}, u32[]{:S(2)}) async-start(f32[16,3,16,128]{3,2,1,0:T(8,128)} %broadcast_in_dim.16), calls=%async_computation.1 | async-start | bytes 786432 | tf_op jit(solution)/shard_map/all_to_all | solution.py:203
  47.5 8.2 %all-to-all-done.1 = f32[16,3,16,128]{3,2,1,0:T(8,128)S(1)} async-done(((f32[16,3,16,128]{3,2,1,0:T(8,128)}), f32[16,3,16,128]{3,2,1,0:T(8,128)S(1)}, u32[]{:S(2)}, u32[]{:S(2)}) %all-to-all-start.1) | async-done | bytes 393248 | tf_op jit(solution)/shard_map/all_to_all | solution.py:203
  55.7 5.7 %collective-permute-start.3 = (f32[3,256,128]{2,1,0:T(8,128)S(1)}, f32[3,256,128]{2,1,0:T(8,128)S(1)}, u32[]{:S(2)}, u32[]{:S(2)}) collective-permute-start(f32[3,256,128]{2,1,0:T(8,128)S(1)} %bitcast.165), channel_id=1, source_target_pairs={{1,0},{2,1},{3,2},{4,3},{5,4},{6,5},{7,6},{9,8},{10,9},{11,10},{12... | collective-permute-start | bytes 1179656 | tf_op jit(solution)/shard_map/ppermute | solution.py:212
  61.4 2.3 %collective-permute-start.2 = (f32[3,256,128]{2,1,0:T(8,128)S(1)}, f32[3,256,128]{2,1,0:T(8,128)S(1)}, u32[]{:S(2)}, u32[]{:S(2)}) collective-permute-start(f32[3,256,128]{2,1,0:T(8,128)S(1)} %bitcast.166), channel_id=1, source_target_pairs={{0,1},{1,2},{2,3},{3,4},{4,5},{5,6},{6,7},{8,9},{9,10},{10,11},{11... | collective-permute-start | bytes 1179656 | tf_op jit(solution)/shard_map/ppermute | solution.py:211
  63.7 3.3 %collective-permute-done.3 = f32[3,256,128]{2,1,0:T(8,128)S(1)} collective-permute-done((f32[3,256,128]{2,1,0:T(8,128)S(1)}, f32[3,256,128]{2,1,0:T(8,128)S(1)}, u32[]{:S(2)}, u32[]{:S(2)}) %collective-permute-start.3) | collective-permute-done | bytes 393248 | tf_op jit(solution)/shard_map/ppermute | solution.py:212
  85.7 3.5 %all-to-all-start.2 = ((f32[16,2,16,128]{3,2,1,0:T(8,128)}), f32[16,2,16,128]{3,2,1,0:T(8,128)S(1)}, u32[]{:S(2)}, u32[]{:S(2)}) async-start(f32[16,2,16,128]{3,2,1,0:T(8,128)} %broadcast_in_dim.18), calls=%async_computation.2 | async-start | bytes 524288 | tf_op jit(solution)/shard_map/all_to_all | solution.py:203
  89.3 7.5 %all-to-all-done.2 = f32[16,2,16,128]{3,2,1,0:T(8,128)S(1)} async-done(((f32[16,2,16,128]{3,2,1,0:T(8,128)}), f32[16,2,16,128]{3,2,1,0:T(8,128)S(1)}, u32[]{:S(2)}, u32[]{:S(2)}) %all-to-all-start.2) | async-done | bytes 262176 | tf_op jit(solution)/shard_map/all_to_all | solution.py:203
  97.4 5.9 %all-to-all-start.3 = ((f32[8,1,2]{2,1,0:T(1,128)}), f32[8,1,2]{2,1,0:T(1,128)S(1)}, u32[]{:S(2)}, u32[]{:S(2)}) async-start(f32[8,1,2]{2,1,0:T(1,128)} %broadcast_in_dim.19), calls=%async_computation.3 | async-start | bytes 8192 | tf_op jit(solution)/shard_map/all_to_all | solution.py:207
  103.3 1.9 %collective-permute-start.5 = (f32[1,256,128]{2,1,0:T(8,128)S(1)}, f32[1,256,128]{2,1,0:T(8,128)S(1)}, u32[]{:S(2)}, u32[]{:S(2)}) collective-permute-start(f32[1,256,128]{2,1,0:T(8,128)S(1)} %bitcast.173), channel_id=1, source_target_pairs={{1,0},{2,1},{3,2},{4,3},{5,4},{6,5},{7,6},{9,8},{10,9},{11,10},{12... | collective-permute-start | bytes 393224 | tf_op jit(solution)/shard_map/ppermute | solution.py:212
  105.2 3.9 %collective-permute-start.4 = (f32[1,256,128]{2,1,0:T(8,128)S(1)}, f32[1,256,128]{2,1,0:T(8,128)S(1)}, u32[]{:S(2)}, u32[]{:S(2)}) collective-permute-start(f32[1,256,128]{2,1,0:T(8,128)S(1)} %bitcast.174), channel_id=1, source_target_pairs={{0,1},{1,2},{2,3},{3,4},{4,5},{5,6},{6,7},{8,9},{9,10},{10,11},{11... | collective-permute-start | bytes 393224 | tf_op jit(solution)/shard_map/ppermute | solution.py:211
  118.9 2.0 %maximum_bitcast_fusion.6 = f32[1,1,3]{2,1,0:T(1,128)S(1)} fusion(f32[1]{0:T(128)} %bitcast.33, f32[1]{0:T(128)} %bitcast.32, f32[1]{0:T(128)} %bitcast.31), kind=kLoop, calls=%fused_computation.1262 | loop fusion | flops 6 | bytes 24 | tf_op jit(solution)/shard_map/reshape.48
  121.6 3.5 %all-to-all-start.4 = ((f32[16,2,16,128]{3,2,1,0:T(8,128)}), f32[16,2,16,128]{3,2,1,0:T(8,128)S(1)}, u32[]{:S(2)}, u32[]{:S(2)}) async-start(f32[16,2,16,128]{3,2,1,0:T(8,128)} %broadcast_in_dim.21), calls=%async_computation.4 | async-start | bytes 524288 | tf_op jit(solution)/shard_map/all_to_all | solution.py:203
  125.9 8.1 %all-to-all-done.4 = f32[16,2,16,128]{3,2,1,0:T(8,128)S(1)} async-done(((f32[16,2,16,128]{3,2,1,0:T(8,128)}), f32[16,2,16,128]{3,2,1,0:T(8,128)S(1)}, u32[]{:S(2)}, u32[]{:S(2)}) %all-to-all-start.4) | async-done | bytes 262176 | tf_op jit(solution)/shard_map/all_to_all | solution.py:203
  134.6 5.4 %all-to-all-start.5 = ((f32[8,1,3]{2,1,0:T(1,128)}), f32[8,1,3]{2,1,0:T(1,128)S(1)}, u32[]{:S(2)}, u32[]{:S(2)}) async-start(f32[8,1,3]{2,1,0:T(1,128)} %broadcast_in_dim.22), calls=%async_computation.5 | async-start | bytes 8192 | tf_op jit(solution)/shard_map/all_to_all | solution.py:207
  141.9 3.6 %collective-permute-start.6 = (f32[1,256,128]{2,1,0:T(8,128)S(1)}, f32[1,256,128]{2,1,0:T(8,128)S(1)}, u32[]{:S(2)}, u32[]{:S(2)}) collective-permute-start(f32[1,256,128]{2,1,0:T(8,128)S(1)} %bitcast.169), channel_id=1, source_target_pairs={{0,1},{1,2},{2,3},{3,4},{4,5},{5,6},{6,7},{8,9},{9,10},{10,11},{11... | collective-permute-start | bytes 393224 | tf_op jit(solution)/shard_map/ppermute | solution.py:211
  157.3 2.0 %pad_maximum_fusion.3 = f32[3]{0:T(128)S(1)} fusion(f32[1]{0:T(128)} %bitcast.42, f32[1]{0:T(128)} %bitcast.41, f32[1]{0:T(128)} %bitcast.40), kind=kLoop, calls=%fused_computation.1263 | loop fusion | flops 6 | bytes 24 | tf_op jit(solution)/shard_map/stack | solution.py:342
  160.0 5.3 %all-to-all-start.6 = ((f32[128,1,3]{2,1,0:T(1,128)}), f32[128,1,3]{2,1,0:T(1,128)S(1)}, u32[]{:S(2)}, u32[]{:S(2)}) async-start(f32[128,1,3]{2,1,0:T(1,128)} %broadcast_in_dim.23), calls=%async_computation.6 | async-start | bytes 131072 | tf_op jit(solution)/shard_map/all_to_all | solution.py:225
  165.5 9.4 %all-to-all-done.6 = f32[128,1,3]{2,1,0:T(1,128)S(1)} async-done(((f32[128,1,3]{2,1,0:T(1,128)}), f32[128,1,3]{2,1,0:T(1,128)S(1)}, u32[]{:S(2)}, u32[]{:S(2)}) %all-to-all-start.6) | async-done | bytes 1568 | tf_op jit(solution)/shard_map/all_to_all | solution.py:225
  (231 shorter events, 53.1 us)
Async XLA Ops:
  0.6 5.7 %copy-start = (bf16[2,20,10240]{2,0,1:T(2,128)(2,1)S(1)}, bf16[2,20,10240]{2,0,1:T(2,128)(2,1)}, u32[]{:S(2)}) copy-start(bf16[2,20,10240]{2,0,1:T(2,128)(2,1)} %param.9) | copy-start | bytes 2457604
  16.3 11.2 %all-to-all-start = ((f32[8,3,4,270]{3,2,1,0:T(4,128)}), f32[8,3,4,270]{3,2,1,0:T(4,128)S(1)}, u32[]{:S(2)}, u32[]{:S(2)}) async-start(f32[8,3,4,270]{3,2,1,0:T(4,128)} %copy.61), calls=%async_computation | async-start | bytes 294912 | tf_op jit(solution)/shard_map/all_to_all | solution.py:269
  27.7 4.5 %collective-permute-start = (f32[3,7,270]{2,1,0:T(8,128)S(1)}, f32[3,7,270]{2,1,0:T(8,128)S(1)}, u32[]{:S(2)}, u32[]{:S(2)}) collective-permute-start(f32[3,7,270]{2,1,0:T(8,128)S(1)} %get-tuple-element.51), channel_id=1, source_target_pairs={{0,8},{8,16},{16,24},{24,32},{32,40},{40,48},{48,56},{56,64},{64,7... | collective-permute-start | bytes 68048 | tf_op jit(solution)/shard_map/ppermute | solution.py:272
  30.9 4.7 %collective-permute-start.1 = (f32[3,7,270]{2,1,0:T(8,128)S(1)}, f32[3,7,270]{2,1,0:T(8,128)S(1)}, u32[]{:S(2)}, u32[]{:S(2)}) collective-permute-start(f32[3,7,270]{2,1,0:T(8,128)S(1)} %get-tuple-element.52), channel_id=1, source_target_pairs={{8,0},{16,8},{24,16},{32,24},{40,32},{48,40},{56,48},{64,56},{72,6... | collective-permute-start | bytes 68048 | tf_op jit(solution)/shard_map/ppermute | solution.py:273
  38.2 17.5 %all-to-all-start.1 = ((f32[16,3,16,128]{3,2,1,0:T(8,128)}), f32[16,3,16,128]{3,2,1,0:T(8,128)S(1)}, u32[]{:S(2)}, u32[]{:S(2)}) async-start(f32[16,3,16,128]{3,2,1,0:T(8,128)} %broadcast_in_dim.16), calls=%async_computation.1 | async-start | bytes 786432 | tf_op jit(solution)/shard_map/all_to_all | solution.py:203
  55.7 11.3 %collective-permute-start.3 = (f32[3,256,128]{2,1,0:T(8,128)S(1)}, f32[3,256,128]{2,1,0:T(8,128)S(1)}, u32[]{:S(2)}, u32[]{:S(2)}) collective-permute-start(f32[3,256,128]{2,1,0:T(8,128)S(1)} %bitcast.165), channel_id=1, source_target_pairs={{1,0},{2,1},{3,2},{4,3},{5,4},{6,5},{7,6},{9,8},{10,9},{11,10},{12... | collective-permute-start | bytes 1179656 | tf_op jit(solution)/shard_map/ppermute | solution.py:212
  61.4 6.8 %collective-permute-start.2 = (f32[3,256,128]{2,1,0:T(8,128)S(1)}, f32[3,256,128]{2,1,0:T(8,128)S(1)}, u32[]{:S(2)}, u32[]{:S(2)}) collective-permute-start(f32[3,256,128]{2,1,0:T(8,128)S(1)} %bitcast.166), channel_id=1, source_target_pairs={{0,1},{1,2},{2,3},{3,4},{4,5},{5,6},{6,7},{8,9},{9,10},{10,11},{11... | collective-permute-start | bytes 1179656 | tf_op jit(solution)/shard_map/ppermute | solution.py:211
  85.7 11.0 %all-to-all-start.2 = ((f32[16,2,16,128]{3,2,1,0:T(8,128)}), f32[16,2,16,128]{3,2,1,0:T(8,128)S(1)}, u32[]{:S(2)}, u32[]{:S(2)}) async-start(f32[16,2,16,128]{3,2,1,0:T(8,128)} %broadcast_in_dim.18), calls=%async_computation.2 | async-start | bytes 524288 | tf_op jit(solution)/shard_map/all_to_all | solution.py:203
  97.4 11.7 %all-to-all-start.3 = ((f32[8,1,2]{2,1,0:T(1,128)}), f32[8,1,2]{2,1,0:T(1,128)S(1)}, u32[]{:S(2)}, u32[]{:S(2)}) async-start(f32[8,1,2]{2,1,0:T(1,128)} %broadcast_in_dim.19), calls=%async_computation.3 | async-start | bytes 8192 | tf_op jit(solution)/shard_map/all_to_all | solution.py:207
  103.3 7.7 %collective-permute-start.5 = (f32[1,256,128]{2,1,0:T(8,128)S(1)}, f32[1,256,128]{2,1,0:T(8,128)S(1)}, u32[]{:S(2)}, u32[]{:S(2)}) collective-permute-start(f32[1,256,128]{2,1,0:T(8,128)S(1)} %bitcast.173), channel_id=1, source_target_pairs={{1,0},{2,1},{3,2},{4,3},{5,4},{6,5},{7,6},{9,8},{10,9},{11,10},{12... | collective-permute-start | bytes 393224 | tf_op jit(solution)/shard_map/ppermute | solution.py:212
  105.2 5.8 %collective-permute-start.4 = (f32[1,256,128]{2,1,0:T(8,128)S(1)}, f32[1,256,128]{2,1,0:T(8,128)S(1)}, u32[]{:S(2)}, u32[]{:S(2)}) collective-permute-start(f32[1,256,128]{2,1,0:T(8,128)S(1)} %bitcast.174), channel_id=1, source_target_pairs={{0,1},{1,2},{2,3},{3,4},{4,5},{5,6},{6,7},{8,9},{9,10},{10,11},{11... | collective-permute-start | bytes 393224 | tf_op jit(solution)/shard_map/ppermute | solution.py:211
  121.6 12.4 %all-to-all-start.4 = ((f32[16,2,16,128]{3,2,1,0:T(8,128)}), f32[16,2,16,128]{3,2,1,0:T(8,128)S(1)}, u32[]{:S(2)}, u32[]{:S(2)}) async-start(f32[16,2,16,128]{3,2,1,0:T(8,128)} %broadcast_in_dim.21), calls=%async_computation.4 | async-start | bytes 524288 | tf_op jit(solution)/shard_map/all_to_all | solution.py:203
  134.6 11.0 %all-to-all-start.5 = ((f32[8,1,3]{2,1,0:T(1,128)}), f32[8,1,3]{2,1,0:T(1,128)S(1)}, u32[]{:S(2)}, u32[]{:S(2)}) async-start(f32[8,1,3]{2,1,0:T(1,128)} %broadcast_in_dim.22), calls=%async_computation.5 | async-start | bytes 8192 | tf_op jit(solution)/shard_map/all_to_all | solution.py:207
  140.0 10.0 %collective-permute-start.7 = (f32[1,256,128]{2,1,0:T(8,128)S(1)}, f32[1,256,128]{2,1,0:T(8,128)S(1)}, u32[]{:S(2)}, u32[]{:S(2)}) collective-permute-start(f32[1,256,128]{2,1,0:T(8,128)S(1)} %bitcast.168), channel_id=1, source_target_pairs={{1,0},{2,1},{3,2},{4,3},{5,4},{6,5},{7,6},{9,8},{10,9},{11,10},{12... | collective-permute-start | bytes 393224 | tf_op jit(solution)/shard_map/ppermute | solution.py:212
  141.9 8.1 %collective-permute-start.6 = (f32[1,256,128]{2,1,0:T(8,128)S(1)}, f32[1,256,128]{2,1,0:T(8,128)S(1)}, u32[]{:S(2)}, u32[]{:S(2)}) collective-permute-start(f32[1,256,128]{2,1,0:T(8,128)S(1)} %bitcast.169), channel_id=1, source_target_pairs={{0,1},{1,2},{2,3},{3,4},{4,5},{5,6},{6,7},{8,9},{9,10},{10,11},{11... | collective-permute-start | bytes 393224 | tf_op jit(solution)/shard_map/ppermute | solution.py:211
  160.0 14.9 %all-to-all-start.6 = ((f32[128,1,3]{2,1,0:T(1,128)}), f32[128,1,3]{2,1,0:T(1,128)S(1)}, u32[]{:S(2)}, u32[]{:S(2)}) async-start(f32[128,1,3]{2,1,0:T(1,128)} %broadcast_in_dim.23), calls=%async_computation.6 | async-start | bytes 131072 | tf_op jit(solution)/shard_map/all_to_all | solution.py:225

commit v12 on v11

--- a/solution.py
+++ b/solution.py
@@ -204,12 +204,14 @@
     summed = None
     if sums is not None:
         column_sums = jnp.sum(got[:, count, 0, :sums.shape[0]], axis=0)
-        rows = lax.all_to_all(jnp.broadcast_to(column_sums[None], (n_rg, sums.shape[0])), "rg", 0, 0, tiled=True)
-        summed = jnp.sum(rows, axis=0)
         got = got[:, :count]
     column = got.transpose(1, 0, 2, 3).reshape(count, n_az * h, w)
     left = lax.ppermute(column, "rg", [(i, i + 1) for i in range(n_rg - 1)])
     right = lax.ppermute(column, "rg", [(i + 1, i) for i in range(n_rg - 1)])
+    if sums is not None:
+        column_sums, left, right = lax.optimization_barrier((column_sums, left, right))
+        rows = lax.all_to_all(jnp.broadcast_to(column_sums[None], (n_rg, sums.shape[0])), "rg", 0, 0, tiled=True)
+        summed = jnp.sum(rows, axis=0)
     return jnp.concatenate([left, column, right], axis=-1), summed
 
 

time: 181 us -> 186 us (1.028)
  waiting for transfers between devices: 46 us -> 49.5 us
    ppermute x3, waiting for transfers between devices: 1.19 us -> 3.51 us  [gather_strip(): left = lax.ppermute(column, 'rg', [(i, i + 1) for i in range(n_rg - 1)])]
  transfers between devices with their start and end apart: 15 -> 15, of which waited for: 8 -> 11; matrix products, arithmetic and copies ran while one was open for 1% -> 7% of each run, Pallas kernels for 0% -> 0%
where the time goes in v12:
time: 186 us; the launch traced here: 185 us
  starting transfers between devices  64 us (34%)
  waiting for transfers between devices  49.5 us (27%)
  matrix products  26.3 us (14%)
  other arithmetic  15.3 us (8%)
  local copies, waits for them, and re-layouts  13.4 us (7%)
  between operations  11.9 us (6%)
  Pallas kernels  4.3 us (2%)
    all_to_all x3, waiting for transfers between devices, gather_strip(): got = lax.all_to_all(sent, 'az', 0, 0, tiled=True)  24.2 us
    all_to_all x3, starting transfers between devices, gather_strip(): got = lax.all_to_all(sent, 'az', 0, 0, tiled=True)  16.3 us
    dot_general x48, matrix products, sandwich(): inner = jnp.dot(left, vector, precision=HIGHEST)  13.8 us
    dot_general x48, matrix products, sandwich(): return jnp.dot(inner, right, precision=HIGHEST)  11 us
    ppermute x3, starting transfers between devices, gather_strip(): left = lax.ppermute(column, 'rg', [(i, i + 1) for i in range(n_rg - 1)])  11 us
    ppermute x3, starting transfers between devices, gather_strip(): right = lax.ppermute(column, 'rg', [(i + 1, i) for i in range(n_rg - 1)])  10.6 us
    all_to_all x2, starting transfers between devices, gather_strip(): lax.all_to_all(jnp.broadcast_to(column_sums[None], (n_rg, sums.shape[0]))...  10.3 us
    all_to_all x1, waiting for transfers between devices, total(): got = lax.all_to_all(sent, ('az', 'rg'), 0, 0, tiled=True)  9.43 us
  transfers between devices with their start and end apart: 15, of which 11 were waited for; matrix products, arithmetic and copies ran while one was open for 7% of the time, Pallas kernels for 0%

profile of v12, /device:TPU:1, one launch (start us, length us, event | category | flops | bytes accessed | tf_op | source)
XLA Modules:
  0.0 184.8 jit_solution(17653432734090857368)
XLA Ops:
  3.9 2.4 %copy.59.lead_ref = bf16[2,20,10240]{2,1,0:T(8,128)(2,1)} copy(bf16[2,20,10240]{2,0,1:T(2,128)(2,1)} %param.8) | data formatting | bytes 1638400 | tf_op args[0]
  9.5 4.3 %shard_map.59 = f32[4,4,16,640]{3,2,1,0:T(8,128)} custom-call(s32[4]{0:T(128)} %pad_add_fusion.bounds_ref, bf16[2,20,10240]{2,1,0:T(8,128)(2,1)} %copy.59.lead_ref, bf16[2,20,10240]{2,1,0:T(8,128)(2,1)} %copy.60.trail_ref), custom_call_target="tpu_custom_call" | custom-call | tf_op jit(solution)/shard_map/pallas_call | solution.py:94
  16.3 5.8 %all-to-all-start = ((f32[8,3,4,270]{3,2,1,0:T(4,128)}), f32[8,3,4,270]{3,2,1,0:T(4,128)S(1)}, u32[]{:S(2)}, u32[]{:S(2)}) async-start(f32[8,3,4,270]{3,2,1,0:T(4,128)} %copy.61), calls=%async_computation | async-start | bytes 294912 | tf_op jit(solution)/shard_map/all_to_all | solution.py:271
  22.5 5.0 %all-to-all-done = f32[8,3,4,270]{3,2,1,0:T(4,128)S(1)} async-done(((f32[8,3,4,270]{3,2,1,0:T(4,128)}), f32[8,3,4,270]{3,2,1,0:T(4,128)S(1)}, u32[]{:S(2)}, u32[]{:S(2)}) %all-to-all-start) | async-done | bytes 103712 | tf_op jit(solution)/shard_map/all_to_all | solution.py:271
  27.7 3.2 %collective-permute-start = (f32[3,7,270]{2,1,0:T(8,128)S(1)}, f32[3,7,270]{2,1,0:T(8,128)S(1)}, u32[]{:S(2)}, u32[]{:S(2)}) collective-permute-start(f32[3,7,270]{2,1,0:T(8,128)S(1)} %get-tuple-element.63), channel_id=1, source_target_pairs={{0,8},{8,16},{16,24},{24,32},{32,40},{40,48},{48,56},{56,64},{64,7... | collective-permute-start | bytes 68048 | tf_op jit(solution)/shard_map/ppermute | solution.py:274
  32.2 3.4 %collective-permute-done.1 = f32[3,7,270]{2,1,0:T(8,128)S(1)} collective-permute-done((f32[3,7,270]{2,1,0:T(8,128)S(1)}, f32[3,7,270]{2,1,0:T(8,128)S(1)}, u32[]{:S(2)}, u32[]{:S(2)}) %collective-permute-start.1) | collective-permute-done | bytes 22712 | tf_op jit(solution)/shard_map/ppermute | solution.py:275
  38.2 9.2 %all-to-all-start.1 = ((f32[16,3,16,128]{3,2,1,0:T(8,128)}), f32[16,3,16,128]{3,2,1,0:T(8,128)S(1)}, u32[]{:S(2)}, u32[]{:S(2)}) async-start(f32[16,3,16,128]{3,2,1,0:T(8,128)} %broadcast_in_dim.16), calls=%async_computation.1 | async-start | bytes 786432 | tf_op jit(solution)/shard_map/all_to_all | solution.py:203
  47.5 8.2 %all-to-all-done.1 = f32[16,3,16,128]{3,2,1,0:T(8,128)S(1)} async-done(((f32[16,3,16,128]{3,2,1,0:T(8,128)}), f32[16,3,16,128]{3,2,1,0:T(8,128)S(1)}, u32[]{:S(2)}, u32[]{:S(2)}) %all-to-all-start.1) | async-done | bytes 393248 | tf_op jit(solution)/shard_map/all_to_all | solution.py:203
  55.7 5.7 %collective-permute-start.3 = (f32[3,256,128]{2,1,0:T(8,128)S(1)}, f32[3,256,128]{2,1,0:T(8,128)S(1)}, u32[]{:S(2)}, u32[]{:S(2)}) collective-permute-start(f32[3,256,128]{2,1,0:T(8,128)S(1)} %bitcast.165), channel_id=1, source_target_pairs={{1,0},{2,1},{3,2},{4,3},{5,4},{6,5},{7,6},{9,8},{10,9},{11,10},{12... | collective-permute-start | bytes 1179656 | tf_op jit(solution)/shard_map/ppermute | solution.py:210
  61.4 2.3 %collective-permute-start.2 = (f32[3,256,128]{2,1,0:T(8,128)S(1)}, f32[3,256,128]{2,1,0:T(8,128)S(1)}, u32[]{:S(2)}, u32[]{:S(2)}) collective-permute-start(f32[3,256,128]{2,1,0:T(8,128)S(1)} %bitcast.166), channel_id=1, source_target_pairs={{0,1},{1,2},{2,3},{3,4},{4,5},{5,6},{6,7},{8,9},{9,10},{10,11},{11... | collective-permute-start | bytes 1179656 | tf_op jit(solution)/shard_map/ppermute | solution.py:209
  63.7 3.3 %collective-permute-done.3 = f32[3,256,128]{2,1,0:T(8,128)S(1)} collective-permute-done((f32[3,256,128]{2,1,0:T(8,128)S(1)}, f32[3,256,128]{2,1,0:T(8,128)S(1)}, u32[]{:S(2)}, u32[]{:S(2)}) %collective-permute-start.3) | collective-permute-done | bytes 393248 | tf_op jit(solution)/shard_map/ppermute | solution.py:210
  85.7 3.5 %all-to-all-start.2 = ((f32[16,2,16,128]{3,2,1,0:T(8,128)}), f32[16,2,16,128]{3,2,1,0:T(8,128)S(1)}, u32[]{:S(2)}, u32[]{:S(2)}) async-start(f32[16,2,16,128]{3,2,1,0:T(8,128)} %broadcast_in_dim.18), calls=%async_computation.2 | async-start | bytes 524288 | tf_op jit(solution)/shard_map/all_to_all | solution.py:203
  89.3 7.5 %all-to-all-done.2 = f32[16,2,16,128]{3,2,1,0:T(8,128)S(1)} async-done(((f32[16,2,16,128]{3,2,1,0:T(8,128)}), f32[16,2,16,128]{3,2,1,0:T(8,128)S(1)}, u32[]{:S(2)}, u32[]{:S(2)}) %all-to-all-start.2) | async-done | bytes 262176 | tf_op jit(solution)/shard_map/all_to_all | solution.py:203
  98.7 5.5 %collective-permute-start.4 = (f32[1,256,128]{2,1,0:T(8,128)S(1)}, f32[1,256,128]{2,1,0:T(8,128)S(1)}, u32[]{:S(2)}, u32[]{:S(2)}) collective-permute-start(f32[1,256,128]{2,1,0:T(8,128)S(1)} %bitcast.174), channel_id=1, source_target_pairs={{0,1},{1,2},{2,3},{3,4},{4,5},{5,6},{6,7},{8,9},{9,10},{10,11},{11... | collective-permute-start | bytes 393224 | tf_op jit(solution)/shard_map/ppermute | solution.py:209
  106.8 4.7 %all-to-all-start.3 = ((f32[8,1,2]{2,1,0:T(1,128)}), f32[8,1,2]{2,1,0:T(1,128)S(1)}, u32[]{:S(2)}, u32[]{:S(2)}) async-start(f32[8,1,2]{2,1,0:T(1,128)} %broadcast_in_dim.19), calls=%async_computation.3 | async-start | bytes 8192 | tf_op jit(solution)/shard_map/all_to_all | solution.py:213
  121.2 2.0 %maximum_bitcast_fusion.6 = f32[1,1,3]{2,1,0:T(1,128)S(1)} fusion(f32[1]{0:T(128)} %bitcast.33, f32[1]{0:T(128)} %bitcast.32, f32[1]{0:T(128)} %bitcast.31), kind=kLoop, calls=%fused_computation.1262 | loop fusion | flops 6 | bytes 24 | tf_op jit(solution)/shard_map/reshape.48
  124.0 3.5 %all-to-all-start.4 = ((f32[16,2,16,128]{3,2,1,0:T(8,128)}), f32[16,2,16,128]{3,2,1,0:T(8,128)S(1)}, u32[]{:S(2)}, u32[]{:S(2)}) async-start(f32[16,2,16,128]{3,2,1,0:T(8,128)} %broadcast_in_dim.21), calls=%async_computation.4 | async-start | bytes 524288 | tf_op jit(solution)/shard_map/all_to_all | solution.py:203
  127.5 8.5 %all-to-all-done.4 = f32[16,2,16,128]{3,2,1,0:T(8,128)S(1)} async-done(((f32[16,2,16,128]{3,2,1,0:T(8,128)}), f32[16,2,16,128]{3,2,1,0:T(8,128)S(1)}, u32[]{:S(2)}, u32[]{:S(2)}) %all-to-all-start.4) | async-done | bytes 262176 | tf_op jit(solution)/shard_map/all_to_all | solution.py:203
  136.0 3.0 %collective-permute-start.7 = (f32[1,256,128]{2,1,0:T(8,128)S(1)}, f32[1,256,128]{2,1,0:T(8,128)S(1)}, u32[]{:S(2)}, u32[]{:S(2)}) collective-permute-start(f32[1,256,128]{2,1,0:T(8,128)S(1)} %bitcast.168), channel_id=1, source_target_pairs={{1,0},{2,1},{3,2},{4,3},{5,4},{6,5},{7,6},{9,8},{10,9},{11,10},{12... | collective-permute-start | bytes 393224 | tf_op jit(solution)/shard_map/ppermute | solution.py:210
  139.0 3.2 %collective-permute-start.6 = (f32[1,256,128]{2,1,0:T(8,128)S(1)}, f32[1,256,128]{2,1,0:T(8,128)S(1)}, u32[]{:S(2)}, u32[]{:S(2)}) collective-permute-start(f32[1,256,128]{2,1,0:T(8,128)S(1)} %bitcast.169), channel_id=1, source_target_pairs={{0,1},{1,2},{2,3},{3,4},{4,5},{5,6},{6,7},{8,9},{9,10},{10,11},{11... | collective-permute-start | bytes 393224 | tf_op jit(solution)/shard_map/ppermute | solution.py:209
  144.8 5.6 %all-to-all-start.5 = ((f32[8,1,3]{2,1,0:T(1,128)}), f32[8,1,3]{2,1,0:T(1,128)S(1)}, u32[]{:S(2)}, u32[]{:S(2)}) async-start(f32[8,1,3]{2,1,0:T(1,128)} %broadcast_in_dim.22), calls=%async_computation.5 | async-start | bytes 8192 | tf_op jit(solution)/shard_map/all_to_all | solution.py:213
  162.0 2.0 %pad_maximum_fusion.3 = f32[3]{0:T(128)S(1)} fusion(f32[1]{0:T(128)} %bitcast.42, f32[1]{0:T(128)} %bitcast.41, f32[1]{0:T(128)} %bitcast.40), kind=kLoop, calls=%fused_computation.1263 | loop fusion | flops 6 | bytes 24 | tf_op jit(solution)/shard_map/stack | solution.py:344
  164.7 5.6 %all-to-all-start.6 = ((f32[128,1,3]{2,1,0:T(1,128)}), f32[128,1,3]{2,1,0:T(1,128)S(1)}, u32[]{:S(2)}, u32[]{:S(2)}) async-start(f32[128,1,3]{2,1,0:T(1,128)} %broadcast_in_dim.23), calls=%async_computation.6 | async-start | bytes 131072 | tf_op jit(solution)/shard_map/all_to_all | solution.py:227
  170.5 9.4 %all-to-all-done.6 = f32[128,1,3]{2,1,0:T(1,128)S(1)} async-done(((f32[128,1,3]{2,1,0:T(1,128)}), f32[128,1,3]{2,1,0:T(1,128)S(1)}, u32[]{:S(2)}, u32[]{:S(2)}) %all-to-all-start.6) | async-done | bytes 1568 | tf_op jit(solution)/shard_map/all_to_all | solution.py:227
  (231 shorter events, 56.0 us)
Async XLA Ops:
  0.6 5.7 %copy-start = (bf16[2,20,10240]{2,0,1:T(2,128)(2,1)S(1)}, bf16[2,20,10240]{2,0,1:T(2,128)(2,1)}, u32[]{:S(2)}) copy-start(bf16[2,20,10240]{2,0,1:T(2,128)(2,1)} %param.9) | copy-start | bytes 2457604
  16.3 11.2 %all-to-all-start = ((f32[8,3,4,270]{3,2,1,0:T(4,128)}), f32[8,3,4,270]{3,2,1,0:T(4,128)S(1)}, u32[]{:S(2)}, u32[]{:S(2)}) async-start(f32[8,3,4,270]{3,2,1,0:T(4,128)} %copy.61), calls=%async_computation | async-start | bytes 294912 | tf_op jit(solution)/shard_map/all_to_all | solution.py:271
  27.7 4.5 %collective-permute-start = (f32[3,7,270]{2,1,0:T(8,128)S(1)}, f32[3,7,270]{2,1,0:T(8,128)S(1)}, u32[]{:S(2)}, u32[]{:S(2)}) collective-permute-start(f32[3,7,270]{2,1,0:T(8,128)S(1)} %get-tuple-element.63), channel_id=1, source_target_pairs={{0,8},{8,16},{16,24},{24,32},{32,40},{40,48},{48,56},{56,64},{64,7... | collective-permute-start | bytes 68048 | tf_op jit(solution)/shard_map/ppermute | solution.py:274
  30.9 4.7 %collective-permute-start.1 = (f32[3,7,270]{2,1,0:T(8,128)S(1)}, f32[3,7,270]{2,1,0:T(8,128)S(1)}, u32[]{:S(2)}, u32[]{:S(2)}) collective-permute-start(f32[3,7,270]{2,1,0:T(8,128)S(1)} %get-tuple-element.64), channel_id=1, source_target_pairs={{8,0},{16,8},{24,16},{32,24},{40,32},{48,40},{56,48},{64,56},{72,6... | collective-permute-start | bytes 68048 | tf_op jit(solution)/shard_map/ppermute | solution.py:275
  38.2 17.5 %all-to-all-start.1 = ((f32[16,3,16,128]{3,2,1,0:T(8,128)}), f32[16,3,16,128]{3,2,1,0:T(8,128)S(1)}, u32[]{:S(2)}, u32[]{:S(2)}) async-start(f32[16,3,16,128]{3,2,1,0:T(8,128)} %broadcast_in_dim.16), calls=%async_computation.1 | async-start | bytes 786432 | tf_op jit(solution)/shard_map/all_to_all | solution.py:203
  55.7 11.3 %collective-permute-start.3 = (f32[3,256,128]{2,1,0:T(8,128)S(1)}, f32[3,256,128]{2,1,0:T(8,128)S(1)}, u32[]{:S(2)}, u32[]{:S(2)}) collective-permute-start(f32[3,256,128]{2,1,0:T(8,128)S(1)} %bitcast.165), channel_id=1, source_target_pairs={{1,0},{2,1},{3,2},{4,3},{5,4},{6,5},{7,6},{9,8},{10,9},{11,10},{12... | collective-permute-start | bytes 1179656 | tf_op jit(solution)/shard_map/ppermute | solution.py:210
  61.4 6.8 %collective-permute-start.2 = (f32[3,256,128]{2,1,0:T(8,128)S(1)}, f32[3,256,128]{2,1,0:T(8,128)S(1)}, u32[]{:S(2)}, u32[]{:S(2)}) collective-permute-start(f32[3,256,128]{2,1,0:T(8,128)S(1)} %bitcast.166), channel_id=1, source_target_pairs={{0,1},{1,2},{2,3},{3,4},{4,5},{5,6},{6,7},{8,9},{9,10},{10,11},{11... | collective-permute-start | bytes 1179656 | tf_op jit(solution)/shard_map/ppermute | solution.py:209
  85.7 11.0 %all-to-all-start.2 = ((f32[16,2,16,128]{3,2,1,0:T(8,128)}), f32[16,2,16,128]{3,2,1,0:T(8,128)S(1)}, u32[]{:S(2)}, u32[]{:S(2)}) async-start(f32[16,2,16,128]{3,2,1,0:T(8,128)} %broadcast_in_dim.18), calls=%async_computation.2 | async-start | bytes 524288 | tf_op jit(solution)/shard_map/all_to_all | solution.py:203
  96.8 8.2 %collective-permute-start.5 = (f32[1,256,128]{2,1,0:T(8,128)S(1)}, f32[1,256,128]{2,1,0:T(8,128)S(1)}, u32[]{:S(2)}, u32[]{:S(2)}) collective-permute-start(f32[1,256,128]{2,1,0:T(8,128)S(1)} %bitcast.173), channel_id=1, source_target_pairs={{1,0},{2,1},{3,2},{4,3},{5,4},{6,5},{7,6},{9,8},{10,9},{11,10},{12... | collective-permute-start | bytes 393224 | tf_op jit(solution)/shard_map/ppermute | solution.py:210
  98.7 7.5 %collective-permute-start.4 = (f32[1,256,128]{2,1,0:T(8,128)S(1)}, f32[1,256,128]{2,1,0:T(8,128)S(1)}, u32[]{:S(2)}, u32[]{:S(2)}) collective-permute-start(f32[1,256,128]{2,1,0:T(8,128)S(1)} %bitcast.174), channel_id=1, source_target_pairs={{0,1},{1,2},{2,3},{3,4},{4,5},{5,6},{6,7},{8,9},{9,10},{10,11},{11... | collective-permute-start | bytes 393224 | tf_op jit(solution)/shard_map/ppermute | solution.py:209
  106.8 10.8 %all-to-all-start.3 = ((f32[8,1,2]{2,1,0:T(1,128)}), f32[8,1,2]{2,1,0:T(1,128)S(1)}, u32[]{:S(2)}, u32[]{:S(2)}) async-start(f32[8,1,2]{2,1,0:T(1,128)} %broadcast_in_dim.19), calls=%async_computation.3 | async-start | bytes 8192 | tf_op jit(solution)/shard_map/all_to_all | solution.py:213
  124.0 12.1 %all-to-all-start.4 = ((f32[16,2,16,128]{3,2,1,0:T(8,128)}), f32[16,2,16,128]{3,2,1,0:T(8,128)S(1)}, u32[]{:S(2)}, u32[]{:S(2)}) async-start(f32[16,2,16,128]{3,2,1,0:T(8,128)} %broadcast_in_dim.21), calls=%async_computation.4 | async-start | bytes 524288 | tf_op jit(solution)/shard_map/all_to_all | solution.py:203
  136.0 7.0 %collective-permute-start.7 = (f32[1,256,128]{2,1,0:T(8,128)S(1)}, f32[1,256,128]{2,1,0:T(8,128)S(1)}, u32[]{:S(2)}, u32[]{:S(2)}) collective-permute-start(f32[1,256,128]{2,1,0:T(8,128)S(1)} %bitcast.168), channel_id=1, source_target_pairs={{1,0},{2,1},{3,2},{4,3},{5,4},{6,5},{7,6},{9,8},{10,9},{11,10},{12... | collective-permute-start | bytes 393224 | tf_op jit(solution)/shard_map/ppermute | solution.py:210
  139.0 5.1 %collective-permute-start.6 = (f32[1,256,128]{2,1,0:T(8,128)S(1)}, f32[1,256,128]{2,1,0:T(8,128)S(1)}, u32[]{:S(2)}, u32[]{:S(2)}) collective-permute-start(f32[1,256,128]{2,1,0:T(8,128)S(1)} %bitcast.169), channel_id=1, source_target_pairs={{0,1},{1,2},{2,3},{3,4},{4,5},{5,6},{6,7},{8,9},{9,10},{10,11},{11... | collective-permute-start | bytes 393224 | tf_op jit(solution)/shard_map/ppermute | solution.py:209
  144.8 11.7 %all-to-all-start.5 = ((f32[8,1,3]{2,1,0:T(1,128)}), f32[8,1,3]{2,1,0:T(1,128)S(1)}, u32[]{:S(2)}, u32[]{:S(2)}) async-start(f32[8,1,3]{2,1,0:T(1,128)} %broadcast_in_dim.22), calls=%async_computation.5 | async-start | bytes 8192 | tf_op jit(solution)/shard_map/all_to_all | solution.py:213
  164.7 15.2 %all-to-all-start.6 = ((f32[128,1,3]{2,1,0:T(1,128)}), f32[128,1,3]{2,1,0:T(1,128)S(1)}, u32[]{:S(2)}, u32[]{:S(2)}) async-start(f32[128,1,3]{2,1,0:T(1,128)} %broadcast_in_dim.23), calls=%async_computation.6 | async-start | bytes 131072 | tf_op jit(solution)/shard_map/all_to_all | solution.py:227

commit v13 on v11

--- a/solution.py
+++ b/solution.py
@@ -62,15 +62,15 @@
 
 
 def multilook_kernel(bounds_ref, lead_ref, trail_ref, out_ref):
-    shape = lead_ref.shape[1:]
+    shape = (lead_ref.shape[0], lead_ref.shape[2])
     line = lax.broadcasted_iota(jnp.int32, shape, 0)
     column = pl.program_id(0) * shape[1] + lax.broadcasted_iota(jnp.int32, shape, 1)
     mask = ((line >= bounds_ref[0]) & (line < bounds_ref[1]) & (column >= bounds_ref[2])
             & (column < bounds_ref[3])).astype(jnp.float32)
-    first_re = lead_ref[0].astype(jnp.float32) * mask
-    first_im = lead_ref[1].astype(jnp.float32) * mask
-    second_re = trail_ref[0].astype(jnp.float32) * mask
-    second_im = trail_ref[1].astype(jnp.float32) * mask
+    first_re = lead_ref[:, 0, :].astype(jnp.float32) * mask
+    first_im = lead_ref[:, 1, :].astype(jnp.float32) * mask
+    second_re = trail_ref[:, 0, :].astype(jnp.float32) * mask
+    second_im = trail_ref[:, 1, :].astype(jnp.float32) * mask
     products = (
         first_re * second_re + first_im * second_im,
         first_im * second_re - first_re * second_im,
@@ -96,12 +96,12 @@
         grid=(width_cols // block,),
         in_specs=[
             pl.BlockSpec(memory_space=pltpu.SMEM),
-            pl.BlockSpec((2, height_rows, block), lambda j: (0, 0, j)),
-            pl.BlockSpec((2, height_rows, block), lambda j: (0, 0, j)),
+            pl.BlockSpec((height_rows, 2, block), lambda j: (0, 0, j)),
+            pl.BlockSpec((height_rows, 2, block), lambda j: (0, 0, j)),
         ],
         out_specs=pl.BlockSpec((4, height_rows // LOOK, block // span, span), lambda j: (0, 0, j, 0)),
         out_shape=jax.ShapeDtypeStruct((4, height_rows // LOOK, width_cols // span, span), jnp.float32),
-    )(bounds, leading, trailing)
+    )(bounds, jnp.transpose(leading, (1, 0, 2)), jnp.transpose(trailing, (1, 0, 2)))
     grouped = rows
     cols = jnp.einsum("pikc,cd->pikd", grouped, group_sum(span, LOOK).T, precision=HIGHEST)
     return cols.reshape(4, height_rows // LOOK, width_cols // LOOK)

time: 181 us -> 178 us (0.983)
  local copies, waits for them, and re-layouts: 13.4 us -> 9.74 us
    unnamed x4 -> x0, local copies, waits for them, and re-layouts: 3.58 us -> none
  transfers between devices with their start and end apart: 15 -> 15, of which waited for: 8 -> 8; matrix products, arithmetic and copies ran while one was open for 1% -> 2% of each run, Pallas kernels for 0% -> 0%
where the time goes in v13:
time: 178 us; the launch traced here: 177 us
  starting transfers between devices  62.3 us (35%)
  waiting for transfers between devices  46 us (26%)
  matrix products  26.3 us (15%)
  other arithmetic  15.2 us (9%)
  between operations  11.9 us (7%)
  local copies, waits for them, and re-layouts  9.74 us (5%)
  Pallas kernels  5.14 us (3%)
    all_to_all x3, waiting for transfers between devices, gather_strip(): got = lax.all_to_all(sent, 'az', 0, 0, tiled=True)  23.7 us
    all_to_all x3, starting transfers between devices, gather_strip(): got = lax.all_to_all(sent, 'az', 0, 0, tiled=True)  16.3 us
    dot_general x48, matrix products, sandwich(): inner = jnp.dot(left, vector, precision=HIGHEST)  13.8 us
    all_to_all x2, starting transfers between devices, gather_strip(): lax.all_to_all(jnp.broadcast_to(column_sums[None], (n_rg, sums.shape[0]))...  11.1 us
    dot_general x48, matrix products, sandwich(): return jnp.dot(inner, right, precision=HIGHEST)  11 us
    ppermute x3, starting transfers between devices, gather_strip(): left = lax.ppermute(column, 'rg', [(i, i + 1) for i in range(n_rg - 1)])  9.78 us
    ppermute x3, starting transfers between devices, gather_strip(): right = lax.ppermute(column, 'rg', [(i + 1, i) for i in range(n_rg - 1)])  9.5 us
    all_to_all x1, waiting for transfers between devices, total(): got = lax.all_to_all(sent, ('az', 'rg'), 0, 0, tiled=True)  9.4 us
  transfers between devices with their start and end apart: 15, of which 8 were waited for; matrix products, arithmetic and copies ran while one was open for 2% of the time, Pallas kernels for 0%

profile of v13, /device:TPU:1, one launch (start us, length us, event | category | flops | bytes accessed | tf_op | source)
XLA Modules:
  0.0 176.7 jit_solution(16618465882444751826)
XLA Ops:
  5.7 5.1 %shard_map.59 = f32[4,4,16,640]{3,2,1,0:T(8,128)} custom-call(s32[4]{0:T(128)} %pad_add_fusion.bounds_ref, bf16[20,2,10240]{2,1,0:T(2,128)(2,1)} %bitcast.180, bf16[20,2,10240]{2,1,0:T(2,128)(2,1)} %bitcast.181), custom_call_target="tpu_custom_call" | custom-call | tf_op jit(solution)/shard_map/pallas_call | solution.py:94
  13.4 5.8 %all-to-all-start = ((f32[8,3,4,270]{3,2,1,0:T(4,128)}), f32[8,3,4,270]{3,2,1,0:T(4,128)S(1)}, u32[]{:S(2)}, u32[]{:S(2)}) async-start(f32[8,3,4,270]{3,2,1,0:T(4,128)} %copy.49), calls=%async_computation | async-start | bytes 294912 | tf_op jit(solution)/shard_map/all_to_all | solution.py:269
  19.6 5.0 %all-to-all-done = f32[8,3,4,270]{3,2,1,0:T(4,128)S(1)} async-done(((f32[8,3,4,270]{3,2,1,0:T(4,128)}), f32[8,3,4,270]{3,2,1,0:T(4,128)S(1)}, u32[]{:S(2)}, u32[]{:S(2)}) %all-to-all-start) | async-done | bytes 103712 | tf_op jit(solution)/shard_map/all_to_all | solution.py:269
  24.7 3.2 %collective-permute-start = (f32[3,7,270]{2,1,0:T(8,128)S(1)}, f32[3,7,270]{2,1,0:T(8,128)S(1)}, u32[]{:S(2)}, u32[]{:S(2)}) collective-permute-start(f32[3,7,270]{2,1,0:T(8,128)S(1)} %get-tuple-element.51), channel_id=1, source_target_pairs={{0,8},{8,16},{16,24},{24,32},{32,40},{40,48},{48,56},{56,64},{64,7... | collective-permute-start | bytes 68048 | tf_op jit(solution)/shard_map/ppermute | solution.py:272
  29.3 3.4 %collective-permute-done.1 = f32[3,7,270]{2,1,0:T(8,128)S(1)} collective-permute-done((f32[3,7,270]{2,1,0:T(8,128)S(1)}, f32[3,7,270]{2,1,0:T(8,128)S(1)}, u32[]{:S(2)}, u32[]{:S(2)}) %collective-permute-start.1) | collective-permute-done | bytes 22712 | tf_op jit(solution)/shard_map/ppermute | solution.py:273
  35.2 9.2 %all-to-all-start.1 = ((f32[16,3,16,128]{3,2,1,0:T(8,128)}), f32[16,3,16,128]{3,2,1,0:T(8,128)S(1)}, u32[]{:S(2)}, u32[]{:S(2)}) async-start(f32[16,3,16,128]{3,2,1,0:T(8,128)} %broadcast_in_dim.16), calls=%async_computation.1 | async-start | bytes 786432 | tf_op jit(solution)/shard_map/all_to_all | solution.py:203
  44.5 8.2 %all-to-all-done.1 = f32[16,3,16,128]{3,2,1,0:T(8,128)S(1)} async-done(((f32[16,3,16,128]{3,2,1,0:T(8,128)}), f32[16,3,16,128]{3,2,1,0:T(8,128)S(1)}, u32[]{:S(2)}, u32[]{:S(2)}) %all-to-all-start.1) | async-done | bytes 393248 | tf_op jit(solution)/shard_map/all_to_all | solution.py:203
  52.8 5.7 %collective-permute-start.3 = (f32[3,256,128]{2,1,0:T(8,128)S(1)}, f32[3,256,128]{2,1,0:T(8,128)S(1)}, u32[]{:S(2)}, u32[]{:S(2)}) collective-permute-start(f32[3,256,128]{2,1,0:T(8,128)S(1)} %bitcast.167), channel_id=1, source_target_pairs={{1,0},{2,1},{3,2},{4,3},{5,4},{6,5},{7,6},{9,8},{10,9},{11,10},{12... | collective-permute-start | bytes 1179656 | tf_op jit(solution)/shard_map/ppermute | solution.py:212
  58.4 2.3 %collective-permute-start.2 = (f32[3,256,128]{2,1,0:T(8,128)S(1)}, f32[3,256,128]{2,1,0:T(8,128)S(1)}, u32[]{:S(2)}, u32[]{:S(2)}) collective-permute-start(f32[3,256,128]{2,1,0:T(8,128)S(1)} %bitcast.168), channel_id=1, source_target_pairs={{0,1},{1,2},{2,3},{3,4},{4,5},{5,6},{6,7},{8,9},{9,10},{10,11},{11... | collective-permute-start | bytes 1179656 | tf_op jit(solution)/shard_map/ppermute | solution.py:211
  60.8 3.3 %collective-permute-done.3 = f32[3,256,128]{2,1,0:T(8,128)S(1)} collective-permute-done((f32[3,256,128]{2,1,0:T(8,128)S(1)}, f32[3,256,128]{2,1,0:T(8,128)S(1)}, u32[]{:S(2)}, u32[]{:S(2)}) %collective-permute-start.3) | collective-permute-done | bytes 393248 | tf_op jit(solution)/shard_map/ppermute | solution.py:212
  82.8 3.5 %all-to-all-start.2 = ((f32[16,2,16,128]{3,2,1,0:T(8,128)}), f32[16,2,16,128]{3,2,1,0:T(8,128)S(1)}, u32[]{:S(2)}, u32[]{:S(2)}) async-start(f32[16,2,16,128]{3,2,1,0:T(8,128)} %broadcast_in_dim.18), calls=%async_computation.2 | async-start | bytes 524288 | tf_op jit(solution)/shard_map/all_to_all | solution.py:203
  86.3 7.5 %all-to-all-done.2 = f32[16,2,16,128]{3,2,1,0:T(8,128)S(1)} async-done(((f32[16,2,16,128]{3,2,1,0:T(8,128)}), f32[16,2,16,128]{3,2,1,0:T(8,128)S(1)}, u32[]{:S(2)}, u32[]{:S(2)}) %all-to-all-start.2) | async-done | bytes 262176 | tf_op jit(solution)/shard_map/all_to_all | solution.py:203
  94.4 5.9 %all-to-all-start.3 = ((f32[8,1,2]{2,1,0:T(1,128)}), f32[8,1,2]{2,1,0:T(1,128)S(1)}, u32[]{:S(2)}, u32[]{:S(2)}) async-start(f32[8,1,2]{2,1,0:T(1,128)} %broadcast_in_dim.19), calls=%async_computation.3 | async-start | bytes 8192 | tf_op jit(solution)/shard_map/all_to_all | solution.py:207
  100.4 1.9 %collective-permute-start.5 = (f32[1,256,128]{2,1,0:T(8,128)S(1)}, f32[1,256,128]{2,1,0:T(8,128)S(1)}, u32[]{:S(2)}, u32[]{:S(2)}) collective-permute-start(f32[1,256,128]{2,1,0:T(8,128)S(1)} %bitcast.175), channel_id=1, source_target_pairs={{1,0},{2,1},{3,2},{4,3},{5,4},{6,5},{7,6},{9,8},{10,9},{11,10},{12... | collective-permute-start | bytes 393224 | tf_op jit(solution)/shard_map/ppermute | solution.py:212
  102.3 3.9 %collective-permute-start.4 = (f32[1,256,128]{2,1,0:T(8,128)S(1)}, f32[1,256,128]{2,1,0:T(8,128)S(1)}, u32[]{:S(2)}, u32[]{:S(2)}) collective-permute-start(f32[1,256,128]{2,1,0:T(8,128)S(1)} %bitcast.176), channel_id=1, source_target_pairs={{0,1},{1,2},{2,3},{3,4},{4,5},{5,6},{6,7},{8,9},{9,10},{10,11},{11... | collective-permute-start | bytes 393224 | tf_op jit(solution)/shard_map/ppermute | solution.py:211
  116.0 2.0 %maximum_bitcast_fusion.6 = f32[1,1,3]{2,1,0:T(1,128)S(1)} fusion(f32[1]{0:T(128)} %bitcast.35, f32[1]{0:T(128)} %bitcast.34, f32[1]{0:T(128)} %bitcast.33), kind=kLoop, calls=%fused_computation.1262 | loop fusion | flops 6 | bytes 24 | tf_op jit(solution)/shard_map/reshape.48
  118.8 3.5 %all-to-all-start.4 = ((f32[16,2,16,128]{3,2,1,0:T(8,128)}), f32[16,2,16,128]{3,2,1,0:T(8,128)S(1)}, u32[]{:S(2)}, u32[]{:S(2)}) async-start(f32[16,2,16,128]{3,2,1,0:T(8,128)} %broadcast_in_dim.21), calls=%async_computation.4 | async-start | bytes 524288 | tf_op jit(solution)/shard_map/all_to_all | solution.py:203
  123.1 8.1 %all-to-all-done.4 = f32[16,2,16,128]{3,2,1,0:T(8,128)S(1)} async-done(((f32[16,2,16,128]{3,2,1,0:T(8,128)}), f32[16,2,16,128]{3,2,1,0:T(8,128)S(1)}, u32[]{:S(2)}, u32[]{:S(2)}) %all-to-all-start.4) | async-done | bytes 262176 | tf_op jit(solution)/shard_map/all_to_all | solution.py:203
  131.8 5.3 %all-to-all-start.5 = ((f32[8,1,3]{2,1,0:T(1,128)}), f32[8,1,3]{2,1,0:T(1,128)S(1)}, u32[]{:S(2)}, u32[]{:S(2)}) async-start(f32[8,1,3]{2,1,0:T(1,128)} %broadcast_in_dim.22), calls=%async_computation.5 | async-start | bytes 8192 | tf_op jit(solution)/shard_map/all_to_all | solution.py:207
  137.1 1.9 %collective-permute-start.7 = (f32[1,256,128]{2,1,0:T(8,128)S(1)}, f32[1,256,128]{2,1,0:T(8,128)S(1)}, u32[]{:S(2)}, u32[]{:S(2)}) collective-permute-start(f32[1,256,128]{2,1,0:T(8,128)S(1)} %bitcast.170), channel_id=1, source_target_pairs={{1,0},{2,1},{3,2},{4,3},{5,4},{6,5},{7,6},{9,8},{10,9},{11,10},{12... | collective-permute-start | bytes 393224 | tf_op jit(solution)/shard_map/ppermute | solution.py:212
  139.0 3.6 %collective-permute-start.6 = (f32[1,256,128]{2,1,0:T(8,128)S(1)}, f32[1,256,128]{2,1,0:T(8,128)S(1)}, u32[]{:S(2)}, u32[]{:S(2)}) collective-permute-start(f32[1,256,128]{2,1,0:T(8,128)S(1)} %bitcast.171), channel_id=1, source_target_pairs={{0,1},{1,2},{2,3},{3,4},{4,5},{5,6},{6,7},{8,9},{9,10},{10,11},{11... | collective-permute-start | bytes 393224 | tf_op jit(solution)/shard_map/ppermute | solution.py:211
  154.5 2.0 %pad_maximum_fusion.3 = f32[3]{0:T(128)S(1)} fusion(f32[1]{0:T(128)} %bitcast.44, f32[1]{0:T(128)} %bitcast.43, f32[1]{0:T(128)} %bitcast.42), kind=kLoop, calls=%fused_computation.1263 | loop fusion | flops 6 | bytes 24 | tf_op jit(solution)/shard_map/stack | solution.py:342
  157.1 5.3 %all-to-all-start.6 = ((f32[128,1,3]{2,1,0:T(1,128)}), f32[128,1,3]{2,1,0:T(1,128)S(1)}, u32[]{:S(2)}, u32[]{:S(2)}) async-start(f32[128,1,3]{2,1,0:T(1,128)} %broadcast_in_dim.23), calls=%async_computation.6 | async-start | bytes 131072 | tf_op jit(solution)/shard_map/all_to_all | solution.py:225
  162.6 9.4 %all-to-all-done.6 = f32[128,1,3]{2,1,0:T(1,128)S(1)} async-done(((f32[128,1,3]{2,1,0:T(1,128)}), f32[128,1,3]{2,1,0:T(1,128)S(1)}, u32[]{:S(2)}, u32[]{:S(2)}) %all-to-all-start.6) | async-done | bytes 1568 | tf_op jit(solution)/shard_map/all_to_all | solution.py:225
  (227 shorter events, 49.8 us)
Async XLA Ops:
  13.4 11.2 %all-to-all-start = ((f32[8,3,4,270]{3,2,1,0:T(4,128)}), f32[8,3,4,270]{3,2,1,0:T(4,128)S(1)}, u32[]{:S(2)}, u32[]{:S(2)}) async-start(f32[8,3,4,270]{3,2,1,0:T(4,128)} %copy.49), calls=%async_computation | async-start | bytes 294912 | tf_op jit(solution)/shard_map/all_to_all | solution.py:269
  24.7 4.5 %collective-permute-start = (f32[3,7,270]{2,1,0:T(8,128)S(1)}, f32[3,7,270]{2,1,0:T(8,128)S(1)}, u32[]{:S(2)}, u32[]{:S(2)}) collective-permute-start(f32[3,7,270]{2,1,0:T(8,128)S(1)} %get-tuple-element.51), channel_id=1, source_target_pairs={{0,8},{8,16},{16,24},{24,32},{32,40},{40,48},{48,56},{56,64},{64,7... | collective-permute-start | bytes 68048 | tf_op jit(solution)/shard_map/ppermute | solution.py:272
  27.9 4.7 %collective-permute-start.1 = (f32[3,7,270]{2,1,0:T(8,128)S(1)}, f32[3,7,270]{2,1,0:T(8,128)S(1)}, u32[]{:S(2)}, u32[]{:S(2)}) collective-permute-start(f32[3,7,270]{2,1,0:T(8,128)S(1)} %get-tuple-element.52), channel_id=1, source_target_pairs={{8,0},{16,8},{24,16},{32,24},{40,32},{48,40},{56,48},{64,56},{72,6... | collective-permute-start | bytes 68048 | tf_op jit(solution)/shard_map/ppermute | solution.py:273
  35.2 17.5 %all-to-all-start.1 = ((f32[16,3,16,128]{3,2,1,0:T(8,128)}), f32[16,3,16,128]{3,2,1,0:T(8,128)S(1)}, u32[]{:S(2)}, u32[]{:S(2)}) async-start(f32[16,3,16,128]{3,2,1,0:T(8,128)} %broadcast_in_dim.16), calls=%async_computation.1 | async-start | bytes 786432 | tf_op jit(solution)/shard_map/all_to_all | solution.py:203
  52.8 11.3 %collective-permute-start.3 = (f32[3,256,128]{2,1,0:T(8,128)S(1)}, f32[3,256,128]{2,1,0:T(8,128)S(1)}, u32[]{:S(2)}, u32[]{:S(2)}) collective-permute-start(f32[3,256,128]{2,1,0:T(8,128)S(1)} %bitcast.167), channel_id=1, source_target_pairs={{1,0},{2,1},{3,2},{4,3},{5,4},{6,5},{7,6},{9,8},{10,9},{11,10},{12... | collective-permute-start | bytes 1179656 | tf_op jit(solution)/shard_map/ppermute | solution.py:212
  58.4 6.8 %collective-permute-start.2 = (f32[3,256,128]{2,1,0:T(8,128)S(1)}, f32[3,256,128]{2,1,0:T(8,128)S(1)}, u32[]{:S(2)}, u32[]{:S(2)}) collective-permute-start(f32[3,256,128]{2,1,0:T(8,128)S(1)} %bitcast.168), channel_id=1, source_target_pairs={{0,1},{1,2},{2,3},{3,4},{4,5},{5,6},{6,7},{8,9},{9,10},{10,11},{11... | collective-permute-start | bytes 1179656 | tf_op jit(solution)/shard_map/ppermute | solution.py:211
  82.8 11.0 %all-to-all-start.2 = ((f32[16,2,16,128]{3,2,1,0:T(8,128)}), f32[16,2,16,128]{3,2,1,0:T(8,128)S(1)}, u32[]{:S(2)}, u32[]{:S(2)}) async-start(f32[16,2,16,128]{3,2,1,0:T(8,128)} %broadcast_in_dim.18), calls=%async_computation.2 | async-start | bytes 524288 | tf_op jit(solution)/shard_map/all_to_all | solution.py:203
  94.4 11.7 %all-to-all-start.3 = ((f32[8,1,2]{2,1,0:T(1,128)}), f32[8,1,2]{2,1,0:T(1,128)S(1)}, u32[]{:S(2)}, u32[]{:S(2)}) async-start(f32[8,1,2]{2,1,0:T(1,128)} %broadcast_in_dim.19), calls=%async_computation.3 | async-start | bytes 8192 | tf_op jit(solution)/shard_map/all_to_all | solution.py:207
  100.4 7.8 %collective-permute-start.5 = (f32[1,256,128]{2,1,0:T(8,128)S(1)}, f32[1,256,128]{2,1,0:T(8,128)S(1)}, u32[]{:S(2)}, u32[]{:S(2)}) collective-permute-start(f32[1,256,128]{2,1,0:T(8,128)S(1)} %bitcast.175), channel_id=1, source_target_pairs={{1,0},{2,1},{3,2},{4,3},{5,4},{6,5},{7,6},{9,8},{10,9},{11,10},{12... | collective-permute-start | bytes 393224 | tf_op jit(solution)/shard_map/ppermute | solution.py:212
  102.3 5.9 %collective-permute-start.4 = (f32[1,256,128]{2,1,0:T(8,128)S(1)}, f32[1,256,128]{2,1,0:T(8,128)S(1)}, u32[]{:S(2)}, u32[]{:S(2)}) collective-permute-start(f32[1,256,128]{2,1,0:T(8,128)S(1)} %bitcast.176), channel_id=1, source_target_pairs={{0,1},{1,2},{2,3},{3,4},{4,5},{5,6},{6,7},{8,9},{9,10},{10,11},{11... | collective-permute-start | bytes 393224 | tf_op jit(solution)/shard_map/ppermute | solution.py:211
  118.8 12.4 %all-to-all-start.4 = ((f32[16,2,16,128]{3,2,1,0:T(8,128)}), f32[16,2,16,128]{3,2,1,0:T(8,128)S(1)}, u32[]{:S(2)}, u32[]{:S(2)}) async-start(f32[16,2,16,128]{3,2,1,0:T(8,128)} %broadcast_in_dim.21), calls=%async_computation.4 | async-start | bytes 524288 | tf_op jit(solution)/shard_map/all_to_all | solution.py:203
  131.8 10.8 %all-to-all-start.5 = ((f32[8,1,3]{2,1,0:T(1,128)}), f32[8,1,3]{2,1,0:T(1,128)S(1)}, u32[]{:S(2)}, u32[]{:S(2)}) async-start(f32[8,1,3]{2,1,0:T(1,128)} %broadcast_in_dim.22), calls=%async_computation.5 | async-start | bytes 8192 | tf_op jit(solution)/shard_map/all_to_all | solution.py:207
  137.1 10.2 %collective-permute-start.7 = (f32[1,256,128]{2,1,0:T(8,128)S(1)}, f32[1,256,128]{2,1,0:T(8,128)S(1)}, u32[]{:S(2)}, u32[]{:S(2)}) collective-permute-start(f32[1,256,128]{2,1,0:T(8,128)S(1)} %bitcast.170), channel_id=1, source_target_pairs={{1,0},{2,1},{3,2},{4,3},{5,4},{6,5},{7,6},{9,8},{10,9},{11,10},{12... | collective-permute-start | bytes 393224 | tf_op jit(solution)/shard_map/ppermute | solution.py:212
  139.0 8.3 %collective-permute-start.6 = (f32[1,256,128]{2,1,0:T(8,128)S(1)}, f32[1,256,128]{2,1,0:T(8,128)S(1)}, u32[]{:S(2)}, u32[]{:S(2)}) collective-permute-start(f32[1,256,128]{2,1,0:T(8,128)S(1)} %bitcast.171), channel_id=1, source_target_pairs={{0,1},{1,2},{2,3},{3,4},{4,5},{5,6},{6,7},{8,9},{9,10},{10,11},{11... | collective-permute-start | bytes 393224 | tf_op jit(solution)/shard_map/ppermute | solution.py:211
  157.1 14.9 %all-to-all-start.6 = ((f32[128,1,3]{2,1,0:T(1,128)}), f32[128,1,3]{2,1,0:T(1,128)S(1)}, u32[]{:S(2)}, u32[]{:S(2)}) async-start(f32[128,1,3]{2,1,0:T(1,128)} %broadcast_in_dim.23), calls=%async_computation.6 | async-start | bytes 131072 | tf_op jit(solution)/shard_map/all_to_all | solution.py:225

commit v14 on v13

--- a/solution.py
+++ b/solution.py
@@ -61,12 +61,15 @@
             - south * padded[2:, 1:-1] - north * padded[:-2, 1:-1])
 
 
-def multilook_kernel(bounds_ref, lead_ref, trail_ref, out_ref):
+def multilook_kernel(track_ref, slant_ref, lead_ref, trail_ref, out_ref):
     shape = (lead_ref.shape[0], lead_ref.shape[2])
-    line = lax.broadcasted_iota(jnp.int32, shape, 0)
+    burst = lax.axis_index("az")
+    first_line = lax.axis_index("rg") * shape[0]
+    line = first_line + lax.broadcasted_iota(jnp.int32, shape, 0)
     column = pl.program_id(0) * shape[1] + lax.broadcasted_iota(jnp.int32, shape, 1)
-    mask = ((line >= bounds_ref[0]) & (line < bounds_ref[1]) & (column >= bounds_ref[2])
-            & (column < bounds_ref[3])).astype(jnp.float32)
+    mask = ((line >= track_ref[burst, 0]) & (line < SEGMENT_HEIGHT - track_ref[burst, 1])
+            & (column >= slant_ref[burst, 0])
+            & (column < pl.num_programs(0) * shape[1] - slant_ref[burst, 1])).astype(jnp.float32)
     first_re = lead_ref[:, 0, :].astype(jnp.float32) * mask
     first_im = lead_ref[:, 1, :].astype(jnp.float32) * mask
     second_re = trail_ref[:, 0, :].astype(jnp.float32) * mask
@@ -87,7 +90,7 @@
                 out_ref[part, group, chunk:chunk + 1, :] = acc[:, chunk * span:(chunk + 1) * span]
 
 
-def mean_multilook(leading, trailing, bounds):
+def mean_multilook(leading, trailing, track_trim, slant_trim):
     _, height_rows, width_cols = leading.shape
     block = 5120
     span = LOOK * 128
@@ -96,12 +99,13 @@
         grid=(width_cols // block,),
         in_specs=[
             pl.BlockSpec(memory_space=pltpu.SMEM),
+            pl.BlockSpec(memory_space=pltpu.SMEM),
             pl.BlockSpec((height_rows, 2, block), lambda j: (0, 0, j)),
             pl.BlockSpec((height_rows, 2, block), lambda j: (0, 0, j)),
         ],
         out_specs=pl.BlockSpec((4, height_rows // LOOK, block // span, span), lambda j: (0, 0, j, 0)),
         out_shape=jax.ShapeDtypeStruct((4, height_rows // LOOK, width_cols // span, span), jnp.float32),
-    )(bounds, jnp.transpose(leading, (1, 0, 2)), jnp.transpose(trailing, (1, 0, 2)))
+    )(track_trim, slant_trim, jnp.transpose(leading, (1, 0, 2)), jnp.transpose(trailing, (1, 0, 2)))
     grouped = rows
     cols = jnp.einsum("pikc,cd->pikd", grouped, group_sum(span, LOOK).T, precision=HIGHEST)
     return cols.reshape(4, height_rows // LOOK, width_cols // LOOK)
@@ -239,14 +243,7 @@
     )
     lines_here = master_phasor_raster.shape[1]
     slant_sample_total = master_phasor_raster.shape[2]
-    first_line = range_index * lines_here
-    bounds = jnp.stack([
-        track_trim_width[0] - first_line,
-        SEGMENT_HEIGHT - track_trim_width[1] - first_line,
-        slant_trim_width[0],
-        slant_sample_total - slant_trim_width[1],
-    ]).astype(jnp.int32)
-    pixel_totals = mean_multilook(master_phasor_raster, slave_phasor_raster, bounds)
+    pixel_totals = mean_multilook(master_phasor_raster, slave_phasor_raster, segment_track_trim, segment_slant_trim)
     look_re, look_im, power_one, power_two = (
         pixel_totals[0],
         pixel_totals[1],

time: 178 us -> 175 us (0.983)
  between operations: 11.9 us -> 9.92 us
    unnamed x0 -> x2, local copies, waits for them, and re-layouts: none -> 2.71 us
    another operation x3 -> x2, other arithmetic: 4.73 us -> 3.37 us
where the time goes in v14:
time: 175 us; the launch traced here: 174 us
  starting transfers between devices  62.4 us (36%)
  waiting for transfers between devices  46 us (26%)
  matrix products  26.3 us (15%)
  other arithmetic  13.8 us (8%)
  local copies, waits for them, and re-layouts  10.6 us (6%)
  between operations  9.92 us (6%)
  Pallas kernels  5.15 us (3%)
    all_to_all x3, waiting for transfers between devices, gather_strip(): got = lax.all_to_all(sent, 'az', 0, 0, tiled=True)  23.7 us
    all_to_all x3, starting transfers between devices, gather_strip(): got = lax.all_to_all(sent, 'az', 0, 0, tiled=True)  16.3 us
    dot_general x48, matrix products, sandwich(): inner = jnp.dot(left, vector, precision=HIGHEST)  13.8 us
    all_to_all x2, starting transfers between devices, gather_strip(): lax.all_to_all(jnp.broadcast_to(column_sums[None], (n_rg, sums.shape[0]))...  11.2 us
    dot_general x48, matrix products, sandwich(): return jnp.dot(inner, right, precision=HIGHEST)  11 us
    ppermute x3, starting transfers between devices, gather_strip(): left = lax.ppermute(column, 'rg', [(i, i + 1) for i in range(n_rg - 1)])  9.78 us
    ppermute x3, starting transfers between devices, gather_strip(): right = lax.ppermute(column, 'rg', [(i + 1, i) for i in range(n_rg - 1)])  9.5 us
    all_to_all x1, waiting for transfers between devices, total(): got = lax.all_to_all(sent, ('az', 'rg'), 0, 0, tiled=True)  9.4 us
  transfers between devices with their start and end apart: 15, of which 8 were waited for; matrix products, arithmetic and copies ran while one was open for 2% of the time, Pallas kernels for 0%

profile of v14, /device:TPU:1, one launch (start us, length us, event | category | flops | bytes accessed | tf_op | source)
XLA Modules:
  0.0 174.2 jit_solution(2357052296115477468)
XLA Ops:
  3.4 5.1 %shard_map.59 = f32[4,4,16,640]{3,2,1,0:T(8,128)} custom-call(s32[16,2]{1,0:T(8,128)} %copy.59.track_ref, s32[16,2]{1,0:T(8,128)} %copy.60.slant_ref, bf16[20,2,10240]{2,1,0:T(2,128)(2,1)} %bitcast.174, bf16[20,2,10240]{2,1,0:T(2,128)(2,1)} %bitcast.175), custom_call_target="tpu_custom_call" | custom-call | tf_op jit(solution)/shard_map/pallas_call | solution.py:97
  11.1 5.8 %all-to-all-start = ((f32[8,3,4,270]{3,2,1,0:T(4,128)}), f32[8,3,4,270]{3,2,1,0:T(4,128)S(1)}, u32[]{:S(2)}, u32[]{:S(2)}) async-start(f32[8,3,4,270]{3,2,1,0:T(4,128)} %copy.61), calls=%async_computation | async-start | bytes 294912 | tf_op jit(solution)/shard_map/all_to_all | solution.py:266
  17.3 5.0 %all-to-all-done = f32[8,3,4,270]{3,2,1,0:T(4,128)S(1)} async-done(((f32[8,3,4,270]{3,2,1,0:T(4,128)}), f32[8,3,4,270]{3,2,1,0:T(4,128)S(1)}, u32[]{:S(2)}, u32[]{:S(2)}) %all-to-all-start) | async-done | bytes 103712 | tf_op jit(solution)/shard_map/all_to_all | solution.py:266
  22.4 3.2 %collective-permute-start = (f32[3,7,270]{2,1,0:T(8,128)S(1)}, f32[3,7,270]{2,1,0:T(8,128)S(1)}, u32[]{:S(2)}, u32[]{:S(2)}) collective-permute-start(f32[3,7,270]{2,1,0:T(8,128)S(1)} %get-tuple-element.51), channel_id=1, source_target_pairs={{0,8},{8,16},{16,24},{24,32},{32,40},{40,48},{48,56},{56,64},{64,7... | collective-permute-start | bytes 68048 | tf_op jit(solution)/shard_map/ppermute | solution.py:269
  26.9 3.4 %collective-permute-done.1 = f32[3,7,270]{2,1,0:T(8,128)S(1)} collective-permute-done((f32[3,7,270]{2,1,0:T(8,128)S(1)}, f32[3,7,270]{2,1,0:T(8,128)S(1)}, u32[]{:S(2)}, u32[]{:S(2)}) %collective-permute-start.1) | collective-permute-done | bytes 22712 | tf_op jit(solution)/shard_map/ppermute | solution.py:270
  32.9 9.2 %all-to-all-start.1 = ((f32[16,3,16,128]{3,2,1,0:T(8,128)}), f32[16,3,16,128]{3,2,1,0:T(8,128)S(1)}, u32[]{:S(2)}, u32[]{:S(2)}) async-start(f32[16,3,16,128]{3,2,1,0:T(8,128)} %broadcast_in_dim.16), calls=%async_computation.1 | async-start | bytes 786432 | tf_op jit(solution)/shard_map/all_to_all | solution.py:207
  42.2 8.2 %all-to-all-done.1 = f32[16,3,16,128]{3,2,1,0:T(8,128)S(1)} async-done(((f32[16,3,16,128]{3,2,1,0:T(8,128)}), f32[16,3,16,128]{3,2,1,0:T(8,128)S(1)}, u32[]{:S(2)}, u32[]{:S(2)}) %all-to-all-start.1) | async-done | bytes 393248 | tf_op jit(solution)/shard_map/all_to_all | solution.py:207
  50.4 5.7 %collective-permute-start.3 = (f32[3,256,128]{2,1,0:T(8,128)S(1)}, f32[3,256,128]{2,1,0:T(8,128)S(1)}, u32[]{:S(2)}, u32[]{:S(2)}) collective-permute-start(f32[3,256,128]{2,1,0:T(8,128)S(1)} %bitcast.161), channel_id=1, source_target_pairs={{1,0},{2,1},{3,2},{4,3},{5,4},{6,5},{7,6},{9,8},{10,9},{11,10},{12... | collective-permute-start | bytes 1179656 | tf_op jit(solution)/shard_map/ppermute | solution.py:216
  56.1 2.3 %collective-permute-start.2 = (f32[3,256,128]{2,1,0:T(8,128)S(1)}, f32[3,256,128]{2,1,0:T(8,128)S(1)}, u32[]{:S(2)}, u32[]{:S(2)}) collective-permute-start(f32[3,256,128]{2,1,0:T(8,128)S(1)} %bitcast.162), channel_id=1, source_target_pairs={{0,1},{1,2},{2,3},{3,4},{4,5},{5,6},{6,7},{8,9},{9,10},{10,11},{11... | collective-permute-start | bytes 1179656 | tf_op jit(solution)/shard_map/ppermute | solution.py:215
  58.4 3.3 %collective-permute-done.3 = f32[3,256,128]{2,1,0:T(8,128)S(1)} collective-permute-done((f32[3,256,128]{2,1,0:T(8,128)S(1)}, f32[3,256,128]{2,1,0:T(8,128)S(1)}, u32[]{:S(2)}, u32[]{:S(2)}) %collective-permute-start.3) | collective-permute-done | bytes 393248 | tf_op jit(solution)/shard_map/ppermute | solution.py:216
  80.4 3.5 %all-to-all-start.2 = ((f32[16,2,16,128]{3,2,1,0:T(8,128)}), f32[16,2,16,128]{3,2,1,0:T(8,128)S(1)}, u32[]{:S(2)}, u32[]{:S(2)}) async-start(f32[16,2,16,128]{3,2,1,0:T(8,128)} %broadcast_in_dim.18), calls=%async_computation.2 | async-start | bytes 524288 | tf_op jit(solution)/shard_map/all_to_all | solution.py:207
  84.0 7.5 %all-to-all-done.2 = f32[16,2,16,128]{3,2,1,0:T(8,128)S(1)} async-done(((f32[16,2,16,128]{3,2,1,0:T(8,128)}), f32[16,2,16,128]{3,2,1,0:T(8,128)S(1)}, u32[]{:S(2)}, u32[]{:S(2)}) %all-to-all-start.2) | async-done | bytes 262176 | tf_op jit(solution)/shard_map/all_to_all | solution.py:207
  92.1 5.9 %all-to-all-start.3 = ((f32[8,1,2]{2,1,0:T(1,128)}), f32[8,1,2]{2,1,0:T(1,128)S(1)}, u32[]{:S(2)}, u32[]{:S(2)}) async-start(f32[8,1,2]{2,1,0:T(1,128)} %broadcast_in_dim.19), calls=%async_computation.3 | async-start | bytes 8192 | tf_op jit(solution)/shard_map/all_to_all | solution.py:211
  98.0 1.9 %collective-permute-start.5 = (f32[1,256,128]{2,1,0:T(8,128)S(1)}, f32[1,256,128]{2,1,0:T(8,128)S(1)}, u32[]{:S(2)}, u32[]{:S(2)}) collective-permute-start(f32[1,256,128]{2,1,0:T(8,128)S(1)} %bitcast.169), channel_id=1, source_target_pairs={{1,0},{2,1},{3,2},{4,3},{5,4},{6,5},{7,6},{9,8},{10,9},{11,10},{12... | collective-permute-start | bytes 393224 | tf_op jit(solution)/shard_map/ppermute | solution.py:216
  99.9 3.9 %collective-permute-start.4 = (f32[1,256,128]{2,1,0:T(8,128)S(1)}, f32[1,256,128]{2,1,0:T(8,128)S(1)}, u32[]{:S(2)}, u32[]{:S(2)}) collective-permute-start(f32[1,256,128]{2,1,0:T(8,128)S(1)} %bitcast.170), channel_id=1, source_target_pairs={{0,1},{1,2},{2,3},{3,4},{4,5},{5,6},{6,7},{8,9},{9,10},{10,11},{11... | collective-permute-start | bytes 393224 | tf_op jit(solution)/shard_map/ppermute | solution.py:215
  113.6 1.9 %maximum_bitcast_fusion.6 = f32[1,1,3]{2,1,0:T(1,128)S(1)} fusion(f32[1]{0:T(128)} %bitcast.29, f32[1]{0:T(128)} %bitcast.28, f32[1]{0:T(128)} %bitcast.27), kind=kLoop, calls=%fused_computation.1261 | loop fusion | flops 6 | bytes 24 | tf_op jit(solution)/shard_map/reshape.48
  116.3 3.5 %all-to-all-start.4 = ((f32[16,2,16,128]{3,2,1,0:T(8,128)}), f32[16,2,16,128]{3,2,1,0:T(8,128)S(1)}, u32[]{:S(2)}, u32[]{:S(2)}) async-start(f32[16,2,16,128]{3,2,1,0:T(8,128)} %broadcast_in_dim.21), calls=%async_computation.4 | async-start | bytes 524288 | tf_op jit(solution)/shard_map/all_to_all | solution.py:207
  120.6 8.1 %all-to-all-done.4 = f32[16,2,16,128]{3,2,1,0:T(8,128)S(1)} async-done(((f32[16,2,16,128]{3,2,1,0:T(8,128)}), f32[16,2,16,128]{3,2,1,0:T(8,128)S(1)}, u32[]{:S(2)}, u32[]{:S(2)}) %all-to-all-start.4) | async-done | bytes 262176 | tf_op jit(solution)/shard_map/all_to_all | solution.py:207
  129.3 5.3 %all-to-all-start.5 = ((f32[8,1,3]{2,1,0:T(1,128)}), f32[8,1,3]{2,1,0:T(1,128)S(1)}, u32[]{:S(2)}, u32[]{:S(2)}) async-start(f32[8,1,3]{2,1,0:T(1,128)} %broadcast_in_dim.22), calls=%async_computation.5 | async-start | bytes 8192 | tf_op jit(solution)/shard_map/all_to_all | solution.py:211
  134.7 1.9 %collective-permute-start.7 = (f32[1,256,128]{2,1,0:T(8,128)S(1)}, f32[1,256,128]{2,1,0:T(8,128)S(1)}, u32[]{:S(2)}, u32[]{:S(2)}) collective-permute-start(f32[1,256,128]{2,1,0:T(8,128)S(1)} %bitcast.164), channel_id=1, source_target_pairs={{1,0},{2,1},{3,2},{4,3},{5,4},{6,5},{7,6},{9,8},{10,9},{11,10},{12... | collective-permute-start | bytes 393224 | tf_op jit(solution)/shard_map/ppermute | solution.py:216
  136.6 3.6 %collective-permute-start.6 = (f32[1,256,128]{2,1,0:T(8,128)S(1)}, f32[1,256,128]{2,1,0:T(8,128)S(1)}, u32[]{:S(2)}, u32[]{:S(2)}) collective-permute-start(f32[1,256,128]{2,1,0:T(8,128)S(1)} %bitcast.165), channel_id=1, source_target_pairs={{0,1},{1,2},{2,3},{3,4},{4,5},{5,6},{6,7},{8,9},{9,10},{10,11},{11... | collective-permute-start | bytes 393224 | tf_op jit(solution)/shard_map/ppermute | solution.py:215
  151.9 2.0 %pad_maximum_fusion.3 = f32[3]{0:T(128)S(1)} fusion(f32[1]{0:T(128)} %bitcast.38, f32[1]{0:T(128)} %bitcast.37, f32[1]{0:T(128)} %bitcast.36), kind=kLoop, calls=%fused_computation.1262 | loop fusion | flops 6 | bytes 24 | tf_op jit(solution)/shard_map/stack | solution.py:339
  154.5 5.3 %all-to-all-start.6 = ((f32[128,1,3]{2,1,0:T(1,128)}), f32[128,1,3]{2,1,0:T(1,128)S(1)}, u32[]{:S(2)}, u32[]{:S(2)}) async-start(f32[128,1,3]{2,1,0:T(1,128)} %broadcast_in_dim.23), calls=%async_computation.6 | async-start | bytes 131072 | tf_op jit(solution)/shard_map/all_to_all | solution.py:229
  160.0 9.4 %all-to-all-done.6 = f32[128,1,3]{2,1,0:T(1,128)S(1)} async-done(((f32[128,1,3]{2,1,0:T(1,128)}), f32[128,1,3]{2,1,0:T(1,128)S(1)}, u32[]{:S(2)}, u32[]{:S(2)}) %all-to-all-start.6) | async-done | bytes 1568 | tf_op jit(solution)/shard_map/all_to_all | solution.py:229
  (225 shorter events, 49.3 us)
Async XLA Ops:
  11.1 11.2 %all-to-all-start = ((f32[8,3,4,270]{3,2,1,0:T(4,128)}), f32[8,3,4,270]{3,2,1,0:T(4,128)S(1)}, u32[]{:S(2)}, u32[]{:S(2)}) async-start(f32[8,3,4,270]{3,2,1,0:T(4,128)} %copy.61), calls=%async_computation | async-start | bytes 294912 | tf_op jit(solution)/shard_map/all_to_all | solution.py:266
  22.4 4.5 %collective-permute-start = (f32[3,7,270]{2,1,0:T(8,128)S(1)}, f32[3,7,270]{2,1,0:T(8,128)S(1)}, u32[]{:S(2)}, u32[]{:S(2)}) collective-permute-start(f32[3,7,270]{2,1,0:T(8,128)S(1)} %get-tuple-element.51), channel_id=1, source_target_pairs={{0,8},{8,16},{16,24},{24,32},{32,40},{40,48},{48,56},{56,64},{64,7... | collective-permute-start | bytes 68048 | tf_op jit(solution)/shard_map/ppermute | solution.py:269
  25.6 4.7 %collective-permute-start.1 = (f32[3,7,270]{2,1,0:T(8,128)S(1)}, f32[3,7,270]{2,1,0:T(8,128)S(1)}, u32[]{:S(2)}, u32[]{:S(2)}) collective-permute-start(f32[3,7,270]{2,1,0:T(8,128)S(1)} %get-tuple-element.52), channel_id=1, source_target_pairs={{8,0},{16,8},{24,16},{32,24},{40,32},{48,40},{56,48},{64,56},{72,6... | collective-permute-start | bytes 68048 | tf_op jit(solution)/shard_map/ppermute | solution.py:270
  32.9 17.5 %all-to-all-start.1 = ((f32[16,3,16,128]{3,2,1,0:T(8,128)}), f32[16,3,16,128]{3,2,1,0:T(8,128)S(1)}, u32[]{:S(2)}, u32[]{:S(2)}) async-start(f32[16,3,16,128]{3,2,1,0:T(8,128)} %broadcast_in_dim.16), calls=%async_computation.1 | async-start | bytes 786432 | tf_op jit(solution)/shard_map/all_to_all | solution.py:207
  50.4 11.3 %collective-permute-start.3 = (f32[3,256,128]{2,1,0:T(8,128)S(1)}, f32[3,256,128]{2,1,0:T(8,128)S(1)}, u32[]{:S(2)}, u32[]{:S(2)}) collective-permute-start(f32[3,256,128]{2,1,0:T(8,128)S(1)} %bitcast.161), channel_id=1, source_target_pairs={{1,0},{2,1},{3,2},{4,3},{5,4},{6,5},{7,6},{9,8},{10,9},{11,10},{12... | collective-permute-start | bytes 1179656 | tf_op jit(solution)/shard_map/ppermute | solution.py:216
  56.1 6.8 %collective-permute-start.2 = (f32[3,256,128]{2,1,0:T(8,128)S(1)}, f32[3,256,128]{2,1,0:T(8,128)S(1)}, u32[]{:S(2)}, u32[]{:S(2)}) collective-permute-start(f32[3,256,128]{2,1,0:T(8,128)S(1)} %bitcast.162), channel_id=1, source_target_pairs={{0,1},{1,2},{2,3},{3,4},{4,5},{5,6},{6,7},{8,9},{9,10},{10,11},{11... | collective-permute-start | bytes 1179656 | tf_op jit(solution)/shard_map/ppermute | solution.py:215
  80.4 11.0 %all-to-all-start.2 = ((f32[16,2,16,128]{3,2,1,0:T(8,128)}), f32[16,2,16,128]{3,2,1,0:T(8,128)S(1)}, u32[]{:S(2)}, u32[]{:S(2)}) async-start(f32[16,2,16,128]{3,2,1,0:T(8,128)} %broadcast_in_dim.18), calls=%async_computation.2 | async-start | bytes 524288 | tf_op jit(solution)/shard_map/all_to_all | solution.py:207
  92.1 11.7 %all-to-all-start.3 = ((f32[8,1,2]{2,1,0:T(1,128)}), f32[8,1,2]{2,1,0:T(1,128)S(1)}, u32[]{:S(2)}, u32[]{:S(2)}) async-start(f32[8,1,2]{2,1,0:T(1,128)} %broadcast_in_dim.19), calls=%async_computation.3 | async-start | bytes 8192 | tf_op jit(solution)/shard_map/all_to_all | solution.py:211
  98.0 7.8 %collective-permute-start.5 = (f32[1,256,128]{2,1,0:T(8,128)S(1)}, f32[1,256,128]{2,1,0:T(8,128)S(1)}, u32[]{:S(2)}, u32[]{:S(2)}) collective-permute-start(f32[1,256,128]{2,1,0:T(8,128)S(1)} %bitcast.169), channel_id=1, source_target_pairs={{1,0},{2,1},{3,2},{4,3},{5,4},{6,5},{7,6},{9,8},{10,9},{11,10},{12... | collective-permute-start | bytes 393224 | tf_op jit(solution)/shard_map/ppermute | solution.py:216
  99.9 5.9 %collective-permute-start.4 = (f32[1,256,128]{2,1,0:T(8,128)S(1)}, f32[1,256,128]{2,1,0:T(8,128)S(1)}, u32[]{:S(2)}, u32[]{:S(2)}) collective-permute-start(f32[1,256,128]{2,1,0:T(8,128)S(1)} %bitcast.170), channel_id=1, source_target_pairs={{0,1},{1,2},{2,3},{3,4},{4,5},{5,6},{6,7},{8,9},{9,10},{10,11},{11... | collective-permute-start | bytes 393224 | tf_op jit(solution)/shard_map/ppermute | solution.py:215
  116.3 12.4 %all-to-all-start.4 = ((f32[16,2,16,128]{3,2,1,0:T(8,128)}), f32[16,2,16,128]{3,2,1,0:T(8,128)S(1)}, u32[]{:S(2)}, u32[]{:S(2)}) async-start(f32[16,2,16,128]{3,2,1,0:T(8,128)} %broadcast_in_dim.21), calls=%async_computation.4 | async-start | bytes 524288 | tf_op jit(solution)/shard_map/all_to_all | solution.py:207
  129.3 10.9 %all-to-all-start.5 = ((f32[8,1,3]{2,1,0:T(1,128)}), f32[8,1,3]{2,1,0:T(1,128)S(1)}, u32[]{:S(2)}, u32[]{:S(2)}) async-start(f32[8,1,3]{2,1,0:T(1,128)} %broadcast_in_dim.22), calls=%async_computation.5 | async-start | bytes 8192 | tf_op jit(solution)/shard_map/all_to_all | solution.py:211
  134.7 10.0 %collective-permute-start.7 = (f32[1,256,128]{2,1,0:T(8,128)S(1)}, f32[1,256,128]{2,1,0:T(8,128)S(1)}, u32[]{:S(2)}, u32[]{:S(2)}) collective-permute-start(f32[1,256,128]{2,1,0:T(8,128)S(1)} %bitcast.164), channel_id=1, source_target_pairs={{1,0},{2,1},{3,2},{4,3},{5,4},{6,5},{7,6},{9,8},{10,9},{11,10},{12... | collective-permute-start | bytes 393224 | tf_op jit(solution)/shard_map/ppermute | solution.py:216
  136.6 8.1 %collective-permute-start.6 = (f32[1,256,128]{2,1,0:T(8,128)S(1)}, f32[1,256,128]{2,1,0:T(8,128)S(1)}, u32[]{:S(2)}, u32[]{:S(2)}) collective-permute-start(f32[1,256,128]{2,1,0:T(8,128)S(1)} %bitcast.165), channel_id=1, source_target_pairs={{0,1},{1,2},{2,3},{3,4},{4,5},{5,6},{6,7},{8,9},{9,10},{10,11},{11... | collective-permute-start | bytes 393224 | tf_op jit(solution)/shard_map/ppermute | solution.py:215
  154.5 14.9 %all-to-all-start.6 = ((f32[128,1,3]{2,1,0:T(1,128)}), f32[128,1,3]{2,1,0:T(1,128)S(1)}, u32[]{:S(2)}, u32[]{:S(2)}) async-start(f32[128,1,3]{2,1,0:T(1,128)} %broadcast_in_dim.23), calls=%async_computation.6 | async-start | bytes 131072 | tf_op jit(solution)/shard_map/all_to_all | solution.py:229
